TPU v7x, 32 devices: a whole 2x2x4 slice. The times are simulated.
32 devices in a mesh: chan: 8 (over z, y), tm: 4 (over x, core).
Axes of the slice: x: 2, y: 2, z: 4, core: 2. Of those that a mesh axis runs over, the one named last changes fastest.
Arguments:
- records: float32 [4, 3200, 512], P('tm', 'chan'), may hold values from -6 to 6
- chan_order: int32 [512], replicated, may hold values from 0 to 511, each once
- live_mask: int32 [512], replicated, may hold values 0 or 1
Outputs:
- stacks: float32 [2, 512, 64, 128], P(None, 'chan', 'tm')
Inputs may be any that keep to these rules, and one draw needn't show every extreme that they name: chan_order holds every channel number once.
All inputs are finite; a program needn't handle non-finite values.
Results may differ from a plain program's by a relative error of at most 0.0041.
Values may be sent and summed in bfloat16 or wider, within the bound.
No kernel may reach another device: no remote copies, remote signals or barrier semaphores. Data moves between devices by JAX's collectives and lax.ppermute only.
A program may use at most 64 MiB of HBM per device.

v0:
```python
import math

import jax
import jax.numpy as jnp
from jax import lax
from jax.sharding import PartitionSpec as P

L = 200
FB = 101
NLAG = 128
ROUNDS = 2
WIN_TM = 16


def shifted(block, axis, distance):
    devices = range(lax.axis_size(axis))
    route = [((i - distance) % len(devices), i) for i in devices]
    return lax.ppermute(block, axis, route)


def forward_table():
    sample_index = jnp.arange(L, dtype=jnp.int32)
    freq_index = jnp.arange(FB, dtype=jnp.int32)
    phase_step = jnp.mod(sample_index[:, None] * freq_index[None, :], L)
    phase_angle = phase_step.astype(jnp.float32) * (2.0 * math.pi / L)
    return jnp.concatenate([jnp.cos(phase_angle), -jnp.sin(phase_angle)], axis=1)


def smoothing_table():
    freq_index = jnp.arange(FB, dtype=jnp.int32)
    nearby = (jnp.abs(freq_index[:, None] - freq_index[None, :]) <= 2).astype(jnp.float32)
    return nearby / jnp.sum(nearby, axis=0, keepdims=True)


def inverse_table():
    freq_index = jnp.arange(FB, dtype=jnp.int32)
    lag_index = jnp.arange(NLAG, dtype=jnp.int32) - NLAG // 2
    phase_step = jnp.mod(freq_index[:, None] * lag_index[None, :], L)
    phase_angle = phase_step.astype(jnp.float32) * (2.0 * math.pi / L)
    edge = (freq_index == 0) | (freq_index == L // 2)
    fold_weight = jnp.where(edge, 1.0, 2.0).astype(jnp.float32) / L
    return jnp.stack(
        [fold_weight[:, None] * jnp.cos(phase_angle), -fold_weight[:, None] * jnp.sin(phase_angle)]
    )


def whiten_spectra(windows, live_block, precision=lax.Precision.HIGHEST):
    window_mean = jnp.mean(windows, axis=-2, keepdims=True)
    centred = windows - window_mean
    normed = centred / jnp.sqrt(jnp.mean(centred * centred, axis=-2, keepdims=True) + 1e-05)
    spectrum = jnp.einsum("...lk,lg->...kg", normed, forward_table(), precision=precision)
    real_part = spectrum[..., :FB]
    imag_part = spectrum[..., FB:]
    power = real_part * real_part + imag_part * imag_part
    smoothed = jnp.einsum("...f,fg->...g", power, smoothing_table(), precision=precision)
    mean_power = jnp.mean(power, axis=-1, keepdims=True)
    scale = live_block.astype(jnp.float32)[:, None] / jnp.sqrt(smoothed + 0.1 * mean_power + 1e-05)
    return jnp.concatenate([real_part * scale, imag_part * scale], axis=-1).astype(jnp.bfloat16)


def correlate(partner, own_spec, inverse):
    partner = partner.reshape(partner.shape[0], partner.shape[1], 2, FB)
    own_spec = own_spec.reshape(own_spec.shape[0], own_spec.shape[1], 2, FB)
    rotated = jnp.concatenate([own_spec[:, :, 1:2], -own_spec[:, :, 0:1]], axis=2)
    real_sum = jnp.einsum("wicf,wjcf->fji", partner, own_spec, preferred_element_type=jnp.float32)
    imag_sum = jnp.einsum("wicf,wjcf->fji", partner, rotated, preferred_element_type=jnp.float32)
    return jnp.einsum(
        "cfji,cfl->jil", jnp.stack([real_sum, imag_sum]), inverse, precision=lax.Precision.HIGHEST
    )


def on_device_reduce(records, chan_order, live_mask):
    chan_count = lax.axis_size("chan")
    position = lax.axis_index("chan")
    blocked = jnp.take(records, chan_order, axis=2)
    own_block = lax.all_to_all(blocked, "chan", split_axis=2, concat_axis=1, tiled=True)
    block_width = own_block.shape[2]
    own_windows = own_block.reshape(WIN_TM, L, block_width)
    live_blocks = jnp.take(live_mask, chan_order).reshape(chan_count, block_width)
    own_live = lax.dynamic_index_in_dim(live_blocks, position, 0, keepdims=False)
    own_spectra = whiten_spectra(own_windows, own_live)
    inverse = inverse_table()
    results = []
    for round_index in range(ROUNDS):
        offset = max(1, round_index * chan_count // 4)
        partner_block = shifted(own_windows, "chan", offset)
        source = jnp.mod(position - offset, chan_count)
        partner_live = lax.dynamic_index_in_dim(live_blocks, source, 0, keepdims=False)
        partner = whiten_spectra(partner_block, partner_live)
        lagged = correlate(partner, own_spectra, inverse)
        lagged = lax.psum_scatter(lagged, "tm", scatter_dimension=1, tiled=True)
        results.append(lagged)
    return jnp.stack(results)


def on_device_local(records, chan_order, live_mask):
    chan_count = lax.axis_size("chan")
    tm_count = lax.axis_size("tm")
    tm_position = lax.axis_index("tm")
    samples, channels = records.shape[1], records.shape[2]
    block_width = channels // chan_count
    slice_width = block_width // tm_count
    windows = records.reshape(samples // L, L, channels)
    spectra = whiten_spectra(windows, live_mask, precision=lax.Precision.HIGH)
    spectra = jnp.take(spectra, chan_order, axis=1)
    own = lax.all_to_all(spectra, "chan", split_axis=1, concat_axis=0, tiled=True)
    gathered = lax.all_gather(own, "tm", axis=0, tiled=True)
    windows_all = gathered.shape[0]
    own_spec = gathered.reshape(windows_all, block_width, 2, FB)
    rotated = jnp.concatenate([own_spec[:, :, 1:2], -own_spec[:, :, 0:1]], axis=2)
    both = jnp.concatenate([own_spec, rotated], axis=1)
    my_slice = lax.dynamic_slice_in_dim(gathered, tm_position * slice_width, slice_width, axis=1)
    partners = []
    for round_index in range(ROUNDS):
        offset = max(1, round_index * chan_count // 4)
        partners.append(shifted(my_slice, "chan", offset))
    partner = jnp.concatenate(partners, axis=1).reshape(windows_all, ROUNDS * slice_width, 2, FB)
    sums = jnp.einsum("wicf,wjcf->fji", partner, both, preferred_element_type=jnp.float32)
    sums = sums.reshape(FB, 2, block_width, ROUNDS, slice_width)
    lagged = jnp.einsum(
        "fcjri,cfl->rjil", sums, inverse_table(), precision=lax.Precision.HIGH
    )
    return lagged


def on_device(records, chan_order, live_mask):
    samples = records.shape[1]
    channels = records.shape[2]
    chan_count = lax.axis_size("chan")
    tm_count = lax.axis_size("tm")
    local_ok = (
        samples % L == 0
        and channels % chan_count == 0
        and (channels // chan_count) % tm_count == 0
        and (samples // L) * chan_count == WIN_TM
    )
    if local_ok:
        return on_device_local(records, chan_order, live_mask)
    return on_device_reduce(records, chan_order, live_mask)


def solution(mesh):
    placed = (P("tm", "chan", None), P(), P())
    return jax.shard_map(
        on_device,
        mesh=mesh,
        in_specs=placed,
        out_specs=P(None, "chan", "tm", None),
        check_vma=False,
    )
```

profile of v0, /device:TPU:6, one launch (start us, length us, event | category | flops | bytes accessed | tf_op | source)
XLA Modules:
  0.0 115.8 jit_solution(12994349782055250445)
XLA Ops:
  7.1 0.7 compare_select_fusion
  7.8 0.7 compare_and_fusion
  8.5 1.2 %reduce_sum.36 = f32[2,512]{1,0:T(2,128)S(1)} reduce(f32[2,200,512]{2,1,0:T(8,128)} %bitcast.33, f32[]{:T(128)} %constant.41.clone.1), dimensions={1}, to_apply=%region_0.0 | reduce | flops 203776 | bytes 823300 | tf_op jit(solution)/shard_map/reduce_sum | solution.py:48
  9.7 1.3 %multiply_reduce_fusion = f32[2,512]{1,0:T(2,128)S(1)} fusion(f32[2,200,512]{2,1,0:T(8,128)} %bitcast.34, f32[2,512]{1,0:T(2,128)S(1)} %broadcast_multiply_fusion.1), kind=kLoop, calls=%fused_computation.18 | loop fusion | flops 613376 | bytes 827392 | tf_op jit(solution)/shard_map/reduce_sum | solution.py:50
  11.0 1.8 %fusion.12 = f32[2,512,202]{1,2,0:T(8,128)S(1)} fusion(f32[2,200,512]{2,1,0:T(8,128)} %bitcast.35, f32[2,512]{1,0:T(2,128)S(1)} %add_sqrt_fusion, f32[2,512]{1,0:T(2,128)S(1)} %broadcast_multiply_fusion.1, f32[200,101]{1,0:T(8,128)S(1)} %get-tuple-element.11, f32[200,101]{1,0:T(8,128)S(1)} %get-tuple-element.12), kind=kOutput, calls=%fused_computation.16 | convolution fusion | flops 248667600 | bytes 1816384 | tf_op jit(solution)/shard_map/...lk,lg->...kg/dot_general | solution.py:51
  14.0 2.6 %gather_fusion = bf16[512,2,202]{2,1,0:T(2,128)(2,1)S(1)} fusion(bf16[2,512,202]{2,0,1:T(2,128)(2,1)S(1)} %copy.16, s32[1024]{0:T(1024)S(1)} %pad_clamp_fusion), kind=kCustom, calls=%fused_computation | custom fusion | bytes 829440 | tf_op jit(solution)/shard_map/jit(_take)/gather | solution.py:105
  16.5 1.8 %fusion.15 = bf16[2,512,202]{2,0,1:T(2,128)(2,1)S(1)} fusion(bf16[512,2,202]{2,1,0:T(2,128)(2,1)S(1)} %gather_fusion, pred[512]{0:T(512)(128)(4,1)S(1)} %compare_and_fusion), kind=kLoop, calls=%fused_computation.20 | loop fusion | flops 206848 | bytes 827904 | tf_op jit(solution)/shard_map/jit(_take)/select_n | solution.py:105
  18.4 20.1 %all_to_all.18 = bf16[2,512,202]{2,0,1:T(2,128)(2,1)S(1)} all-to-all(bf16[2,512,202]{2,0,1:T(2,128)(2,1)S(1)} %fusion.15), channel_id=1, replica_groups=mesh['chan'=8,'tm'=4] {'chan'}, dimensions={1} | all-to-all | bytes 827392 | tf_op jit(solution)/shard_map/all_to_all | solution.py:106
  38.5 0.8 copy.18
  39.4 20.8 %all-gather.2.cloned.1.call-done = bf16[64,64,202]{2,1,0:T(8,128)(2,1)} async-done(((bf16[16,64,202]{2,1,0:T(8,128)(2,1)}), bf16[64,64,202]{2,1,0:T(8,128)(2,1)}) %all-gather.2.cloned.1.call-update) | async-done | bytes 1654800 | tf_op jit(solution)/shard_map/all_gather | solution.py:107
  60.2 1.9 %constant_dynamic-slice_fusion = bf16[64,16,202]{2,1,0:T(8,128)(2,1)} fusion(bf16[64,64,202]{2,1,0:T(8,128)(2,1)} %all-gather.2.cloned.1.call-done, s32[]{:T(128)S(6)} %select_n.58), kind=kLoop, calls=%fused_computation.67 | loop fusion | bytes 827396 | tf_op jit(solution)/shard_map/dynamic_slice | solution.py:112
  62.1 1.5 %collective-permute-start = (bf16[64,16,202]{2,1,0:T(8,128)(2,1)}, bf16[64,16,202]{2,1,0:T(8,128)(2,1)}, u32[]{:S(2)}, u32[]{:S(2)}) collective-permute-start(bf16[64,16,202]{2,1,0:T(8,128)(2,1)} %constant_dynamic-slice_fusion), channel_id=1, source_target_pairs={{28,0},{0,4},{4,8},{8,12},{12,16},{16,20},{20,24},{24,28},{29,1},{... | collective-permute-start | bytes 1241096 | tf_op jit(solution)/shard_map/ppermute | solution.py:18
  63.5 1.5 %collective-permute-start.1 = (bf16[64,16,202]{2,1,0:T(8,128)(2,1)}, bf16[64,16,202]{2,1,0:T(8,128)(2,1)}, u32[]{:S(2)}, u32[]{:S(2)}) collective-permute-start(bf16[64,16,202]{2,1,0:T(8,128)(2,1)} %constant_dynamic-slice_fusion), channel_id=1, source_target_pairs={{24,0},{28,4},{0,8},{4,12},{8,16},{12,20},{16,24},{20,28},{25,1},{... | collective-permute-start | bytes 1241096 | tf_op jit(solution)/shard_map/ppermute | solution.py:18
  65.3 4.3 %reshape.185 = bf16[64,64,2,101]{3,2,1,0:T(2,128)(2,1)} reshape(bf16[64,64,202]{2,1,0:T(8,128)(2,1)} %all-gather.2.cloned.1.call-done) | data formatting | bytes 3309568 | tf_op jit(solution)/shard_map/reshape | solution.py:109
  69.6 6.4 %copy.21 = bf16[64,64,2,101]{1,0,2,3:T(8,128)(2,1)S(1)} copy(bf16[64,64,2,101]{3,2,1,0:T(2,128)(2,1)} %reshape.185) | data formatting | bytes 3309568 | tf_op jit(solution)/shard_map/reshape | solution.py:109
  76.0 2.0 %fusion.44 = (bf16[64,64,1,101]{1,0,2,3:T(8,128)(2,1)}, bf16[64,64,1,101]{1,0,2,3:T(8,128)(2,1)}) fusion(bf16[64,64,2,101]{1,0,2,3:T(8,128)(2,1)S(1)} %copy.21), kind=kLoop, calls=%fused_computation.73 | loop fusion | flops 413696 | bytes 3309568 | tf_op jit(solution)/shard_map/slice | solution.py:110
  78.0 11.2 %collective-permute-done.1 = bf16[64,16,202]{2,1,0:T(8,128)(2,1)} collective-permute-done((bf16[64,16,202]{2,1,0:T(8,128)(2,1)}, bf16[64,16,202]{2,1,0:T(8,128)(2,1)}, u32[]{:S(2)}, u32[]{:S(2)}) %collective-permute-start.1) | collective-permute-done | bytes 413728 | tf_op jit(solution)/shard_map/ppermute | solution.py:18
  89.3 2.4 %pad_maximum_fusion = bf16[64,32,202]{2,1,0:T(8,128)(2,1)} fusion(bf16[64,16,202]{2,1,0:T(8,128)(2,1)} %collective-permute-done.1, bf16[64,16,202]{2,1,0:T(8,128)(2,1)} %collective-permute-done), kind=kLoop, calls=%fused_computation.14 | loop fusion | flops 1654784 | bytes 1654784 | tf_op jit(solution)/shard_map/concatenate | solution.py:117
  91.7 2.5 %reshape.186 = bf16[64,32,2,101]{3,2,1,0:T(2,128)(2,1)} reshape(bf16[64,32,202]{2,1,0:T(8,128)(2,1)} %pad_maximum_fusion) | data formatting | bytes 1654784 | tf_op jit(solution)/shard_map/reshape | solution.py:117
  94.2 4.5 %copy.22 = bf16[64,32,2,101]{0,1,2,3:T(8,128)(2,1)} copy(bf16[64,32,2,101]{3,2,1,0:T(2,128)(2,1)} %reshape.186) | data formatting | bytes 1654784 | tf_op jit(solution)/shard_map/reshape | solution.py:117
  98.7 5.8 %fusion.6 = f32[101,128,32]{1,2,0:T(8,128)} fusion(bf16[64,32,2,101]{0,1,2,3:T(8,128)(2,1)} %copy.22, bf16[64,64,1,101]{1,0,2,3:T(8,128)(2,1)} %get-tuple-element.6, bf16[64,64,1,101]{1,0,2,3:T(8,128)(2,1)} %get-tuple-element.5, bf16[64,64,2,101]{1,0,2,3:T(8,128)(2,1)S(1)} %copy.21), kind=kOutput, calls=%fused_computation.8 | convolution fusion | flops 115834880 | bytes 5791744 | tf_op jit(solution)/shard_map/wicf,wjcf->fji/dot_general | solution.py:118
  104.4 1.9 %copy.29 = f32[101,128,32]{0,1,2:T(8,128)S(1)} copy(f32[101,128,32]{1,2,0:T(8,128)} %fusion.6) | data formatting | bytes 3309568 | tf_op jit(solution)/shard_map/reshape | solution.py:119
  106.3 1.0 convolution_bitcast_fusion
  107.4 1.6 %copy.25 = f32[2,64,16,128]{3,2,1,0:T(8,128)} copy(f32[2,64,16,128]{3,1,2,0:T(8,128)S(1)} %convolution_bitcast_fusion) | data formatting | bytes 2097152 | tf_op jit(solution)/shard_map/fcjri,cfl->rjil/transpose | solution.py:120
  (20 shorter events, 2.1 us)
Async XLA Ops:
  6.5 53.6 %all-gather.2.cloned.1.call-start = ((), (), s32[]{:S(2)}) async-start(), calls=%async_computation.1 | async-start | bytes 2621440 | tf_op jit(solution)/shard_map/all_gather | solution.py:107
  11.0 1.9 %copy-start = (s32[512]{0:T(512)S(1)}, s32[512]{0:T(512)}, u32[]{:S(2)}) copy-start(s32[512]{0:T(512)} %param.5) | copy-start | bytes 6148
  62.1 16.0 %collective-permute-start = (bf16[64,16,202]{2,1,0:T(8,128)(2,1)}, bf16[64,16,202]{2,1,0:T(8,128)(2,1)}, u32[]{:S(2)}, u32[]{:S(2)}) collective-permute-start(bf16[64,16,202]{2,1,0:T(8,128)(2,1)} %constant_dynamic-slice_fusion), channel_id=1, source_target_pairs={{28,0},{0,4},{4,8},{8,12},{12,16},{16,20},{20,24},{24,28},{29,1},{... | collective-permute-start | bytes 1241096 | tf_op jit(solution)/shard_map/ppermute | solution.py:18
  63.5 25.7 %collective-permute-start.1 = (bf16[64,16,202]{2,1,0:T(8,128)(2,1)}, bf16[64,16,202]{2,1,0:T(8,128)(2,1)}, u32[]{:S(2)}, u32[]{:S(2)}) collective-permute-start(bf16[64,16,202]{2,1,0:T(8,128)(2,1)} %constant_dynamic-slice_fusion), channel_id=1, source_target_pairs={{24,0},{28,4},{0,8},{4,12},{8,16},{12,20},{16,24},{20,28},{25,1},{... | collective-permute-start | bytes 1241096 | tf_op jit(solution)/shard_map/ppermute | solution.py:18
Sparse Core Ops, SparseCore 0:
  39.5 20.6 all-gather.1
where the time goes:
time: 118 us; the launch traced here: 116 us
  waiting for transfers between devices  32.1 us (27%)
  local copies, waits for them, and re-layouts  27 us (23%)
  blocking collectives  20.1 us (17%)
  between operations  13.5 us (11%)
  other arithmetic  11.1 us (9%)
  matrix products  9.09 us (8%)
  starting transfers between devices  2.96 us (3%)
    all_gather x1, waiting for transfers between devices, on_device_local(): gathered = lax.all_gather(own, 'tm', axis=0, tiled=True)  20.8 us
    all_to_all x1, blocking collectives, on_device_local(): lax.all_to_all(spectra, 'chan', split_axis=1, concat_axis=0, tiled=True)  20.1 us
    ppermute x2, waiting for transfers between devices, shifted(): return lax.ppermute(block, axis, route)  11.2 us
    reshape x2, local copies, waits for them, and re-layouts, on_device_local(): own_spec = gathered.reshape(windows_all, block_width, 2, FB)  10.8 us
    reshape x2, local copies, waits for them, and re-layouts, on_device_local(): jnp.concatenate(partners, axis=1)  6.96 us
    dot_general x1, matrix products, on_device_local(): jnp.einsum('wicf,wjcf->fji', partner, both, preferred_element_type=jnp.fl...  5.77 us
    ppermute x2, starting transfers between devices, shifted(): return lax.ppermute(block, axis, route)  2.96 us
    gather x1, local copies, waits for them, and re-layouts, on_device_local(): spectra = jnp.take(spectra, chan_order, axis=1)  2.57 us
  transfers between devices with their start and end apart: 3, of which 2 were waited for; matrix products, arithmetic and copies ran while one was open for 11% of the time, Pallas kernels for 0%

commit v1 on v0

--- a/solution.py
+++ b/solution.py
@@ -93,32 +93,71 @@
     return jnp.stack(results)
 
 
+def whiten_planes(windows, live, precision):
+    window_mean = jnp.mean(windows, axis=-2, keepdims=True)
+    centred = windows - window_mean
+    normed = centred / jnp.sqrt(jnp.mean(centred * centred, axis=-2, keepdims=True) + 1e-05)
+    table = forward_table()
+    real_part = jnp.einsum("wlk,lg->wkg", normed, table[:, :FB], precision=precision)
+    imag_part = jnp.einsum("wlk,lg->wkg", normed, table[:, FB:], precision=precision)
+    power = real_part * real_part + imag_part * imag_part
+    smoothed = jnp.einsum("wkf,fg->wkg", power, smoothing_table(), precision=precision)
+    mean_power = jnp.mean(power, axis=-1, keepdims=True)
+    scale = live.astype(jnp.float32)[:, None] / jnp.sqrt(smoothed + 0.1 * mean_power + 1e-05)
+    return jnp.stack([real_part * scale, imag_part * scale], axis=1).astype(jnp.bfloat16)
+
+
 def on_device_local(records, chan_order, live_mask):
     chan_count = lax.axis_size("chan")
     tm_count = lax.axis_size("tm")
+    chan_position = lax.axis_index("chan")
     tm_position = lax.axis_index("tm")
     samples, channels = records.shape[1], records.shape[2]
     block_width = channels // chan_count
     slice_width = block_width // tm_count
     windows = records.reshape(samples // L, L, channels)
-    spectra = whiten_spectra(windows, live_mask, precision=lax.Precision.HIGH)
-    spectra = jnp.take(spectra, chan_order, axis=1)
-    own = lax.all_to_all(spectra, "chan", split_axis=1, concat_axis=0, tiled=True)
-    gathered = lax.all_gather(own, "tm", axis=0, tiled=True)
-    windows_all = gathered.shape[0]
-    own_spec = gathered.reshape(windows_all, block_width, 2, FB)
-    rotated = jnp.concatenate([own_spec[:, :, 1:2], -own_spec[:, :, 0:1]], axis=2)
-    both = jnp.concatenate([own_spec, rotated], axis=1)
-    my_slice = lax.dynamic_slice_in_dim(gathered, tm_position * slice_width, slice_width, axis=1)
+    spectra = whiten_planes(windows, live_mask, lax.Precision.HIGH)
+    sorted_spec = jnp.take(spectra, chan_order, axis=2)
+    sorted_spec = sorted_spec.reshape(spectra.shape[0], 2, chan_count, block_width, FB)
+    sorted_spec = jnp.moveaxis(sorted_spec, 2, 0)
+    pieces = []
+    for distance in range(chan_count):
+        target = jnp.mod(chan_position + distance, chan_count)
+        piece = lax.dynamic_index_in_dim(sorted_spec, target, 0, keepdims=False)
+        pieces.append(piece if distance == 0 else shifted(piece, "chan", distance))
+    own = jnp.stack(pieces)
+    grid = [(c, q) for c in range(chan_count) for q in range(tm_count)]
     partners = []
     for round_index in range(ROUNDS):
         offset = max(1, round_index * chan_count // 4)
-        partners.append(shifted(my_slice, "chan", offset))
-    partner = jnp.concatenate(partners, axis=1).reshape(windows_all, ROUNDS * slice_width, 2, FB)
-    sums = jnp.einsum("wicf,wjcf->fji", partner, both, preferred_element_type=jnp.float32)
-    sums = sums.reshape(FB, 2, block_width, ROUNDS, slice_width)
+        per_source = []
+        for tm_shift in range(tm_count):
+            target_tm = jnp.mod(tm_position + tm_shift, tm_count)
+            piece = lax.dynamic_slice_in_dim(own, target_tm * slice_width, slice_width, axis=3)
+            if offset % chan_count == 0 and tm_shift == 0:
+                per_source.append(piece)
+                continue
+            route = [
+                (c * tm_count + q, ((c + offset) % chan_count) * tm_count + (q + tm_shift) % tm_count)
+                for c, q in grid
+            ]
+            per_source.append(lax.ppermute(piece, ("chan", "tm"), route))
+        by_shift = jnp.stack(per_source)
+        by_time = jnp.concatenate([by_shift[::-1], by_shift[::-1]], axis=0)
+        start = jnp.mod(tm_count - 1 - tm_position, tm_count)
+        by_time = lax.dynamic_slice_in_dim(by_time, start, tm_count, axis=0)
+        by_time = jnp.roll(by_time, offset, axis=1)
+        partners.append(by_time)
+    gathered = lax.all_gather(own, "tm", axis=0, tiled=False)
+    windows_all = tm_count * chan_count * spectra.shape[0]
+    own_spec = gathered.reshape(windows_all, 2, block_width, FB)
+    partner = jnp.concatenate(partners, axis=4).reshape(windows_all, 2, ROUNDS * slice_width, FB)
+    rotated = jnp.stack([-partner[:, 1], partner[:, 0]], axis=1)
+    both = jnp.concatenate([partner, rotated], axis=2)
+    sums = jnp.einsum("xcnf,xcjf->fjn", both, own_spec, preferred_element_type=jnp.float32)
+    sums = sums.reshape(FB, block_width, 2, ROUNDS, slice_width)
     lagged = jnp.einsum(
-        "fcjri,cfl->rjil", sums, inverse_table(), precision=lax.Precision.HIGH
+        "fjcri,cfl->rjil", sums, inverse_table(), precision=lax.Precision.HIGH
     )
     return lagged
 

time: 118 us -> 103 us (0.87)
  starting transfers between devices: 2.96 us -> 28.8 us
  blocking collectives: 20.1 us -> 0 us
  waiting for transfers between devices: 32.1 us -> 12.7 us
  matrix products: 9.09 us -> 12.4 us
  other arithmetic: 11.1 us -> 8.65 us
  local copies, waits for them, and re-layouts: 27 us -> 25.3 us
    all_gather x1, waiting for transfers between devices: 20.8 us -> 0.01 us  [on_device_local(): gathered = lax.all_gather(own, 'tm', axis=0, tiled=False)]
    all_to_all x1 -> x0, blocking collectives: 20.1 us -> none  [on_device_local(): lax.all_to_all(spectra, 'chan', split_axis=1, concat_axis=0, tiled=True)]
    ppermute x0 -> x8, starting transfers between devices: none -> 17.3 us  [on_device_local(): per_source.append(lax.ppermute(piece, ('chan', 'tm'), route))]
    reshape x5 -> x1, local copies, waits for them, and re-layouts: 19.6 us -> 7.66 us  [on_device_local(): own_spec = gathered.reshape(windows_all, 2, block_width, FB)]
    ppermute x2 -> x7, starting transfers between devices: 2.96 us -> 11.5 us  [shifted(): return lax.ppermute(block, axis, route)]
    ppermute x0 -> x8, waiting for transfers between devices: none -> 8.18 us  [on_device_local(): per_source.append(lax.ppermute(piece, ('chan', 'tm'), route))]
    concatenate x1, local copies, waits for them, and re-layouts: 0.45 us -> 7.64 us  [on_device_local(): jnp.concatenate(partners, axis=4)]
    ppermute x2 -> x7, waiting for transfers between devices: 11.2 us -> 4.49 us  [shifted(): return lax.ppermute(block, axis, route)]
  transfers between devices with their start and end apart: 3 -> 16, of which waited for: 2 -> 6; matrix products, arithmetic and copies ran while one was open for 11% -> 13% of each run, Pallas kernels for 0% -> 0%
where the time goes in v1:
time: 103 us; the launch traced here: 102 us
  starting transfers between devices  28.8 us (28%)
  local copies, waits for them, and re-layouts  25.3 us (25%)
  between operations  13.8 us (13%)
  waiting for transfers between devices  12.7 us (12%)
  matrix products  12.4 us (12%)
  other arithmetic  8.65 us (8%)
    ppermute x8, starting transfers between devices, on_device_local(): per_source.append(lax.ppermute(piece, ('chan', 'tm'), route))  17.3 us
    ppermute x7, starting transfers between devices, shifted(): return lax.ppermute(block, axis, route)  11.5 us
    ppermute x8, waiting for transfers between devices, on_device_local(): per_source.append(lax.ppermute(piece, ('chan', 'tm'), route))  8.18 us
    reshape x1, local copies, waits for them, and re-layouts, on_device_local(): own_spec = gathered.reshape(windows_all, 2, block_width, FB)  7.66 us
    concatenate x1, local copies, waits for them, and re-layouts, on_device_local(): jnp.concatenate(partners, axis=4)  7.64 us
    dot_general x1, matrix products, on_device_local(): jnp.einsum('xcnf,xcjf->fjn', both, own_spec, preferred_element_type=jnp.f...  7.1 us
    ppermute x7, waiting for transfers between devices, shifted(): return lax.ppermute(block, axis, route)  4.49 us
    dot_general x1, local copies, waits for them, and re-layouts, on_device_local(): jnp.einsum('xcnf,xcjf->fjn', both, own_spec, preferred_element_type=jnp.f...  3.3 us
  transfers between devices with their start and end apart: 16, of which 6 were waited for; matrix products, arithmetic and copies ran while one was open for 13% of the time, Pallas kernels for 0%

profile of v1, /device:TPU:6, one launch (start us, length us, event | category | flops | bytes accessed | tf_op | source)
XLA Modules:
  0.0 101.6 jit_solution(6989024324684574363)
XLA Ops:
  10.6 1.9 %fusion.20 = f32[2,512,101]{1,2,0:T(8,128)S(1)} fusion(f32[2,200,512]{2,1,0:T(8,128)} %bitcast.80, f32[2,512]{1,0:T(2,128)S(1)} %add_sqrt_fusion, f32[2,512]{1,0:T(2,128)S(1)} %broadcast_multiply_fusion.1), kind=kOutput, calls=%fused_computation.33 | convolution fusion | flops 124700200 | bytes 1241088 | tf_op jit(solution)/shard_map/wlk,lg->wkg/dot_general | solution.py:101
  14.4 2.3 %gather_fusion = bf16[512,2,2,101]{3,2,1,0:T(2,128)(2,1)S(1)} fusion(bf16[2,2,512,101]{3,1,2,0:T(2,128)(2,1)S(1)} %copy.28, s32[1024]{0:T(1024)S(1)} %pad_clamp_fusion), kind=kCustom, calls=%fused_computation | custom fusion | bytes 829440 | tf_op jit(solution)/shard_map/jit(_take)/gather | solution.py:120
  17.1 1.6 %collective-permute-start = (bf16[2,2,64,101]{3,2,1,0:T(8,128)(2,1)S(1)}, bf16[2,2,64,101]{3,2,1,0:T(8,128)(2,1)S(1)}, u32[]{:S(2)}, u32[]{:S(2)}) collective-permute-start(bf16[2,2,64,101]{3,2,1,0:T(8,128)(2,1)S(1)} %get-tuple-element.17), channel_id=1, source_target_pairs={{28,0},{0,4},{4,8},{8,12},{12,16},{16,20},{20,24},{24,28},{29,1},{... | collective-permute-start | bytes 155144 | tf_op jit(solution)/shard_map/ppermute | solution.py:18
  18.7 1.6 %collective-permute-start.1 = (bf16[2,2,64,101]{3,2,1,0:T(8,128)(2,1)S(1)}, bf16[2,2,64,101]{3,2,1,0:T(8,128)(2,1)S(1)}, u32[]{:S(2)}, u32[]{:S(2)}) collective-permute-start(bf16[2,2,64,101]{3,2,1,0:T(8,128)(2,1)S(1)} %get-tuple-element.16), channel_id=1, source_target_pairs={{24,0},{28,4},{0,8},{4,12},{8,16},{12,20},{16,24},{20,28},{25,1},{... | collective-permute-start | bytes 155144 | tf_op jit(solution)/shard_map/ppermute | solution.py:18
  20.2 2.5 %collective-permute-start.2 = (bf16[2,2,64,101]{3,2,1,0:T(8,128)(2,1)S(1)}, bf16[2,2,64,101]{3,2,1,0:T(8,128)(2,1)S(1)}, u32[]{:S(2)}, u32[]{:S(2)}) collective-permute-start(bf16[2,2,64,101]{3,2,1,0:T(8,128)(2,1)S(1)} %get-tuple-element.15), channel_id=1, source_target_pairs={{20,0},{24,4},{28,8},{0,12},{4,16},{8,20},{12,24},{16,28},{21,1},{... | collective-permute-start | bytes 155144 | tf_op jit(solution)/shard_map/ppermute | solution.py:18
  23.1 2.2 %collective-permute-start.4 = (bf16[2,2,64,101]{3,2,1,0:T(8,128)(2,1)S(1)}, bf16[2,2,64,101]{3,2,1,0:T(8,128)(2,1)S(1)}, u32[]{:S(2)}, u32[]{:S(2)}) collective-permute-start(bf16[2,2,64,101]{3,2,1,0:T(8,128)(2,1)S(1)} %get-tuple-element.13), channel_id=1, source_target_pairs={{12,0},{16,4},{20,8},{24,12},{28,16},{0,20},{4,24},{8,28},{13,1},{... | collective-permute-start | bytes 155144 | tf_op jit(solution)/shard_map/ppermute | solution.py:18
  25.3 1.9 %collective-permute-start.5 = (bf16[2,2,64,101]{3,2,1,0:T(8,128)(2,1)S(1)}, bf16[2,2,64,101]{3,2,1,0:T(8,128)(2,1)S(1)}, u32[]{:S(2)}, u32[]{:S(2)}) collective-permute-start(bf16[2,2,64,101]{3,2,1,0:T(8,128)(2,1)S(1)} %get-tuple-element.12), channel_id=1, source_target_pairs={{8,0},{12,4},{16,8},{20,12},{24,16},{28,20},{0,24},{4,28},{9,1},{1... | collective-permute-start | bytes 155144 | tf_op jit(solution)/shard_map/ppermute | solution.py:18
  27.2 1.5 %collective-permute-start.6 = (bf16[2,2,64,101]{3,2,1,0:T(8,128)(2,1)S(1)}, bf16[2,2,64,101]{3,2,1,0:T(8,128)(2,1)S(1)}, u32[]{:S(2)}, u32[]{:S(2)}) collective-permute-start(bf16[2,2,64,101]{3,2,1,0:T(8,128)(2,1)S(1)} %get-tuple-element.11), channel_id=1, source_target_pairs={{4,0},{8,4},{12,8},{16,12},{20,16},{24,20},{28,24},{0,28},{5,1},{9... | collective-permute-start | bytes 155144 | tf_op jit(solution)/shard_map/ppermute | solution.py:18
  28.7 1.6 %collective-permute-done.3 = bf16[2,2,64,101]{3,2,1,0:T(8,128)(2,1)S(1)} collective-permute-done((bf16[2,2,64,101]{3,2,1,0:T(8,128)(2,1)S(1)}, bf16[2,2,64,101]{3,2,1,0:T(8,128)(2,1)S(1)}, u32[]{:S(2)}, u32[]{:S(2)}) %collective-permute-start.3) | collective-permute-done | bytes 51744 | tf_op jit(solution)/shard_map/ppermute | solution.py:18
  30.3 1.8 %collective-permute-done.4 = bf16[2,2,64,101]{3,2,1,0:T(8,128)(2,1)S(1)} collective-permute-done((bf16[2,2,64,101]{3,2,1,0:T(8,128)(2,1)S(1)}, bf16[2,2,64,101]{3,2,1,0:T(8,128)(2,1)S(1)}, u32[]{:S(2)}, u32[]{:S(2)}) %collective-permute-start.4) | collective-permute-done | bytes 51744 | tf_op jit(solution)/shard_map/ppermute | solution.py:18
  36.3 1.7 %collective-permute-start.8 = (bf16[8,2,2,16,101]{4,3,2,1,0:T(8,128)(2,1)S(1)}, bf16[8,2,2,16,101]{4,3,2,1,0:T(8,128)(2,1)S(1)}, u32[]{:S(2)}, u32[]{:S(2)}) collective-permute-start(bf16[8,2,2,16,101]{4,3,2,1,0:T(8,128)(2,1)S(1)} %get-tuple-element.10), channel_id=1, source_target_pairs={{0,5},{1,6},{2,7},{3,4},{4,9},{5,10},{6,11},{7,8},{8,13},{9,14},{1... | collective-permute-start | bytes 310280 | tf_op jit(solution)/shard_map/ppermute | solution.py:144
  38.8 3.5 %collective-permute-start.10 = (bf16[8,2,2,16,101]{4,3,2,1,0:T(8,128)(2,1)S(1)}, bf16[8,2,2,16,101]{4,3,2,1,0:T(8,128)(2,1)S(1)}, u32[]{:S(2)}, u32[]{:S(2)}) collective-permute-start(bf16[8,2,2,16,101]{4,3,2,1,0:T(8,128)(2,1)S(1)} %get-tuple-element.8), channel_id=1, source_target_pairs={{0,7},{1,4},{2,5},{3,6},{4,11},{5,8},{6,9},{7,10},{8,15},{9,12},{1... | collective-permute-start | bytes 310280 | tf_op jit(solution)/shard_map/ppermute | solution.py:144
  42.7 5.9 %collective-permute-start.13 = (bf16[8,2,2,16,101]{4,3,2,1,0:T(8,128)(2,1)S(1)}, bf16[8,2,2,16,101]{4,3,2,1,0:T(8,128)(2,1)S(1)}, u32[]{:S(2)}, u32[]{:S(2)}) collective-permute-start(bf16[8,2,2,16,101]{4,3,2,1,0:T(8,128)(2,1)S(1)} %get-tuple-element.9), channel_id=1, source_target_pairs={{0,10},{1,11},{2,8},{3,9},{4,14},{5,15},{6,12},{7,13},{8,18},{9,19... | collective-permute-start | bytes 310280 | tf_op jit(solution)/shard_map/ppermute | solution.py:144
  48.7 4.1 %collective-permute-start.14 = (bf16[8,2,2,16,101]{4,3,2,1,0:T(8,128)(2,1)S(1)}, bf16[8,2,2,16,101]{4,3,2,1,0:T(8,128)(2,1)S(1)}, u32[]{:S(2)}, u32[]{:S(2)}) collective-permute-start(bf16[8,2,2,16,101]{4,3,2,1,0:T(8,128)(2,1)S(1)} %get-tuple-element.8), channel_id=1, source_target_pairs={{0,11},{1,8},{2,9},{3,10},{4,15},{5,12},{6,13},{7,14},{8,19},{9,16... | collective-permute-start | bytes 310280 | tf_op jit(solution)/shard_map/ppermute | solution.py:144
  53.0 3.1 %collective-permute-done.12 = bf16[8,2,2,16,101]{4,3,2,1,0:T(8,128)(2,1)S(1)} collective-permute-done((bf16[8,2,2,16,101]{4,3,2,1,0:T(8,128)(2,1)S(1)}, bf16[8,2,2,16,101]{4,3,2,1,0:T(8,128)(2,1)S(1)}, u32[]{:S(2)}, u32[]{:S(2)}) %collective-permute-start.12) | collective-permute-done | bytes 103456 | tf_op jit(solution)/shard_map/ppermute | solution.py:144
  56.1 2.4 %collective-permute-done.13 = bf16[8,2,2,16,101]{4,3,2,1,0:T(8,128)(2,1)S(1)} collective-permute-done((bf16[8,2,2,16,101]{4,3,2,1,0:T(8,128)(2,1)S(1)}, bf16[8,2,2,16,101]{4,3,2,1,0:T(8,128)(2,1)S(1)}, u32[]{:S(2)}, u32[]{:S(2)}) %collective-permute-start.13) | collective-permute-done | bytes 103456 | tf_op jit(solution)/shard_map/ppermute | solution.py:144
  58.6 2.6 %collective-permute-done.14 = bf16[8,2,2,16,101]{4,3,2,1,0:T(8,128)(2,1)S(1)} collective-permute-done((bf16[8,2,2,16,101]{4,3,2,1,0:T(8,128)(2,1)S(1)}, bf16[8,2,2,16,101]{4,3,2,1,0:T(8,128)(2,1)S(1)}, u32[]{:S(2)}, u32[]{:S(2)}) %collective-permute-start.14) | collective-permute-done | bytes 103456 | tf_op jit(solution)/shard_map/ppermute | solution.py:144
  63.3 7.6 %copy.30 = bf16[4,8,2,2,32,101]{4,2,1,0,3,5:T(2,128)(2,1)S(1)} copy(bf16[4,8,2,2,32,101]{5,4,3,2,1,0:T(8,128)(2,1)} %maximum_maximum_fusion) | data formatting | bytes 1654784 | tf_op jit(solution)/shard_map/concatenate | solution.py:154
  71.0 2.1 %slice_negate_fusion = (bf16[64,1,32,101]{2,0,1,3:T(8,128)(2,1)}, bf16[64,1,32,101]{2,0,1,3:T(8,128)(2,1)}) fusion(bf16[64,2,32,101]{2,0,1,3:T(8,128)(2,1)S(1)} %bitcast.75), kind=kLoop, calls=%fused_computation.10 | loop fusion | flops 206848 | bytes 1654784 | tf_op jit(solution)/shard_map/neg | solution.py:155
  73.0 7.7 %copy.31 = bf16[64,2,64,101]{0,2,1,3:T(8,128)(2,1)} copy(bf16[64,2,64,101]{3,2,1,0:T(8,128)(2,1)} %bitcast.84) | data formatting | bytes 3309568 | tf_op jit(solution)/shard_map/reshape | solution.py:153
  80.7 7.1 %fusion.8 = f32[101,64,64]{2,1,0:T(8,128)} fusion(bf16[64,2,64,101]{0,2,1,3:T(8,128)(2,1)} %copy.31, bf16[64,1,32,101]{2,0,1,3:T(8,128)(2,1)} %get-tuple-element.6, bf16[64,1,32,101]{2,0,1,3:T(8,128)(2,1)} %get-tuple-element.5, bf16[64,2,32,101]{2,0,1,3:T(8,128)(2,1)S(1)} %bitcast.76), kind=kOutput, calls=%fused_computation.9 | convolution fusion | flops 110870528 | bytes 4964352 | tf_op jit(solution)/shard_map/xcnf,xcjf->fjn/dot_general | solution.py:157
  87.8 3.3 %copy.32 = f32[101,64,64]{0,2,1:T(8,128)S(1)} copy(f32[101,64,64]{2,1,0:T(8,128)} %fusion.8) | data formatting | bytes 3309568 | tf_op jit(solution)/shard_map/xcnf,xcjf->fjn/dot_general | solution.py:157
  91.1 2.1 %fusion.11 = f32[2,64,16,128]{3,1,2,0:T(8,128)S(1)} fusion(f32[101,64,2,2,16]{0,4,3,2,1:T(8,128)S(1)} %bitcast.77, f32[1,101,128]{2,1,0:T(8,128)S(1)} %get-tuple-element.21, f32[1,101,128]{2,1,0:T(8,128)S(1)} %get-tuple-element.20), kind=kOutput, calls=%fused_computation.11 | convolution fusion | flops 317744384 | bytes 2806784 | tf_op jit(solution)/shard_map/fjcri,cfl->rjil/dot_general | solution.py:159
  93.2 1.6 %copy.34 = f32[2,64,16,128]{3,2,1,0:T(8,128)} copy(f32[2,64,16,128]{3,1,2,0:T(8,128)S(1)} %fusion.11) | data formatting | bytes 2097152 | tf_op jit(solution)/shard_map/fjcri,cfl->rjil/transpose | solution.py:159
  (64 shorter events, 14.2 us)
Async XLA Ops:
  6.5 66.5 %all-gather.3.cloned.1.call-start = ((), (), s32[]{:S(2)}) async-start(), calls=%async_computation | async-start | bytes 2621440 | tf_op jit(solution)/shard_map/all_gather | solution.py:151
  9.2 3.3 %copy-start = (f32[1,400,512]{2,1,0:T(8,128)S(1)}, f32[1,400,512]{2,1,0:T(8,128)}, u32[]{:S(2)}) copy-start(f32[1,400,512]{2,1,0:T(8,128)} %param.3) | copy-start | bytes 2457604
  12.6 0.9 copy-start.2
  17.1 8.2 %collective-permute-start = (bf16[2,2,64,101]{3,2,1,0:T(8,128)(2,1)S(1)}, bf16[2,2,64,101]{3,2,1,0:T(8,128)(2,1)S(1)}, u32[]{:S(2)}, u32[]{:S(2)}) collective-permute-start(bf16[2,2,64,101]{3,2,1,0:T(8,128)(2,1)S(1)} %get-tuple-element.17), channel_id=1, source_target_pairs={{28,0},{0,4},{4,8},{8,12},{12,16},{16,20},{20,24},{24,28},{29,1},{... | collective-permute-start | bytes 155144 | tf_op jit(solution)/shard_map/ppermute | solution.py:18
  18.7 8.5 %collective-permute-start.1 = (bf16[2,2,64,101]{3,2,1,0:T(8,128)(2,1)S(1)}, bf16[2,2,64,101]{3,2,1,0:T(8,128)(2,1)S(1)}, u32[]{:S(2)}, u32[]{:S(2)}) collective-permute-start(bf16[2,2,64,101]{3,2,1,0:T(8,128)(2,1)S(1)} %get-tuple-element.16), channel_id=1, source_target_pairs={{24,0},{28,4},{0,8},{4,12},{8,16},{12,20},{16,24},{20,28},{25,1},{... | collective-permute-start | bytes 155144 | tf_op jit(solution)/shard_map/ppermute | solution.py:18
  20.2 8.4 %collective-permute-start.2 = (bf16[2,2,64,101]{3,2,1,0:T(8,128)(2,1)S(1)}, bf16[2,2,64,101]{3,2,1,0:T(8,128)(2,1)S(1)}, u32[]{:S(2)}, u32[]{:S(2)}) collective-permute-start(bf16[2,2,64,101]{3,2,1,0:T(8,128)(2,1)S(1)} %get-tuple-element.15), channel_id=1, source_target_pairs={{20,0},{24,4},{28,8},{0,12},{4,16},{8,20},{12,24},{16,28},{21,1},{... | collective-permute-start | bytes 155144 | tf_op jit(solution)/shard_map/ppermute | solution.py:18
  22.8 7.6 %collective-permute-start.3 = (bf16[2,2,64,101]{3,2,1,0:T(8,128)(2,1)S(1)}, bf16[2,2,64,101]{3,2,1,0:T(8,128)(2,1)S(1)}, u32[]{:S(2)}, u32[]{:S(2)}) collective-permute-start(bf16[2,2,64,101]{3,2,1,0:T(8,128)(2,1)S(1)} %get-tuple-element.14), channel_id=1, source_target_pairs={{16,0},{20,4},{24,8},{28,12},{0,16},{4,20},{8,24},{12,28},{17,1},{... | collective-permute-start | bytes 155144 | tf_op jit(solution)/shard_map/ppermute | solution.py:18
  23.1 9.0 %collective-permute-start.4 = (bf16[2,2,64,101]{3,2,1,0:T(8,128)(2,1)S(1)}, bf16[2,2,64,101]{3,2,1,0:T(8,128)(2,1)S(1)}, u32[]{:S(2)}, u32[]{:S(2)}) collective-permute-start(bf16[2,2,64,101]{3,2,1,0:T(8,128)(2,1)S(1)} %get-tuple-element.13), channel_id=1, source_target_pairs={{12,0},{16,4},{20,8},{24,12},{28,16},{0,20},{4,24},{8,28},{13,1},{... | collective-permute-start | bytes 155144 | tf_op jit(solution)/shard_map/ppermute | solution.py:18
  25.3 6.8 %collective-permute-start.5 = (bf16[2,2,64,101]{3,2,1,0:T(8,128)(2,1)S(1)}, bf16[2,2,64,101]{3,2,1,0:T(8,128)(2,1)S(1)}, u32[]{:S(2)}, u32[]{:S(2)}) collective-permute-start(bf16[2,2,64,101]{3,2,1,0:T(8,128)(2,1)S(1)} %get-tuple-element.12), channel_id=1, source_target_pairs={{8,0},{12,4},{16,8},{20,12},{24,16},{28,20},{0,24},{4,28},{9,1},{1... | collective-permute-start | bytes 155144 | tf_op jit(solution)/shard_map/ppermute | solution.py:18
  27.2 6.0 %collective-permute-start.6 = (bf16[2,2,64,101]{3,2,1,0:T(8,128)(2,1)S(1)}, bf16[2,2,64,101]{3,2,1,0:T(8,128)(2,1)S(1)}, u32[]{:S(2)}, u32[]{:S(2)}) collective-permute-start(bf16[2,2,64,101]{3,2,1,0:T(8,128)(2,1)S(1)} %get-tuple-element.11), channel_id=1, source_target_pairs={{4,0},{8,4},{12,8},{16,12},{20,16},{24,20},{28,24},{0,28},{5,1},{9... | collective-permute-start | bytes 155144 | tf_op jit(solution)/shard_map/ppermute | solution.py:18
  33.2 0.8 copy-start.1
  35.3 7.4 %collective-permute-start.7 = (bf16[8,2,2,16,101]{4,3,2,1,0:T(8,128)(2,1)S(1)}, bf16[8,2,2,16,101]{4,3,2,1,0:T(8,128)(2,1)S(1)}, u32[]{:S(2)}, u32[]{:S(2)}) collective-permute-start(bf16[8,2,2,16,101]{4,3,2,1,0:T(8,128)(2,1)S(1)} %get-tuple-element.7), channel_id=1, source_target_pairs={{0,4},{1,5},{2,6},{3,7},{4,8},{5,9},{6,10},{7,11},{8,12},{9,13},{1... | collective-permute-start | bytes 310280 | tf_op jit(solution)/shard_map/ppermute | solution.py:144
  36.3 6.5 %collective-permute-start.8 = (bf16[8,2,2,16,101]{4,3,2,1,0:T(8,128)(2,1)S(1)}, bf16[8,2,2,16,101]{4,3,2,1,0:T(8,128)(2,1)S(1)}, u32[]{:S(2)}, u32[]{:S(2)}) collective-permute-start(bf16[8,2,2,16,101]{4,3,2,1,0:T(8,128)(2,1)S(1)} %get-tuple-element.10), channel_id=1, source_target_pairs={{0,5},{1,6},{2,7},{3,4},{4,9},{5,10},{6,11},{7,8},{8,13},{9,14},{1... | collective-permute-start | bytes 310280 | tf_op jit(solution)/shard_map/ppermute | solution.py:144
  37.9 10.8 %collective-permute-start.9 = (bf16[8,2,2,16,101]{4,3,2,1,0:T(8,128)(2,1)S(1)}, bf16[8,2,2,16,101]{4,3,2,1,0:T(8,128)(2,1)S(1)}, u32[]{:S(2)}, u32[]{:S(2)}) collective-permute-start(bf16[8,2,2,16,101]{4,3,2,1,0:T(8,128)(2,1)S(1)} %get-tuple-element.9), channel_id=1, source_target_pairs={{0,6},{1,7},{2,4},{3,5},{4,10},{5,11},{6,8},{7,9},{8,14},{9,15},{1... | collective-permute-start | bytes 310280 | tf_op jit(solution)/shard_map/ppermute | solution.py:144
  38.8 14.1 %collective-permute-start.10 = (bf16[8,2,2,16,101]{4,3,2,1,0:T(8,128)(2,1)S(1)}, bf16[8,2,2,16,101]{4,3,2,1,0:T(8,128)(2,1)S(1)}, u32[]{:S(2)}, u32[]{:S(2)}) collective-permute-start(bf16[8,2,2,16,101]{4,3,2,1,0:T(8,128)(2,1)S(1)} %get-tuple-element.8), channel_id=1, source_target_pairs={{0,7},{1,4},{2,5},{3,6},{4,11},{5,8},{6,9},{7,10},{8,15},{9,12},{1... | collective-permute-start | bytes 310280 | tf_op jit(solution)/shard_map/ppermute | solution.py:144
  42.5 10.5 %collective-permute-start.11 = (bf16[8,2,2,16,101]{4,3,2,1,0:T(8,128)(2,1)S(1)}, bf16[8,2,2,16,101]{4,3,2,1,0:T(8,128)(2,1)S(1)}, u32[]{:S(2)}, u32[]{:S(2)}) collective-permute-start(bf16[8,2,2,16,101]{4,3,2,1,0:T(8,128)(2,1)S(1)} %get-tuple-element.7), channel_id=1, source_target_pairs={{0,8},{1,9},{2,10},{3,11},{4,12},{5,13},{6,14},{7,15},{8,16},{9,17... | collective-permute-start | bytes 310280 | tf_op jit(solution)/shard_map/ppermute | solution.py:144
  42.7 13.4 %collective-permute-start.12 = (bf16[8,2,2,16,101]{4,3,2,1,0:T(8,128)(2,1)S(1)}, bf16[8,2,2,16,101]{4,3,2,1,0:T(8,128)(2,1)S(1)}, u32[]{:S(2)}, u32[]{:S(2)}) collective-permute-start(bf16[8,2,2,16,101]{4,3,2,1,0:T(8,128)(2,1)S(1)} %get-tuple-element.10), channel_id=1, source_target_pairs={{0,9},{1,10},{2,11},{3,8},{4,13},{5,14},{6,15},{7,12},{8,17},{9,18... | collective-permute-start | bytes 310280 | tf_op jit(solution)/shard_map/ppermute | solution.py:144
  42.7 15.8 %collective-permute-start.13 = (bf16[8,2,2,16,101]{4,3,2,1,0:T(8,128)(2,1)S(1)}, bf16[8,2,2,16,101]{4,3,2,1,0:T(8,128)(2,1)S(1)}, u32[]{:S(2)}, u32[]{:S(2)}) collective-permute-start(bf16[8,2,2,16,101]{4,3,2,1,0:T(8,128)(2,1)S(1)} %get-tuple-element.9), channel_id=1, source_target_pairs={{0,10},{1,11},{2,8},{3,9},{4,14},{5,15},{6,12},{7,13},{8,18},{9,19... | collective-permute-start | bytes 310280 | tf_op jit(solution)/shard_map/ppermute | solution.py:144
  48.7 12.5 %collective-permute-start.14 = (bf16[8,2,2,16,101]{4,3,2,1,0:T(8,128)(2,1)S(1)}, bf16[8,2,2,16,101]{4,3,2,1,0:T(8,128)(2,1)S(1)}, u32[]{:S(2)}, u32[]{:S(2)}) collective-permute-start(bf16[8,2,2,16,101]{4,3,2,1,0:T(8,128)(2,1)S(1)} %get-tuple-element.8), channel_id=1, source_target_pairs={{0,11},{1,8},{2,9},{3,10},{4,15},{5,12},{6,13},{7,14},{8,19},{9,16... | collective-permute-start | bytes 310280 | tf_op jit(solution)/shard_map/ppermute | solution.py:144
Sparse Core Ops, SparseCore 0:
  34.2 32.5 all-gather.2

commit v2 on v1

--- a/solution.py
+++ b/solution.py
@@ -148,16 +148,20 @@
         by_time = lax.dynamic_slice_in_dim(by_time, start, tm_count, axis=0)
         by_time = jnp.roll(by_time, offset, axis=1)
         partners.append(by_time)
-    gathered = lax.all_gather(own, "tm", axis=0, tiled=False)
-    windows_all = tm_count * chan_count * spectra.shape[0]
-    own_spec = gathered.reshape(windows_all, 2, block_width, FB)
-    partner = jnp.concatenate(partners, axis=4).reshape(windows_all, 2, ROUNDS * slice_width, FB)
-    rotated = jnp.stack([-partner[:, 1], partner[:, 0]], axis=1)
-    both = jnp.concatenate([partner, rotated], axis=2)
-    sums = jnp.einsum("xcnf,xcjf->fjn", both, own_spec, preferred_element_type=jnp.float32)
-    sums = sums.reshape(FB, block_width, 2, ROUNDS, slice_width)
+    windows_here = chan_count * spectra.shape[0]
+    own_t = jnp.transpose(own, (4, 2, 0, 1, 3)).reshape(FB, 2, windows_here, block_width)
+    gathered = lax.all_gather(own_t, "tm", axis=2, tiled=False)
+    contraction = 2 * tm_count * windows_here
+    own_spec = gathered.reshape(FB, contraction, block_width)
+    partner = jnp.concatenate(partners, axis=4)
+    rotated = jnp.stack([-partner[:, :, :, 1], partner[:, :, :, 0]], axis=3)
+    both = jnp.stack([partner, rotated])
+    both = jnp.transpose(both, (6, 0, 5, 4, 1, 2, 3))
+    both = both.reshape(FB, 2 * ROUNDS * slice_width, contraction)
+    sums = jnp.einsum("fnk,fkj->fnj", both, own_spec, preferred_element_type=jnp.float32)
+    sums = sums.reshape(FB, 2, ROUNDS, slice_width, block_width)
     lagged = jnp.einsum(
-        "fjcri,cfl->rjil", sums, inverse_table(), precision=lax.Precision.HIGH
+        "fcrij,cfl->rjil", sums, inverse_table(), precision=lax.Precision.HIGH
     )
     return lagged
 

time: 103 us -> 84.8 us (0.82)
  local copies, waits for them, and re-layouts: 25.3 us -> 13.5 us
  matrix products: 12.4 us -> 8.27 us
  other arithmetic: 8.65 us -> 6.63 us
    concatenate x1 -> x0, local copies, waits for them, and re-layouts: 7.64 us -> none  [on_device_local(): jnp.concatenate(partners, axis=4)]
    dot_general x2, matrix products: 9.18 us -> 5.03 us  [the longest x1 4.04 us: on_device_local(): jnp.einsum('fcrij,cfl->rjil', sums, inverse_table(), precision=lax.Precis...]
    dot_general x1 -> x0, local copies, waits for them, and re-layouts: 3.3 us -> none  [on_device_local(): jnp.einsum('xcnf,xcjf->fjn', both, own_spec, preferred_element_type=jnp.f...]
    neg x1, other arithmetic: 2.06 us -> 0.1 us  [on_device_local(): rotated = jnp.stack([-partner[:, :, :, 1], partner[:, :, :, 0]], axis=3)]
    transpose x1 -> x3, local copies, waits for them, and re-layouts: 1.58 us -> 3.09 us  [the longest x1 1.58 us: on_device_local(): jnp.einsum('fcrij,cfl->rjil', sums, inverse_table(), precision=lax.Precis...]
    concatenate x1 -> x0, other arithmetic: 1.28 us -> none  [on_device_local(): jnp.concatenate(partners, axis=4)]
    dynamic_slice x1, local copies, waits for them, and re-layouts: 1.16 us -> 0.08 us  [on_device_local(): lax.dynamic_slice_in_dim(own, target_tm * slice_width, slice_width, axis=3)]
    reshape x1 -> x2, local copies, waits for them, and re-layouts: 7.66 us -> 7.14 us  [the longest x1 3.91 us: on_device_local(): own_spec = gathered.reshape(FB, contraction, block_width)]
  transfers between devices with their start and end apart: 16 -> 16, of which waited for: 6 -> 6; matrix products, arithmetic and copies ran while one was open for 13% -> 8% of each run, Pallas kernels for 0% -> 0%
where the time goes in v2:
time: 84.8 us; the launch traced here: 83.7 us
  starting transfers between devices  28.8 us (34%)
  between operations  13.8 us (16%)
  local copies, waits for them, and re-layouts  13.5 us (16%)
  waiting for transfers between devices  12.7 us (15%)
  matrix products  8.27 us (10%)
  other arithmetic  6.63 us (8%)
    ppermute x8, starting transfers between devices, on_device_local(): per_source.append(lax.ppermute(piece, ('chan', 'tm'), route))  17.3 us
    ppermute x7, starting transfers between devices, shifted(): return lax.ppermute(block, axis, route)  11.5 us
    ppermute x8, waiting for transfers between devices, on_device_local(): per_source.append(lax.ppermute(piece, ('chan', 'tm'), route))  8.18 us
    ppermute x7, waiting for transfers between devices, shifted(): return lax.ppermute(block, axis, route)  4.49 us
    dot_general x1, matrix products, on_device_local(): jnp.einsum('fcrij,cfl->rjil', sums, inverse_table(), precision=lax.Precis...  4.04 us
    reshape x1, local copies, waits for them, and re-layouts, on_device_local(): own_spec = gathered.reshape(FB, contraction, block_width)  3.91 us
    reshape x1, local copies, waits for them, and re-layouts, on_device_local(): both = both.reshape(FB, 2 * ROUNDS * slice_width, contraction)  3.23 us
    gather x2, local copies, waits for them, and re-layouts, on_device_local(): sorted_spec = jnp.take(spectra, chan_order, axis=2)  2.36 us
  transfers between devices with their start and end apart: 16, of which 6 were waited for; matrix products, arithmetic and copies ran while one was open for 8% of the time, Pallas kernels for 0%

profile of v2, /device:TPU:6, one launch (start us, length us, event | category | flops | bytes accessed | tf_op | source)
XLA Modules:
  0.0 83.7 jit_solution(9974662559899389448)
XLA Ops:
  8.0 1.2 %reduce_sum.36 = f32[2,512]{1,0:T(2,128)S(1)} reduce(f32[2,200,512]{2,1,0:T(8,128)} %bitcast.84, f32[]{:T(128)} %constant.164.clone.1), dimensions={1}, to_apply=%region_0.0 | reduce | flops 203776 | bytes 823300 | tf_op jit(solution)/shard_map/reduce_sum | solution.py:97
  9.3 1.3 %multiply_reduce_fusion = f32[2,512]{1,0:T(2,128)S(1)} fusion(f32[2,200,512]{2,1,0:T(8,128)} %bitcast.85, f32[2,512]{1,0:T(2,128)S(1)} %broadcast_multiply_fusion.1), kind=kLoop, calls=%fused_computation.15 | loop fusion | flops 613376 | bytes 827392 | tf_op jit(solution)/shard_map/reduce_sum | solution.py:99
  10.6 1.9 %fusion.11 = f32[2,512,101]{1,2,0:T(8,128)S(1)} fusion(f32[2,200,512]{2,1,0:T(8,128)} %bitcast.86, f32[2,512]{1,0:T(2,128)S(1)} %add_sqrt_fusion, f32[2,512]{1,0:T(2,128)S(1)} %broadcast_multiply_fusion.1), kind=kOutput, calls=%fused_computation.28 | convolution fusion | flops 124700200 | bytes 1241088 | tf_op jit(solution)/shard_map/wlk,lg->wkg/dot_general | solution.py:101
  14.4 2.3 %gather_fusion = bf16[512,2,2,101]{3,2,1,0:T(2,128)(2,1)S(1)} fusion(bf16[2,2,512,101]{3,1,2,0:T(2,128)(2,1)S(1)} %copy.11, s32[1024]{0:T(1024)S(1)} %pad_clamp_fusion), kind=kCustom, calls=%fused_computation | custom fusion | bytes 829440 | tf_op jit(solution)/shard_map/jit(_take)/gather | solution.py:120
  17.1 1.6 %collective-permute-start = (bf16[2,2,64,101]{3,2,1,0:T(8,128)(2,1)S(1)}, bf16[2,2,64,101]{3,2,1,0:T(8,128)(2,1)S(1)}, u32[]{:S(2)}, u32[]{:S(2)}) collective-permute-start(bf16[2,2,64,101]{3,2,1,0:T(8,128)(2,1)S(1)} %get-tuple-element.19), channel_id=1, source_target_pairs={{28,0},{0,4},{4,8},{8,12},{12,16},{16,20},{20,24},{24,28},{29,1},{... | collective-permute-start | bytes 155144 | tf_op jit(solution)/shard_map/ppermute | solution.py:18
  18.7 1.6 %collective-permute-start.1 = (bf16[2,2,64,101]{3,2,1,0:T(8,128)(2,1)S(1)}, bf16[2,2,64,101]{3,2,1,0:T(8,128)(2,1)S(1)}, u32[]{:S(2)}, u32[]{:S(2)}) collective-permute-start(bf16[2,2,64,101]{3,2,1,0:T(8,128)(2,1)S(1)} %get-tuple-element.18), channel_id=1, source_target_pairs={{24,0},{28,4},{0,8},{4,12},{8,16},{12,20},{16,24},{20,28},{25,1},{... | collective-permute-start | bytes 155144 | tf_op jit(solution)/shard_map/ppermute | solution.py:18
  20.2 2.5 %collective-permute-start.2 = (bf16[2,2,64,101]{3,2,1,0:T(8,128)(2,1)S(1)}, bf16[2,2,64,101]{3,2,1,0:T(8,128)(2,1)S(1)}, u32[]{:S(2)}, u32[]{:S(2)}) collective-permute-start(bf16[2,2,64,101]{3,2,1,0:T(8,128)(2,1)S(1)} %get-tuple-element.17), channel_id=1, source_target_pairs={{20,0},{24,4},{28,8},{0,12},{4,16},{8,20},{12,24},{16,28},{21,1},{... | collective-permute-start | bytes 155144 | tf_op jit(solution)/shard_map/ppermute | solution.py:18
  23.1 2.2 %collective-permute-start.4 = (bf16[2,2,64,101]{3,2,1,0:T(8,128)(2,1)S(1)}, bf16[2,2,64,101]{3,2,1,0:T(8,128)(2,1)S(1)}, u32[]{:S(2)}, u32[]{:S(2)}) collective-permute-start(bf16[2,2,64,101]{3,2,1,0:T(8,128)(2,1)S(1)} %get-tuple-element.15), channel_id=1, source_target_pairs={{12,0},{16,4},{20,8},{24,12},{28,16},{0,20},{4,24},{8,28},{13,1},{... | collective-permute-start | bytes 155144 | tf_op jit(solution)/shard_map/ppermute | solution.py:18
  25.3 1.9 %collective-permute-start.5 = (bf16[2,2,64,101]{3,2,1,0:T(8,128)(2,1)S(1)}, bf16[2,2,64,101]{3,2,1,0:T(8,128)(2,1)S(1)}, u32[]{:S(2)}, u32[]{:S(2)}) collective-permute-start(bf16[2,2,64,101]{3,2,1,0:T(8,128)(2,1)S(1)} %get-tuple-element.14), channel_id=1, source_target_pairs={{8,0},{12,4},{16,8},{20,12},{24,16},{28,20},{0,24},{4,28},{9,1},{1... | collective-permute-start | bytes 155144 | tf_op jit(solution)/shard_map/ppermute | solution.py:18
  27.2 1.5 %collective-permute-start.6 = (bf16[2,2,64,101]{3,2,1,0:T(8,128)(2,1)S(1)}, bf16[2,2,64,101]{3,2,1,0:T(8,128)(2,1)S(1)}, u32[]{:S(2)}, u32[]{:S(2)}) collective-permute-start(bf16[2,2,64,101]{3,2,1,0:T(8,128)(2,1)S(1)} %get-tuple-element.13), channel_id=1, source_target_pairs={{4,0},{8,4},{12,8},{16,12},{20,16},{24,20},{28,24},{0,28},{5,1},{9... | collective-permute-start | bytes 155144 | tf_op jit(solution)/shard_map/ppermute | solution.py:18
  28.7 1.6 %collective-permute-done.3 = bf16[2,2,64,101]{3,2,1,0:T(8,128)(2,1)S(1)} collective-permute-done((bf16[2,2,64,101]{3,2,1,0:T(8,128)(2,1)S(1)}, bf16[2,2,64,101]{3,2,1,0:T(8,128)(2,1)S(1)}, u32[]{:S(2)}, u32[]{:S(2)}) %collective-permute-start.3) | collective-permute-done | bytes 51744 | tf_op jit(solution)/shard_map/ppermute | solution.py:18
  30.3 1.8 %collective-permute-done.4 = bf16[2,2,64,101]{3,2,1,0:T(8,128)(2,1)S(1)} collective-permute-done((bf16[2,2,64,101]{3,2,1,0:T(8,128)(2,1)S(1)}, bf16[2,2,64,101]{3,2,1,0:T(8,128)(2,1)S(1)}, u32[]{:S(2)}, u32[]{:S(2)}) %collective-permute-start.4) | collective-permute-done | bytes 51744 | tf_op jit(solution)/shard_map/ppermute | solution.py:18
  32.2 1.1 %collective-permute-done.6 = bf16[2,2,64,101]{3,2,1,0:T(8,128)(2,1)S(1)} collective-permute-done((bf16[2,2,64,101]{3,2,1,0:T(8,128)(2,1)S(1)}, bf16[2,2,64,101]{3,2,1,0:T(8,128)(2,1)S(1)}, u32[]{:S(2)}, u32[]{:S(2)}) %collective-permute-start.6) | collective-permute-done | bytes 51744 | tf_op jit(solution)/shard_map/ppermute | solution.py:18
  35.2 1.7 %collective-permute-start.8 = (bf16[8,2,2,16,101]{4,3,2,1,0:T(8,128)(2,1)S(1)}, bf16[8,2,2,16,101]{4,3,2,1,0:T(8,128)(2,1)S(1)}, u32[]{:S(2)}, u32[]{:S(2)}) collective-permute-start(bf16[8,2,2,16,101]{4,3,2,1,0:T(8,128)(2,1)S(1)} %get-tuple-element.12), channel_id=1, source_target_pairs={{0,5},{1,6},{2,7},{3,4},{4,9},{5,10},{6,11},{7,8},{8,13},{9,14},{1... | collective-permute-start | bytes 310280 | tf_op jit(solution)/shard_map/ppermute | solution.py:144
  37.7 3.5 %collective-permute-start.10 = (bf16[8,2,2,16,101]{4,3,2,1,0:T(8,128)(2,1)S(1)}, bf16[8,2,2,16,101]{4,3,2,1,0:T(8,128)(2,1)S(1)}, u32[]{:S(2)}, u32[]{:S(2)}) collective-permute-start(bf16[8,2,2,16,101]{4,3,2,1,0:T(8,128)(2,1)S(1)} %get-tuple-element.10), channel_id=1, source_target_pairs={{0,7},{1,4},{2,5},{3,6},{4,11},{5,8},{6,9},{7,10},{8,15},{9,12},{1... | collective-permute-start | bytes 310280 | tf_op jit(solution)/shard_map/ppermute | solution.py:144
  41.7 6.4 %collective-permute-start.13 = (bf16[8,2,2,16,101]{4,3,2,1,0:T(8,128)(2,1)S(1)}, bf16[8,2,2,16,101]{4,3,2,1,0:T(8,128)(2,1)S(1)}, u32[]{:S(2)}, u32[]{:S(2)}) collective-permute-start(bf16[8,2,2,16,101]{4,3,2,1,0:T(8,128)(2,1)S(1)} %get-tuple-element.11), channel_id=1, source_target_pairs={{0,10},{1,11},{2,8},{3,9},{4,14},{5,15},{6,12},{7,13},{8,18},{9,19... | collective-permute-start | bytes 310280 | tf_op jit(solution)/shard_map/ppermute | solution.py:144
  48.1 3.7 %collective-permute-start.14 = (bf16[8,2,2,16,101]{4,3,2,1,0:T(8,128)(2,1)S(1)}, bf16[8,2,2,16,101]{4,3,2,1,0:T(8,128)(2,1)S(1)}, u32[]{:S(2)}, u32[]{:S(2)}) collective-permute-start(bf16[8,2,2,16,101]{4,3,2,1,0:T(8,128)(2,1)S(1)} %get-tuple-element.10), channel_id=1, source_target_pairs={{0,11},{1,8},{2,9},{3,10},{4,15},{5,12},{6,13},{7,14},{8,19},{9,16... | collective-permute-start | bytes 310280 | tf_op jit(solution)/shard_map/ppermute | solution.py:144
  52.0 3.1 %collective-permute-done.12 = bf16[8,2,2,16,101]{4,3,2,1,0:T(8,128)(2,1)S(1)} collective-permute-done((bf16[8,2,2,16,101]{4,3,2,1,0:T(8,128)(2,1)S(1)}, bf16[8,2,2,16,101]{4,3,2,1,0:T(8,128)(2,1)S(1)}, u32[]{:S(2)}, u32[]{:S(2)}) %collective-permute-start.12) | collective-permute-done | bytes 103456 | tf_op jit(solution)/shard_map/ppermute | solution.py:144
  55.1 2.4 %collective-permute-done.13 = bf16[8,2,2,16,101]{4,3,2,1,0:T(8,128)(2,1)S(1)} collective-permute-done((bf16[8,2,2,16,101]{4,3,2,1,0:T(8,128)(2,1)S(1)}, bf16[8,2,2,16,101]{4,3,2,1,0:T(8,128)(2,1)S(1)}, u32[]{:S(2)}, u32[]{:S(2)}) %collective-permute-start.13) | collective-permute-done | bytes 103456 | tf_op jit(solution)/shard_map/ppermute | solution.py:144
  57.5 2.6 %collective-permute-done.14 = bf16[8,2,2,16,101]{4,3,2,1,0:T(8,128)(2,1)S(1)} collective-permute-done((bf16[8,2,2,16,101]{4,3,2,1,0:T(8,128)(2,1)S(1)}, bf16[8,2,2,16,101]{4,3,2,1,0:T(8,128)(2,1)S(1)}, u32[]{:S(2)}, u32[]{:S(2)}) %collective-permute-start.14) | collective-permute-done | bytes 103456 | tf_op jit(solution)/shard_map/ppermute | solution.py:144
  63.0 3.2 %copy.15 = bf16[101,64,128]{2,1,0:T(8,128)(2,1)} copy(bf16[101,64,128]{0,1,2:T(8,128)(2,1)S(1)} %bitcast.83) | data formatting | bytes 3309568 | tf_op jit(solution)/shard_map/reshape | solution.py:160
  66.3 3.9 %copy.16 = bf16[101,128,64]{1,2,0:T(8,128)(2,1)S(1)} copy(bf16[101,128,64]{0,2,1:T(8,128)(2,1)} %bitcast.89) | data formatting | bytes 3309568 | tf_op jit(solution)/shard_map/reshape | solution.py:155
  71.2 4.0 %fusion.2 = f32[2,64,16,128]{3,1,2,0:T(8,128)S(1)} fusion(f32[101,2,2,16,64]{4,3,2,1,0:T(8,128)S(1)} %bitcast.82, f32[1,101,128]{2,1,0:T(8,128)S(1)} %get-tuple-element.23, f32[1,101,128]{2,1,0:T(8,128)S(1)} %get-tuple-element.22), kind=kOutput, calls=%fused_computation.4 | convolution fusion | flops 317744384 | bytes 2806784 | tf_op jit(solution)/shard_map/fcrij,cfl->rjil/dot_general | solution.py:163
  75.2 1.6 %copy.18 = f32[2,64,16,128]{3,2,1,0:T(8,128)} copy(f32[2,64,16,128]{3,1,2,0:T(8,128)S(1)} %fusion.2) | data formatting | bytes 2097152 | tf_op jit(solution)/shard_map/fcrij,cfl->rjil/transpose | solution.py:163
  (67 shorter events, 11.3 us)
Async XLA Ops:
  6.5 59.7 %all-gather.2.cloned.1.call-start = ((), (), s32[]{:S(2)}) async-start(), calls=%async_computation | async-start | bytes 2621440 | tf_op jit(solution)/shard_map/all_gather | solution.py:153
  9.2 3.3 %copy-start.1 = (f32[1,400,512]{2,1,0:T(8,128)S(1)}, f32[1,400,512]{2,1,0:T(8,128)}, u32[]{:S(2)}) copy-start(f32[1,400,512]{2,1,0:T(8,128)} %param.3) | copy-start | bytes 2457604
  12.6 0.9 %copy-start.2 = (s32[512]{0:T(512)S(1)}, s32[512]{0:T(512)}, u32[]{:S(2)}) copy-start(s32[512]{0:T(512)} %param.5) | copy-start | bytes 6148
  17.1 8.2 %collective-permute-start = (bf16[2,2,64,101]{3,2,1,0:T(8,128)(2,1)S(1)}, bf16[2,2,64,101]{3,2,1,0:T(8,128)(2,1)S(1)}, u32[]{:S(2)}, u32[]{:S(2)}) collective-permute-start(bf16[2,2,64,101]{3,2,1,0:T(8,128)(2,1)S(1)} %get-tuple-element.19), channel_id=1, source_target_pairs={{28,0},{0,4},{4,8},{8,12},{12,16},{16,20},{20,24},{24,28},{29,1},{... | collective-permute-start | bytes 155144 | tf_op jit(solution)/shard_map/ppermute | solution.py:18
  18.7 8.5 %collective-permute-start.1 = (bf16[2,2,64,101]{3,2,1,0:T(8,128)(2,1)S(1)}, bf16[2,2,64,101]{3,2,1,0:T(8,128)(2,1)S(1)}, u32[]{:S(2)}, u32[]{:S(2)}) collective-permute-start(bf16[2,2,64,101]{3,2,1,0:T(8,128)(2,1)S(1)} %get-tuple-element.18), channel_id=1, source_target_pairs={{24,0},{28,4},{0,8},{4,12},{8,16},{12,20},{16,24},{20,28},{25,1},{... | collective-permute-start | bytes 155144 | tf_op jit(solution)/shard_map/ppermute | solution.py:18
  20.2 8.4 %collective-permute-start.2 = (bf16[2,2,64,101]{3,2,1,0:T(8,128)(2,1)S(1)}, bf16[2,2,64,101]{3,2,1,0:T(8,128)(2,1)S(1)}, u32[]{:S(2)}, u32[]{:S(2)}) collective-permute-start(bf16[2,2,64,101]{3,2,1,0:T(8,128)(2,1)S(1)} %get-tuple-element.17), channel_id=1, source_target_pairs={{20,0},{24,4},{28,8},{0,12},{4,16},{8,20},{12,24},{16,28},{21,1},{... | collective-permute-start | bytes 155144 | tf_op jit(solution)/shard_map/ppermute | solution.py:18
  22.8 7.6 %collective-permute-start.3 = (bf16[2,2,64,101]{3,2,1,0:T(8,128)(2,1)S(1)}, bf16[2,2,64,101]{3,2,1,0:T(8,128)(2,1)S(1)}, u32[]{:S(2)}, u32[]{:S(2)}) collective-permute-start(bf16[2,2,64,101]{3,2,1,0:T(8,128)(2,1)S(1)} %get-tuple-element.16), channel_id=1, source_target_pairs={{16,0},{20,4},{24,8},{28,12},{0,16},{4,20},{8,24},{12,28},{17,1},{... | collective-permute-start | bytes 155144 | tf_op jit(solution)/shard_map/ppermute | solution.py:18
  23.1 9.0 %collective-permute-start.4 = (bf16[2,2,64,101]{3,2,1,0:T(8,128)(2,1)S(1)}, bf16[2,2,64,101]{3,2,1,0:T(8,128)(2,1)S(1)}, u32[]{:S(2)}, u32[]{:S(2)}) collective-permute-start(bf16[2,2,64,101]{3,2,1,0:T(8,128)(2,1)S(1)} %get-tuple-element.15), channel_id=1, source_target_pairs={{12,0},{16,4},{20,8},{24,12},{28,16},{0,20},{4,24},{8,28},{13,1},{... | collective-permute-start | bytes 155144 | tf_op jit(solution)/shard_map/ppermute | solution.py:18
  25.3 6.8 %collective-permute-start.5 = (bf16[2,2,64,101]{3,2,1,0:T(8,128)(2,1)S(1)}, bf16[2,2,64,101]{3,2,1,0:T(8,128)(2,1)S(1)}, u32[]{:S(2)}, u32[]{:S(2)}) collective-permute-start(bf16[2,2,64,101]{3,2,1,0:T(8,128)(2,1)S(1)} %get-tuple-element.14), channel_id=1, source_target_pairs={{8,0},{12,4},{16,8},{20,12},{24,16},{28,20},{0,24},{4,28},{9,1},{1... | collective-permute-start | bytes 155144 | tf_op jit(solution)/shard_map/ppermute | solution.py:18
  27.2 6.0 %collective-permute-start.6 = (bf16[2,2,64,101]{3,2,1,0:T(8,128)(2,1)S(1)}, bf16[2,2,64,101]{3,2,1,0:T(8,128)(2,1)S(1)}, u32[]{:S(2)}, u32[]{:S(2)}) collective-permute-start(bf16[2,2,64,101]{3,2,1,0:T(8,128)(2,1)S(1)} %get-tuple-element.13), channel_id=1, source_target_pairs={{4,0},{8,4},{12,8},{16,12},{20,16},{24,20},{28,24},{0,28},{5,1},{9... | collective-permute-start | bytes 155144 | tf_op jit(solution)/shard_map/ppermute | solution.py:18
  34.3 7.4 %collective-permute-start.7 = (bf16[8,2,2,16,101]{4,3,2,1,0:T(8,128)(2,1)S(1)}, bf16[8,2,2,16,101]{4,3,2,1,0:T(8,128)(2,1)S(1)}, u32[]{:S(2)}, u32[]{:S(2)}) collective-permute-start(bf16[8,2,2,16,101]{4,3,2,1,0:T(8,128)(2,1)S(1)} %get-tuple-element.9), channel_id=1, source_target_pairs={{0,4},{1,5},{2,6},{3,7},{4,8},{5,9},{6,10},{7,11},{8,12},{9,13},{1... | collective-permute-start | bytes 310280 | tf_op jit(solution)/shard_map/ppermute | solution.py:144
  35.2 6.5 %collective-permute-start.8 = (bf16[8,2,2,16,101]{4,3,2,1,0:T(8,128)(2,1)S(1)}, bf16[8,2,2,16,101]{4,3,2,1,0:T(8,128)(2,1)S(1)}, u32[]{:S(2)}, u32[]{:S(2)}) collective-permute-start(bf16[8,2,2,16,101]{4,3,2,1,0:T(8,128)(2,1)S(1)} %get-tuple-element.12), channel_id=1, source_target_pairs={{0,5},{1,6},{2,7},{3,4},{4,9},{5,10},{6,11},{7,8},{8,13},{9,14},{1... | collective-permute-start | bytes 310280 | tf_op jit(solution)/shard_map/ppermute | solution.py:144
  36.9 11.2 %collective-permute-start.9 = (bf16[8,2,2,16,101]{4,3,2,1,0:T(8,128)(2,1)S(1)}, bf16[8,2,2,16,101]{4,3,2,1,0:T(8,128)(2,1)S(1)}, u32[]{:S(2)}, u32[]{:S(2)}) collective-permute-start(bf16[8,2,2,16,101]{4,3,2,1,0:T(8,128)(2,1)S(1)} %get-tuple-element.11), channel_id=1, source_target_pairs={{0,6},{1,7},{2,4},{3,5},{4,10},{5,11},{6,8},{7,9},{8,14},{9,15},{1... | collective-permute-start | bytes 310280 | tf_op jit(solution)/shard_map/ppermute | solution.py:144
  37.7 14.1 %collective-permute-start.10 = (bf16[8,2,2,16,101]{4,3,2,1,0:T(8,128)(2,1)S(1)}, bf16[8,2,2,16,101]{4,3,2,1,0:T(8,128)(2,1)S(1)}, u32[]{:S(2)}, u32[]{:S(2)}) collective-permute-start(bf16[8,2,2,16,101]{4,3,2,1,0:T(8,128)(2,1)S(1)} %get-tuple-element.10), channel_id=1, source_target_pairs={{0,7},{1,4},{2,5},{3,6},{4,11},{5,8},{6,9},{7,10},{8,15},{9,12},{1... | collective-permute-start | bytes 310280 | tf_op jit(solution)/shard_map/ppermute | solution.py:144
  41.5 10.5 %collective-permute-start.11 = (bf16[8,2,2,16,101]{4,3,2,1,0:T(8,128)(2,1)S(1)}, bf16[8,2,2,16,101]{4,3,2,1,0:T(8,128)(2,1)S(1)}, u32[]{:S(2)}, u32[]{:S(2)}) collective-permute-start(bf16[8,2,2,16,101]{4,3,2,1,0:T(8,128)(2,1)S(1)} %get-tuple-element.9), channel_id=1, source_target_pairs={{0,8},{1,9},{2,10},{3,11},{4,12},{5,13},{6,14},{7,15},{8,16},{9,17... | collective-permute-start | bytes 310280 | tf_op jit(solution)/shard_map/ppermute | solution.py:144
  41.7 13.4 %collective-permute-start.12 = (bf16[8,2,2,16,101]{4,3,2,1,0:T(8,128)(2,1)S(1)}, bf16[8,2,2,16,101]{4,3,2,1,0:T(8,128)(2,1)S(1)}, u32[]{:S(2)}, u32[]{:S(2)}) collective-permute-start(bf16[8,2,2,16,101]{4,3,2,1,0:T(8,128)(2,1)S(1)} %get-tuple-element.12), channel_id=1, source_target_pairs={{0,9},{1,10},{2,11},{3,8},{4,13},{5,14},{6,15},{7,12},{8,17},{9,18... | collective-permute-start | bytes 310280 | tf_op jit(solution)/shard_map/ppermute | solution.py:144
  41.7 15.8 %collective-permute-start.13 = (bf16[8,2,2,16,101]{4,3,2,1,0:T(8,128)(2,1)S(1)}, bf16[8,2,2,16,101]{4,3,2,1,0:T(8,128)(2,1)S(1)}, u32[]{:S(2)}, u32[]{:S(2)}) collective-permute-start(bf16[8,2,2,16,101]{4,3,2,1,0:T(8,128)(2,1)S(1)} %get-tuple-element.11), channel_id=1, source_target_pairs={{0,10},{1,11},{2,8},{3,9},{4,14},{5,15},{6,12},{7,13},{8,18},{9,19... | collective-permute-start | bytes 310280 | tf_op jit(solution)/shard_map/ppermute | solution.py:144
  48.1 12.1 %collective-permute-start.14 = (bf16[8,2,2,16,101]{4,3,2,1,0:T(8,128)(2,1)S(1)}, bf16[8,2,2,16,101]{4,3,2,1,0:T(8,128)(2,1)S(1)}, u32[]{:S(2)}, u32[]{:S(2)}) collective-permute-start(bf16[8,2,2,16,101]{4,3,2,1,0:T(8,128)(2,1)S(1)} %get-tuple-element.10), channel_id=1, source_target_pairs={{0,11},{1,8},{2,9},{3,10},{4,15},{5,12},{6,13},{7,14},{8,19},{9,16... | collective-permute-start | bytes 310280 | tf_op jit(solution)/shard_map/ppermute | solution.py:144
  66.3 3.9 %copy-start = (bf16[101,64,128]{2,1,0:T(8,128)(2,1)S(1)}, bf16[101,64,128]{2,1,0:T(8,128)(2,1)}, u32[]{:S(2)}) copy-start(bf16[101,64,128]{2,1,0:T(8,128)(2,1)} %copy.15) | copy-start | bytes 4964356
Sparse Core Ops, SparseCore 0:
  34.2 31.7 all-gather.1

commit v3 on v2

--- a/solution.py
+++ b/solution.py
@@ -126,31 +126,35 @@
         piece = lax.dynamic_index_in_dim(sorted_spec, target, 0, keepdims=False)
         pieces.append(piece if distance == 0 else shifted(piece, "chan", distance))
     own = jnp.stack(pieces)
+    masks = [0]
+    step = tm_count // 2
+    while step >= 1:
+        masks = masks + [m ^ step for m in masks]
+        step //= 2
     grid = [(c, q) for c in range(chan_count) for q in range(tm_count)]
     partners = []
     for round_index in range(ROUNDS):
         offset = max(1, round_index * chan_count // 4)
         per_source = []
-        for tm_shift in range(tm_count):
-            target_tm = jnp.mod(tm_position + tm_shift, tm_count)
+        for mask in masks:
+            target_tm = jnp.bitwise_xor(tm_position, mask)
             piece = lax.dynamic_slice_in_dim(own, target_tm * slice_width, slice_width, axis=3)
-            if offset % chan_count == 0 and tm_shift == 0:
-                per_source.append(piece)
-                continue
             route = [
-                (c * tm_count + q, ((c + offset) % chan_count) * tm_count + (q + tm_shift) % tm_count)
+                (c * tm_count + q, ((c + offset) % chan_count) * tm_count + (q ^ mask))
                 for c, q in grid
             ]
             per_source.append(lax.ppermute(piece, ("chan", "tm"), route))
-        by_shift = jnp.stack(per_source)
-        by_time = jnp.concatenate([by_shift[::-1], by_shift[::-1]], axis=0)
-        start = jnp.mod(tm_count - 1 - tm_position, tm_count)
-        by_time = lax.dynamic_slice_in_dim(by_time, start, tm_count, axis=0)
+        by_time = jnp.stack(per_source)
         by_time = jnp.roll(by_time, offset, axis=1)
         partners.append(by_time)
     windows_here = chan_count * spectra.shape[0]
     own_t = jnp.transpose(own, (4, 2, 0, 1, 3)).reshape(FB, 2, windows_here, block_width)
-    gathered = lax.all_gather(own_t, "tm", axis=2, tiled=False)
+    gathered = own_t[:, :, None]
+    step = tm_count // 2
+    while step >= 1:
+        route = [(q, q ^ step) for q in range(tm_count)]
+        gathered = jnp.concatenate([gathered, lax.ppermute(gathered, "tm", route)], axis=2)
+        step //= 2
     contraction = 2 * tm_count * windows_here
     own_spec = gathered.reshape(FB, contraction, block_width)
     partner = jnp.concatenate(partners, axis=4)

time: 84.8 us -> 81.9 us (0.966)
  between operations: 13.8 us -> 0.29 us
  waiting for transfers between devices: 12.7 us -> 25 us
  starting transfers between devices: 28.8 us -> 24.2 us
  other arithmetic: 6.63 us -> 8.83 us
  matrix products: 8.27 us -> 10.2 us
  local copies, waits for them, and re-layouts: 13.5 us -> 11.9 us
    ppermute x0 -> x2, waiting for transfers between devices: none -> 8.19 us  [on_device_local(): lax.ppermute(gathered, 'tm', route)]
    ppermute x8, starting transfers between devices: 17.3 us -> 10.9 us  [on_device_local(): per_source.append(lax.ppermute(piece, ('chan', 'tm'), route))]
    ppermute x8, waiting for transfers between devices: 8.18 us -> 12.3 us  [on_device_local(): per_source.append(lax.ppermute(piece, ('chan', 'tm'), route))]
    concatenate x1 -> x3, other arithmetic: 0.53 us -> 3.21 us  [the longest x2 2.89 us: on_device_local(): jnp.concatenate([gathered, lax.ppermute(gathered, 'tm', route)], axis=2)]
    dot_general x1, matrix products: 0.99 us -> 2.92 us  [on_device_local(): jnp.einsum('fnk,fkj->fnj', both, own_spec, preferred_element_type=jnp.flo...]
    ppermute x0 -> x2, starting transfers between devices: none -> 1.79 us  [on_device_local(): lax.ppermute(gathered, 'tm', route)]
  transfers between devices with their start and end apart: 16 -> 17, of which waited for: 6 -> 9; matrix products, arithmetic and copies ran while one was open for 8% -> 7% of each run, Pallas kernels for 0% -> 0%
where the time goes in v3:
time: 81.9 us; the launch traced here: 80.4 us
  waiting for transfers between devices  25 us (31%)
  starting transfers between devices  24.2 us (30%)
  local copies, waits for them, and re-layouts  11.9 us (15%)
  matrix products  10.2 us (12%)
  other arithmetic  8.83 us (11%)
    ppermute x8, waiting for transfers between devices, on_device_local(): per_source.append(lax.ppermute(piece, ('chan', 'tm'), route))  12.3 us
    ppermute x7, starting transfers between devices, shifted(): return lax.ppermute(block, axis, route)  11.5 us
    ppermute x8, starting transfers between devices, on_device_local(): per_source.append(lax.ppermute(piece, ('chan', 'tm'), route))  10.9 us
    ppermute x2, waiting for transfers between devices, on_device_local(): lax.ppermute(gathered, 'tm', route)  8.19 us
    ppermute x7, waiting for transfers between devices, shifted(): return lax.ppermute(block, axis, route)  4.46 us
    dot_general x1, matrix products, on_device_local(): jnp.einsum('fcrij,cfl->rjil', sums, inverse_table(), precision=lax.Precis...  4.04 us
    reshape x1, local copies, waits for them, and re-layouts, on_device_local(): own_spec = gathered.reshape(FB, contraction, block_width)  3.3 us
    reshape x1, local copies, waits for them, and re-layouts, on_device_local(): both = both.reshape(FB, 2 * ROUNDS * slice_width, contraction)  3.23 us
  transfers between devices with their start and end apart: 17, of which 9 were waited for; matrix products, arithmetic and copies ran while one was open for 7% of the time, Pallas kernels for 0%

profile of v3, /device:TPU:6, one launch (start us, length us, event | category | flops | bytes accessed | tf_op | source)
XLA Modules:
  0.0 80.4 jit_solution(15858013550006933423)
XLA Ops:
  4.1 1.9 %fusion.12 = f32[2,512,101]{1,2,0:T(8,128)S(1)} fusion(f32[2,200,512]{2,1,0:T(8,128)} %bitcast.90, f32[2,512]{1,0:T(2,128)S(1)} %add_sqrt_fusion, f32[2,512]{1,0:T(2,128)S(1)} %broadcast_multiply_fusion.1), kind=kOutput, calls=%fused_computation.36 | convolution fusion | flops 124700200 | bytes 1241088 | tf_op jit(solution)/shard_map/wlk,lg->wkg/dot_general | solution.py:101
  7.9 2.3 %gather_fusion = bf16[512,2,2,101]{3,2,1,0:T(2,128)(2,1)S(1)} fusion(bf16[2,2,512,101]{3,1,2,0:T(2,128)(2,1)S(1)} %copy.11, s32[1024]{0:T(1024)S(1)} %pad_clamp_fusion), kind=kCustom, calls=%fused_computation | custom fusion | bytes 829440 | tf_op jit(solution)/shard_map/jit(_take)/gather | solution.py:120
  10.6 1.6 %collective-permute-start = (bf16[2,2,64,101]{3,2,1,0:T(8,128)(2,1)S(1)}, bf16[2,2,64,101]{3,2,1,0:T(8,128)(2,1)S(1)}, u32[]{:S(2)}, u32[]{:S(2)}) collective-permute-start(bf16[2,2,64,101]{3,2,1,0:T(8,128)(2,1)S(1)} %get-tuple-element.17), channel_id=1, source_target_pairs={{28,0},{0,4},{4,8},{8,12},{12,16},{16,20},{20,24},{24,28},{29,1},{... | collective-permute-start | bytes 155144 | tf_op jit(solution)/shard_map/ppermute | solution.py:18
  12.1 1.6 %collective-permute-start.1 = (bf16[2,2,64,101]{3,2,1,0:T(8,128)(2,1)S(1)}, bf16[2,2,64,101]{3,2,1,0:T(8,128)(2,1)S(1)}, u32[]{:S(2)}, u32[]{:S(2)}) collective-permute-start(bf16[2,2,64,101]{3,2,1,0:T(8,128)(2,1)S(1)} %get-tuple-element.16), channel_id=1, source_target_pairs={{24,0},{28,4},{0,8},{4,12},{8,16},{12,20},{16,24},{20,28},{25,1},{... | collective-permute-start | bytes 155144 | tf_op jit(solution)/shard_map/ppermute | solution.py:18
  13.7 2.5 %collective-permute-start.2 = (bf16[2,2,64,101]{3,2,1,0:T(8,128)(2,1)S(1)}, bf16[2,2,64,101]{3,2,1,0:T(8,128)(2,1)S(1)}, u32[]{:S(2)}, u32[]{:S(2)}) collective-permute-start(bf16[2,2,64,101]{3,2,1,0:T(8,128)(2,1)S(1)} %get-tuple-element.15), channel_id=1, source_target_pairs={{20,0},{24,4},{28,8},{0,12},{4,16},{8,20},{12,24},{16,28},{21,1},{... | collective-permute-start | bytes 155144 | tf_op jit(solution)/shard_map/ppermute | solution.py:18
  16.6 2.2 %collective-permute-start.4 = (bf16[2,2,64,101]{3,2,1,0:T(8,128)(2,1)S(1)}, bf16[2,2,64,101]{3,2,1,0:T(8,128)(2,1)S(1)}, u32[]{:S(2)}, u32[]{:S(2)}) collective-permute-start(bf16[2,2,64,101]{3,2,1,0:T(8,128)(2,1)S(1)} %get-tuple-element.13), channel_id=1, source_target_pairs={{12,0},{16,4},{20,8},{24,12},{28,16},{0,20},{4,24},{8,28},{13,1},{... | collective-permute-start | bytes 155144 | tf_op jit(solution)/shard_map/ppermute | solution.py:18
  18.8 1.9 %collective-permute-start.5 = (bf16[2,2,64,101]{3,2,1,0:T(8,128)(2,1)S(1)}, bf16[2,2,64,101]{3,2,1,0:T(8,128)(2,1)S(1)}, u32[]{:S(2)}, u32[]{:S(2)}) collective-permute-start(bf16[2,2,64,101]{3,2,1,0:T(8,128)(2,1)S(1)} %get-tuple-element.12), channel_id=1, source_target_pairs={{8,0},{12,4},{16,8},{20,12},{24,16},{28,20},{0,24},{4,28},{9,1},{1... | collective-permute-start | bytes 155144 | tf_op jit(solution)/shard_map/ppermute | solution.py:18
  22.2 1.6 %collective-permute-done.3 = bf16[2,2,64,101]{3,2,1,0:T(8,128)(2,1)S(1)} collective-permute-done((bf16[2,2,64,101]{3,2,1,0:T(8,128)(2,1)S(1)}, bf16[2,2,64,101]{3,2,1,0:T(8,128)(2,1)S(1)}, u32[]{:S(2)}, u32[]{:S(2)}) %collective-permute-start.3) | collective-permute-done | bytes 51744 | tf_op jit(solution)/shard_map/ppermute | solution.py:18
  23.8 1.8 %collective-permute-done.4 = bf16[2,2,64,101]{3,2,1,0:T(8,128)(2,1)S(1)} collective-permute-done((bf16[2,2,64,101]{3,2,1,0:T(8,128)(2,1)S(1)}, bf16[2,2,64,101]{3,2,1,0:T(8,128)(2,1)S(1)}, u32[]{:S(2)}, u32[]{:S(2)}) %collective-permute-start.4) | collective-permute-done | bytes 51744 | tf_op jit(solution)/shard_map/ppermute | solution.py:18
  27.7 2.5 %collective-permute-start.8 = (bf16[8,2,2,16,101]{4,3,2,1,0:T(8,128)(2,1)S(1)}, bf16[8,2,2,16,101]{4,3,2,1,0:T(8,128)(2,1)S(1)}, u32[]{:S(2)}, u32[]{:S(2)}) collective-permute-start(bf16[8,2,2,16,101]{4,3,2,1,0:T(8,128)(2,1)S(1)} %get-tuple-element.10), channel_id=1, source_target_pairs={{0,6},{1,7},{2,4},{3,5},{4,10},{5,11},{6,8},{7,9},{8,14},{9,15},{1... | collective-permute-start | bytes 310280 | tf_op jit(solution)/shard_map/ppermute | solution.py:146
  30.3 3.9 %collective-permute-start.10 = (bf16[8,2,2,16,101]{4,3,2,1,0:T(8,128)(2,1)S(1)}, bf16[8,2,2,16,101]{4,3,2,1,0:T(8,128)(2,1)S(1)}, u32[]{:S(2)}, u32[]{:S(2)}) collective-permute-start(bf16[8,2,2,16,101]{4,3,2,1,0:T(8,128)(2,1)S(1)} %get-tuple-element.8), channel_id=1, source_target_pairs={{0,7},{1,6},{2,5},{3,4},{4,11},{5,10},{6,9},{7,8},{8,15},{9,14},{1... | collective-permute-start | bytes 310280 | tf_op jit(solution)/shard_map/ppermute | solution.py:146
  34.4 4.1 %collective-permute-done.7 = bf16[8,2,2,16,101]{4,3,2,1,0:T(8,128)(2,1)S(1)} collective-permute-done((bf16[8,2,2,16,101]{4,3,2,1,0:T(8,128)(2,1)S(1)}, bf16[8,2,2,16,101]{4,3,2,1,0:T(8,128)(2,1)S(1)}, u32[]{:S(2)}, u32[]{:S(2)}) %collective-permute-start.7) | collective-permute-done | bytes 103456 | tf_op jit(solution)/shard_map/ppermute | solution.py:146
  38.5 2.1 %collective-permute-start.12 = (bf16[8,2,2,16,101]{4,3,2,1,0:T(8,128)(2,1)S(1)}, bf16[8,2,2,16,101]{4,3,2,1,0:T(8,128)(2,1)S(1)}, u32[]{:S(2)}, u32[]{:S(2)}) collective-permute-start(bf16[8,2,2,16,101]{4,3,2,1,0:T(8,128)(2,1)S(1)} %get-tuple-element.10), channel_id=1, source_target_pairs={{0,10},{1,11},{2,8},{3,9},{4,14},{5,15},{6,12},{7,13},{8,18},{9,19... | collective-permute-start | bytes 310280 | tf_op jit(solution)/shard_map/ppermute | solution.py:146
  41.9 1.8 %collective-permute-start.15 = (bf16[101,2,1,16,64]{0,4,3,2,1:T(8,128)(2,1)S(1)}, bf16[101,2,1,16,64]{0,4,3,2,1:T(8,128)(2,1)S(1)}, u32[]{:S(2)}, u32[]{:S(2)}) collective-permute-start(bf16[101,2,1,16,64]{0,4,3,2,1:T(8,128)(2,1)S(1)} %bitcast.85), channel_id=1, source_target_pairs={{0,2},{1,3},{2,0},{3,1},{4,6},{5,7},{6,4},{7,5},{8,10},{9,11},{10,... | collective-permute-start | bytes 1241096 | tf_op jit(solution)/shard_map/ppermute | solution.py:156
  43.9 1.7 %collective-permute-done.11 = bf16[8,2,2,16,101]{4,3,2,1,0:T(8,128)(2,1)S(1)} collective-permute-done((bf16[8,2,2,16,101]{4,3,2,1,0:T(8,128)(2,1)S(1)}, bf16[8,2,2,16,101]{4,3,2,1,0:T(8,128)(2,1)S(1)}, u32[]{:S(2)}, u32[]{:S(2)}) %collective-permute-start.11) | collective-permute-done | bytes 103456 | tf_op jit(solution)/shard_map/ppermute | solution.py:146
  45.6 2.5 %collective-permute-done.12 = bf16[8,2,2,16,101]{4,3,2,1,0:T(8,128)(2,1)S(1)} collective-permute-done((bf16[8,2,2,16,101]{4,3,2,1,0:T(8,128)(2,1)S(1)}, bf16[8,2,2,16,101]{4,3,2,1,0:T(8,128)(2,1)S(1)}, u32[]{:S(2)}, u32[]{:S(2)}) %collective-permute-start.12) | collective-permute-done | bytes 103456 | tf_op jit(solution)/shard_map/ppermute | solution.py:146
  48.2 3.9 %collective-permute-done.14 = bf16[8,2,2,16,101]{4,3,2,1,0:T(8,128)(2,1)S(1)} collective-permute-done((bf16[8,2,2,16,101]{4,3,2,1,0:T(8,128)(2,1)S(1)}, bf16[8,2,2,16,101]{4,3,2,1,0:T(8,128)(2,1)S(1)}, u32[]{:S(2)}, u32[]{:S(2)}) %collective-permute-start.14) | collective-permute-done | bytes 103456 | tf_op jit(solution)/shard_map/ppermute | solution.py:146
  52.5 8.2 %collective-permute-done.15 = bf16[101,2,1,16,64]{0,4,3,2,1:T(8,128)(2,1)S(1)} collective-permute-done((bf16[101,2,1,16,64]{0,4,3,2,1:T(8,128)(2,1)S(1)}, bf16[101,2,1,16,64]{0,4,3,2,1:T(8,128)(2,1)S(1)}, u32[]{:S(2)}, u32[]{:S(2)}) %collective-permute-start.15) | collective-permute-done | bytes 413728 | tf_op jit(solution)/shard_map/ppermute | solution.py:156
  63.7 3.2 %copy.15 = bf16[101,64,128]{2,1,0:T(8,128)(2,1)} copy(bf16[101,64,128]{0,1,2:T(8,128)(2,1)S(1)} %bitcast.84) | data formatting | bytes 3309568 | tf_op jit(solution)/shard_map/reshape | solution.py:164
  66.9 1.7 %pad_maximum_fusion = bf16[101,2,4,16,64]{0,4,3,2,1:T(8,128)(2,1)S(1)} fusion(bf16[101,2,2,16,64]{0,4,3,2,1:T(8,128)(2,1)} %collective-permute-done.16, bf16[101,2,1,16,64]{0,4,3,2,1:T(8,128)(2,1)S(1)} %collective-permute-done.15, bf16[101,2,1,16,64]{0,4,3,2,1:T(8,128)(2,1)S(1)} %bitcast.87), kind=kLoop, calls=%fused_computation.4 | loop fusion | flops 1654784 | bytes 3309568 | tf_op jit(solution)/shard_map/concatenate | solution.py:156
  68.6 3.3 %copy.16 = bf16[101,128,64]{1,2,0:T(8,128)(2,1)} copy(bf16[101,128,64]{0,2,1:T(8,128)(2,1)S(1)} %bitcast.83) | data formatting | bytes 3309568 | tf_op jit(solution)/shard_map/reshape | solution.py:159
  71.9 2.9 %fusion.57 = f32[101,64,64]{2,1,0:T(8,128)S(1)} fusion(bf16[101,64,128]{2,1,0:T(8,128)(2,1)} %copy.15, bf16[101,128,64]{1,2,0:T(8,128)(2,1)} %copy.16), kind=kOutput, calls=%fused_computation.111 | convolution fusion | flops 105906176 | bytes 4964352 | tf_op jit(solution)/shard_map/fnk,fkj->fnj/dot_general | solution.py:165
  74.8 4.0 %fusion.2 = f32[2,64,16,128]{3,1,2,0:T(8,128)S(1)} fusion(f32[101,2,2,16,64]{4,3,2,1,0:T(8,128)S(1)} %bitcast.82, f32[1,101,128]{2,1,0:T(8,128)S(1)} %get-tuple-element.21, f32[1,101,128]{2,1,0:T(8,128)S(1)} %get-tuple-element.20), kind=kOutput, calls=%fused_computation.5 | convolution fusion | flops 317744384 | bytes 2806784 | tf_op jit(solution)/shard_map/fcrij,cfl->rjil/dot_general | solution.py:167
  78.9 1.6 %copy.18 = f32[2,64,16,128]{3,2,1,0:T(8,128)} copy(f32[2,64,16,128]{3,1,2,0:T(8,128)S(1)} %fusion.2) | data formatting | bytes 2097152 | tf_op jit(solution)/shard_map/fcrij,cfl->rjil/transpose | solution.py:167
  (60 shorter events, 15.5 us)
Async XLA Ops:
  2.7 3.3 %copy-start = (f32[1,400,512]{2,1,0:T(8,128)S(1)}, f32[1,400,512]{2,1,0:T(8,128)}, u32[]{:S(2)}) copy-start(f32[1,400,512]{2,1,0:T(8,128)} %param.3) | copy-start | bytes 2457604
  6.0 0.9 %copy-start.1 = (s32[512]{0:T(512)S(1)}, s32[512]{0:T(512)}, u32[]{:S(2)}) copy-start(s32[512]{0:T(512)} %param.5) | copy-start | bytes 6148
  10.6 8.2 %collective-permute-start = (bf16[2,2,64,101]{3,2,1,0:T(8,128)(2,1)S(1)}, bf16[2,2,64,101]{3,2,1,0:T(8,128)(2,1)S(1)}, u32[]{:S(2)}, u32[]{:S(2)}) collective-permute-start(bf16[2,2,64,101]{3,2,1,0:T(8,128)(2,1)S(1)} %get-tuple-element.17), channel_id=1, source_target_pairs={{28,0},{0,4},{4,8},{8,12},{12,16},{16,20},{20,24},{24,28},{29,1},{... | collective-permute-start | bytes 155144 | tf_op jit(solution)/shard_map/ppermute | solution.py:18
  12.1 8.6 %collective-permute-start.1 = (bf16[2,2,64,101]{3,2,1,0:T(8,128)(2,1)S(1)}, bf16[2,2,64,101]{3,2,1,0:T(8,128)(2,1)S(1)}, u32[]{:S(2)}, u32[]{:S(2)}) collective-permute-start(bf16[2,2,64,101]{3,2,1,0:T(8,128)(2,1)S(1)} %get-tuple-element.16), channel_id=1, source_target_pairs={{24,0},{28,4},{0,8},{4,12},{8,16},{12,20},{16,24},{20,28},{25,1},{... | collective-permute-start | bytes 155144 | tf_op jit(solution)/shard_map/ppermute | solution.py:18
  13.7 8.5 %collective-permute-start.2 = (bf16[2,2,64,101]{3,2,1,0:T(8,128)(2,1)S(1)}, bf16[2,2,64,101]{3,2,1,0:T(8,128)(2,1)S(1)}, u32[]{:S(2)}, u32[]{:S(2)}) collective-permute-start(bf16[2,2,64,101]{3,2,1,0:T(8,128)(2,1)S(1)} %get-tuple-element.15), channel_id=1, source_target_pairs={{20,0},{24,4},{28,8},{0,12},{4,16},{8,20},{12,24},{16,28},{21,1},{... | collective-permute-start | bytes 155144 | tf_op jit(solution)/shard_map/ppermute | solution.py:18
  16.2 7.6 %collective-permute-start.3 = (bf16[2,2,64,101]{3,2,1,0:T(8,128)(2,1)S(1)}, bf16[2,2,64,101]{3,2,1,0:T(8,128)(2,1)S(1)}, u32[]{:S(2)}, u32[]{:S(2)}) collective-permute-start(bf16[2,2,64,101]{3,2,1,0:T(8,128)(2,1)S(1)} %get-tuple-element.14), channel_id=1, source_target_pairs={{16,0},{20,4},{24,8},{28,12},{0,16},{4,20},{8,24},{12,28},{17,1},{... | collective-permute-start | bytes 155144 | tf_op jit(solution)/shard_map/ppermute | solution.py:18
  16.6 9.0 %collective-permute-start.4 = (bf16[2,2,64,101]{3,2,1,0:T(8,128)(2,1)S(1)}, bf16[2,2,64,101]{3,2,1,0:T(8,128)(2,1)S(1)}, u32[]{:S(2)}, u32[]{:S(2)}) collective-permute-start(bf16[2,2,64,101]{3,2,1,0:T(8,128)(2,1)S(1)} %get-tuple-element.13), channel_id=1, source_target_pairs={{12,0},{16,4},{20,8},{24,12},{28,16},{0,20},{4,24},{8,28},{13,1},{... | collective-permute-start | bytes 155144 | tf_op jit(solution)/shard_map/ppermute | solution.py:18
  18.8 6.8 %collective-permute-start.5 = (bf16[2,2,64,101]{3,2,1,0:T(8,128)(2,1)S(1)}, bf16[2,2,64,101]{3,2,1,0:T(8,128)(2,1)S(1)}, u32[]{:S(2)}, u32[]{:S(2)}) collective-permute-start(bf16[2,2,64,101]{3,2,1,0:T(8,128)(2,1)S(1)} %get-tuple-element.12), channel_id=1, source_target_pairs={{8,0},{12,4},{16,8},{20,12},{24,16},{28,20},{0,24},{4,28},{9,1},{1... | collective-permute-start | bytes 155144 | tf_op jit(solution)/shard_map/ppermute | solution.py:18
  20.7 6.0 %collective-permute-start.6 = (bf16[2,2,64,101]{3,2,1,0:T(8,128)(2,1)S(1)}, bf16[2,2,64,101]{3,2,1,0:T(8,128)(2,1)S(1)}, u32[]{:S(2)}, u32[]{:S(2)}) collective-permute-start(bf16[2,2,64,101]{3,2,1,0:T(8,128)(2,1)S(1)} %get-tuple-element.11), channel_id=1, source_target_pairs={{4,0},{8,4},{12,8},{16,12},{20,16},{24,20},{28,24},{0,28},{5,1},{9... | collective-permute-start | bytes 155144 | tf_op jit(solution)/shard_map/ppermute | solution.py:18
  26.8 11.7 %collective-permute-start.7 = (bf16[8,2,2,16,101]{4,3,2,1,0:T(8,128)(2,1)S(1)}, bf16[8,2,2,16,101]{4,3,2,1,0:T(8,128)(2,1)S(1)}, u32[]{:S(2)}, u32[]{:S(2)}) collective-permute-start(bf16[8,2,2,16,101]{4,3,2,1,0:T(8,128)(2,1)S(1)} %get-tuple-element.7), channel_id=1, source_target_pairs={{0,4},{1,5},{2,6},{3,7},{4,8},{5,9},{6,10},{7,11},{8,12},{9,13},{1... | collective-permute-start | bytes 310280 | tf_op jit(solution)/shard_map/ppermute | solution.py:146
  27.7 12.8 %collective-permute-start.8 = (bf16[8,2,2,16,101]{4,3,2,1,0:T(8,128)(2,1)S(1)}, bf16[8,2,2,16,101]{4,3,2,1,0:T(8,128)(2,1)S(1)}, u32[]{:S(2)}, u32[]{:S(2)}) collective-permute-start(bf16[8,2,2,16,101]{4,3,2,1,0:T(8,128)(2,1)S(1)} %get-tuple-element.10), channel_id=1, source_target_pairs={{0,6},{1,7},{2,4},{3,5},{4,10},{5,11},{6,8},{7,9},{8,14},{9,15},{1... | collective-permute-start | bytes 310280 | tf_op jit(solution)/shard_map/ppermute | solution.py:146
  30.3 10.3 %collective-permute-start.9 = (bf16[8,2,2,16,101]{4,3,2,1,0:T(8,128)(2,1)S(1)}, bf16[8,2,2,16,101]{4,3,2,1,0:T(8,128)(2,1)S(1)}, u32[]{:S(2)}, u32[]{:S(2)}) collective-permute-start(bf16[8,2,2,16,101]{4,3,2,1,0:T(8,128)(2,1)S(1)} %get-tuple-element.9), channel_id=1, source_target_pairs={{0,5},{1,4},{2,7},{3,6},{4,9},{5,8},{6,11},{7,10},{8,13},{9,12},{1... | collective-permute-start | bytes 310280 | tf_op jit(solution)/shard_map/ppermute | solution.py:146
  30.3 11.6 %collective-permute-start.10 = (bf16[8,2,2,16,101]{4,3,2,1,0:T(8,128)(2,1)S(1)}, bf16[8,2,2,16,101]{4,3,2,1,0:T(8,128)(2,1)S(1)}, u32[]{:S(2)}, u32[]{:S(2)}) collective-permute-start(bf16[8,2,2,16,101]{4,3,2,1,0:T(8,128)(2,1)S(1)} %get-tuple-element.8), channel_id=1, source_target_pairs={{0,7},{1,6},{2,5},{3,4},{4,11},{5,10},{6,9},{7,8},{8,15},{9,14},{1... | collective-permute-start | bytes 310280 | tf_op jit(solution)/shard_map/ppermute | solution.py:146
  34.1 11.4 %collective-permute-start.11 = (bf16[8,2,2,16,101]{4,3,2,1,0:T(8,128)(2,1)S(1)}, bf16[8,2,2,16,101]{4,3,2,1,0:T(8,128)(2,1)S(1)}, u32[]{:S(2)}, u32[]{:S(2)}) collective-permute-start(bf16[8,2,2,16,101]{4,3,2,1,0:T(8,128)(2,1)S(1)} %get-tuple-element.7), channel_id=1, source_target_pairs={{0,8},{1,9},{2,10},{3,11},{4,12},{5,13},{6,14},{7,15},{8,16},{9,17... | collective-permute-start | bytes 310280 | tf_op jit(solution)/shard_map/ppermute | solution.py:146
  38.5 9.6 %collective-permute-start.12 = (bf16[8,2,2,16,101]{4,3,2,1,0:T(8,128)(2,1)S(1)}, bf16[8,2,2,16,101]{4,3,2,1,0:T(8,128)(2,1)S(1)}, u32[]{:S(2)}, u32[]{:S(2)}) collective-permute-start(bf16[8,2,2,16,101]{4,3,2,1,0:T(8,128)(2,1)S(1)} %get-tuple-element.10), channel_id=1, source_target_pairs={{0,10},{1,11},{2,8},{3,9},{4,14},{5,15},{6,12},{7,13},{8,18},{9,19... | collective-permute-start | bytes 310280 | tf_op jit(solution)/shard_map/ppermute | solution.py:146
  40.5 7.7 %collective-permute-start.13 = (bf16[8,2,2,16,101]{4,3,2,1,0:T(8,128)(2,1)S(1)}, bf16[8,2,2,16,101]{4,3,2,1,0:T(8,128)(2,1)S(1)}, u32[]{:S(2)}, u32[]{:S(2)}) collective-permute-start(bf16[8,2,2,16,101]{4,3,2,1,0:T(8,128)(2,1)S(1)} %get-tuple-element.9), channel_id=1, source_target_pairs={{0,9},{1,8},{2,11},{3,10},{4,13},{5,12},{6,15},{7,14},{8,17},{9,16... | collective-permute-start | bytes 310280 | tf_op jit(solution)/shard_map/ppermute | solution.py:146
  40.5 11.6 %collective-permute-start.14 = (bf16[8,2,2,16,101]{4,3,2,1,0:T(8,128)(2,1)S(1)}, bf16[8,2,2,16,101]{4,3,2,1,0:T(8,128)(2,1)S(1)}, u32[]{:S(2)}, u32[]{:S(2)}) collective-permute-start(bf16[8,2,2,16,101]{4,3,2,1,0:T(8,128)(2,1)S(1)} %get-tuple-element.8), channel_id=1, source_target_pairs={{0,11},{1,10},{2,9},{3,8},{4,15},{5,14},{6,13},{7,12},{8,19},{9,18... | collective-permute-start | bytes 310280 | tf_op jit(solution)/shard_map/ppermute | solution.py:146
  41.9 18.8 %collective-permute-start.15 = (bf16[101,2,1,16,64]{0,4,3,2,1:T(8,128)(2,1)S(1)}, bf16[101,2,1,16,64]{0,4,3,2,1:T(8,128)(2,1)S(1)}, u32[]{:S(2)}, u32[]{:S(2)}) collective-permute-start(bf16[101,2,1,16,64]{0,4,3,2,1:T(8,128)(2,1)S(1)} %bitcast.85), channel_id=1, source_target_pairs={{0,2},{1,3},{2,0},{3,1},{4,6},{5,7},{6,4},{7,5},{8,10},{9,11},{10,... | collective-permute-start | bytes 1241096 | tf_op jit(solution)/shard_map/ppermute | solution.py:156
  61.8 5.1 %collective-permute-start.16 = (bf16[101,2,2,16,64]{0,4,3,2,1:T(8,128)(2,1)}, bf16[101,2,2,16,64]{0,4,3,2,1:T(8,128)(2,1)}, u32[]{:S(2)}, u32[]{:S(2)}) collective-permute-start(bf16[101,2,2,16,64]{0,4,3,2,1:T(8,128)(2,1)} %pad_maximum_fusion.13), channel_id=1, source_target_pairs={{0,1},{1,0},{2,3},{3,2},{4,5},{5,4},{6,7},{7,6},{8,9},{9,8},{10,11... | collective-permute-start | bytes 2482184 | tf_op jit(solution)/shard_map/ppermute | solution.py:156

commit v4 on v3

--- a/solution.py
+++ b/solution.py
@@ -120,41 +120,42 @@
     sorted_spec = jnp.take(spectra, chan_order, axis=2)
     sorted_spec = sorted_spec.reshape(spectra.shape[0], 2, chan_count, block_width, FB)
     sorted_spec = jnp.moveaxis(sorted_spec, 2, 0)
+    offsets = [max(1, round_index * chan_count // 4) for round_index in range(ROUNDS)]
     pieces = []
     for distance in range(chan_count):
-        target = jnp.mod(chan_position + distance, chan_count)
-        piece = lax.dynamic_index_in_dim(sorted_spec, target, 0, keepdims=False)
+        wanted = [chan_position + distance] + [chan_position + distance - o for o in offsets]
+        piece = jnp.stack(
+            [lax.dynamic_index_in_dim(sorted_spec, jnp.mod(b, chan_count), 0, keepdims=False) for b in wanted]
+        )
         pieces.append(piece if distance == 0 else shifted(piece, "chan", distance))
-    own = jnp.stack(pieces)
-    masks = [0]
-    step = tm_count // 2
-    while step >= 1:
-        masks = masks + [m ^ step for m in masks]
-        step //= 2
-    grid = [(c, q) for c in range(chan_count) for q in range(tm_count)]
-    partners = []
-    for round_index in range(ROUNDS):
-        offset = max(1, round_index * chan_count // 4)
-        per_source = []
-        for mask in masks:
-            target_tm = jnp.bitwise_xor(tm_position, mask)
-            piece = lax.dynamic_slice_in_dim(own, target_tm * slice_width, slice_width, axis=3)
-            route = [
-                (c * tm_count + q, ((c + offset) % chan_count) * tm_count + (q ^ mask))
-                for c, q in grid
-            ]
-            per_source.append(lax.ppermute(piece, ("chan", "tm"), route))
-        by_time = jnp.stack(per_source)
-        by_time = jnp.roll(by_time, offset, axis=1)
-        partners.append(by_time)
+    exchanged = jnp.stack(pieces)
+    own = exchanged[:, 0]
     windows_here = chan_count * spectra.shape[0]
     own_t = jnp.transpose(own, (4, 2, 0, 1, 3)).reshape(FB, 2, windows_here, block_width)
+    targets = list(range(tm_count))
+    held = []
+    for round_index in range(ROUNDS):
+        block = exchanged[:, 1 + round_index]
+        held.append(jnp.stack([
+            lax.dynamic_slice_in_dim(block, jnp.bitwise_xor(tm_position, r) * slice_width, slice_width, axis=3)
+            for r in targets
+        ])[None])
     gathered = own_t[:, :, None]
     step = tm_count // 2
     while step >= 1:
+        send_at = [n for n, r in enumerate(targets) if r & step]
+        keep_at = [n for n, r in enumerate(targets) if not r & step]
         route = [(q, q ^ step) for q in range(tm_count)]
-        gathered = jnp.concatenate([gathered, lax.ppermute(gathered, "tm", route)], axis=2)
+        payload = (gathered, [h[:, send_at[0]:send_at[-1] + 1] for h in held])
+        got_own, got_held = lax.ppermute(payload, "tm", route)
+        gathered = jnp.concatenate([gathered, got_own], axis=2)
+        held = [
+            jnp.concatenate([h[:, keep_at[0]:keep_at[-1] + 1], g], axis=0)
+            for h, g in zip(held, got_held)
+        ]
+        targets = [targets[n] for n in keep_at]
         step //= 2
+    partners = [h[:, 0] for h in held]
     contraction = 2 * tm_count * windows_here
     own_spec = gathered.reshape(FB, contraction, block_width)
     partner = jnp.concatenate(partners, axis=4)

time: 81.9 us -> 92.4 us (1.13)
  the two profiles are of different devices: /device:TPU:6 before, /device:TPU:13 now
where the time goes in v4:
time: 92.4 us; the launch traced here: 92.1 us
  waiting for transfers between devices  44.6 us (48%)
  starting transfers between devices  17.1 us (19%)
  local copies, waits for them, and re-layouts  12.5 us (14%)
  matrix products  9.06 us (10%)
  other arithmetic  8.5 us (9%)
    ppermute x7, waiting for transfers between devices, shifted(): return lax.ppermute(block, axis, route)  26.6 us
    ppermute x6, waiting for transfers between devices, on_device_local(): got_own, got_held = lax.ppermute(payload, 'tm', route)  18.1 us
    ppermute x7, starting transfers between devices, shifted(): return lax.ppermute(block, axis, route)  10.5 us
    ppermute x6, starting transfers between devices, on_device_local(): got_own, got_held = lax.ppermute(payload, 'tm', route)  6.67 us
    dot_general x1, matrix products, on_device_local(): jnp.einsum('fcrij,cfl->rjil', sums, inverse_table(), precision=lax.Precis...  4.04 us
    reshape x1, local copies, waits for them, and re-layouts, on_device_local(): own_spec = gathered.reshape(FB, contraction, block_width)  3.3 us
    reshape x1, local copies, waits for them, and re-layouts, on_device_local(): both = both.reshape(FB, 2 * ROUNDS * slice_width, contraction)  3.22 us
    dot_general x1, matrix products, on_device_local(): jnp.einsum('fnk,fkj->fnj', both, own_spec, preferred_element_type=jnp.flo...  2.92 us
  transfers between devices with their start and end apart: 13, of which 6 were waited for; matrix products, arithmetic and copies ran while one was open for 9% of the time, Pallas kernels for 0%

profile of v4, /device:TPU:13, one launch (start us, length us, event | category | flops | bytes accessed | tf_op | source)
XLA Modules:
  0.0 92.1 jit_solution(7147941969544683917)
XLA Ops:
  1.6 1.2 %reduce_sum.36 = f32[2,512]{1,0:T(2,128)S(1)} reduce(f32[2,200,512]{2,1,0:T(8,128)} %bitcast.115, f32[]{:T(128)} %constant.265.clone.1), dimensions={1}, to_apply=%region_0.0 | reduce | flops 203776 | bytes 823300 | tf_op jit(solution)/shard_map/reduce_sum | solution.py:97
  5.6 2.3 %gather_fusion = bf16[512,2,2,101]{3,2,1,0:T(2,128)(2,1)S(1)} fusion(bf16[2,2,512,101]{3,1,2,0:T(2,128)(2,1)S(1)} %copy.23, s32[1024]{0:T(1024)S(1)} %pad_clamp_fusion), kind=kCustom, calls=%fused_computation | custom fusion | bytes 829440 | tf_op jit(solution)/shard_map/jit(_take)/gather | solution.py:120
  8.4 1.3 %collective-permute-start.1 = (bf16[3,2,2,64,101]{4,3,2,1,0:T(8,128)(2,1)S(1)}, bf16[3,2,2,64,101]{4,3,2,1,0:T(8,128)(2,1)S(1)}, u32[]{:S(2)}, u32[]{:S(2)}) collective-permute-start(bf16[3,2,2,64,101]{4,3,2,1,0:T(8,128)(2,1)S(1)} %get-tuple-element.43), channel_id=1, source_target_pairs={{24,0},{28,4},{0,8},{4,12},{8,16},{12,20},{16,24},{20,28},{25,1},{... | collective-permute-start | bytes 465416 | tf_op jit(solution)/shard_map/ppermute | solution.py:18
  9.8 1.3 %collective-permute-start = (bf16[3,2,2,64,101]{4,3,2,1,0:T(8,128)(2,1)S(1)}, bf16[3,2,2,64,101]{4,3,2,1,0:T(8,128)(2,1)S(1)}, u32[]{:S(2)}, u32[]{:S(2)}) collective-permute-start(bf16[3,2,2,64,101]{4,3,2,1,0:T(8,128)(2,1)S(1)} %pad_maximum_fusion.6), channel_id=1, source_target_pairs={{28,0},{0,4},{4,8},{8,12},{12,16},{16,20},{20,24},{24,28},{29,1},{... | collective-permute-start | bytes 465416 | tf_op jit(solution)/shard_map/ppermute | solution.py:18
  12.1 1.3 %collective-permute-start.3 = (bf16[3,2,2,64,101]{4,3,2,1,0:T(8,128)(2,1)S(1)}, bf16[3,2,2,64,101]{4,3,2,1,0:T(8,128)(2,1)S(1)}, u32[]{:S(2)}, u32[]{:S(2)}) collective-permute-start(bf16[3,2,2,64,101]{4,3,2,1,0:T(8,128)(2,1)S(1)} %get-tuple-element.41), channel_id=1, source_target_pairs={{16,0},{20,4},{24,8},{28,12},{0,16},{4,20},{8,24},{12,28},{17,1},{... | collective-permute-start | bytes 465416 | tf_op jit(solution)/shard_map/ppermute | solution.py:18
  13.4 1.0 %collective-permute-start.4 = (bf16[3,2,2,64,101]{4,3,2,1,0:T(8,128)(2,1)S(1)}, bf16[3,2,2,64,101]{4,3,2,1,0:T(8,128)(2,1)S(1)}, u32[]{:S(2)}, u32[]{:S(2)}) collective-permute-start(bf16[3,2,2,64,101]{4,3,2,1,0:T(8,128)(2,1)S(1)} %get-tuple-element.40), channel_id=1, source_target_pairs={{12,0},{16,4},{20,8},{24,12},{28,16},{0,20},{4,24},{8,28},{13,1},{... | collective-permute-start | bytes 465416 | tf_op jit(solution)/shard_map/ppermute | solution.py:18
  14.5 3.1 %collective-permute-done = bf16[3,2,2,64,101]{4,3,2,1,0:T(8,128)(2,1)S(1)} collective-permute-done((bf16[3,2,2,64,101]{4,3,2,1,0:T(8,128)(2,1)S(1)}, bf16[3,2,2,64,101]{4,3,2,1,0:T(8,128)(2,1)S(1)}, u32[]{:S(2)}, u32[]{:S(2)}) %collective-permute-start) | collective-permute-done | bytes 155168 | tf_op jit(solution)/shard_map/ppermute | solution.py:18
  17.8 4.3 %collective-permute-start.6 = (bf16[3,2,2,64,101]{4,3,2,1,0:T(8,128)(2,1)S(1)}, bf16[3,2,2,64,101]{4,3,2,1,0:T(8,128)(2,1)S(1)}, u32[]{:S(2)}, u32[]{:S(2)}) collective-permute-start(bf16[3,2,2,64,101]{4,3,2,1,0:T(8,128)(2,1)S(1)} %get-tuple-element.38), channel_id=1, source_target_pairs={{4,0},{8,4},{12,8},{16,12},{20,16},{24,20},{28,24},{0,28},{5,1},{9... | collective-permute-start | bytes 465416 | tf_op jit(solution)/shard_map/ppermute | solution.py:18
  22.2 16.5 %collective-permute-done.2 = bf16[3,2,2,64,101]{4,3,2,1,0:T(8,128)(2,1)S(1)} collective-permute-done((bf16[3,2,2,64,101]{4,3,2,1,0:T(8,128)(2,1)S(1)}, bf16[3,2,2,64,101]{4,3,2,1,0:T(8,128)(2,1)S(1)}, u32[]{:S(2)}, u32[]{:S(2)}) %collective-permute-start.2) | collective-permute-done | bytes 155168 | tf_op jit(solution)/shard_map/ppermute | solution.py:18
  38.7 4.2 %collective-permute-done.3 = bf16[3,2,2,64,101]{4,3,2,1,0:T(8,128)(2,1)S(1)} collective-permute-done((bf16[3,2,2,64,101]{4,3,2,1,0:T(8,128)(2,1)S(1)}, bf16[3,2,2,64,101]{4,3,2,1,0:T(8,128)(2,1)S(1)}, u32[]{:S(2)}, u32[]{:S(2)}) %collective-permute-start.3) | collective-permute-done | bytes 155168 | tf_op jit(solution)/shard_map/ppermute | solution.py:18
  43.0 2.8 %collective-permute-done.5 = bf16[3,2,2,64,101]{4,3,2,1,0:T(8,128)(2,1)S(1)} collective-permute-done((bf16[3,2,2,64,101]{4,3,2,1,0:T(8,128)(2,1)S(1)}, bf16[3,2,2,64,101]{4,3,2,1,0:T(8,128)(2,1)S(1)}, u32[]{:S(2)}, u32[]{:S(2)}) %collective-permute-start.5) | collective-permute-done | bytes 155168 | tf_op jit(solution)/shard_map/ppermute | solution.py:18
  46.1 1.3 %collective-permute-start.11 = (bf16[101,2,1,16,64]{0,4,3,2,1:T(8,128)(2,1)S(1)}, bf16[101,2,1,16,64]{0,4,3,2,1:T(8,128)(2,1)S(1)}, u32[]{:S(2)}, u32[]{:S(2)}) collective-permute-start(bf16[101,2,1,16,64]{0,4,3,2,1:T(8,128)(2,1)S(1)} %bitcast.112), channel_id=1, source_target_pairs={{0,2},{1,3},{2,0},{3,1},{4,6},{5,7},{6,4},{7,5},{8,10},{9,11},{10,... | collective-permute-start | bytes 1241096 | tf_op jit(solution)/shard_map/ppermute | solution.py:150
  48.3 1.3 %collective-permute-start.7 = (bf16[1,2,8,2,2,16,101]{6,5,4,3,2,1,0:T(8,128)(2,1)S(1)}, bf16[1,2,8,2,2,16,101]{6,5,4,3,2,1,0:T(8,128)(2,1)S(1)}, u32[]{:S(2)}, u32[]{:S(2)}) collective-permute-start(bf16[1,2,8,2,2,16,101]{6,5,4,3,2,1,0:T(8,128)(2,1)S(1)} %get-tuple-element.21), channel_id=1, source_target_pairs={{0,2},{1,3},{2,0},{3,1},{4,6},{5,7},{6,4},{7,5},{8,10},{9,11},{10,... | collective-permute-start | bytes 620552 | tf_op jit(solution)/shard_map/ppermute | solution.py:150
  49.9 14.9 %collective-permute-done.9 = bf16[1,2,8,2,2,16,101]{6,5,4,3,2,0,1:T(8,128)(2,1)S(1)} collective-permute-done((bf16[1,2,8,2,2,16,101]{6,5,4,3,2,0,1:T(8,128)(2,1)S(1)}, bf16[1,2,8,2,2,16,101]{6,5,4,3,2,0,1:T(8,128)(2,1)S(1)}, u32[]{:S(2)}, u32[]{:S(2)}) %collective-permute-start.9) | collective-permute-done | bytes 206880 | tf_op jit(solution)/shard_map/ppermute | solution.py:150
  64.9 2.4 %collective-permute-start.10 = (bf16[2,1,8,2,2,16,101]{6,5,4,3,2,0,1:T(8,128)(2,1)S(1)}, bf16[2,1,8,2,2,16,101]{6,5,4,3,2,0,1:T(8,128)(2,1)S(1)}, u32[]{:S(2)}, u32[]{:S(2)}) collective-permute-start(bf16[2,1,8,2,2,16,101]{6,5,4,3,2,0,1:T(8,128)(2,1)S(1)} %get-tuple-element.11), channel_id=1, source_target_pairs={{0,1},{1,0},{2,3},{3,2},{4,5},{5,4},{6,7},{7,6},{8,9},{9,8},{10,11... | collective-permute-start | bytes 620552 | tf_op jit(solution)/shard_map/ppermute | solution.py:150
  67.2 3.1 %collective-permute-done.7 = bf16[1,2,8,2,2,16,101]{6,5,4,3,2,1,0:T(8,128)(2,1)S(1)} collective-permute-done((bf16[1,2,8,2,2,16,101]{6,5,4,3,2,1,0:T(8,128)(2,1)S(1)}, bf16[1,2,8,2,2,16,101]{6,5,4,3,2,1,0:T(8,128)(2,1)S(1)}, u32[]{:S(2)}, u32[]{:S(2)}) %collective-permute-start.7) | collective-permute-done | bytes 206880 | tf_op jit(solution)/shard_map/ppermute | solution.py:150
  70.5 1.4 %collective-permute-start.8 = (bf16[2,1,8,2,2,16,101]{6,5,4,3,2,1,0:T(8,128)(2,1)S(1)}, bf16[2,1,8,2,2,16,101]{6,5,4,3,2,1,0:T(8,128)(2,1)S(1)}, u32[]{:S(2)}, u32[]{:S(2)}) collective-permute-start(bf16[2,1,8,2,2,16,101]{6,5,4,3,2,1,0:T(8,128)(2,1)S(1)} %get-tuple-element.19), channel_id=1, source_target_pairs={{0,1},{1,0},{2,3},{3,2},{4,5},{5,4},{6,7},{7,6},{8,9},{9,8},{10,11... | collective-permute-start | bytes 620552 | tf_op jit(solution)/shard_map/ppermute | solution.py:150
  71.9 1.2 %pad_maximum_fusion.2 = bf16[101,2,2,16,64]{0,4,3,2,1:T(8,128)(2,1)} fusion(bf16[101,2,1,16,64]{0,4,3,2,1:T(8,128)(2,1)S(1)} %collective-permute-done.11, bf16[101,2,1,16,64]{0,4,3,2,1:T(8,128)(2,1)S(1)} %bitcast.113), kind=kLoop, calls=%fused_computation.17 | loop fusion | flops 413696 | bytes 1654784 | tf_op jit(solution)/shard_map/concatenate | solution.py:151
  75.4 3.2 %copy.27 = bf16[101,64,128]{2,1,0:T(8,128)(2,1)} copy(bf16[101,64,128]{0,1,2:T(8,128)(2,1)S(1)} %bitcast.111) | data formatting | bytes 3309568 | tf_op jit(solution)/shard_map/reshape | solution.py:165
  78.6 1.7 %pad_maximum_fusion = bf16[101,2,4,16,64]{0,4,3,2,1:T(8,128)(2,1)S(1)} fusion(bf16[101,2,2,16,64]{0,4,3,2,1:T(8,128)(2,1)} %collective-permute-done.12, bf16[101,2,1,16,64]{0,4,3,2,1:T(8,128)(2,1)S(1)} %collective-permute-done.11, bf16[101,2,1,16,64]{0,4,3,2,1:T(8,128)(2,1)S(1)} %bitcast.114), kind=kLoop, calls=%fused_computation.4 | loop fusion | flops 1654784 | bytes 3309568 | tf_op jit(solution)/shard_map/concatenate | solution.py:151
  80.3 3.3 %copy.28 = bf16[101,128,64]{1,2,0:T(8,128)(2,1)} copy(bf16[101,128,64]{0,2,1:T(8,128)(2,1)S(1)} %bitcast.110) | data formatting | bytes 3309568 | tf_op jit(solution)/shard_map/reshape | solution.py:160
  83.6 2.9 %fusion.63 = f32[101,64,64]{2,1,0:T(8,128)S(1)} fusion(bf16[101,64,128]{2,1,0:T(8,128)(2,1)} %copy.27, bf16[101,128,64]{1,2,0:T(8,128)(2,1)} %copy.28), kind=kOutput, calls=%fused_computation.134 | convolution fusion | flops 105906176 | bytes 4964352 | tf_op jit(solution)/shard_map/fnk,fkj->fnj/dot_general | solution.py:166
  86.5 4.0 %fusion.2 = f32[2,64,16,128]{3,1,2,0:T(8,128)S(1)} fusion(f32[101,2,2,16,64]{4,3,2,1,0:T(8,128)S(1)} %bitcast.109, f32[1,101,128]{2,1,0:T(8,128)S(1)} %get-tuple-element.45, f32[1,101,128]{2,1,0:T(8,128)S(1)} %get-tuple-element.44), kind=kOutput, calls=%fused_computation.5 | convolution fusion | flops 317744384 | bytes 2806784 | tf_op jit(solution)/shard_map/fcrij,cfl->rjil/dot_general | solution.py:168
  90.5 1.6 %copy.30 = f32[2,64,16,128]{3,2,1,0:T(8,128)} copy(f32[2,64,16,128]{3,1,2,0:T(8,128)S(1)} %fusion.2) | data formatting | bytes 2097152 | tf_op jit(solution)/shard_map/fcrij,cfl->rjil/transpose | solution.py:168
  (62 shorter events, 10.1 us)
Async XLA Ops:
  0.0 2.8 %copy-start = (f32[1,400,512]{2,1,0:T(8,128)S(1)}, f32[1,400,512]{2,1,0:T(8,128)}, u32[]{:S(2)}) copy-start(f32[1,400,512]{2,1,0:T(8,128)} %param.3) | copy-start | bytes 2457604
  3.7 0.9 copy-start.1
  8.4 9.4 %collective-permute-start.1 = (bf16[3,2,2,64,101]{4,3,2,1,0:T(8,128)(2,1)S(1)}, bf16[3,2,2,64,101]{4,3,2,1,0:T(8,128)(2,1)S(1)}, u32[]{:S(2)}, u32[]{:S(2)}) collective-permute-start(bf16[3,2,2,64,101]{4,3,2,1,0:T(8,128)(2,1)S(1)} %get-tuple-element.43), channel_id=1, source_target_pairs={{24,0},{28,4},{0,8},{4,12},{8,16},{12,20},{16,24},{20,28},{25,1},{... | collective-permute-start | bytes 465416 | tf_op jit(solution)/shard_map/ppermute | solution.py:18
  9.8 7.7 %collective-permute-start = (bf16[3,2,2,64,101]{4,3,2,1,0:T(8,128)(2,1)S(1)}, bf16[3,2,2,64,101]{4,3,2,1,0:T(8,128)(2,1)S(1)}, u32[]{:S(2)}, u32[]{:S(2)}) collective-permute-start(bf16[3,2,2,64,101]{4,3,2,1,0:T(8,128)(2,1)S(1)} %pad_maximum_fusion.6), channel_id=1, source_target_pairs={{28,0},{0,4},{4,8},{8,12},{12,16},{16,20},{20,24},{24,28},{29,1},{... | collective-permute-start | bytes 465416 | tf_op jit(solution)/shard_map/ppermute | solution.py:18
  11.1 27.5 %collective-permute-start.2 = (bf16[3,2,2,64,101]{4,3,2,1,0:T(8,128)(2,1)S(1)}, bf16[3,2,2,64,101]{4,3,2,1,0:T(8,128)(2,1)S(1)}, u32[]{:S(2)}, u32[]{:S(2)}) collective-permute-start(bf16[3,2,2,64,101]{4,3,2,1,0:T(8,128)(2,1)S(1)} %get-tuple-element.42), channel_id=1, source_target_pairs={{20,0},{24,4},{28,8},{0,12},{4,16},{8,20},{12,24},{16,28},{21,1},{... | collective-permute-start | bytes 465416 | tf_op jit(solution)/shard_map/ppermute | solution.py:18
  12.1 30.8 %collective-permute-start.3 = (bf16[3,2,2,64,101]{4,3,2,1,0:T(8,128)(2,1)S(1)}, bf16[3,2,2,64,101]{4,3,2,1,0:T(8,128)(2,1)S(1)}, u32[]{:S(2)}, u32[]{:S(2)}) collective-permute-start(bf16[3,2,2,64,101]{4,3,2,1,0:T(8,128)(2,1)S(1)} %get-tuple-element.41), channel_id=1, source_target_pairs={{16,0},{20,4},{24,8},{28,12},{0,16},{4,20},{8,24},{12,28},{17,1},{... | collective-permute-start | bytes 465416 | tf_op jit(solution)/shard_map/ppermute | solution.py:18
  13.4 29.5 %collective-permute-start.4 = (bf16[3,2,2,64,101]{4,3,2,1,0:T(8,128)(2,1)S(1)}, bf16[3,2,2,64,101]{4,3,2,1,0:T(8,128)(2,1)S(1)}, u32[]{:S(2)}, u32[]{:S(2)}) collective-permute-start(bf16[3,2,2,64,101]{4,3,2,1,0:T(8,128)(2,1)S(1)} %get-tuple-element.40), channel_id=1, source_target_pairs={{12,0},{16,4},{20,8},{24,12},{28,16},{0,20},{4,24},{8,28},{13,1},{... | collective-permute-start | bytes 465416 | tf_op jit(solution)/shard_map/ppermute | solution.py:18
  17.6 28.2 %collective-permute-start.5 = (bf16[3,2,2,64,101]{4,3,2,1,0:T(8,128)(2,1)S(1)}, bf16[3,2,2,64,101]{4,3,2,1,0:T(8,128)(2,1)S(1)}, u32[]{:S(2)}, u32[]{:S(2)}) collective-permute-start(bf16[3,2,2,64,101]{4,3,2,1,0:T(8,128)(2,1)S(1)} %get-tuple-element.39), channel_id=1, source_target_pairs={{8,0},{12,4},{16,8},{20,12},{24,16},{28,20},{0,24},{4,28},{9,1},{1... | collective-permute-start | bytes 465416 | tf_op jit(solution)/shard_map/ppermute | solution.py:18
  17.8 28.0 %collective-permute-start.6 = (bf16[3,2,2,64,101]{4,3,2,1,0:T(8,128)(2,1)S(1)}, bf16[3,2,2,64,101]{4,3,2,1,0:T(8,128)(2,1)S(1)}, u32[]{:S(2)}, u32[]{:S(2)}) collective-permute-start(bf16[3,2,2,64,101]{4,3,2,1,0:T(8,128)(2,1)S(1)} %get-tuple-element.38), channel_id=1, source_target_pairs={{4,0},{8,4},{12,8},{16,12},{20,16},{24,20},{28,24},{0,28},{5,1},{9... | collective-permute-start | bytes 465416 | tf_op jit(solution)/shard_map/ppermute | solution.py:18
  46.1 25.8 %collective-permute-start.11 = (bf16[101,2,1,16,64]{0,4,3,2,1:T(8,128)(2,1)S(1)}, bf16[101,2,1,16,64]{0,4,3,2,1:T(8,128)(2,1)S(1)}, u32[]{:S(2)}, u32[]{:S(2)}) collective-permute-start(bf16[101,2,1,16,64]{0,4,3,2,1:T(8,128)(2,1)S(1)} %bitcast.112), channel_id=1, source_target_pairs={{0,2},{1,3},{2,0},{3,1},{4,6},{5,7},{6,4},{7,5},{8,10},{9,11},{10,... | collective-permute-start | bytes 1241096 | tf_op jit(solution)/shard_map/ppermute | solution.py:150
  47.8 16.9 %collective-permute-start.9 = (bf16[1,2,8,2,2,16,101]{6,5,4,3,2,0,1:T(8,128)(2,1)S(1)}, bf16[1,2,8,2,2,16,101]{6,5,4,3,2,0,1:T(8,128)(2,1)S(1)}, u32[]{:S(2)}, u32[]{:S(2)}) collective-permute-start(bf16[1,2,8,2,2,16,101]{6,5,4,3,2,0,1:T(8,128)(2,1)S(1)} %get-tuple-element.13), channel_id=1, source_target_pairs={{0,2},{1,3},{2,0},{3,1},{4,6},{5,7},{6,4},{7,5},{8,10},{9,11},{10,... | collective-permute-start | bytes 620552 | tf_op jit(solution)/shard_map/ppermute | solution.py:150
  48.3 22.0 %collective-permute-start.7 = (bf16[1,2,8,2,2,16,101]{6,5,4,3,2,1,0:T(8,128)(2,1)S(1)}, bf16[1,2,8,2,2,16,101]{6,5,4,3,2,1,0:T(8,128)(2,1)S(1)}, u32[]{:S(2)}, u32[]{:S(2)}) collective-permute-start(bf16[1,2,8,2,2,16,101]{6,5,4,3,2,1,0:T(8,128)(2,1)S(1)} %get-tuple-element.21), channel_id=1, source_target_pairs={{0,2},{1,3},{2,0},{3,1},{4,6},{5,7},{6,4},{7,5},{8,10},{9,11},{10,... | collective-permute-start | bytes 620552 | tf_op jit(solution)/shard_map/ppermute | solution.py:150
  64.9 8.3 %collective-permute-start.10 = (bf16[2,1,8,2,2,16,101]{6,5,4,3,2,0,1:T(8,128)(2,1)S(1)}, bf16[2,1,8,2,2,16,101]{6,5,4,3,2,0,1:T(8,128)(2,1)S(1)}, u32[]{:S(2)}, u32[]{:S(2)}) collective-permute-start(bf16[2,1,8,2,2,16,101]{6,5,4,3,2,0,1:T(8,128)(2,1)S(1)} %get-tuple-element.11), channel_id=1, source_target_pairs={{0,1},{1,0},{2,3},{3,2},{4,5},{5,4},{6,7},{7,6},{8,9},{9,8},{10,11... | collective-permute-start | bytes 620552 | tf_op jit(solution)/shard_map/ppermute | solution.py:150
  70.5 2.8 %collective-permute-start.8 = (bf16[2,1,8,2,2,16,101]{6,5,4,3,2,1,0:T(8,128)(2,1)S(1)}, bf16[2,1,8,2,2,16,101]{6,5,4,3,2,1,0:T(8,128)(2,1)S(1)}, u32[]{:S(2)}, u32[]{:S(2)}) collective-permute-start(bf16[2,1,8,2,2,16,101]{6,5,4,3,2,1,0:T(8,128)(2,1)S(1)} %get-tuple-element.19), channel_id=1, source_target_pairs={{0,1},{1,0},{2,3},{3,2},{4,5},{5,4},{6,7},{7,6},{8,9},{9,8},{10,11... | collective-permute-start | bytes 620552 | tf_op jit(solution)/shard_map/ppermute | solution.py:150
  73.1 5.5 %collective-permute-start.12 = (bf16[101,2,2,16,64]{0,4,3,2,1:T(8,128)(2,1)}, bf16[101,2,2,16,64]{0,4,3,2,1:T(8,128)(2,1)}, u32[]{:S(2)}, u32[]{:S(2)}) collective-permute-start(bf16[101,2,2,16,64]{0,4,3,2,1:T(8,128)(2,1)} %pad_maximum_fusion.2), channel_id=1, source_target_pairs={{0,1},{1,0},{2,3},{3,2},{4,5},{5,4},{6,7},{7,6},{8,9},{9,8},{10,11... | collective-permute-start | bytes 2482184 | tf_op jit(solution)/shard_map/ppermute | solution.py:150

commit v5 on v1

--- a/solution.py
+++ b/solution.py
@@ -126,40 +126,30 @@
         piece = lax.dynamic_index_in_dim(sorted_spec, target, 0, keepdims=False)
         pieces.append(piece if distance == 0 else shifted(piece, "chan", distance))
     own = jnp.stack(pieces)
-    grid = [(c, q) for c in range(chan_count) for q in range(tm_count)]
-    partners = []
+    gathered = own[None]
+    step = tm_count // 2
+    while step >= 1:
+        route = [(q, q ^ step) for q in range(tm_count)]
+        gathered = jnp.concatenate([gathered, lax.ppermute(gathered, "tm", route)], axis=0)
+        step //= 2
+    windows_all = gathered.shape[0] * gathered.shape[1] * gathered.shape[2]
+    own_spec = jnp.transpose(gathered, (5, 3, 0, 1, 2, 4)).reshape(FB, 2 * windows_all, block_width)
+    my_slice = lax.dynamic_slice_in_dim(gathered, tm_position * slice_width, slice_width, axis=4)
+    inverse = inverse_table()
+    results = []
     for round_index in range(ROUNDS):
         offset = max(1, round_index * chan_count // 4)
-        per_source = []
-        for tm_shift in range(tm_count):
-            target_tm = jnp.mod(tm_position + tm_shift, tm_count)
-            piece = lax.dynamic_slice_in_dim(own, target_tm * slice_width, slice_width, axis=3)
-            if offset % chan_count == 0 and tm_shift == 0:
-                per_source.append(piece)
-                continue
-            route = [
-                (c * tm_count + q, ((c + offset) % chan_count) * tm_count + (q + tm_shift) % tm_count)
-                for c, q in grid
-            ]
-            per_source.append(lax.ppermute(piece, ("chan", "tm"), route))
-        by_shift = jnp.stack(per_source)
-        by_time = jnp.concatenate([by_shift[::-1], by_shift[::-1]], axis=0)
-        start = jnp.mod(tm_count - 1 - tm_position, tm_count)
-        by_time = lax.dynamic_slice_in_dim(by_time, start, tm_count, axis=0)
-        by_time = jnp.roll(by_time, offset, axis=1)
-        partners.append(by_time)
-    gathered = lax.all_gather(own, "tm", axis=0, tiled=False)
-    windows_all = tm_count * chan_count * spectra.shape[0]
-    own_spec = gathered.reshape(windows_all, 2, block_width, FB)
-    partner = jnp.concatenate(partners, axis=4).reshape(windows_all, 2, ROUNDS * slice_width, FB)
-    rotated = jnp.stack([-partner[:, 1], partner[:, 0]], axis=1)
-    both = jnp.concatenate([partner, rotated], axis=2)
-    sums = jnp.einsum("xcnf,xcjf->fjn", both, own_spec, preferred_element_type=jnp.float32)
-    sums = sums.reshape(FB, block_width, 2, ROUNDS, slice_width)
-    lagged = jnp.einsum(
-        "fjcri,cfl->rjil", sums, inverse_table(), precision=lax.Precision.HIGH
-    )
-    return lagged
+        partner = shifted(my_slice, "chan", offset)
+        partner = jnp.roll(partner, offset, axis=1)
+        rotated = jnp.stack([-partner[:, :, :, 1], partner[:, :, :, 0]], axis=3)
+        both = jnp.stack([partner, rotated])
+        both = jnp.transpose(both, (6, 0, 5, 4, 1, 2, 3)).reshape(FB, 2 * slice_width, 2 * windows_all)
+        sums = jnp.einsum("fnk,fkj->fnj", both, own_spec, preferred_element_type=jnp.float32)
+        sums = sums.reshape(FB, 2, slice_width, block_width)
+        results.append(
+            jnp.einsum("fcij,cfl->jil", sums, inverse, precision=lax.Precision.HIGH)
+        )
+    return jnp.stack(results)
 
 
 def on_device(records, chan_order, live_mask):

time: 103 us -> 81.8 us (0.79)
  waiting for transfers between devices: 12.7 us -> 33.2 us
  starting transfers between devices: 28.8 us -> 15.2 us
  between operations: 13.8 us -> 0.32 us
  local copies, waits for them, and re-layouts: 25.3 us -> 17.3 us
  matrix products: 12.4 us -> 8.23 us
  other arithmetic: 8.65 us -> 7.13 us
    ppermute x8 -> x2, starting transfers between devices: 17.3 us -> 0.67 us  [on_device_local(): lax.ppermute(gathered, 'tm', route)]
    ppermute x7 -> x9, waiting for transfers between devices: 4.49 us -> 18.3 us  [shifted(): return lax.ppermute(block, axis, route)]
    concatenate x1 -> x0, local copies, waits for them, and re-layouts: 7.64 us -> none  [on_device_local(): jnp.concatenate(partners, axis=4)]
    ppermute x8 -> x2, waiting for transfers between devices: 8.18 us -> 14.9 us  [on_device_local(): lax.ppermute(gathered, 'tm', route)]
    dot_general x1 -> x0, local copies, waits for them, and re-layouts: 3.3 us -> none  [on_device_local(): jnp.einsum('xcnf,xcjf->fjn', both, own_spec, preferred_element_type=jnp.f...]
    dot_general x2 -> x4, matrix products: 9.18 us -> 6.13 us  [the longest x2 4.19 us: on_device_local(): jnp.einsum('fcij,cfl->jil', sums, inverse, precision=lax.Precision.HIGH)]
    ppermute x7 -> x9, starting transfers between devices: 11.5 us -> 14.5 us  [shifted(): return lax.ppermute(block, axis, route)]
    slice x4, local copies, waits for them, and re-layouts: 0.08 us -> 1.98 us  [on_device_local(): partner = jnp.roll(partner, offset, axis=1)]
  transfers between devices with their start and end apart: 16 -> 11, of which waited for: 6 -> 7; matrix products, arithmetic and copies ran while one was open for 13% -> 11% of each run, Pallas kernels for 0% -> 0%
where the time goes in v5:
time: 81.8 us; the launch traced here: 81.4 us
  waiting for transfers between devices  33.2 us (41%)
  local copies, waits for them, and re-layouts  17.3 us (21%)
  starting transfers between devices  15.2 us (19%)
  matrix products  8.23 us (10%)
  other arithmetic  7.13 us (9%)
    ppermute x9, waiting for transfers between devices, shifted(): return lax.ppermute(block, axis, route)  18.3 us
    ppermute x2, waiting for transfers between devices, on_device_local(): lax.ppermute(gathered, 'tm', route)  14.9 us
    ppermute x9, starting transfers between devices, shifted(): return lax.ppermute(block, axis, route)  14.5 us
    dot_general x2, matrix products, on_device_local(): jnp.einsum('fcij,cfl->jil', sums, inverse, precision=lax.Precision.HIGH)  4.19 us
    reshape x1, local copies, waits for them, and re-layouts, on_device_local(): jnp.transpose(gathered, (5, 3, 0, 1, 2, 4))  3.79 us
    reshape x2, local copies, waits for them, and re-layouts, on_device_local(): jnp.transpose(both, (6, 0, 5, 4, 1, 2, 3))  3.62 us
    gather x2, local copies, waits for them, and re-layouts, on_device_local(): sorted_spec = jnp.take(spectra, chan_order, axis=2)  2.36 us
    slice x4, local copies, waits for them, and re-layouts, on_device_local(): partner = jnp.roll(partner, offset, axis=1)  1.98 us
  transfers between devices with their start and end apart: 11, of which 7 were waited for; matrix products, arithmetic and copies ran while one was open for 11% of the time, Pallas kernels for 0%

profile of v5, /device:TPU:6, one launch (start us, length us, event | category | flops | bytes accessed | tf_op | source)
XLA Modules:
  0.0 81.4 jit_solution(2628676703228473395)
XLA Ops:
  1.6 1.2 %reduce_sum.36 = f32[2,512]{1,0:T(2,128)S(1)} reduce(f32[2,200,512]{2,1,0:T(8,128)} %bitcast.99, f32[]{:T(128)} %constant.131.clone.1), dimensions={1}, to_apply=%region_0.0 | reduce | flops 203776 | bytes 823300 | tf_op jit(solution)/shard_map/reduce_sum | solution.py:97
  2.8 1.3 %multiply_reduce_fusion = f32[2,512]{1,0:T(2,128)S(1)} fusion(f32[2,200,512]{2,1,0:T(8,128)} %bitcast.100, f32[2,512]{1,0:T(2,128)S(1)} %broadcast_multiply_fusion.1), kind=kLoop, calls=%fused_computation.19 | loop fusion | flops 613376 | bytes 827392 | tf_op jit(solution)/shard_map/reduce_sum | solution.py:99
  6.7 2.3 %gather_fusion = bf16[512,2,2,101]{3,2,1,0:T(2,128)(2,1)S(1)} fusion(bf16[2,2,512,101]{3,1,2,0:T(2,128)(2,1)S(1)} %copy.9, s32[1024]{0:T(1024)S(1)} %pad_clamp_fusion), kind=kCustom, calls=%fused_computation | custom fusion | bytes 829440 | tf_op jit(solution)/shard_map/jit(_take)/gather | solution.py:120
  9.4 1.6 %collective-permute-start = (bf16[2,2,64,101]{3,2,1,0:T(8,128)(2,1)S(1)}, bf16[2,2,64,101]{3,2,1,0:T(8,128)(2,1)S(1)}, u32[]{:S(2)}, u32[]{:S(2)}) collective-permute-start(bf16[2,2,64,101]{3,2,1,0:T(8,128)(2,1)S(1)} %get-tuple-element.17), channel_id=1, source_target_pairs={{28,0},{0,4},{4,8},{8,12},{12,16},{16,20},{20,24},{24,28},{29,1},{... | collective-permute-start | bytes 155144 | tf_op jit(solution)/shard_map/ppermute | solution.py:18
  11.0 1.6 %collective-permute-start.1 = (bf16[2,2,64,101]{3,2,1,0:T(8,128)(2,1)S(1)}, bf16[2,2,64,101]{3,2,1,0:T(8,128)(2,1)S(1)}, u32[]{:S(2)}, u32[]{:S(2)}) collective-permute-start(bf16[2,2,64,101]{3,2,1,0:T(8,128)(2,1)S(1)} %get-tuple-element.16), channel_id=1, source_target_pairs={{24,0},{28,4},{0,8},{4,12},{8,16},{12,20},{16,24},{20,28},{25,1},{... | collective-permute-start | bytes 155144 | tf_op jit(solution)/shard_map/ppermute | solution.py:18
  12.5 2.5 %collective-permute-start.2 = (bf16[2,2,64,101]{3,2,1,0:T(8,128)(2,1)S(1)}, bf16[2,2,64,101]{3,2,1,0:T(8,128)(2,1)S(1)}, u32[]{:S(2)}, u32[]{:S(2)}) collective-permute-start(bf16[2,2,64,101]{3,2,1,0:T(8,128)(2,1)S(1)} %get-tuple-element.15), channel_id=1, source_target_pairs={{20,0},{24,4},{28,8},{0,12},{4,16},{8,20},{12,24},{16,28},{21,1},{... | collective-permute-start | bytes 155144 | tf_op jit(solution)/shard_map/ppermute | solution.py:18
  15.4 2.2 %collective-permute-start.4 = (bf16[2,2,64,101]{3,2,1,0:T(8,128)(2,1)S(1)}, bf16[2,2,64,101]{3,2,1,0:T(8,128)(2,1)S(1)}, u32[]{:S(2)}, u32[]{:S(2)}) collective-permute-start(bf16[2,2,64,101]{3,2,1,0:T(8,128)(2,1)S(1)} %get-tuple-element.13), channel_id=1, source_target_pairs={{12,0},{16,4},{20,8},{24,12},{28,16},{0,20},{4,24},{8,28},{13,1},{... | collective-permute-start | bytes 155144 | tf_op jit(solution)/shard_map/ppermute | solution.py:18
  17.6 1.9 %collective-permute-start.5 = (bf16[2,2,64,101]{3,2,1,0:T(8,128)(2,1)S(1)}, bf16[2,2,64,101]{3,2,1,0:T(8,128)(2,1)S(1)}, u32[]{:S(2)}, u32[]{:S(2)}) collective-permute-start(bf16[2,2,64,101]{3,2,1,0:T(8,128)(2,1)S(1)} %get-tuple-element.12), channel_id=1, source_target_pairs={{8,0},{12,4},{16,8},{20,12},{24,16},{28,20},{0,24},{4,28},{9,1},{1... | collective-permute-start | bytes 155144 | tf_op jit(solution)/shard_map/ppermute | solution.py:18
  19.5 1.5 %collective-permute-start.6 = (bf16[2,2,64,101]{3,2,1,0:T(8,128)(2,1)S(1)}, bf16[2,2,64,101]{3,2,1,0:T(8,128)(2,1)S(1)}, u32[]{:S(2)}, u32[]{:S(2)}) collective-permute-start(bf16[2,2,64,101]{3,2,1,0:T(8,128)(2,1)S(1)} %get-tuple-element.11), channel_id=1, source_target_pairs={{4,0},{8,4},{12,8},{16,12},{20,16},{24,20},{28,24},{0,28},{5,1},{9... | collective-permute-start | bytes 155144 | tf_op jit(solution)/shard_map/ppermute | solution.py:18
  21.0 1.6 %collective-permute-done.3 = bf16[2,2,64,101]{3,2,1,0:T(8,128)(2,1)S(1)} collective-permute-done((bf16[2,2,64,101]{3,2,1,0:T(8,128)(2,1)S(1)}, bf16[2,2,64,101]{3,2,1,0:T(8,128)(2,1)S(1)}, u32[]{:S(2)}, u32[]{:S(2)}) %collective-permute-start.3) | collective-permute-done | bytes 51744 | tf_op jit(solution)/shard_map/ppermute | solution.py:18
  22.7 1.8 %collective-permute-done.4 = bf16[2,2,64,101]{3,2,1,0:T(8,128)(2,1)S(1)} collective-permute-done((bf16[2,2,64,101]{3,2,1,0:T(8,128)(2,1)S(1)}, bf16[2,2,64,101]{3,2,1,0:T(8,128)(2,1)S(1)}, u32[]{:S(2)}, u32[]{:S(2)}) %collective-permute-start.4) | collective-permute-done | bytes 51744 | tf_op jit(solution)/shard_map/ppermute | solution.py:18
  26.2 12.3 %collective-permute-done.7 = bf16[1,8,2,2,64,101]{5,4,3,2,1,0:T(8,128)(2,1)S(1)} collective-permute-done((bf16[1,8,2,2,64,101]{5,4,3,2,1,0:T(8,128)(2,1)S(1)}, bf16[1,8,2,2,64,101]{5,4,3,2,1,0:T(8,128)(2,1)S(1)}, u32[]{:S(2)}, u32[]{:S(2)}) %collective-permute-start.7) | collective-permute-done | bytes 413728 | tf_op jit(solution)/shard_map/ppermute | solution.py:133
  38.8 2.6 %collective-permute-done.8 = bf16[2,8,2,2,64,101]{5,4,3,2,1,0:T(8,128)(2,1)S(1)} collective-permute-done((bf16[2,8,2,2,64,101]{5,4,3,2,1,0:T(8,128)(2,1)S(1)}, bf16[2,8,2,2,64,101]{5,4,3,2,1,0:T(8,128)(2,1)S(1)}, u32[]{:S(2)}, u32[]{:S(2)}) %collective-permute-start.8) | collective-permute-done | bytes 827424 | tf_op jit(solution)/shard_map/ppermute | solution.py:133
  42.8 1.4 %collective-permute-start.9 = (bf16[4,8,2,2,16,101]{5,4,3,2,1,0:T(8,128)(2,1)}, bf16[4,8,2,2,16,101]{5,4,3,2,1,0:T(8,128)(2,1)S(1)}, u32[]{:S(2)}, u32[]{:S(2)}) collective-permute-start(bf16[4,8,2,2,16,101]{5,4,3,2,1,0:T(8,128)(2,1)} %constant_dynamic-slice_fusion), channel_id=1, source_target_pairs={{28,0},{0,4},{4,8},{8,12},{12,16},{16,20},{20,24},{24,28},{29,1},{... | collective-permute-start | bytes 1241096 | tf_op jit(solution)/shard_map/ppermute | solution.py:18
  44.2 1.6 %collective-permute-start.10 = (bf16[4,8,2,2,16,101]{5,4,3,2,1,0:T(8,128)(2,1)}, bf16[4,8,2,2,16,101]{5,4,3,2,1,0:T(8,128)(2,1)}, u32[]{:S(2)}, u32[]{:S(2)}) collective-permute-start(bf16[4,8,2,2,16,101]{5,4,3,2,1,0:T(8,128)(2,1)} %constant_dynamic-slice_fusion), channel_id=1, source_target_pairs={{24,0},{28,4},{0,8},{4,12},{8,16},{12,20},{16,24},{20,28},{25,1},{... | collective-permute-start | bytes 1241096 | tf_op jit(solution)/shard_map/ppermute | solution.py:18
  46.7 1.6 %copy.12 = bf16[101,2,4,8,2,64]{0,5,4,3,2,1:T(8,128)(2,1)} copy(bf16[101,2,4,8,2,64]{0,5,1,4,3,2:T(8,128)(2,1)S(1)} %get-tuple-element.5) | data formatting | bytes 3309568 | tf_op jit(solution)/shard_map/transpose | solution.py:136
  48.3 3.8 %copy.14 = bf16[101,128,64]{1,2,0:T(8,128)(2,1)S(1)} copy(bf16[101,128,64]{0,2,1:T(8,128)(2,1)} %bitcast.94) | data formatting | bytes 3309568 | tf_op jit(solution)/shard_map/reshape | solution.py:136
  52.1 4.9 %collective-permute-done.9 = bf16[4,8,2,2,16,101]{5,4,3,2,1,0:T(8,128)(2,1)S(1)} collective-permute-done((bf16[4,8,2,2,16,101]{5,4,3,2,1,0:T(8,128)(2,1)}, bf16[4,8,2,2,16,101]{5,4,3,2,1,0:T(8,128)(2,1)S(1)}, u32[]{:S(2)}, u32[]{:S(2)}) %collective-permute-start.9) | collective-permute-done | bytes 413728 | tf_op jit(solution)/shard_map/ppermute | solution.py:18
  57.9 1.5 %copy.13 = bf16[101,32,128]{2,1,0:T(8,128)(2,1)S(1)} copy(bf16[101,32,128]{0,1,2:T(8,128)(2,1)S(1)} %bitcast.97) | data formatting | bytes 1654784 | tf_op jit(solution)/shard_map/reshape | solution.py:146
  59.4 8.9 %collective-permute-done.10 = bf16[4,8,2,2,16,101]{5,4,3,2,1,0:T(8,128)(2,1)} collective-permute-done((bf16[4,8,2,2,16,101]{5,4,3,2,1,0:T(8,128)(2,1)}, bf16[4,8,2,2,16,101]{5,4,3,2,1,0:T(8,128)(2,1)}, u32[]{:S(2)}, u32[]{:S(2)}) %collective-permute-start.10) | collective-permute-done | bytes 413728 | tf_op jit(solution)/shard_map/ppermute | solution.py:18
  71.2 2.2 %copy.17 = bf16[101,32,128]{2,1,0:T(8,128)(2,1)} copy(bf16[101,32,128]{0,1,2:T(8,128)(2,1)S(1)} %bitcast.98) | data formatting | bytes 1654784 | tf_op jit(solution)/shard_map/reshape | solution.py:146
  75.5 2.1 %fusion.4 = f32[1,64,16,128]{3,1,2,0:T(8,128)S(1)} fusion(f32[101,2,16,64]{3,2,1,0:T(8,128)S(1)} %bitcast.96, f32[1,101,128]{2,1,0:T(8,128)S(1)} %copy-done.3, f32[1,101,128]{2,1,0:T(8,128)S(1)} %copy-done.2), kind=kOutput, calls=%fused_computation.6 | convolution fusion | flops 158885120 | bytes 1455104 | tf_op jit(solution)/shard_map/fcij,cfl->jil/dot_general | solution.py:150
  77.6 2.1 %fusion.7 = f32[1,64,16,128]{3,1,2,0:T(8,128)S(1)} fusion(f32[101,2,16,64]{3,2,1,0:T(8,128)S(1)} %bitcast.95, f32[1,101,128]{2,1,0:T(8,128)S(1)} %copy-done.3, f32[1,101,128]{2,1,0:T(8,128)S(1)} %copy-done.2), kind=kOutput, calls=%fused_computation.7 | convolution fusion | flops 158885120 | bytes 1455104 | tf_op jit(solution)/shard_map/fcij,cfl->jil/dot_general | solution.py:150
  79.8 1.6 %copy.20 = f32[2,64,16,128]{3,2,1,0:T(8,128)} copy(f32[2,64,16,128]{3,1,2,0:T(8,128)S(1)} %pad_maximum_fusion.2) | data formatting | bytes 2097152 | tf_op jit(solution)/shard_map/stack | solution.py:152
  (64 shorter events, 15.2 us)
Async XLA Ops:
  0.0 4.1 %copy-start.1 = (f32[1,400,512]{2,1,0:T(8,128)S(1)}, f32[1,400,512]{2,1,0:T(8,128)}, u32[]{:S(2)}) copy-start(f32[1,400,512]{2,1,0:T(8,128)} %param.3) | copy-start | bytes 2457604
  4.9 0.9 %copy-start.4 = (s32[512]{0:T(512)S(1)}, s32[512]{0:T(512)}, u32[]{:S(2)}) copy-start(s32[512]{0:T(512)} %param.5) | copy-start | bytes 6148
  9.4 8.2 %collective-permute-start = (bf16[2,2,64,101]{3,2,1,0:T(8,128)(2,1)S(1)}, bf16[2,2,64,101]{3,2,1,0:T(8,128)(2,1)S(1)}, u32[]{:S(2)}, u32[]{:S(2)}) collective-permute-start(bf16[2,2,64,101]{3,2,1,0:T(8,128)(2,1)S(1)} %get-tuple-element.17), channel_id=1, source_target_pairs={{28,0},{0,4},{4,8},{8,12},{12,16},{16,20},{20,24},{24,28},{29,1},{... | collective-permute-start | bytes 155144 | tf_op jit(solution)/shard_map/ppermute | solution.py:18
  11.0 8.5 %collective-permute-start.1 = (bf16[2,2,64,101]{3,2,1,0:T(8,128)(2,1)S(1)}, bf16[2,2,64,101]{3,2,1,0:T(8,128)(2,1)S(1)}, u32[]{:S(2)}, u32[]{:S(2)}) collective-permute-start(bf16[2,2,64,101]{3,2,1,0:T(8,128)(2,1)S(1)} %get-tuple-element.16), channel_id=1, source_target_pairs={{24,0},{28,4},{0,8},{4,12},{8,16},{12,20},{16,24},{20,28},{25,1},{... | collective-permute-start | bytes 155144 | tf_op jit(solution)/shard_map/ppermute | solution.py:18
  12.5 8.4 %collective-permute-start.2 = (bf16[2,2,64,101]{3,2,1,0:T(8,128)(2,1)S(1)}, bf16[2,2,64,101]{3,2,1,0:T(8,128)(2,1)S(1)}, u32[]{:S(2)}, u32[]{:S(2)}) collective-permute-start(bf16[2,2,64,101]{3,2,1,0:T(8,128)(2,1)S(1)} %get-tuple-element.15), channel_id=1, source_target_pairs={{20,0},{24,4},{28,8},{0,12},{4,16},{8,20},{12,24},{16,28},{21,1},{... | collective-permute-start | bytes 155144 | tf_op jit(solution)/shard_map/ppermute | solution.py:18
  15.1 7.6 %collective-permute-start.3 = (bf16[2,2,64,101]{3,2,1,0:T(8,128)(2,1)S(1)}, bf16[2,2,64,101]{3,2,1,0:T(8,128)(2,1)S(1)}, u32[]{:S(2)}, u32[]{:S(2)}) collective-permute-start(bf16[2,2,64,101]{3,2,1,0:T(8,128)(2,1)S(1)} %get-tuple-element.14), channel_id=1, source_target_pairs={{16,0},{20,4},{24,8},{28,12},{0,16},{4,20},{8,24},{12,28},{17,1},{... | collective-permute-start | bytes 155144 | tf_op jit(solution)/shard_map/ppermute | solution.py:18
  15.4 9.0 %collective-permute-start.4 = (bf16[2,2,64,101]{3,2,1,0:T(8,128)(2,1)S(1)}, bf16[2,2,64,101]{3,2,1,0:T(8,128)(2,1)S(1)}, u32[]{:S(2)}, u32[]{:S(2)}) collective-permute-start(bf16[2,2,64,101]{3,2,1,0:T(8,128)(2,1)S(1)} %get-tuple-element.13), channel_id=1, source_target_pairs={{12,0},{16,4},{20,8},{24,12},{28,16},{0,20},{4,24},{8,28},{13,1},{... | collective-permute-start | bytes 155144 | tf_op jit(solution)/shard_map/ppermute | solution.py:18
  17.6 6.8 %collective-permute-start.5 = (bf16[2,2,64,101]{3,2,1,0:T(8,128)(2,1)S(1)}, bf16[2,2,64,101]{3,2,1,0:T(8,128)(2,1)S(1)}, u32[]{:S(2)}, u32[]{:S(2)}) collective-permute-start(bf16[2,2,64,101]{3,2,1,0:T(8,128)(2,1)S(1)} %get-tuple-element.12), channel_id=1, source_target_pairs={{8,0},{12,4},{16,8},{20,12},{24,16},{28,20},{0,24},{4,28},{9,1},{1... | collective-permute-start | bytes 155144 | tf_op jit(solution)/shard_map/ppermute | solution.py:18
  19.5 6.0 %collective-permute-start.6 = (bf16[2,2,64,101]{3,2,1,0:T(8,128)(2,1)S(1)}, bf16[2,2,64,101]{3,2,1,0:T(8,128)(2,1)S(1)}, u32[]{:S(2)}, u32[]{:S(2)}) collective-permute-start(bf16[2,2,64,101]{3,2,1,0:T(8,128)(2,1)S(1)} %get-tuple-element.11), channel_id=1, source_target_pairs={{4,0},{8,4},{12,8},{16,12},{20,16},{24,20},{28,24},{0,28},{5,1},{9... | collective-permute-start | bytes 155144 | tf_op jit(solution)/shard_map/ppermute | solution.py:18
  25.6 12.9 %collective-permute-start.7 = (bf16[1,8,2,2,64,101]{5,4,3,2,1,0:T(8,128)(2,1)S(1)}, bf16[1,8,2,2,64,101]{5,4,3,2,1,0:T(8,128)(2,1)S(1)}, u32[]{:S(2)}, u32[]{:S(2)}) collective-permute-start(bf16[1,8,2,2,64,101]{5,4,3,2,1,0:T(8,128)(2,1)S(1)} %bitcast.103), channel_id=1, source_target_pairs={{0,2},{1,3},{2,0},{3,1},{4,6},{5,7},{6,4},{7,5},{8,10},{9,11},{10,... | collective-permute-start | bytes 1241096 | tf_op jit(solution)/shard_map/ppermute | solution.py:133
  38.7 2.7 %collective-permute-start.8 = (bf16[2,8,2,2,64,101]{5,4,3,2,1,0:T(8,128)(2,1)S(1)}, bf16[2,8,2,2,64,101]{5,4,3,2,1,0:T(8,128)(2,1)S(1)}, u32[]{:S(2)}, u32[]{:S(2)}) collective-permute-start(bf16[2,8,2,2,64,101]{5,4,3,2,1,0:T(8,128)(2,1)S(1)} %pad_maximum_fusion.1), channel_id=1, source_target_pairs={{0,1},{1,0},{2,3},{3,2},{4,5},{5,4},{6,7},{7,6},{8,9},{9,8},{10,11... | collective-permute-start | bytes 2482184 | tf_op jit(solution)/shard_map/ppermute | solution.py:133
  42.8 14.2 %collective-permute-start.9 = (bf16[4,8,2,2,16,101]{5,4,3,2,1,0:T(8,128)(2,1)}, bf16[4,8,2,2,16,101]{5,4,3,2,1,0:T(8,128)(2,1)S(1)}, u32[]{:S(2)}, u32[]{:S(2)}) collective-permute-start(bf16[4,8,2,2,16,101]{5,4,3,2,1,0:T(8,128)(2,1)} %constant_dynamic-slice_fusion), channel_id=1, source_target_pairs={{28,0},{0,4},{4,8},{8,12},{12,16},{16,20},{20,24},{24,28},{29,1},{... | collective-permute-start | bytes 1241096 | tf_op jit(solution)/shard_map/ppermute | solution.py:18
  44.2 24.1 %collective-permute-start.10 = (bf16[4,8,2,2,16,101]{5,4,3,2,1,0:T(8,128)(2,1)}, bf16[4,8,2,2,16,101]{5,4,3,2,1,0:T(8,128)(2,1)}, u32[]{:S(2)}, u32[]{:S(2)}) collective-permute-start(bf16[4,8,2,2,16,101]{5,4,3,2,1,0:T(8,128)(2,1)} %constant_dynamic-slice_fusion), channel_id=1, source_target_pairs={{24,0},{28,4},{0,8},{4,12},{8,16},{12,20},{16,24},{20,28},{25,1},{... | collective-permute-start | bytes 1241096 | tf_op jit(solution)/shard_map/ppermute | solution.py:18
  73.4 1.1 %copy-start = (bf16[101,32,128]{2,1,0:T(8,128)(2,1)S(1)}, bf16[101,32,128]{2,1,0:T(8,128)(2,1)}, u32[]{:S(2)}) copy-start(bf16[101,32,128]{2,1,0:T(8,128)(2,1)} %copy.17) | copy-start | bytes 2482180
  74.5 1.0 %copy-start.2 = (f32[1,101,128]{2,1,0:T(8,128)S(1)}, f32[1,101,128]{2,1,0:T(8,128)}, u32[]{:S(2)}) copy-start(f32[1,101,128]{2,1,0:T(8,128)} %get-tuple-element.20) | copy-start | bytes 155140
  74.5 1.0 %copy-start.3 = (f32[1,101,128]{2,1,0:T(8,128)S(1)}, f32[1,101,128]{2,1,0:T(8,128)}, u32[]{:S(2)}) copy-start(f32[1,101,128]{2,1,0:T(8,128)} %get-tuple-element.21) | copy-start | bytes 155140

commit v6 on v5

--- a/solution.py
+++ b/solution.py
@@ -126,20 +126,92 @@
         piece = lax.dynamic_index_in_dim(sorted_spec, target, 0, keepdims=False)
         pieces.append(piece if distance == 0 else shifted(piece, "chan", distance))
     own = jnp.stack(pieces)
+    offsets = [max(1, round_index * chan_count // 4) for round_index in range(ROUNDS)]
+
+    def send_slices(group):
+        piece = lax.dynamic_slice_in_dim(group, tm_position * slice_width, slice_width, axis=4)
+        return [shifted(piece, "chan", offset) for offset in offsets]
+
     gathered = own[None]
+    partner_groups = [send_slices(gathered)]
     step = tm_count // 2
     while step >= 1:
         route = [(q, q ^ step) for q in range(tm_count)]
-        gathered = jnp.concatenate([gathered, lax.ppermute(gathered, "tm", route)], axis=0)
+        arrived = lax.ppermute(gathered, "tm", route)
+        partner_groups.append(send_slices(arrived))
+        gathered = jnp.concatenate([gathered, arrived], axis=0)
         step //= 2
     windows_all = gathered.shape[0] * gathered.shape[1] * gathered.shape[2]
     own_spec = jnp.transpose(gathered, (5, 3, 0, 1, 2, 4)).reshape(FB, 2 * windows_all, block_width)
-    my_slice = lax.dynamic_slice_in_dim(gathered, tm_position * slice_width, slice_width, axis=4)
     inverse = inverse_table()
     results = []
     for round_index in range(ROUNDS):
         offset = max(1, round_index * chan_count // 4)
-        partner = shifted(my_slice, "chan", offset)
+        partner_block = shifted(own_windows, "chan", offset)
+        source = jnp.mod(position - offset, chan_count)
+        partner_live = lax.dynamic_index_in_dim(live_blocks, source, 0, keepdims=False)
+        partner = whiten_spectra(partner_block, partner_live)
+        lagged = correlate(partner, own_spectra, inverse)
+        lagged = lax.psum_scatter(lagged, "tm", scatter_dimension=1, tiled=True)
+        results.append(lagged)
+    return jnp.stack(results)
+
+
+def whiten_planes(windows, live, precision):
+    window_mean = jnp.mean(windows, axis=-2, keepdims=True)
+    centred = windows - window_mean
+    normed = centred / jnp.sqrt(jnp.mean(centred * centred, axis=-2, keepdims=True) + 1e-05)
+    table = forward_table()
+    real_part = jnp.einsum("wlk,lg->wkg", normed, table[:, :FB], precision=precision)
+    imag_part = jnp.einsum("wlk,lg->wkg", normed, table[:, FB:], precision=precision)
+    power = real_part * real_part + imag_part * imag_part
+    smoothed = jnp.einsum("wkf,fg->wkg", power, smoothing_table(), precision=precision)
+    mean_power = jnp.mean(power, axis=-1, keepdims=True)
+    scale = live.astype(jnp.float32)[:, None] / jnp.sqrt(smoothed + 0.1 * mean_power + 1e-05)
+    return jnp.stack([real_part * scale, imag_part * scale], axis=1).astype(jnp.bfloat16)
+
+
+def on_device_local(records, chan_order, live_mask):
+    chan_count = lax.axis_size("chan")
+    tm_count = lax.axis_size("tm")
+    chan_position = lax.axis_index("chan")
+    tm_position = lax.axis_index("tm")
+    samples, channels = records.shape[1], records.shape[2]
+    block_width = channels // chan_count
+    slice_width = block_width // tm_count
+    windows = records.reshape(samples // L, L, channels)
+    spectra = whiten_planes(windows, live_mask, lax.Precision.HIGH)
+    sorted_spec = jnp.take(spectra, chan_order, axis=2)
+    sorted_spec = sorted_spec.reshape(spectra.shape[0], 2, chan_count, block_width, FB)
+    sorted_spec = jnp.moveaxis(sorted_spec, 2, 0)
+    pieces = []
+    for distance in range(chan_count):
+        target = jnp.mod(chan_position + distance, chan_count)
+        piece = lax.dynamic_index_in_dim(sorted_spec, target, 0, keepdims=False)
+        pieces.append(piece if distance == 0 else shifted(piece, "chan", distance))
+    own = jnp.stack(pieces)
+    offsets = [max(1, round_index * chan_count // 4) for round_index in range(ROUNDS)]
+
+    def send_slices(group):
+        piece = lax.dynamic_slice_in_dim(group, tm_position * slice_width, slice_width, axis=4)
+        return [shifted(piece, "chan", offset) for offset in offsets]
+
+    gathered = own[None]
+    partner_groups = [send_slices(gathered)]
+    step = tm_count // 2
+    while step >= 1:
+        route = [(q, q ^ step) for q in range(tm_count)]
+        arrived = lax.ppermute(gathered, "tm", route)
+        partner_groups.append(send_slices(arrived))
+        gathered = jnp.concatenate([gathered, arrived], axis=0)
+        step //= 2
+    windows_all = gathered.shape[0] * gathered.shape[1] * gathered.shape[2]
+    own_spec = jnp.transpose(gathered, (5, 3, 0, 1, 2, 4)).reshape(FB, 2 * windows_all, block_width)
+    inverse = inverse_table()
+    results = []
+    for round_index in range(ROUNDS):
+        offset = offsets[round_index]
+        partner = jnp.concatenate([group[round_index] for group in partner_groups], axis=0)
         partner = jnp.roll(partner, offset, axis=1)
         rotated = jnp.stack([-partner[:, :, :, 1], partner[:, :, :, 0]], axis=3)
         both = jnp.stack([partner, rotated])

time: 81.8 us -> 82.7 us (1.011)
  starting transfers between devices: 15.2 us -> 23.1 us
  waiting for transfers between devices: 33.2 us -> 27.2 us
  local copies, waits for them, and re-layouts: 17.3 us -> 16.3 us
    ppermute x9 -> x13, starting transfers between devices: 14.5 us -> 22.4 us  [shifted(): return lax.ppermute(block, axis, route)]
    ppermute x9 -> x13, waiting for transfers between devices: 18.3 us -> 14.9 us  [shifted(): return lax.ppermute(block, axis, route)]
    ppermute x2, waiting for transfers between devices: 14.9 us -> 12.3 us  [on_device_local(): arrived = lax.ppermute(gathered, 'tm', route)]
    slice x4, local copies, waits for them, and re-layouts: 1.98 us -> 0.08 us  [on_device_local(): partner = jnp.roll(partner, offset, axis=1)]
    unnamed x17 -> x31, local copies, waits for them, and re-layouts: 0.28 us -> 1.14 us
  transfers between devices with their start and end apart: 11 -> 15, of which waited for: 7 -> 9; matrix products, arithmetic and copies ran while one was open for 11% -> 9% of each run, Pallas kernels for 0% -> 0%
where the time goes in v6:
time: 82.7 us; the launch traced here: 82.4 us
  waiting for transfers between devices  27.2 us (33%)
  starting transfers between devices  23.1 us (28%)
  local copies, waits for them, and re-layouts  16.3 us (20%)
  matrix products  8.23 us (10%)
  other arithmetic  7.12 us (9%)
    ppermute x13, starting transfers between devices, shifted(): return lax.ppermute(block, axis, route)  22.4 us
    ppermute x13, waiting for transfers between devices, shifted(): return lax.ppermute(block, axis, route)  14.9 us
    ppermute x2, waiting for transfers between devices, on_device_local(): arrived = lax.ppermute(gathered, 'tm', route)  12.3 us
    reshape x2, local copies, waits for them, and re-layouts, on_device_local(): jnp.transpose(both, (6, 0, 5, 4, 1, 2, 3))  4.37 us
    dot_general x2, matrix products, on_device_local(): jnp.einsum('fcij,cfl->jil', sums, inverse, precision=lax.Precision.HIGH)  4.19 us
    reshape x1, local copies, waits for them, and re-layouts, on_device_local(): jnp.transpose(gathered, (5, 3, 0, 1, 2, 4))  3.88 us
    gather x2, local copies, waits for them, and re-layouts, on_device_local(): sorted_spec = jnp.take(spectra, chan_order, axis=2)  2.36 us
    dot_general x2, matrix products, on_device_local(): jnp.einsum('fnk,fkj->fnj', both, own_spec, preferred_element_type=jnp.flo...  1.94 us
  transfers between devices with their start and end apart: 15, of which 9 were waited for; matrix products, arithmetic and copies ran while one was open for 9% of the time, Pallas kernels for 0%

profile of v6, /device:TPU:6, one launch (start us, length us, event | category | flops | bytes accessed | tf_op | source)
XLA Modules:
  0.0 82.4 jit_solution(16522557159755574255)
XLA Ops:
  6.7 2.3 %gather_fusion = bf16[512,2,2,101]{3,2,1,0:T(2,128)(2,1)S(1)} fusion(bf16[2,2,512,101]{3,1,2,0:T(2,128)(2,1)S(1)} %copy.9, s32[1024]{0:T(1024)S(1)} %pad_clamp_fusion), kind=kCustom, calls=%fused_computation | custom fusion | bytes 829440 | tf_op jit(solution)/shard_map/jit(_take)/gather | solution.py:184
  9.4 1.6 %collective-permute-start = (bf16[2,2,64,101]{3,2,1,0:T(8,128)(2,1)S(1)}, bf16[2,2,64,101]{3,2,1,0:T(8,128)(2,1)S(1)}, u32[]{:S(2)}, u32[]{:S(2)}) collective-permute-start(bf16[2,2,64,101]{3,2,1,0:T(8,128)(2,1)S(1)} %get-tuple-element.15), channel_id=1, source_target_pairs={{28,0},{0,4},{4,8},{8,12},{12,16},{16,20},{20,24},{24,28},{29,1},{... | collective-permute-start | bytes 155144 | tf_op jit(solution)/shard_map/ppermute | solution.py:18
  11.0 1.6 %collective-permute-start.1 = (bf16[2,2,64,101]{3,2,1,0:T(8,128)(2,1)S(1)}, bf16[2,2,64,101]{3,2,1,0:T(8,128)(2,1)S(1)}, u32[]{:S(2)}, u32[]{:S(2)}) collective-permute-start(bf16[2,2,64,101]{3,2,1,0:T(8,128)(2,1)S(1)} %get-tuple-element.14), channel_id=1, source_target_pairs={{24,0},{28,4},{0,8},{4,12},{8,16},{12,20},{16,24},{20,28},{25,1},{... | collective-permute-start | bytes 155144 | tf_op jit(solution)/shard_map/ppermute | solution.py:18
  12.5 2.5 %collective-permute-start.2 = (bf16[2,2,64,101]{3,2,1,0:T(8,128)(2,1)S(1)}, bf16[2,2,64,101]{3,2,1,0:T(8,128)(2,1)S(1)}, u32[]{:S(2)}, u32[]{:S(2)}) collective-permute-start(bf16[2,2,64,101]{3,2,1,0:T(8,128)(2,1)S(1)} %get-tuple-element.13), channel_id=1, source_target_pairs={{20,0},{24,4},{28,8},{0,12},{4,16},{8,20},{12,24},{16,28},{21,1},{... | collective-permute-start | bytes 155144 | tf_op jit(solution)/shard_map/ppermute | solution.py:18
  15.4 2.2 %collective-permute-start.4 = (bf16[2,2,64,101]{3,2,1,0:T(8,128)(2,1)S(1)}, bf16[2,2,64,101]{3,2,1,0:T(8,128)(2,1)S(1)}, u32[]{:S(2)}, u32[]{:S(2)}) collective-permute-start(bf16[2,2,64,101]{3,2,1,0:T(8,128)(2,1)S(1)} %get-tuple-element.11), channel_id=1, source_target_pairs={{12,0},{16,4},{20,8},{24,12},{28,16},{0,20},{4,24},{8,28},{13,1},{... | collective-permute-start | bytes 155144 | tf_op jit(solution)/shard_map/ppermute | solution.py:18
  17.6 1.9 %collective-permute-start.5 = (bf16[2,2,64,101]{3,2,1,0:T(8,128)(2,1)S(1)}, bf16[2,2,64,101]{3,2,1,0:T(8,128)(2,1)S(1)}, u32[]{:S(2)}, u32[]{:S(2)}) collective-permute-start(bf16[2,2,64,101]{3,2,1,0:T(8,128)(2,1)S(1)} %get-tuple-element.10), channel_id=1, source_target_pairs={{8,0},{12,4},{16,8},{20,12},{24,16},{28,20},{0,24},{4,28},{9,1},{1... | collective-permute-start | bytes 155144 | tf_op jit(solution)/shard_map/ppermute | solution.py:18
  19.5 1.5 %collective-permute-start.6 = (bf16[2,2,64,101]{3,2,1,0:T(8,128)(2,1)S(1)}, bf16[2,2,64,101]{3,2,1,0:T(8,128)(2,1)S(1)}, u32[]{:S(2)}, u32[]{:S(2)}) collective-permute-start(bf16[2,2,64,101]{3,2,1,0:T(8,128)(2,1)S(1)} %get-tuple-element.9), channel_id=1, source_target_pairs={{4,0},{8,4},{12,8},{16,12},{20,16},{24,20},{28,24},{0,28},{5,1},{9... | collective-permute-start | bytes 155144 | tf_op jit(solution)/shard_map/ppermute | solution.py:18
  21.0 1.6 %collective-permute-done.3 = bf16[2,2,64,101]{3,2,1,0:T(8,128)(2,1)S(1)} collective-permute-done((bf16[2,2,64,101]{3,2,1,0:T(8,128)(2,1)S(1)}, bf16[2,2,64,101]{3,2,1,0:T(8,128)(2,1)S(1)}, u32[]{:S(2)}, u32[]{:S(2)}) %collective-permute-start.3) | collective-permute-done | bytes 51744 | tf_op jit(solution)/shard_map/ppermute | solution.py:18
  22.7 1.8 %collective-permute-done.4 = bf16[2,2,64,101]{3,2,1,0:T(8,128)(2,1)S(1)} collective-permute-done((bf16[2,2,64,101]{3,2,1,0:T(8,128)(2,1)S(1)}, bf16[2,2,64,101]{3,2,1,0:T(8,128)(2,1)S(1)}, u32[]{:S(2)}, u32[]{:S(2)}) %collective-permute-start.4) | collective-permute-done | bytes 51744 | tf_op jit(solution)/shard_map/ppermute | solution.py:18
  26.2 12.3 %collective-permute-done.8 = bf16[1,8,2,2,64,101]{5,4,3,2,1,0:T(8,128)(2,1)S(1)} collective-permute-done((bf16[1,8,2,2,64,101]{5,4,3,2,1,0:T(8,128)(2,1)S(1)}, bf16[1,8,2,2,64,101]{5,4,3,2,1,0:T(8,128)(2,1)S(1)}, u32[]{:S(2)}, u32[]{:S(2)}) %collective-permute-start.8) | collective-permute-done | bytes 413728 | tf_op jit(solution)/shard_map/ppermute | solution.py:204
  38.8 1.5 %collective-permute-start.7 = (bf16[1,8,2,2,16,101]{5,4,3,2,1,0:T(8,128)(2,1)S(1)}, bf16[1,8,2,2,16,101]{5,4,3,2,1,0:T(8,128)(2,1)S(1)}, u32[]{:S(2)}, u32[]{:S(2)}) collective-permute-start(bf16[1,8,2,2,16,101]{5,4,3,2,1,0:T(8,128)(2,1)S(1)} %dynamic-slice_bitcast_fusion), channel_id=1, source_target_pairs={{28,0},{0,4},{4,8},{8,12},{12,16},{16,20},{20,24},{24,28},{29,1},{... | collective-permute-start | bytes 310280 | tf_op jit(solution)/shard_map/ppermute | solution.py:18
  41.2 1.4 %collective-permute-start.12 = (bf16[1,8,2,2,16,101]{5,4,3,2,1,0:T(8,128)(2,1)S(1)}, bf16[1,8,2,2,16,101]{5,4,3,2,1,0:T(8,128)(2,1)S(1)}, u32[]{:S(2)}, u32[]{:S(2)}) collective-permute-start(bf16[1,8,2,2,16,101]{5,4,3,2,1,0:T(8,128)(2,1)S(1)} %dynamic-slice_bitcast_fusion), channel_id=1, source_target_pairs={{24,0},{28,4},{0,8},{4,12},{8,16},{12,20},{16,24},{20,28},{25,1},{... | collective-permute-start | bytes 310280 | tf_op jit(solution)/shard_map/ppermute | solution.py:18
  42.6 2.2 %collective-permute-done.7 = bf16[1,8,2,2,16,101]{5,4,3,2,1,0:T(8,128)(2,1)S(1)} collective-permute-done((bf16[1,8,2,2,16,101]{5,4,3,2,1,0:T(8,128)(2,1)S(1)}, bf16[1,8,2,2,16,101]{5,4,3,2,1,0:T(8,128)(2,1)S(1)}, u32[]{:S(2)}, u32[]{:S(2)}) %collective-permute-start.7) | collective-permute-done | bytes 103456 | tf_op jit(solution)/shard_map/ppermute | solution.py:18
  44.8 2.9 %collective-permute-start.9 = (bf16[1,8,2,2,16,101]{5,4,3,2,1,0:T(8,128)(2,1)S(1)}, bf16[1,8,2,2,16,101]{5,4,3,2,1,0:T(8,128)(2,1)S(1)}, u32[]{:S(2)}, u32[]{:S(2)}) collective-permute-start(bf16[1,8,2,2,16,101]{5,4,3,2,1,0:T(8,128)(2,1)S(1)} %constant_dynamic-slice_fusion.1), channel_id=1, source_target_pairs={{28,0},{0,4},{4,8},{8,12},{12,16},{16,20},{20,24},{24,28},{29,1},{... | collective-permute-start | bytes 310280 | tf_op jit(solution)/shard_map/ppermute | solution.py:18
  49.1 2.4 %collective-permute-done.9 = bf16[1,8,2,2,16,101]{5,4,3,2,1,0:T(8,128)(2,1)S(1)} collective-permute-done((bf16[1,8,2,2,16,101]{5,4,3,2,1,0:T(8,128)(2,1)S(1)}, bf16[1,8,2,2,16,101]{5,4,3,2,1,0:T(8,128)(2,1)S(1)}, u32[]{:S(2)}, u32[]{:S(2)}) %collective-permute-start.9) | collective-permute-done | bytes 103456 | tf_op jit(solution)/shard_map/ppermute | solution.py:18
  51.6 3.4 %collective-permute-start.11 = (bf16[2,8,2,2,16,101]{5,4,3,2,1,0:T(8,128)(2,1)S(1)}, bf16[2,8,2,2,16,101]{5,4,3,2,1,0:T(8,128)(2,1)S(1)}, u32[]{:S(2)}, u32[]{:S(2)}) collective-permute-start(bf16[2,8,2,2,16,101]{5,4,3,2,1,0:T(8,128)(2,1)S(1)} %constant_dynamic-slice_fusion), channel_id=1, source_target_pairs={{28,0},{0,4},{4,8},{8,12},{12,16},{16,20},{20,24},{24,28},{29,1},{... | collective-permute-start | bytes 620552 | tf_op jit(solution)/shard_map/ppermute | solution.py:18
  57.9 1.5 %copy.12 = bf16[101,2,4,8,2,64]{0,5,4,3,2,1:T(8,128)(2,1)} copy(bf16[101,2,4,8,2,64]{0,5,1,4,3,2:T(8,128)(2,1)S(1)} %maximum_bitcast_fusion) | data formatting | bytes 3309568 | tf_op jit(solution)/shard_map/transpose | solution.py:209
  59.5 3.9 %copy.14 = bf16[101,128,64]{1,2,0:T(8,128)(2,1)S(1)} copy(bf16[101,128,64]{0,2,1:T(8,128)(2,1)} %bitcast.96) | data formatting | bytes 3309568 | tf_op jit(solution)/shard_map/reshape | solution.py:209
  63.5 4.5 %collective-permute-done.14 = bf16[2,8,2,2,16,101]{5,4,3,2,1,0:T(8,128)(2,1)S(1)} collective-permute-done((bf16[2,8,2,2,16,101]{5,4,3,2,1,0:T(8,128)(2,1)S(1)}, bf16[2,8,2,2,16,101]{5,4,3,2,1,0:T(8,128)(2,1)S(1)}, u32[]{:S(2)}, u32[]{:S(2)}) %collective-permute-start.14) | collective-permute-done | bytes 206880 | tf_op jit(solution)/shard_map/ppermute | solution.py:18
  69.0 2.2 %copy.13 = bf16[101,32,128]{2,1,0:T(8,128)(2,1)} copy(bf16[101,32,128]{0,1,2:T(8,128)(2,1)S(1)} %bitcast.99) | data formatting | bytes 1654784 | tf_op jit(solution)/shard_map/reshape | solution.py:218
  72.2 2.2 %copy.17 = bf16[101,32,128]{2,1,0:T(8,128)(2,1)} copy(bf16[101,32,128]{0,1,2:T(8,128)(2,1)S(1)} %bitcast.100) | data formatting | bytes 1654784 | tf_op jit(solution)/shard_map/reshape | solution.py:218
  76.5 2.1 %fusion.4 = f32[1,64,16,128]{3,1,2,0:T(8,128)S(1)} fusion(f32[101,2,16,64]{3,2,1,0:T(8,128)S(1)} %bitcast.98, f32[1,101,128]{2,1,0:T(8,128)S(1)} %copy-done.8, f32[1,101,128]{2,1,0:T(8,128)S(1)} %copy-done.7), kind=kOutput, calls=%fused_computation.6 | convolution fusion | flops 158885120 | bytes 1455104 | tf_op jit(solution)/shard_map/fcij,cfl->jil/dot_general | solution.py:222
  78.6 2.1 %fusion.7 = f32[1,64,16,128]{3,1,2,0:T(8,128)S(1)} fusion(f32[101,2,16,64]{3,2,1,0:T(8,128)S(1)} %bitcast.97, f32[1,101,128]{2,1,0:T(8,128)S(1)} %copy-done.8, f32[1,101,128]{2,1,0:T(8,128)S(1)} %copy-done.7), kind=kOutput, calls=%fused_computation.7 | convolution fusion | flops 158885120 | bytes 1455104 | tf_op jit(solution)/shard_map/fcij,cfl->jil/dot_general | solution.py:222
  80.8 1.6 %copy.20 = f32[2,64,16,128]{3,2,1,0:T(8,128)} copy(f32[2,64,16,128]{3,1,2,0:T(8,128)S(1)} %pad_maximum_fusion.1) | data formatting | bytes 2097152 | tf_op jit(solution)/shard_map/stack | solution.py:224
  (90 shorter events, 19.0 us)
Async XLA Ops:
  0.0 4.1 %copy-start.2 = (f32[1,400,512]{2,1,0:T(8,128)S(1)}, f32[1,400,512]{2,1,0:T(8,128)}, u32[]{:S(2)}) copy-start(f32[1,400,512]{2,1,0:T(8,128)} %param.3) | copy-start | bytes 2457604
  4.9 0.9 %copy-start.9 = (s32[512]{0:T(512)S(1)}, s32[512]{0:T(512)}, u32[]{:S(2)}) copy-start(s32[512]{0:T(512)} %param.5) | copy-start | bytes 6148
  9.4 8.2 %collective-permute-start = (bf16[2,2,64,101]{3,2,1,0:T(8,128)(2,1)S(1)}, bf16[2,2,64,101]{3,2,1,0:T(8,128)(2,1)S(1)}, u32[]{:S(2)}, u32[]{:S(2)}) collective-permute-start(bf16[2,2,64,101]{3,2,1,0:T(8,128)(2,1)S(1)} %get-tuple-element.15), channel_id=1, source_target_pairs={{28,0},{0,4},{4,8},{8,12},{12,16},{16,20},{20,24},{24,28},{29,1},{... | collective-permute-start | bytes 155144 | tf_op jit(solution)/shard_map/ppermute | solution.py:18
  11.0 8.5 %collective-permute-start.1 = (bf16[2,2,64,101]{3,2,1,0:T(8,128)(2,1)S(1)}, bf16[2,2,64,101]{3,2,1,0:T(8,128)(2,1)S(1)}, u32[]{:S(2)}, u32[]{:S(2)}) collective-permute-start(bf16[2,2,64,101]{3,2,1,0:T(8,128)(2,1)S(1)} %get-tuple-element.14), channel_id=1, source_target_pairs={{24,0},{28,4},{0,8},{4,12},{8,16},{12,20},{16,24},{20,28},{25,1},{... | collective-permute-start | bytes 155144 | tf_op jit(solution)/shard_map/ppermute | solution.py:18
  12.5 8.4 %collective-permute-start.2 = (bf16[2,2,64,101]{3,2,1,0:T(8,128)(2,1)S(1)}, bf16[2,2,64,101]{3,2,1,0:T(8,128)(2,1)S(1)}, u32[]{:S(2)}, u32[]{:S(2)}) collective-permute-start(bf16[2,2,64,101]{3,2,1,0:T(8,128)(2,1)S(1)} %get-tuple-element.13), channel_id=1, source_target_pairs={{20,0},{24,4},{28,8},{0,12},{4,16},{8,20},{12,24},{16,28},{21,1},{... | collective-permute-start | bytes 155144 | tf_op jit(solution)/shard_map/ppermute | solution.py:18
  15.1 7.6 %collective-permute-start.3 = (bf16[2,2,64,101]{3,2,1,0:T(8,128)(2,1)S(1)}, bf16[2,2,64,101]{3,2,1,0:T(8,128)(2,1)S(1)}, u32[]{:S(2)}, u32[]{:S(2)}) collective-permute-start(bf16[2,2,64,101]{3,2,1,0:T(8,128)(2,1)S(1)} %get-tuple-element.12), channel_id=1, source_target_pairs={{16,0},{20,4},{24,8},{28,12},{0,16},{4,20},{8,24},{12,28},{17,1},{... | collective-permute-start | bytes 155144 | tf_op jit(solution)/shard_map/ppermute | solution.py:18
  15.4 9.0 %collective-permute-start.4 = (bf16[2,2,64,101]{3,2,1,0:T(8,128)(2,1)S(1)}, bf16[2,2,64,101]{3,2,1,0:T(8,128)(2,1)S(1)}, u32[]{:S(2)}, u32[]{:S(2)}) collective-permute-start(bf16[2,2,64,101]{3,2,1,0:T(8,128)(2,1)S(1)} %get-tuple-element.11), channel_id=1, source_target_pairs={{12,0},{16,4},{20,8},{24,12},{28,16},{0,20},{4,24},{8,28},{13,1},{... | collective-permute-start | bytes 155144 | tf_op jit(solution)/shard_map/ppermute | solution.py:18
  17.6 6.8 %collective-permute-start.5 = (bf16[2,2,64,101]{3,2,1,0:T(8,128)(2,1)S(1)}, bf16[2,2,64,101]{3,2,1,0:T(8,128)(2,1)S(1)}, u32[]{:S(2)}, u32[]{:S(2)}) collective-permute-start(bf16[2,2,64,101]{3,2,1,0:T(8,128)(2,1)S(1)} %get-tuple-element.10), channel_id=1, source_target_pairs={{8,0},{12,4},{16,8},{20,12},{24,16},{28,20},{0,24},{4,28},{9,1},{1... | collective-permute-start | bytes 155144 | tf_op jit(solution)/shard_map/ppermute | solution.py:18
  19.5 6.0 %collective-permute-start.6 = (bf16[2,2,64,101]{3,2,1,0:T(8,128)(2,1)S(1)}, bf16[2,2,64,101]{3,2,1,0:T(8,128)(2,1)S(1)}, u32[]{:S(2)}, u32[]{:S(2)}) collective-permute-start(bf16[2,2,64,101]{3,2,1,0:T(8,128)(2,1)S(1)} %get-tuple-element.9), channel_id=1, source_target_pairs={{4,0},{8,4},{12,8},{16,12},{20,16},{24,20},{28,24},{0,28},{5,1},{9... | collective-permute-start | bytes 155144 | tf_op jit(solution)/shard_map/ppermute | solution.py:18
  25.6 12.9 %collective-permute-start.8 = (bf16[1,8,2,2,64,101]{5,4,3,2,1,0:T(8,128)(2,1)S(1)}, bf16[1,8,2,2,64,101]{5,4,3,2,1,0:T(8,128)(2,1)S(1)}, u32[]{:S(2)}, u32[]{:S(2)}) collective-permute-start(bf16[1,8,2,2,64,101]{5,4,3,2,1,0:T(8,128)(2,1)S(1)} %bitcast.105), channel_id=1, source_target_pairs={{0,2},{1,3},{2,0},{3,1},{4,6},{5,7},{6,4},{7,5},{8,10},{9,11},{10,... | collective-permute-start | bytes 1241096 | tf_op jit(solution)/shard_map/ppermute | solution.py:204
  38.7 12.9 %collective-permute-start.10 = (bf16[2,8,2,2,64,101]{5,4,3,2,1,0:T(8,128)(2,1)S(1)}, bf16[2,8,2,2,64,101]{5,4,3,2,1,0:T(8,128)(2,1)S(1)}, u32[]{:S(2)}, u32[]{:S(2)}) collective-permute-start(bf16[2,8,2,2,64,101]{5,4,3,2,1,0:T(8,128)(2,1)S(1)} %pad_maximum_fusion), channel_id=1, source_target_pairs={{0,1},{1,0},{2,3},{3,2},{4,5},{5,4},{6,7},{7,6},{8,9},{9,8},{10,11... | collective-permute-start | bytes 2482184 | tf_op jit(solution)/shard_map/ppermute | solution.py:204
  38.8 5.9 %collective-permute-start.7 = (bf16[1,8,2,2,16,101]{5,4,3,2,1,0:T(8,128)(2,1)S(1)}, bf16[1,8,2,2,16,101]{5,4,3,2,1,0:T(8,128)(2,1)S(1)}, u32[]{:S(2)}, u32[]{:S(2)}) collective-permute-start(bf16[1,8,2,2,16,101]{5,4,3,2,1,0:T(8,128)(2,1)S(1)} %dynamic-slice_bitcast_fusion), channel_id=1, source_target_pairs={{28,0},{0,4},{4,8},{8,12},{12,16},{16,20},{20,24},{24,28},{29,1},{... | collective-permute-start | bytes 310280 | tf_op jit(solution)/shard_map/ppermute | solution.py:18
  41.2 7.4 %collective-permute-start.12 = (bf16[1,8,2,2,16,101]{5,4,3,2,1,0:T(8,128)(2,1)S(1)}, bf16[1,8,2,2,16,101]{5,4,3,2,1,0:T(8,128)(2,1)S(1)}, u32[]{:S(2)}, u32[]{:S(2)}) collective-permute-start(bf16[1,8,2,2,16,101]{5,4,3,2,1,0:T(8,128)(2,1)S(1)} %dynamic-slice_bitcast_fusion), channel_id=1, source_target_pairs={{24,0},{28,4},{0,8},{4,12},{8,16},{12,20},{16,24},{20,28},{25,1},{... | collective-permute-start | bytes 310280 | tf_op jit(solution)/shard_map/ppermute | solution.py:18
  44.8 6.7 %collective-permute-start.9 = (bf16[1,8,2,2,16,101]{5,4,3,2,1,0:T(8,128)(2,1)S(1)}, bf16[1,8,2,2,16,101]{5,4,3,2,1,0:T(8,128)(2,1)S(1)}, u32[]{:S(2)}, u32[]{:S(2)}) collective-permute-start(bf16[1,8,2,2,16,101]{5,4,3,2,1,0:T(8,128)(2,1)S(1)} %constant_dynamic-slice_fusion.1), channel_id=1, source_target_pairs={{28,0},{0,4},{4,8},{8,12},{12,16},{16,20},{20,24},{24,28},{29,1},{... | collective-permute-start | bytes 310280 | tf_op jit(solution)/shard_map/ppermute | solution.py:18
  48.6 6.8 %collective-permute-start.13 = (bf16[1,8,2,2,16,101]{5,4,3,2,1,0:T(8,128)(2,1)S(1)}, bf16[1,8,2,2,16,101]{5,4,3,2,1,0:T(8,128)(2,1)S(1)}, u32[]{:S(2)}, u32[]{:S(2)}) collective-permute-start(bf16[1,8,2,2,16,101]{5,4,3,2,1,0:T(8,128)(2,1)S(1)} %constant_dynamic-slice_fusion.1), channel_id=1, source_target_pairs={{24,0},{28,4},{0,8},{4,12},{8,16},{12,20},{16,24},{20,28},{25,1},{... | collective-permute-start | bytes 310280 | tf_op jit(solution)/shard_map/ppermute | solution.py:18
  51.5 3.9 %copy-start.5 = (bf16[4,8,2,2,16,101]{5,4,3,2,1,0:T(8,128)(2,1)}, bf16[4,8,2,2,16,101]{5,4,3,2,1,0:T(8,128)(2,1)S(1)}, u32[]{:S(2)}) copy-start(bf16[4,8,2,2,16,101]{5,4,3,2,1,0:T(8,128)(2,1)S(1)} %constant_dynamic-update-slice_fusion.1) | copy-start | bytes 1241092
  51.6 11.8 %collective-permute-start.11 = (bf16[2,8,2,2,16,101]{5,4,3,2,1,0:T(8,128)(2,1)S(1)}, bf16[2,8,2,2,16,101]{5,4,3,2,1,0:T(8,128)(2,1)S(1)}, u32[]{:S(2)}, u32[]{:S(2)}) collective-permute-start(bf16[2,8,2,2,16,101]{5,4,3,2,1,0:T(8,128)(2,1)S(1)} %constant_dynamic-slice_fusion), channel_id=1, source_target_pairs={{28,0},{0,4},{4,8},{8,12},{12,16},{16,20},{20,24},{24,28},{29,1},{... | collective-permute-start | bytes 620552 | tf_op jit(solution)/shard_map/ppermute | solution.py:18
  56.2 11.8 %collective-permute-start.14 = (bf16[2,8,2,2,16,101]{5,4,3,2,1,0:T(8,128)(2,1)S(1)}, bf16[2,8,2,2,16,101]{5,4,3,2,1,0:T(8,128)(2,1)S(1)}, u32[]{:S(2)}, u32[]{:S(2)}) collective-permute-start(bf16[2,8,2,2,16,101]{5,4,3,2,1,0:T(8,128)(2,1)S(1)} %constant_dynamic-slice_fusion), channel_id=1, source_target_pairs={{24,0},{28,4},{0,8},{4,12},{8,16},{12,20},{16,24},{20,28},{25,1},{... | collective-permute-start | bytes 620552 | tf_op jit(solution)/shard_map/ppermute | solution.py:18
  59.5 3.9 %copy-start.6 = (bf16[4,8,2,2,16,101]{5,4,3,2,1,0:T(8,128)(2,1)S(1)}, bf16[4,8,2,2,16,101]{5,4,3,2,1,0:T(8,128)(2,1)}, u32[]{:S(2)}) copy-start(bf16[4,8,2,2,16,101]{5,4,3,2,1,0:T(8,128)(2,1)} %copy-done.5) | copy-start | bytes 1241092
  59.5 8.5 %copy-start.4 = (bf16[4,8,2,2,16,101]{5,4,3,2,1,0:T(8,128)(2,1)S(1)}, bf16[4,8,2,2,16,101]{5,4,3,2,1,0:T(8,128)(2,1)}, u32[]{:S(2)}) copy-start(bf16[4,8,2,2,16,101]{5,4,3,2,1,0:T(8,128)(2,1)} %copy-done.3) | copy-start | bytes 1241092
  71.8 2.5 %copy-start = (bf16[101,32,128]{2,1,0:T(8,128)(2,1)S(1)}, bf16[101,32,128]{2,1,0:T(8,128)(2,1)}, u32[]{:S(2)}) copy-start(bf16[101,32,128]{2,1,0:T(8,128)(2,1)} %copy.13) | copy-start | bytes 2482180
  74.4 1.1 %copy-start.1 = (bf16[101,32,128]{2,1,0:T(8,128)(2,1)S(1)}, bf16[101,32,128]{2,1,0:T(8,128)(2,1)}, u32[]{:S(2)}) copy-start(bf16[101,32,128]{2,1,0:T(8,128)(2,1)} %copy.17) | copy-start | bytes 2482180
  75.5 1.0 %copy-start.7 = (f32[1,101,128]{2,1,0:T(8,128)S(1)}, f32[1,101,128]{2,1,0:T(8,128)}, u32[]{:S(2)}) copy-start(f32[1,101,128]{2,1,0:T(8,128)} %get-tuple-element.18) | copy-start | bytes 155140
  75.5 1.0 %copy-start.8 = (f32[1,101,128]{2,1,0:T(8,128)S(1)}, f32[1,101,128]{2,1,0:T(8,128)}, u32[]{:S(2)}) copy-start(f32[1,101,128]{2,1,0:T(8,128)} %get-tuple-element.19) | copy-start | bytes 155140
  (1 other events, 0.8 us)

commit v7 on v5

--- a/solution.py
+++ b/solution.py
@@ -4,6 +4,7 @@
 import jax.numpy as jnp
 from jax import lax
 from jax.sharding import PartitionSpec as P
+
 
 L = 200
 FB = 101
@@ -126,25 +127,44 @@
         piece = lax.dynamic_index_in_dim(sorted_spec, target, 0, keepdims=False)
         pieces.append(piece if distance == 0 else shifted(piece, "chan", distance))
     own = jnp.stack(pieces)
+    offsets = [max(1, round_index * chan_count // 4) for round_index in range(ROUNDS)]
+
+    def send_slices(group):
+        piece = lax.dynamic_slice_in_dim(group, tm_position * slice_width, slice_width, axis=4)
+        return [shifted(piece, "chan", offset) for offset in offsets]
+
     gathered = own[None]
+    partner_groups = [send_slices(gathered)]
     step = tm_count // 2
     while step >= 1:
         route = [(q, q ^ step) for q in range(tm_count)]
-        gathered = jnp.concatenate([gathered, lax.ppermute(gathered, "tm", route)], axis=0)
+        arrived = lax.ppermute(gathered, "tm", route)
+        partner_groups.append(send_slices(arrived))
+        gathered = jnp.concatenate([gathered, arrived], axis=0)
         step //= 2
-    windows_all = gathered.shape[0] * gathered.shape[1] * gathered.shape[2]
-    own_spec = jnp.transpose(gathered, (5, 3, 0, 1, 2, 4)).reshape(FB, 2 * windows_all, block_width)
-    my_slice = lax.dynamic_slice_in_dim(gathered, tm_position * slice_width, slice_width, axis=4)
+    early = 2 if gathered.shape[0] > 2 else gathered.shape[0]
+    groups = [(0, early), (early, gathered.shape[0])] if early < gathered.shape[0] else [(0, early)]
+
+    def own_operand(lo, hi):
+        part = gathered[lo:hi]
+        width = 2 * part.shape[0] * part.shape[1] * part.shape[2]
+        return jnp.transpose(part, (5, 3, 0, 1, 2, 4)).reshape(FB, width, block_width)
+
+    own_ops = [own_operand(lo, hi) for lo, hi in groups]
     inverse = inverse_table()
     results = []
     for round_index in range(ROUNDS):
-        offset = max(1, round_index * chan_count // 4)
-        partner = shifted(my_slice, "chan", offset)
+        offset = offsets[round_index]
+        partner = jnp.concatenate([group[round_index] for group in partner_groups], axis=0)
         partner = jnp.roll(partner, offset, axis=1)
-        rotated = jnp.stack([-partner[:, :, :, 1], partner[:, :, :, 0]], axis=3)
-        both = jnp.stack([partner, rotated])
-        both = jnp.transpose(both, (6, 0, 5, 4, 1, 2, 3)).reshape(FB, 2 * slice_width, 2 * windows_all)
-        sums = jnp.einsum("fnk,fkj->fnj", both, own_spec, preferred_element_type=jnp.float32)
+        sums = None
+        for (lo, hi), own_op in zip(groups, own_ops):
+            part = partner[lo:hi]
+            rotated = jnp.stack([-part[:, :, :, 1], part[:, :, :, 0]], axis=3)
+            both = jnp.stack([part, rotated])
+            both = jnp.transpose(both, (6, 0, 5, 4, 1, 2, 3)).reshape(FB, 2 * slice_width, own_op.shape[1])
+            term = jnp.einsum("fnk,fkj->fnj", both, own_op, preferred_element_type=jnp.float32)
+            sums = term if sums is None else sums + term
         sums = sums.reshape(FB, 2, slice_width, block_width)
         results.append(
             jnp.einsum("fcij,cfl->jil", sums, inverse, precision=lax.Precision.HIGH)

time: 81.8 us -> 112 us (1.37)
  the two profiles are of different devices: /device:TPU:6 before, /device:TPU:0 now
where the time goes in v7:
time: 112 us
  local copies, waits for them, and re-layouts  42.9 us (38%)
  starting transfers between devices  24.8 us (22%)
  waiting for transfers between devices  21 us (19%)
  other arithmetic  12.7 us (11%)
  matrix products  9.86 us (9%)
    ppermute x13, starting transfers between devices, shifted(): return lax.ppermute(block, axis, route)  23.3 us
    reshape x4, local copies, waits for them, and re-layouts, on_device_local(): jnp.transpose(both, (6, 0, 5, 4, 1, 2, 3))  13.4 us
    ppermute x13, waiting for transfers between devices, shifted(): return lax.ppermute(block, axis, route)  10.9 us
    ppermute x2, waiting for transfers between devices, on_device_local(): arrived = lax.ppermute(gathered, 'tm', route)  10.1 us
    transpose x2, local copies, waits for them, and re-layouts, own_operand(): jnp.transpose(part, (5, 3, 0, 1, 2, 4)).reshape(FB, width, block_width)  6.62 us
    unnamed x23, local copies, waits for them, and re-layouts  5.16 us
    slice x4, local copies, waits for them, and re-layouts, on_device_local(): partner = jnp.roll(partner, offset, axis=1)  4.61 us
    dot_general x2, matrix products, on_device_local(): jnp.einsum('fcij,cfl->jil', sums, inverse, precision=lax.Precision.HIGH)  4.19 us
  transfers between devices with their start and end apart: 15, of which 9 were waited for; matrix products, arithmetic and copies ran while one was open for 14% of the time, Pallas kernels for 0%

profile of v7, /device:TPU:0, one launch (start us, length us, event | category | flops | bytes accessed | tf_op | source)
XLA Modules:
  0.0 111.5 jit_solution(11774564882698437436)
XLA Ops:
  6.7 2.3 %gather_fusion = bf16[512,2,2,101]{3,2,1,0:T(2,128)(2,1)S(1)} fusion(bf16[2,2,512,101]{3,1,2,0:T(2,128)(2,1)S(1)} %copy.11, s32[1024]{0:T(1024)S(1)} %pad_clamp_fusion), kind=kCustom, calls=%fused_computation | custom fusion | bytes 829440 | tf_op jit(solution)/shard_map/jit(_take)/gather | solution.py:121
  9.4 3.0 %collective-permute-start = (bf16[2,2,64,101]{3,2,1,0:T(8,128)(2,1)S(1)}, bf16[2,2,64,101]{3,2,1,0:T(8,128)(2,1)S(1)}, u32[]{:S(2)}, u32[]{:S(2)}) collective-permute-start(bf16[2,2,64,101]{3,2,1,0:T(8,128)(2,1)S(1)} %get-tuple-element.25), channel_id=1, source_target_pairs={{28,0},{0,4},{4,8},{8,12},{12,16},{16,20},{20,24},{24,28},{29,1},{... | collective-permute-start | bytes 155144 | tf_op jit(solution)/shard_map/ppermute | solution.py:19
  14.0 2.5 %collective-permute-start.2 = (bf16[2,2,64,101]{3,2,1,0:T(8,128)(2,1)S(1)}, bf16[2,2,64,101]{3,2,1,0:T(8,128)(2,1)S(1)}, u32[]{:S(2)}, u32[]{:S(2)}) collective-permute-start(bf16[2,2,64,101]{3,2,1,0:T(8,128)(2,1)S(1)} %get-tuple-element.23), channel_id=1, source_target_pairs={{20,0},{24,4},{28,8},{0,12},{4,16},{8,20},{12,24},{16,28},{21,1},{... | collective-permute-start | bytes 155144 | tf_op jit(solution)/shard_map/ppermute | solution.py:19
  17.8 2.6 %collective-permute-start.4 = (bf16[2,2,64,101]{3,2,1,0:T(8,128)(2,1)S(1)}, bf16[2,2,64,101]{3,2,1,0:T(8,128)(2,1)S(1)}, u32[]{:S(2)}, u32[]{:S(2)}) collective-permute-start(bf16[2,2,64,101]{3,2,1,0:T(8,128)(2,1)S(1)} %get-tuple-element.21), channel_id=1, source_target_pairs={{12,0},{16,4},{20,8},{24,12},{28,16},{0,20},{4,24},{8,28},{13,1},{... | collective-permute-start | bytes 155144 | tf_op jit(solution)/shard_map/ppermute | solution.py:19
  28.0 10.1 %collective-permute-done.8 = bf16[1,8,2,2,64,101]{5,4,3,2,1,0:T(8,128)(2,1)S(1)} collective-permute-done((bf16[1,8,2,2,64,101]{5,4,3,2,1,0:T(8,128)(2,1)S(1)}, bf16[1,8,2,2,64,101]{5,4,3,2,1,0:T(8,128)(2,1)S(1)}, u32[]{:S(2)}, u32[]{:S(2)}) %collective-permute-start.8) | collective-permute-done | bytes 413728 | tf_op jit(solution)/shard_map/ppermute | solution.py:141
  39.3 3.4 %collective-permute-start.7 = (bf16[1,8,2,2,16,101]{5,4,3,2,1,0:T(8,128)(2,1)S(1)}, bf16[1,8,2,2,16,101]{5,4,3,2,1,0:T(8,128)(2,1)S(1)}, u32[]{:S(2)}, u32[]{:S(2)}) collective-permute-start(bf16[1,8,2,2,16,101]{5,4,3,2,1,0:T(8,128)(2,1)S(1)} %dynamic-slice_bitcast_fusion), channel_id=1, source_target_pairs={{28,0},{0,4},{4,8},{8,12},{12,16},{16,20},{20,24},{24,28},{29,1},{... | collective-permute-start | bytes 310280 | tf_op jit(solution)/shard_map/ppermute | solution.py:19
  43.0 2.8 %collective-permute-start.12 = (bf16[1,8,2,2,16,101]{5,4,3,2,1,0:T(8,128)(2,1)S(1)}, bf16[1,8,2,2,16,101]{5,4,3,2,1,0:T(8,128)(2,1)S(1)}, u32[]{:S(2)}, u32[]{:S(2)}) collective-permute-start(bf16[1,8,2,2,16,101]{5,4,3,2,1,0:T(8,128)(2,1)S(1)} %dynamic-slice_bitcast_fusion), channel_id=1, source_target_pairs={{24,0},{28,4},{0,8},{4,12},{8,16},{12,20},{16,24},{20,28},{25,1},{... | collective-permute-start | bytes 310280 | tf_op jit(solution)/shard_map/ppermute | solution.py:19
  45.9 2.1 %collective-permute-done.7 = bf16[1,8,2,2,16,101]{5,4,3,2,1,0:T(8,128)(2,1)S(1)} collective-permute-done((bf16[1,8,2,2,16,101]{5,4,3,2,1,0:T(8,128)(2,1)S(1)}, bf16[1,8,2,2,16,101]{5,4,3,2,1,0:T(8,128)(2,1)S(1)}, u32[]{:S(2)}, u32[]{:S(2)}) %collective-permute-start.7) | collective-permute-done | bytes 103456 | tf_op jit(solution)/shard_map/ppermute | solution.py:19
  48.6 1.8 %collective-permute-done.12 = bf16[1,8,2,2,16,101]{5,4,3,2,1,0:T(8,128)(2,1)S(1)} collective-permute-done((bf16[1,8,2,2,16,101]{5,4,3,2,1,0:T(8,128)(2,1)S(1)}, bf16[1,8,2,2,16,101]{5,4,3,2,1,0:T(8,128)(2,1)S(1)}, u32[]{:S(2)}, u32[]{:S(2)}) %collective-permute-start.12) | collective-permute-done | bytes 103456 | tf_op jit(solution)/shard_map/ppermute | solution.py:19
  53.0 2.3 %copy.14 = bf16[101,2,2,8,2,64]{5,4,3,2,1,0:T(2,128)(2,1)S(1)} copy(bf16[101,2,2,8,2,64]{0,5,1,4,3,2:T(8,128)(2,1)S(1)} %get-tuple-element.5) | data formatting | bytes 1654784 | tf_op jit(solution)/shard_map/transpose | solution.py:151
  55.3 1.7 %constant_dynamic-slice_fusion = bf16[2,8,2,2,16,101]{5,4,3,2,1,0:T(8,128)(2,1)} fusion(bf16[2,8,2,2,64,101]{5,4,3,2,1,0:T(8,128)(2,1)} %collective-permute-done.10, s32[]{:T(128)S(6)} %select_n.136), kind=kLoop, calls=%fused_computation.135 | loop fusion | bytes 413700 | tf_op jit(solution)/shard_map/dynamic_slice | solution.py:133
  57.6 1.9 %collective-permute-done.9 = bf16[1,8,2,2,16,101]{5,4,3,2,1,0:T(8,128)(2,1)} collective-permute-done((bf16[1,8,2,2,16,101]{5,4,3,2,1,0:T(8,128)(2,1)S(1)}, bf16[1,8,2,2,16,101]{5,4,3,2,1,0:T(8,128)(2,1)}, u32[]{:S(2)}, u32[]{:S(2)}) %collective-permute-start.9) | collective-permute-done | bytes 103456 | tf_op jit(solution)/shard_map/ppermute | solution.py:19
  62.8 4.3 %copy.17 = bf16[101,2,2,8,2,64]{5,4,3,2,1,0:T(2,128)(2,1)S(1)} copy(bf16[101,2,2,8,2,64]{0,5,1,4,3,2:T(8,128)(2,1)} %bitcast.35) | data formatting | bytes 1654784 | tf_op jit(solution)/shard_map/transpose | solution.py:151
  67.2 2.0 %collective-permute-done.11 = bf16[2,8,2,2,16,101]{5,4,3,2,1,0:T(8,128)(2,1)} collective-permute-done((bf16[2,8,2,2,16,101]{5,4,3,2,1,0:T(8,128)(2,1)}, bf16[2,8,2,2,16,101]{5,4,3,2,1,0:T(8,128)(2,1)}, u32[]{:S(2)}, u32[]{:S(2)}) %collective-permute-start.11) | collective-permute-done | bytes 206880 | tf_op jit(solution)/shard_map/ppermute | solution.py:19
  69.2 1.7 %constant_dynamic-update-slice_fusion = bf16[4,8,2,2,16,101]{5,4,3,2,1,0:T(8,128)(2,1)} fusion(bf16[4,8,2,2,16,101]{5,4,3,2,1,0:T(8,128)(2,1)} %constant_dynamic-update-slice_fusion.1, bf16[2,8,2,2,16,101]{5,4,3,2,1,0:T(8,128)(2,1)} %collective-permute-done.11), kind=kLoop, calls=%fused_computation.123 | loop fusion | bytes 524288 | tf_op jit(solution)/shard_map/concatenate | solution.py:158
  74.4 1.8 %slice.91 = bf16[4,6,2,2,16,101]{5,4,3,2,1,0:T(8,128)(2,1)} slice(bf16[4,8,2,2,16,101]{5,4,3,2,1,0:T(8,128)(2,1)} %constant_dynamic-update-slice_fusion.3), slice={[0:4], [0:6], [0:2], [0:2], [0:16], [0:101]} | slice | bytes 620544 | tf_op jit(solution)/shard_map/jit(_roll_static)/slice | solution.py:159
  79.3 3.4 %copy.18 = bf16[101,32,64]{2,1,0:T(8,128)(2,1)} copy(bf16[101,32,64]{0,1,2:T(8,128)(2,1)} %bitcast.128) | data formatting | bytes 827392 | tf_op jit(solution)/shard_map/reshape | solution.py:165
  84.6 3.4 %copy.15 = bf16[101,32,64]{2,1,0:T(8,128)(2,1)} copy(bf16[101,32,64]{0,1,2:T(8,128)(2,1)} %bitcast.129) | data formatting | bytes 827392 | tf_op jit(solution)/shard_map/reshape | solution.py:165
  89.1 2.1 %fusion.22 = (bf16[1,2,8,2,2,16,101]{6,5,4,3,2,1,0:T(8,128)(2,1)S(1)}, bf16[1,2,8,2,2,16,101]{6,5,4,3,2,1,0:T(8,128)(2,1)}, bf16[1,2,8,2,2,16,101]{6,5,4,3,2,1,0...) fusion(bf16[4,6,2,2,16,101]{5,4,3,2,1,0:T(8,128)(2,1)} %slice.91, bf16[4,2,2,2,16,101]{5,4,3,2,1,0:T(8,128)(2,1)S(1)} %slice.90, ...), kind=kLoop, calls=%fused_computation.55 | loop fusion | flops 517120 | bytes 1551360 | tf_op jit(solution)/shard_map/stack | solution.py:164
  92.2 3.4 %copy.23 = bf16[101,32,64]{2,1,0:T(8,128)(2,1)} copy(bf16[101,32,64]{0,1,2:T(8,128)(2,1)} %bitcast.130) | data formatting | bytes 827392 | tf_op jit(solution)/shard_map/reshape | solution.py:165
  97.6 3.3 %copy.21 = bf16[101,32,64]{2,1,0:T(8,128)(2,1)} copy(bf16[101,32,64]{0,1,2:T(8,128)(2,1)} %bitcast.131) | data formatting | bytes 827392 | tf_op jit(solution)/shard_map/reshape | solution.py:165
  100.9 1.8 %fusion.81 = f32[101,32,64]{2,1,0:T(8,128)S(1)} fusion(bf16[101,32,64]{2,1,0:T(8,128)(2,1)} %copy.15, bf16[101,64,64]{2,1,0:T(8,128)(2,1)S(1)} %bitcast.118), kind=kOutput, calls=%fused_computation.153 | convolution fusion | flops 26476544 | bytes 2068480 | tf_op jit(solution)/shard_map/fnk,fkj->fnj/dot_general | solution.py:166
  105.6 2.1 %fusion.4 = f32[1,64,16,128]{3,1,2,0:T(8,128)S(1)} fusion(f32[101,2,16,64]{3,2,1,0:T(8,128)S(1)} %bitcast.121, f32[1,101,128]{2,1,0:T(8,128)S(1)} %get-tuple-element.29, f32[1,101,128]{2,1,0:T(8,128)S(1)} %get-tuple-element.28), kind=kOutput, calls=%fused_computation.7 | convolution fusion | flops 158885120 | bytes 1455104 | tf_op jit(solution)/shard_map/fcij,cfl->jil/dot_general | solution.py:170
  107.7 2.1 %fusion.7 = f32[1,64,16,128]{3,1,2,0:T(8,128)S(1)} fusion(f32[101,2,16,64]{3,2,1,0:T(8,128)S(1)} %bitcast.120, f32[1,101,128]{2,1,0:T(8,128)S(1)} %get-tuple-element.29, f32[1,101,128]{2,1,0:T(8,128)S(1)} %get-tuple-element.28), kind=kOutput, calls=%fused_computation.8 | convolution fusion | flops 158885120 | bytes 1455104 | tf_op jit(solution)/shard_map/fcij,cfl->jil/dot_general | solution.py:170
  (89 shorter events, 43.1 us)
Async XLA Ops:
  0.0 4.1 %copy-start.3 = (f32[1,400,512]{2,1,0:T(8,128)S(1)}, f32[1,400,512]{2,1,0:T(8,128)}, u32[]{:S(2)}) copy-start(f32[1,400,512]{2,1,0:T(8,128)} %param.3) | copy-start | bytes 2457604
  4.9 0.9 copy-start.5
  9.4 11.0 %collective-permute-start = (bf16[2,2,64,101]{3,2,1,0:T(8,128)(2,1)S(1)}, bf16[2,2,64,101]{3,2,1,0:T(8,128)(2,1)S(1)}, u32[]{:S(2)}, u32[]{:S(2)}) collective-permute-start(bf16[2,2,64,101]{3,2,1,0:T(8,128)(2,1)S(1)} %get-tuple-element.25), channel_id=1, source_target_pairs={{28,0},{0,4},{4,8},{8,12},{12,16},{16,20},{20,24},{24,28},{29,1},{... | collective-permute-start | bytes 155144 | tf_op jit(solution)/shard_map/ppermute | solution.py:19
  12.5 9.4 %collective-permute-start.1 = (bf16[2,2,64,101]{3,2,1,0:T(8,128)(2,1)S(1)}, bf16[2,2,64,101]{3,2,1,0:T(8,128)(2,1)S(1)}, u32[]{:S(2)}, u32[]{:S(2)}) collective-permute-start(bf16[2,2,64,101]{3,2,1,0:T(8,128)(2,1)S(1)} %get-tuple-element.24), channel_id=1, source_target_pairs={{24,0},{28,4},{0,8},{4,12},{8,16},{12,20},{16,24},{20,28},{25,1},{... | collective-permute-start | bytes 155144 | tf_op jit(solution)/shard_map/ppermute | solution.py:19
  14.0 9.7 %collective-permute-start.2 = (bf16[2,2,64,101]{3,2,1,0:T(8,128)(2,1)S(1)}, bf16[2,2,64,101]{3,2,1,0:T(8,128)(2,1)S(1)}, u32[]{:S(2)}, u32[]{:S(2)}) collective-permute-start(bf16[2,2,64,101]{3,2,1,0:T(8,128)(2,1)S(1)} %get-tuple-element.23), channel_id=1, source_target_pairs={{20,0},{24,4},{28,8},{0,12},{4,16},{8,20},{12,24},{16,28},{21,1},{... | collective-permute-start | bytes 155144 | tf_op jit(solution)/shard_map/ppermute | solution.py:19
  16.6 7.8 %collective-permute-start.3 = (bf16[2,2,64,101]{3,2,1,0:T(8,128)(2,1)S(1)}, bf16[2,2,64,101]{3,2,1,0:T(8,128)(2,1)S(1)}, u32[]{:S(2)}, u32[]{:S(2)}) collective-permute-start(bf16[2,2,64,101]{3,2,1,0:T(8,128)(2,1)S(1)} %get-tuple-element.22), channel_id=1, source_target_pairs={{16,0},{20,4},{24,8},{28,12},{0,16},{4,20},{8,24},{12,28},{17,1},{... | collective-permute-start | bytes 155144 | tf_op jit(solution)/shard_map/ppermute | solution.py:19
  17.8 7.4 %collective-permute-start.4 = (bf16[2,2,64,101]{3,2,1,0:T(8,128)(2,1)S(1)}, bf16[2,2,64,101]{3,2,1,0:T(8,128)(2,1)S(1)}, u32[]{:S(2)}, u32[]{:S(2)}) collective-permute-start(bf16[2,2,64,101]{3,2,1,0:T(8,128)(2,1)S(1)} %get-tuple-element.21), channel_id=1, source_target_pairs={{12,0},{16,4},{20,8},{24,12},{28,16},{0,20},{4,24},{8,28},{13,1},{... | collective-permute-start | bytes 155144 | tf_op jit(solution)/shard_map/ppermute | solution.py:19
  20.5 5.9 %collective-permute-start.5 = (bf16[2,2,64,101]{3,2,1,0:T(8,128)(2,1)S(1)}, bf16[2,2,64,101]{3,2,1,0:T(8,128)(2,1)S(1)}, u32[]{:S(2)}, u32[]{:S(2)}) collective-permute-start(bf16[2,2,64,101]{3,2,1,0:T(8,128)(2,1)S(1)} %get-tuple-element.20), channel_id=1, source_target_pairs={{8,0},{12,4},{16,8},{20,12},{24,16},{28,20},{0,24},{4,28},{9,1},{1... | collective-permute-start | bytes 155144 | tf_op jit(solution)/shard_map/ppermute | solution.py:19
  21.9 4.5 %collective-permute-start.6 = (bf16[2,2,64,101]{3,2,1,0:T(8,128)(2,1)S(1)}, bf16[2,2,64,101]{3,2,1,0:T(8,128)(2,1)S(1)}, u32[]{:S(2)}, u32[]{:S(2)}) collective-permute-start(bf16[2,2,64,101]{3,2,1,0:T(8,128)(2,1)S(1)} %get-tuple-element.19), channel_id=1, source_target_pairs={{4,0},{8,4},{12,8},{16,12},{20,16},{24,20},{28,24},{0,28},{5,1},{9... | collective-permute-start | bytes 155144 | tf_op jit(solution)/shard_map/ppermute | solution.py:19
  26.4 11.6 %collective-permute-start.8 = (bf16[1,8,2,2,64,101]{5,4,3,2,1,0:T(8,128)(2,1)S(1)}, bf16[1,8,2,2,64,101]{5,4,3,2,1,0:T(8,128)(2,1)S(1)}, u32[]{:S(2)}, u32[]{:S(2)}) collective-permute-start(bf16[1,8,2,2,64,101]{5,4,3,2,1,0:T(8,128)(2,1)S(1)} %bitcast.132), channel_id=1, source_target_pairs={{0,2},{1,3},{2,0},{3,1},{4,6},{5,7},{6,4},{7,5},{8,10},{9,11},{10,... | collective-permute-start | bytes 1241096 | tf_op jit(solution)/shard_map/ppermute | solution.py:141
  39.3 16.0 %collective-permute-start.10 = (bf16[2,8,2,2,64,101]{5,4,3,2,1,0:T(8,128)(2,1)}, bf16[2,8,2,2,64,101]{5,4,3,2,1,0:T(8,128)(2,1)}, u32[]{:S(2)}, u32[]{:S(2)}) collective-permute-start(bf16[2,8,2,2,64,101]{5,4,3,2,1,0:T(8,128)(2,1)} %get-tuple-element.6), channel_id=1, source_target_pairs={{0,1},{1,0},{2,3},{3,2},{4,5},{5,4},{6,7},{7,6},{8,9},{9,8},{10,11... | collective-permute-start | bytes 2482184 | tf_op jit(solution)/shard_map/ppermute | solution.py:141
  39.3 8.6 %collective-permute-start.7 = (bf16[1,8,2,2,16,101]{5,4,3,2,1,0:T(8,128)(2,1)S(1)}, bf16[1,8,2,2,16,101]{5,4,3,2,1,0:T(8,128)(2,1)S(1)}, u32[]{:S(2)}, u32[]{:S(2)}) collective-permute-start(bf16[1,8,2,2,16,101]{5,4,3,2,1,0:T(8,128)(2,1)S(1)} %dynamic-slice_bitcast_fusion), channel_id=1, source_target_pairs={{28,0},{0,4},{4,8},{8,12},{12,16},{16,20},{20,24},{24,28},{29,1},{... | collective-permute-start | bytes 310280 | tf_op jit(solution)/shard_map/ppermute | solution.py:19
  43.0 7.5 %collective-permute-start.12 = (bf16[1,8,2,2,16,101]{5,4,3,2,1,0:T(8,128)(2,1)S(1)}, bf16[1,8,2,2,16,101]{5,4,3,2,1,0:T(8,128)(2,1)S(1)}, u32[]{:S(2)}, u32[]{:S(2)}) collective-permute-start(bf16[1,8,2,2,16,101]{5,4,3,2,1,0:T(8,128)(2,1)S(1)} %dynamic-slice_bitcast_fusion), channel_id=1, source_target_pairs={{24,0},{28,4},{0,8},{4,12},{8,16},{12,20},{16,24},{20,28},{25,1},{... | collective-permute-start | bytes 310280 | tf_op jit(solution)/shard_map/ppermute | solution.py:19
  50.5 9.0 %collective-permute-start.9 = (bf16[1,8,2,2,16,101]{5,4,3,2,1,0:T(8,128)(2,1)S(1)}, bf16[1,8,2,2,16,101]{5,4,3,2,1,0:T(8,128)(2,1)}, u32[]{:S(2)}, u32[]{:S(2)}) collective-permute-start(bf16[1,8,2,2,16,101]{5,4,3,2,1,0:T(8,128)(2,1)S(1)} %constant_dynamic-slice_fusion.1), channel_id=1, source_target_pairs={{28,0},{0,4},{4,8},{8,12},{12,16},{16,20},{20,24},{24,28},{29,1},{... | collective-permute-start | bytes 310280 | tf_op jit(solution)/shard_map/ppermute | solution.py:19
  52.0 9.1 %collective-permute-start.13 = (bf16[1,8,2,2,16,101]{5,4,3,2,1,0:T(8,128)(2,1)S(1)}, bf16[1,8,2,2,16,101]{5,4,3,2,1,0:T(8,128)(2,1)}, u32[]{:S(2)}, u32[]{:S(2)}) collective-permute-start(bf16[1,8,2,2,16,101]{5,4,3,2,1,0:T(8,128)(2,1)S(1)} %constant_dynamic-slice_fusion.1), channel_id=1, source_target_pairs={{24,0},{28,4},{0,8},{4,12},{8,16},{12,20},{16,24},{20,28},{25,1},{... | collective-permute-start | bytes 310280 | tf_op jit(solution)/shard_map/ppermute | solution.py:19
  57.0 12.2 %collective-permute-start.11 = (bf16[2,8,2,2,16,101]{5,4,3,2,1,0:T(8,128)(2,1)}, bf16[2,8,2,2,16,101]{5,4,3,2,1,0:T(8,128)(2,1)}, u32[]{:S(2)}, u32[]{:S(2)}) collective-permute-start(bf16[2,8,2,2,16,101]{5,4,3,2,1,0:T(8,128)(2,1)} %constant_dynamic-slice_fusion), channel_id=1, source_target_pairs={{28,0},{0,4},{4,8},{8,12},{12,16},{16,20},{20,24},{24,28},{29,1},{... | collective-permute-start | bytes 620552 | tf_op jit(solution)/shard_map/ppermute | solution.py:19
  61.1 11.7 %collective-permute-start.14 = (bf16[2,8,2,2,16,101]{5,4,3,2,1,0:T(8,128)(2,1)}, bf16[2,8,2,2,16,101]{5,4,3,2,1,0:T(8,128)(2,1)}, u32[]{:S(2)}, u32[]{:S(2)}) collective-permute-start(bf16[2,8,2,2,16,101]{5,4,3,2,1,0:T(8,128)(2,1)} %constant_dynamic-slice_fusion), channel_id=1, source_target_pairs={{24,0},{28,4},{0,8},{4,12},{8,16},{12,20},{16,24},{20,28},{25,1},{... | collective-permute-start | bytes 620552 | tf_op jit(solution)/shard_map/ppermute | solution.py:19
  62.0 0.8 copy-start.4
  100.9 1.8 %copy-start.2 = (bf16[101,32,64]{2,1,0:T(8,128)(2,1)S(1)}, bf16[101,32,64]{2,1,0:T(8,128)(2,1)}, u32[]{:S(2)}) copy-start(bf16[101,32,64]{2,1,0:T(8,128)(2,1)} %copy.21) | copy-start | bytes 1241092
  102.7 1.1 %copy-start = (bf16[101,32,64]{2,1,0:T(8,128)(2,1)S(1)}, bf16[101,32,64]{2,1,0:T(8,128)(2,1)}, u32[]{:S(2)}) copy-start(bf16[101,32,64]{2,1,0:T(8,128)(2,1)} %copy.18) | copy-start | bytes 1241092
  103.8 1.1 %copy-start.1 = (bf16[101,32,64]{2,1,0:T(8,128)(2,1)S(1)}, bf16[101,32,64]{2,1,0:T(8,128)(2,1)}, u32[]{:S(2)}) copy-start(bf16[101,32,64]{2,1,0:T(8,128)(2,1)} %copy.23) | copy-start | bytes 1241092

commit v8 on v6

--- a/solution.py
+++ b/solution.py
@@ -4,6 +4,7 @@
 import jax.numpy as jnp
 from jax import lax
 from jax.sharding import PartitionSpec as P
+
 
 L = 200
 FB = 101
@@ -117,7 +118,10 @@
     slice_width = block_width // tm_count
     windows = records.reshape(samples // L, L, channels)
     spectra = whiten_planes(windows, live_mask, lax.Precision.HIGH)
-    sorted_spec = jnp.take(spectra, chan_order, axis=2)
+    picks = (chan_order[:, None] == jnp.arange(channels, dtype=chan_order.dtype)[None, :])
+    sorted_spec = jnp.einsum(
+        "kh,wchf->wckf", picks.astype(jnp.bfloat16), spectra, preferred_element_type=jnp.float32
+    ).astype(jnp.bfloat16)
     sorted_spec = sorted_spec.reshape(spectra.shape[0], 2, chan_count, block_width, FB)
     sorted_spec = jnp.moveaxis(sorted_spec, 2, 0)
     pieces = []
@@ -181,7 +185,10 @@
     slice_width = block_width // tm_count
     windows = records.reshape(samples // L, L, channels)
     spectra = whiten_planes(windows, live_mask, lax.Precision.HIGH)
-    sorted_spec = jnp.take(spectra, chan_order, axis=2)
+    picks = (chan_order[:, None] == jnp.arange(channels, dtype=chan_order.dtype)[None, :])
+    sorted_spec = jnp.einsum(
+        "kh,wchf->wckf", picks.astype(jnp.bfloat16), spectra, preferred_element_type=jnp.float32
+    ).astype(jnp.bfloat16)
     sorted_spec = sorted_spec.reshape(spectra.shape[0], 2, chan_count, block_width, FB)
     sorted_spec = jnp.moveaxis(sorted_spec, 2, 0)
     pieces = []

time: 82.7 us -> 79.1 us (0.956)
  local copies, waits for them, and re-layouts: 16.3 us -> 13.8 us
  other arithmetic: 7.12 us -> 5.55 us
    gather x2 -> x0, local copies, waits for them, and re-layouts: 2.36 us -> none  [on_device_local(): sorted_spec = jnp.take(spectra, chan_order, axis=2)]
    select_n x2 -> x0, other arithmetic: 0.91 us -> none  [on_device_local(): sorted_spec = jnp.take(spectra, chan_order, axis=2)]
where the time goes in v8:
time: 79.1 us; the launch traced here: 78.8 us
  waiting for transfers between devices  27.1 us (34%)
  starting transfers between devices  23.2 us (29%)
  local copies, waits for them, and re-layouts  13.8 us (17%)
  matrix products  8.79 us (11%)
  other arithmetic  5.55 us (7%)
    ppermute x13, starting transfers between devices, shifted(): return lax.ppermute(block, axis, route)  22.5 us
    ppermute x13, waiting for transfers between devices, shifted(): return lax.ppermute(block, axis, route)  14.8 us
    ppermute x2, waiting for transfers between devices, on_device_local(): arrived = lax.ppermute(gathered, 'tm', route)  12.3 us
    reshape x2, local copies, waits for them, and re-layouts, on_device_local(): jnp.transpose(both, (6, 0, 5, 4, 1, 2, 3))  4.37 us
    dot_general x2, matrix products, on_device_local(): jnp.einsum('fcij,cfl->jil', sums, inverse, precision=lax.Precision.HIGH)  4.19 us
    reshape x1, local copies, waits for them, and re-layouts, on_device_local(): jnp.transpose(gathered, (5, 3, 0, 1, 2, 4))  3.88 us
    dot_general x2, matrix products, on_device_local(): jnp.einsum('fnk,fkj->fnj', both, own_spec, preferred_element_type=jnp.flo...  1.94 us
    another operation x1, local copies, waits for them, and re-layouts, on_device_local(): return jnp.stack(results)  1.59 us
  transfers between devices with their start and end apart: 15, of which 9 were waited for; matrix products, arithmetic and copies ran while one was open for 9% of the time, Pallas kernels for 0%

profile of v8, /device:TPU:6, one launch (start us, length us, event | category | flops | bytes accessed | tf_op | source)
XLA Modules:
  0.0 78.8 jit_solution(1869025042919904163)
XLA Ops:
  0.1 1.3 %reduce_sum.36 = f32[2,512]{1,0:T(2,128)S(1)} reduce(f32[2,200,512]{2,1,0:T(8,128)} %bitcast.107, f32[]{:T(128)} %constant.117.clone.1), dimensions={1}, to_apply=%region_0.0 | reduce | flops 203776 | bytes 823300 | tf_op jit(solution)/shard_map/reduce_sum | solution.py:165
  5.8 1.6 %collective-permute-start = (bf16[2,2,64,101]{3,2,1,0:T(8,128)(2,1)S(1)}, bf16[2,2,64,101]{3,2,1,0:T(8,128)(2,1)S(1)}, u32[]{:S(2)}, u32[]{:S(2)}) collective-permute-start(bf16[2,2,64,101]{3,2,1,0:T(8,128)(2,1)S(1)} %get-tuple-element.15), channel_id=1, source_target_pairs={{28,0},{0,4},{4,8},{8,12},{12,16},{16,20},{20,24},{24,28},{29,1},{... | collective-permute-start | bytes 155144 | tf_op jit(solution)/shard_map/ppermute | solution.py:19
  7.4 1.6 %collective-permute-start.1 = (bf16[2,2,64,101]{3,2,1,0:T(8,128)(2,1)S(1)}, bf16[2,2,64,101]{3,2,1,0:T(8,128)(2,1)S(1)}, u32[]{:S(2)}, u32[]{:S(2)}) collective-permute-start(bf16[2,2,64,101]{3,2,1,0:T(8,128)(2,1)S(1)} %get-tuple-element.14), channel_id=1, source_target_pairs={{24,0},{28,4},{0,8},{4,12},{8,16},{12,20},{16,24},{20,28},{25,1},{... | collective-permute-start | bytes 155144 | tf_op jit(solution)/shard_map/ppermute | solution.py:19
  9.0 2.5 %collective-permute-start.2 = (bf16[2,2,64,101]{3,2,1,0:T(8,128)(2,1)S(1)}, bf16[2,2,64,101]{3,2,1,0:T(8,128)(2,1)S(1)}, u32[]{:S(2)}, u32[]{:S(2)}) collective-permute-start(bf16[2,2,64,101]{3,2,1,0:T(8,128)(2,1)S(1)} %get-tuple-element.13), channel_id=1, source_target_pairs={{20,0},{24,4},{28,8},{0,12},{4,16},{8,20},{12,24},{16,28},{21,1},{... | collective-permute-start | bytes 155144 | tf_op jit(solution)/shard_map/ppermute | solution.py:19
  11.9 2.2 %collective-permute-start.4 = (bf16[2,2,64,101]{3,2,1,0:T(8,128)(2,1)S(1)}, bf16[2,2,64,101]{3,2,1,0:T(8,128)(2,1)S(1)}, u32[]{:S(2)}, u32[]{:S(2)}) collective-permute-start(bf16[2,2,64,101]{3,2,1,0:T(8,128)(2,1)S(1)} %get-tuple-element.11), channel_id=1, source_target_pairs={{12,0},{16,4},{20,8},{24,12},{28,16},{0,20},{4,24},{8,28},{13,1},{... | collective-permute-start | bytes 155144 | tf_op jit(solution)/shard_map/ppermute | solution.py:19
  14.1 1.9 %collective-permute-start.5 = (bf16[2,2,64,101]{3,2,1,0:T(8,128)(2,1)S(1)}, bf16[2,2,64,101]{3,2,1,0:T(8,128)(2,1)S(1)}, u32[]{:S(2)}, u32[]{:S(2)}) collective-permute-start(bf16[2,2,64,101]{3,2,1,0:T(8,128)(2,1)S(1)} %get-tuple-element.10), channel_id=1, source_target_pairs={{8,0},{12,4},{16,8},{20,12},{24,16},{28,20},{0,24},{4,28},{9,1},{1... | collective-permute-start | bytes 155144 | tf_op jit(solution)/shard_map/ppermute | solution.py:19
  15.9 1.5 %collective-permute-start.6 = (bf16[2,2,64,101]{3,2,1,0:T(8,128)(2,1)S(1)}, bf16[2,2,64,101]{3,2,1,0:T(8,128)(2,1)S(1)}, u32[]{:S(2)}, u32[]{:S(2)}) collective-permute-start(bf16[2,2,64,101]{3,2,1,0:T(8,128)(2,1)S(1)} %get-tuple-element.9), channel_id=1, source_target_pairs={{4,0},{8,4},{12,8},{16,12},{20,16},{24,20},{28,24},{0,28},{5,1},{9... | collective-permute-start | bytes 155144 | tf_op jit(solution)/shard_map/ppermute | solution.py:19
  17.4 1.6 %collective-permute-done.3 = bf16[2,2,64,101]{3,2,1,0:T(8,128)(2,1)S(1)} collective-permute-done((bf16[2,2,64,101]{3,2,1,0:T(8,128)(2,1)S(1)}, bf16[2,2,64,101]{3,2,1,0:T(8,128)(2,1)S(1)}, u32[]{:S(2)}, u32[]{:S(2)}) %collective-permute-start.3) | collective-permute-done | bytes 51744 | tf_op jit(solution)/shard_map/ppermute | solution.py:19
  19.1 1.8 %collective-permute-done.4 = bf16[2,2,64,101]{3,2,1,0:T(8,128)(2,1)S(1)} collective-permute-done((bf16[2,2,64,101]{3,2,1,0:T(8,128)(2,1)S(1)}, bf16[2,2,64,101]{3,2,1,0:T(8,128)(2,1)S(1)}, u32[]{:S(2)}, u32[]{:S(2)}) %collective-permute-start.4) | collective-permute-done | bytes 51744 | tf_op jit(solution)/shard_map/ppermute | solution.py:19
  22.6 12.3 %collective-permute-done.8 = bf16[1,8,2,2,64,101]{5,4,3,2,1,0:T(8,128)(2,1)S(1)} collective-permute-done((bf16[1,8,2,2,64,101]{5,4,3,2,1,0:T(8,128)(2,1)S(1)}, bf16[1,8,2,2,64,101]{5,4,3,2,1,0:T(8,128)(2,1)S(1)}, u32[]{:S(2)}, u32[]{:S(2)}) %collective-permute-start.8) | collective-permute-done | bytes 413728 | tf_op jit(solution)/shard_map/ppermute | solution.py:211
  35.2 1.5 %collective-permute-start.7 = (bf16[1,8,2,2,16,101]{5,4,3,2,1,0:T(8,128)(2,1)S(1)}, bf16[1,8,2,2,16,101]{5,4,3,2,1,0:T(8,128)(2,1)S(1)}, u32[]{:S(2)}, u32[]{:S(2)}) collective-permute-start(bf16[1,8,2,2,16,101]{5,4,3,2,1,0:T(8,128)(2,1)S(1)} %dynamic-slice_bitcast_fusion), channel_id=1, source_target_pairs={{28,0},{0,4},{4,8},{8,12},{12,16},{16,20},{20,24},{24,28},{29,1},{... | collective-permute-start | bytes 310280 | tf_op jit(solution)/shard_map/ppermute | solution.py:19
  37.6 1.4 %collective-permute-start.12 = (bf16[1,8,2,2,16,101]{5,4,3,2,1,0:T(8,128)(2,1)S(1)}, bf16[1,8,2,2,16,101]{5,4,3,2,1,0:T(8,128)(2,1)S(1)}, u32[]{:S(2)}, u32[]{:S(2)}) collective-permute-start(bf16[1,8,2,2,16,101]{5,4,3,2,1,0:T(8,128)(2,1)S(1)} %dynamic-slice_bitcast_fusion), channel_id=1, source_target_pairs={{24,0},{28,4},{0,8},{4,12},{8,16},{12,20},{16,24},{20,28},{25,1},{... | collective-permute-start | bytes 310280 | tf_op jit(solution)/shard_map/ppermute | solution.py:19
  39.0 2.2 %collective-permute-done.7 = bf16[1,8,2,2,16,101]{5,4,3,2,1,0:T(8,128)(2,1)S(1)} collective-permute-done((bf16[1,8,2,2,16,101]{5,4,3,2,1,0:T(8,128)(2,1)S(1)}, bf16[1,8,2,2,16,101]{5,4,3,2,1,0:T(8,128)(2,1)S(1)}, u32[]{:S(2)}, u32[]{:S(2)}) %collective-permute-start.7) | collective-permute-done | bytes 103456 | tf_op jit(solution)/shard_map/ppermute | solution.py:19
  41.2 2.9 %collective-permute-start.9 = (bf16[1,8,2,2,16,101]{5,4,3,2,1,0:T(8,128)(2,1)S(1)}, bf16[1,8,2,2,16,101]{5,4,3,2,1,0:T(8,128)(2,1)S(1)}, u32[]{:S(2)}, u32[]{:S(2)}) collective-permute-start(bf16[1,8,2,2,16,101]{5,4,3,2,1,0:T(8,128)(2,1)S(1)} %constant_dynamic-slice_fusion.1), channel_id=1, source_target_pairs={{28,0},{0,4},{4,8},{8,12},{12,16},{16,20},{20,24},{24,28},{29,1},{... | collective-permute-start | bytes 310280 | tf_op jit(solution)/shard_map/ppermute | solution.py:19
  45.6 2.4 %collective-permute-done.9 = bf16[1,8,2,2,16,101]{5,4,3,2,1,0:T(8,128)(2,1)S(1)} collective-permute-done((bf16[1,8,2,2,16,101]{5,4,3,2,1,0:T(8,128)(2,1)S(1)}, bf16[1,8,2,2,16,101]{5,4,3,2,1,0:T(8,128)(2,1)S(1)}, u32[]{:S(2)}, u32[]{:S(2)}) %collective-permute-start.9) | collective-permute-done | bytes 103456 | tf_op jit(solution)/shard_map/ppermute | solution.py:19
  48.1 3.4 %collective-permute-start.11 = (bf16[2,8,2,2,16,101]{5,4,3,2,1,0:T(8,128)(2,1)S(1)}, bf16[2,8,2,2,16,101]{5,4,3,2,1,0:T(8,128)(2,1)S(1)}, u32[]{:S(2)}, u32[]{:S(2)}) collective-permute-start(bf16[2,8,2,2,16,101]{5,4,3,2,1,0:T(8,128)(2,1)S(1)} %constant_dynamic-slice_fusion), channel_id=1, source_target_pairs={{28,0},{0,4},{4,8},{8,12},{12,16},{16,20},{20,24},{24,28},{29,1},{... | collective-permute-start | bytes 620552 | tf_op jit(solution)/shard_map/ppermute | solution.py:19
  54.4 1.5 %copy.13 = bf16[101,2,4,8,2,64]{0,5,4,3,2,1:T(8,128)(2,1)} copy(bf16[101,2,4,8,2,64]{0,5,1,4,3,2:T(8,128)(2,1)S(1)} %maximum_bitcast_fusion) | data formatting | bytes 3309568 | tf_op jit(solution)/shard_map/transpose | solution.py:216
  55.9 3.9 %copy.15 = bf16[101,128,64]{1,2,0:T(8,128)(2,1)S(1)} copy(bf16[101,128,64]{0,2,1:T(8,128)(2,1)} %bitcast.102) | data formatting | bytes 3309568 | tf_op jit(solution)/shard_map/reshape | solution.py:216
  59.9 4.5 %collective-permute-done.14 = bf16[2,8,2,2,16,101]{5,4,3,2,1,0:T(8,128)(2,1)S(1)} collective-permute-done((bf16[2,8,2,2,16,101]{5,4,3,2,1,0:T(8,128)(2,1)S(1)}, bf16[2,8,2,2,16,101]{5,4,3,2,1,0:T(8,128)(2,1)S(1)}, u32[]{:S(2)}, u32[]{:S(2)}) %collective-permute-start.14) | collective-permute-done | bytes 206880 | tf_op jit(solution)/shard_map/ppermute | solution.py:19
  65.5 2.2 %copy.14 = bf16[101,32,128]{2,1,0:T(8,128)(2,1)} copy(bf16[101,32,128]{0,1,2:T(8,128)(2,1)S(1)} %bitcast.105) | data formatting | bytes 1654784 | tf_op jit(solution)/shard_map/reshape | solution.py:225
  68.6 2.2 %copy.18 = bf16[101,32,128]{2,1,0:T(8,128)(2,1)} copy(bf16[101,32,128]{0,1,2:T(8,128)(2,1)S(1)} %bitcast.106) | data formatting | bytes 1654784 | tf_op jit(solution)/shard_map/reshape | solution.py:225
  72.9 2.1 %fusion.4 = f32[1,64,16,128]{3,1,2,0:T(8,128)S(1)} fusion(f32[101,2,16,64]{3,2,1,0:T(8,128)S(1)} %bitcast.104, f32[1,101,128]{2,1,0:T(8,128)S(1)} %copy-done.8, f32[1,101,128]{2,1,0:T(8,128)S(1)} %copy-done.7), kind=kOutput, calls=%fused_computation.6 | convolution fusion | flops 158885120 | bytes 1455104 | tf_op jit(solution)/shard_map/fcij,cfl->jil/dot_general | solution.py:229
  75.0 2.1 %fusion.7 = f32[1,64,16,128]{3,1,2,0:T(8,128)S(1)} fusion(f32[101,2,16,64]{3,2,1,0:T(8,128)S(1)} %bitcast.103, f32[1,101,128]{2,1,0:T(8,128)S(1)} %copy-done.8, f32[1,101,128]{2,1,0:T(8,128)S(1)} %copy-done.7), kind=kOutput, calls=%fused_computation.7 | convolution fusion | flops 158885120 | bytes 1455104 | tf_op jit(solution)/shard_map/fcij,cfl->jil/dot_general | solution.py:229
  77.2 1.6 %copy.21 = f32[2,64,16,128]{3,2,1,0:T(8,128)} copy(f32[2,64,16,128]{3,1,2,0:T(8,128)S(1)} %pad_maximum_fusion.1) | data formatting | bytes 2097152 | tf_op jit(solution)/shard_map/stack | solution.py:231
  (85 shorter events, 16.4 us)
Async XLA Ops:
  0.0 2.7 %copy-start.2 = (f32[1,400,512]{2,1,0:T(8,128)S(1)}, f32[1,400,512]{2,1,0:T(8,128)}, u32[]{:S(2)}) copy-start(f32[1,400,512]{2,1,0:T(8,128)} %param.3) | copy-start | bytes 2457604
  3.5 1.4 %copy-start.10 = (s32[512]{0:T(512)S(1)}, s32[512]{0:T(512)}, u32[]{:S(2)}) copy-start(s32[512]{0:T(512)} %param.4) | copy-start | bytes 6148
  5.8 8.2 %collective-permute-start = (bf16[2,2,64,101]{3,2,1,0:T(8,128)(2,1)S(1)}, bf16[2,2,64,101]{3,2,1,0:T(8,128)(2,1)S(1)}, u32[]{:S(2)}, u32[]{:S(2)}) collective-permute-start(bf16[2,2,64,101]{3,2,1,0:T(8,128)(2,1)S(1)} %get-tuple-element.15), channel_id=1, source_target_pairs={{28,0},{0,4},{4,8},{8,12},{12,16},{16,20},{20,24},{24,28},{29,1},{... | collective-permute-start | bytes 155144 | tf_op jit(solution)/shard_map/ppermute | solution.py:19
  7.4 8.5 %collective-permute-start.1 = (bf16[2,2,64,101]{3,2,1,0:T(8,128)(2,1)S(1)}, bf16[2,2,64,101]{3,2,1,0:T(8,128)(2,1)S(1)}, u32[]{:S(2)}, u32[]{:S(2)}) collective-permute-start(bf16[2,2,64,101]{3,2,1,0:T(8,128)(2,1)S(1)} %get-tuple-element.14), channel_id=1, source_target_pairs={{24,0},{28,4},{0,8},{4,12},{8,16},{12,20},{16,24},{20,28},{25,1},{... | collective-permute-start | bytes 155144 | tf_op jit(solution)/shard_map/ppermute | solution.py:19
  9.0 8.4 %collective-permute-start.2 = (bf16[2,2,64,101]{3,2,1,0:T(8,128)(2,1)S(1)}, bf16[2,2,64,101]{3,2,1,0:T(8,128)(2,1)S(1)}, u32[]{:S(2)}, u32[]{:S(2)}) collective-permute-start(bf16[2,2,64,101]{3,2,1,0:T(8,128)(2,1)S(1)} %get-tuple-element.13), channel_id=1, source_target_pairs={{20,0},{24,4},{28,8},{0,12},{4,16},{8,20},{12,24},{16,28},{21,1},{... | collective-permute-start | bytes 155144 | tf_op jit(solution)/shard_map/ppermute | solution.py:19
  11.5 7.6 %collective-permute-start.3 = (bf16[2,2,64,101]{3,2,1,0:T(8,128)(2,1)S(1)}, bf16[2,2,64,101]{3,2,1,0:T(8,128)(2,1)S(1)}, u32[]{:S(2)}, u32[]{:S(2)}) collective-permute-start(bf16[2,2,64,101]{3,2,1,0:T(8,128)(2,1)S(1)} %get-tuple-element.12), channel_id=1, source_target_pairs={{16,0},{20,4},{24,8},{28,12},{0,16},{4,20},{8,24},{12,28},{17,1},{... | collective-permute-start | bytes 155144 | tf_op jit(solution)/shard_map/ppermute | solution.py:19
  11.9 9.0 %collective-permute-start.4 = (bf16[2,2,64,101]{3,2,1,0:T(8,128)(2,1)S(1)}, bf16[2,2,64,101]{3,2,1,0:T(8,128)(2,1)S(1)}, u32[]{:S(2)}, u32[]{:S(2)}) collective-permute-start(bf16[2,2,64,101]{3,2,1,0:T(8,128)(2,1)S(1)} %get-tuple-element.11), channel_id=1, source_target_pairs={{12,0},{16,4},{20,8},{24,12},{28,16},{0,20},{4,24},{8,28},{13,1},{... | collective-permute-start | bytes 155144 | tf_op jit(solution)/shard_map/ppermute | solution.py:19
  14.1 6.8 %collective-permute-start.5 = (bf16[2,2,64,101]{3,2,1,0:T(8,128)(2,1)S(1)}, bf16[2,2,64,101]{3,2,1,0:T(8,128)(2,1)S(1)}, u32[]{:S(2)}, u32[]{:S(2)}) collective-permute-start(bf16[2,2,64,101]{3,2,1,0:T(8,128)(2,1)S(1)} %get-tuple-element.10), channel_id=1, source_target_pairs={{8,0},{12,4},{16,8},{20,12},{24,16},{28,20},{0,24},{4,28},{9,1},{1... | collective-permute-start | bytes 155144 | tf_op jit(solution)/shard_map/ppermute | solution.py:19
  15.9 6.0 %collective-permute-start.6 = (bf16[2,2,64,101]{3,2,1,0:T(8,128)(2,1)S(1)}, bf16[2,2,64,101]{3,2,1,0:T(8,128)(2,1)S(1)}, u32[]{:S(2)}, u32[]{:S(2)}) collective-permute-start(bf16[2,2,64,101]{3,2,1,0:T(8,128)(2,1)S(1)} %get-tuple-element.9), channel_id=1, source_target_pairs={{4,0},{8,4},{12,8},{16,12},{20,16},{24,20},{28,24},{0,28},{5,1},{9... | collective-permute-start | bytes 155144 | tf_op jit(solution)/shard_map/ppermute | solution.py:19
  22.0 12.9 %collective-permute-start.8 = (bf16[1,8,2,2,64,101]{5,4,3,2,1,0:T(8,128)(2,1)S(1)}, bf16[1,8,2,2,64,101]{5,4,3,2,1,0:T(8,128)(2,1)S(1)}, u32[]{:S(2)}, u32[]{:S(2)}) collective-permute-start(bf16[1,8,2,2,64,101]{5,4,3,2,1,0:T(8,128)(2,1)S(1)} %bitcast.111), channel_id=1, source_target_pairs={{0,2},{1,3},{2,0},{3,1},{4,6},{5,7},{6,4},{7,5},{8,10},{9,11},{10,... | collective-permute-start | bytes 1241096 | tf_op jit(solution)/shard_map/ppermute | solution.py:211
  35.1 12.9 %collective-permute-start.10 = (bf16[2,8,2,2,64,101]{5,4,3,2,1,0:T(8,128)(2,1)S(1)}, bf16[2,8,2,2,64,101]{5,4,3,2,1,0:T(8,128)(2,1)S(1)}, u32[]{:S(2)}, u32[]{:S(2)}) collective-permute-start(bf16[2,8,2,2,64,101]{5,4,3,2,1,0:T(8,128)(2,1)S(1)} %pad_maximum_fusion), channel_id=1, source_target_pairs={{0,1},{1,0},{2,3},{3,2},{4,5},{5,4},{6,7},{7,6},{8,9},{9,8},{10,11... | collective-permute-start | bytes 2482184 | tf_op jit(solution)/shard_map/ppermute | solution.py:211
  35.2 5.9 %collective-permute-start.7 = (bf16[1,8,2,2,16,101]{5,4,3,2,1,0:T(8,128)(2,1)S(1)}, bf16[1,8,2,2,16,101]{5,4,3,2,1,0:T(8,128)(2,1)S(1)}, u32[]{:S(2)}, u32[]{:S(2)}) collective-permute-start(bf16[1,8,2,2,16,101]{5,4,3,2,1,0:T(8,128)(2,1)S(1)} %dynamic-slice_bitcast_fusion), channel_id=1, source_target_pairs={{28,0},{0,4},{4,8},{8,12},{12,16},{16,20},{20,24},{24,28},{29,1},{... | collective-permute-start | bytes 310280 | tf_op jit(solution)/shard_map/ppermute | solution.py:19
  37.6 7.4 %collective-permute-start.12 = (bf16[1,8,2,2,16,101]{5,4,3,2,1,0:T(8,128)(2,1)S(1)}, bf16[1,8,2,2,16,101]{5,4,3,2,1,0:T(8,128)(2,1)S(1)}, u32[]{:S(2)}, u32[]{:S(2)}) collective-permute-start(bf16[1,8,2,2,16,101]{5,4,3,2,1,0:T(8,128)(2,1)S(1)} %dynamic-slice_bitcast_fusion), channel_id=1, source_target_pairs={{24,0},{28,4},{0,8},{4,12},{8,16},{12,20},{16,24},{20,28},{25,1},{... | collective-permute-start | bytes 310280 | tf_op jit(solution)/shard_map/ppermute | solution.py:19
  41.2 6.7 %collective-permute-start.9 = (bf16[1,8,2,2,16,101]{5,4,3,2,1,0:T(8,128)(2,1)S(1)}, bf16[1,8,2,2,16,101]{5,4,3,2,1,0:T(8,128)(2,1)S(1)}, u32[]{:S(2)}, u32[]{:S(2)}) collective-permute-start(bf16[1,8,2,2,16,101]{5,4,3,2,1,0:T(8,128)(2,1)S(1)} %constant_dynamic-slice_fusion.1), channel_id=1, source_target_pairs={{28,0},{0,4},{4,8},{8,12},{12,16},{16,20},{20,24},{24,28},{29,1},{... | collective-permute-start | bytes 310280 | tf_op jit(solution)/shard_map/ppermute | solution.py:19
  45.0 6.8 %collective-permute-start.13 = (bf16[1,8,2,2,16,101]{5,4,3,2,1,0:T(8,128)(2,1)S(1)}, bf16[1,8,2,2,16,101]{5,4,3,2,1,0:T(8,128)(2,1)S(1)}, u32[]{:S(2)}, u32[]{:S(2)}) collective-permute-start(bf16[1,8,2,2,16,101]{5,4,3,2,1,0:T(8,128)(2,1)S(1)} %constant_dynamic-slice_fusion.1), channel_id=1, source_target_pairs={{24,0},{28,4},{0,8},{4,12},{8,16},{12,20},{16,24},{20,28},{25,1},{... | collective-permute-start | bytes 310280 | tf_op jit(solution)/shard_map/ppermute | solution.py:19
  48.0 3.9 %copy-start.5 = (bf16[4,8,2,2,16,101]{5,4,3,2,1,0:T(8,128)(2,1)}, bf16[4,8,2,2,16,101]{5,4,3,2,1,0:T(8,128)(2,1)S(1)}, u32[]{:S(2)}) copy-start(bf16[4,8,2,2,16,101]{5,4,3,2,1,0:T(8,128)(2,1)S(1)} %constant_dynamic-update-slice_fusion.1) | copy-start | bytes 1241092
  48.1 11.8 %collective-permute-start.11 = (bf16[2,8,2,2,16,101]{5,4,3,2,1,0:T(8,128)(2,1)S(1)}, bf16[2,8,2,2,16,101]{5,4,3,2,1,0:T(8,128)(2,1)S(1)}, u32[]{:S(2)}, u32[]{:S(2)}) collective-permute-start(bf16[2,8,2,2,16,101]{5,4,3,2,1,0:T(8,128)(2,1)S(1)} %constant_dynamic-slice_fusion), channel_id=1, source_target_pairs={{28,0},{0,4},{4,8},{8,12},{12,16},{16,20},{20,24},{24,28},{29,1},{... | collective-permute-start | bytes 620552 | tf_op jit(solution)/shard_map/ppermute | solution.py:19
  52.7 11.8 %collective-permute-start.14 = (bf16[2,8,2,2,16,101]{5,4,3,2,1,0:T(8,128)(2,1)S(1)}, bf16[2,8,2,2,16,101]{5,4,3,2,1,0:T(8,128)(2,1)S(1)}, u32[]{:S(2)}, u32[]{:S(2)}) collective-permute-start(bf16[2,8,2,2,16,101]{5,4,3,2,1,0:T(8,128)(2,1)S(1)} %constant_dynamic-slice_fusion), channel_id=1, source_target_pairs={{24,0},{28,4},{0,8},{4,12},{8,16},{12,20},{16,24},{20,28},{25,1},{... | collective-permute-start | bytes 620552 | tf_op jit(solution)/shard_map/ppermute | solution.py:19
  55.9 3.9 %copy-start.6 = (bf16[4,8,2,2,16,101]{5,4,3,2,1,0:T(8,128)(2,1)S(1)}, bf16[4,8,2,2,16,101]{5,4,3,2,1,0:T(8,128)(2,1)}, u32[]{:S(2)}) copy-start(bf16[4,8,2,2,16,101]{5,4,3,2,1,0:T(8,128)(2,1)} %copy-done.5) | copy-start | bytes 1241092
  55.9 8.5 %copy-start.4 = (bf16[4,8,2,2,16,101]{5,4,3,2,1,0:T(8,128)(2,1)S(1)}, bf16[4,8,2,2,16,101]{5,4,3,2,1,0:T(8,128)(2,1)}, u32[]{:S(2)}) copy-start(bf16[4,8,2,2,16,101]{5,4,3,2,1,0:T(8,128)(2,1)} %copy-done.3) | copy-start | bytes 1241092
  68.3 2.5 %copy-start = (bf16[101,32,128]{2,1,0:T(8,128)(2,1)S(1)}, bf16[101,32,128]{2,1,0:T(8,128)(2,1)}, u32[]{:S(2)}) copy-start(bf16[101,32,128]{2,1,0:T(8,128)(2,1)} %copy.14) | copy-start | bytes 2482180
  70.8 1.1 %copy-start.1 = (bf16[101,32,128]{2,1,0:T(8,128)(2,1)S(1)}, bf16[101,32,128]{2,1,0:T(8,128)(2,1)}, u32[]{:S(2)}) copy-start(bf16[101,32,128]{2,1,0:T(8,128)(2,1)} %copy.18) | copy-start | bytes 2482180
  71.9 1.0 %copy-start.7 = (f32[1,101,128]{2,1,0:T(8,128)S(1)}, f32[1,101,128]{2,1,0:T(8,128)}, u32[]{:S(2)}) copy-start(f32[1,101,128]{2,1,0:T(8,128)} %get-tuple-element.18) | copy-start | bytes 155140
  71.9 1.0 %copy-start.8 = (f32[1,101,128]{2,1,0:T(8,128)S(1)}, f32[1,101,128]{2,1,0:T(8,128)}, u32[]{:S(2)}) copy-start(f32[1,101,128]{2,1,0:T(8,128)} %get-tuple-element.19) | copy-start | bytes 155140
  (2 other events, 1.7 us)

commit v9 on v8

--- a/solution.py
+++ b/solution.py
@@ -134,7 +134,10 @@
 
     def send_slices(group):
         piece = lax.dynamic_slice_in_dim(group, tm_position * slice_width, slice_width, axis=4)
-        return [shifted(piece, "chan", offset) for offset in offsets]
+        sent = []
+        for offset in offsets:
+            sent.append(shifted(piece, "chan", offset))
+        return sent
 
     gathered = own[None]
     partner_groups = [send_slices(gathered)]
@@ -201,7 +204,10 @@
 
     def send_slices(group):
         piece = lax.dynamic_slice_in_dim(group, tm_position * slice_width, slice_width, axis=4)
-        return [shifted(piece, "chan", offset) for offset in offsets]
+        sent = []
+        for offset in offsets:
+            sent.append(shifted(piece, "chan", offset))
+        return sent
 
     gathered = own[None]
     partner_groups = [send_slices(gathered)]

time: 79.1 us -> 79.1 us (level)
  no operation moved by 1% of the time
where the time goes in v9:
time: 79.1 us; the launch traced here: 78.8 us
  waiting for transfers between devices  27.1 us (34%)
  starting transfers between devices  23.2 us (29%)
  local copies, waits for them, and re-layouts  13.8 us (17%)
  matrix products  8.79 us (11%)
  other arithmetic  5.55 us (7%)
    ppermute x13, starting transfers between devices, shifted(): return lax.ppermute(block, axis, route)  22.5 us
    ppermute x13, waiting for transfers between devices, shifted(): return lax.ppermute(block, axis, route)  14.8 us
    ppermute x2, waiting for transfers between devices, on_device_local(): arrived = lax.ppermute(gathered, 'tm', route)  12.3 us
    reshape x2, local copies, waits for them, and re-layouts, on_device_local(): jnp.transpose(both, (6, 0, 5, 4, 1, 2, 3))  4.37 us
    dot_general x2, matrix products, on_device_local(): jnp.einsum('fcij,cfl->jil', sums, inverse, precision=lax.Precision.HIGH)  4.19 us
    reshape x1, local copies, waits for them, and re-layouts, on_device_local(): jnp.transpose(gathered, (5, 3, 0, 1, 2, 4))  3.88 us
    dot_general x2, matrix products, on_device_local(): jnp.einsum('fnk,fkj->fnj', both, own_spec, preferred_element_type=jnp.flo...  1.94 us
    another operation x1, local copies, waits for them, and re-layouts, on_device_local(): return jnp.stack(results)  1.59 us
  transfers between devices with their start and end apart: 15, of which 9 were waited for; matrix products, arithmetic and copies ran while one was open for 9% of the time, Pallas kernels for 0%

profile of v9, /device:TPU:6, one launch (start us, length us, event | category | flops | bytes accessed | tf_op | source)
XLA Modules:
  0.0 78.8 jit_solution(1869025042919904163)
XLA Ops:
  0.1 1.3 %reduce_sum.36 = f32[2,512]{1,0:T(2,128)S(1)} reduce(f32[2,200,512]{2,1,0:T(8,128)} %bitcast.107, f32[]{:T(128)} %constant.117.clone.1), dimensions={1}, to_apply=%region_0.0 | reduce | flops 203776 | bytes 823300 | tf_op jit(solution)/shard_map/reduce_sum | solution.py:168
  5.8 1.6 %collective-permute-start = (bf16[2,2,64,101]{3,2,1,0:T(8,128)(2,1)S(1)}, bf16[2,2,64,101]{3,2,1,0:T(8,128)(2,1)S(1)}, u32[]{:S(2)}, u32[]{:S(2)}) collective-permute-start(bf16[2,2,64,101]{3,2,1,0:T(8,128)(2,1)S(1)} %get-tuple-element.15), channel_id=1, source_target_pairs={{28,0},{0,4},{4,8},{8,12},{12,16},{16,20},{20,24},{24,28},{29,1},{... | collective-permute-start | bytes 155144 | tf_op jit(solution)/shard_map/ppermute | solution.py:19
  7.4 1.6 %collective-permute-start.1 = (bf16[2,2,64,101]{3,2,1,0:T(8,128)(2,1)S(1)}, bf16[2,2,64,101]{3,2,1,0:T(8,128)(2,1)S(1)}, u32[]{:S(2)}, u32[]{:S(2)}) collective-permute-start(bf16[2,2,64,101]{3,2,1,0:T(8,128)(2,1)S(1)} %get-tuple-element.14), channel_id=1, source_target_pairs={{24,0},{28,4},{0,8},{4,12},{8,16},{12,20},{16,24},{20,28},{25,1},{... | collective-permute-start | bytes 155144 | tf_op jit(solution)/shard_map/ppermute | solution.py:19
  9.0 2.5 %collective-permute-start.2 = (bf16[2,2,64,101]{3,2,1,0:T(8,128)(2,1)S(1)}, bf16[2,2,64,101]{3,2,1,0:T(8,128)(2,1)S(1)}, u32[]{:S(2)}, u32[]{:S(2)}) collective-permute-start(bf16[2,2,64,101]{3,2,1,0:T(8,128)(2,1)S(1)} %get-tuple-element.13), channel_id=1, source_target_pairs={{20,0},{24,4},{28,8},{0,12},{4,16},{8,20},{12,24},{16,28},{21,1},{... | collective-permute-start | bytes 155144 | tf_op jit(solution)/shard_map/ppermute | solution.py:19
  11.9 2.2 %collective-permute-start.4 = (bf16[2,2,64,101]{3,2,1,0:T(8,128)(2,1)S(1)}, bf16[2,2,64,101]{3,2,1,0:T(8,128)(2,1)S(1)}, u32[]{:S(2)}, u32[]{:S(2)}) collective-permute-start(bf16[2,2,64,101]{3,2,1,0:T(8,128)(2,1)S(1)} %get-tuple-element.11), channel_id=1, source_target_pairs={{12,0},{16,4},{20,8},{24,12},{28,16},{0,20},{4,24},{8,28},{13,1},{... | collective-permute-start | bytes 155144 | tf_op jit(solution)/shard_map/ppermute | solution.py:19
  14.1 1.9 %collective-permute-start.5 = (bf16[2,2,64,101]{3,2,1,0:T(8,128)(2,1)S(1)}, bf16[2,2,64,101]{3,2,1,0:T(8,128)(2,1)S(1)}, u32[]{:S(2)}, u32[]{:S(2)}) collective-permute-start(bf16[2,2,64,101]{3,2,1,0:T(8,128)(2,1)S(1)} %get-tuple-element.10), channel_id=1, source_target_pairs={{8,0},{12,4},{16,8},{20,12},{24,16},{28,20},{0,24},{4,28},{9,1},{1... | collective-permute-start | bytes 155144 | tf_op jit(solution)/shard_map/ppermute | solution.py:19
  15.9 1.5 %collective-permute-start.6 = (bf16[2,2,64,101]{3,2,1,0:T(8,128)(2,1)S(1)}, bf16[2,2,64,101]{3,2,1,0:T(8,128)(2,1)S(1)}, u32[]{:S(2)}, u32[]{:S(2)}) collective-permute-start(bf16[2,2,64,101]{3,2,1,0:T(8,128)(2,1)S(1)} %get-tuple-element.9), channel_id=1, source_target_pairs={{4,0},{8,4},{12,8},{16,12},{20,16},{24,20},{28,24},{0,28},{5,1},{9... | collective-permute-start | bytes 155144 | tf_op jit(solution)/shard_map/ppermute | solution.py:19
  17.4 1.6 %collective-permute-done.3 = bf16[2,2,64,101]{3,2,1,0:T(8,128)(2,1)S(1)} collective-permute-done((bf16[2,2,64,101]{3,2,1,0:T(8,128)(2,1)S(1)}, bf16[2,2,64,101]{3,2,1,0:T(8,128)(2,1)S(1)}, u32[]{:S(2)}, u32[]{:S(2)}) %collective-permute-start.3) | collective-permute-done | bytes 51744 | tf_op jit(solution)/shard_map/ppermute | solution.py:19
  19.1 1.8 %collective-permute-done.4 = bf16[2,2,64,101]{3,2,1,0:T(8,128)(2,1)S(1)} collective-permute-done((bf16[2,2,64,101]{3,2,1,0:T(8,128)(2,1)S(1)}, bf16[2,2,64,101]{3,2,1,0:T(8,128)(2,1)S(1)}, u32[]{:S(2)}, u32[]{:S(2)}) %collective-permute-start.4) | collective-permute-done | bytes 51744 | tf_op jit(solution)/shard_map/ppermute | solution.py:19
  22.6 12.3 %collective-permute-done.8 = bf16[1,8,2,2,64,101]{5,4,3,2,1,0:T(8,128)(2,1)S(1)} collective-permute-done((bf16[1,8,2,2,64,101]{5,4,3,2,1,0:T(8,128)(2,1)S(1)}, bf16[1,8,2,2,64,101]{5,4,3,2,1,0:T(8,128)(2,1)S(1)}, u32[]{:S(2)}, u32[]{:S(2)}) %collective-permute-start.8) | collective-permute-done | bytes 413728 | tf_op jit(solution)/shard_map/ppermute | solution.py:217
  35.2 1.5 %collective-permute-start.7 = (bf16[1,8,2,2,16,101]{5,4,3,2,1,0:T(8,128)(2,1)S(1)}, bf16[1,8,2,2,16,101]{5,4,3,2,1,0:T(8,128)(2,1)S(1)}, u32[]{:S(2)}, u32[]{:S(2)}) collective-permute-start(bf16[1,8,2,2,16,101]{5,4,3,2,1,0:T(8,128)(2,1)S(1)} %dynamic-slice_bitcast_fusion), channel_id=1, source_target_pairs={{28,0},{0,4},{4,8},{8,12},{12,16},{16,20},{20,24},{24,28},{29,1},{... | collective-permute-start | bytes 310280 | tf_op jit(solution)/shard_map/ppermute | solution.py:19
  37.6 1.4 %collective-permute-start.12 = (bf16[1,8,2,2,16,101]{5,4,3,2,1,0:T(8,128)(2,1)S(1)}, bf16[1,8,2,2,16,101]{5,4,3,2,1,0:T(8,128)(2,1)S(1)}, u32[]{:S(2)}, u32[]{:S(2)}) collective-permute-start(bf16[1,8,2,2,16,101]{5,4,3,2,1,0:T(8,128)(2,1)S(1)} %dynamic-slice_bitcast_fusion), channel_id=1, source_target_pairs={{24,0},{28,4},{0,8},{4,12},{8,16},{12,20},{16,24},{20,28},{25,1},{... | collective-permute-start | bytes 310280 | tf_op jit(solution)/shard_map/ppermute | solution.py:19
  39.0 2.2 %collective-permute-done.7 = bf16[1,8,2,2,16,101]{5,4,3,2,1,0:T(8,128)(2,1)S(1)} collective-permute-done((bf16[1,8,2,2,16,101]{5,4,3,2,1,0:T(8,128)(2,1)S(1)}, bf16[1,8,2,2,16,101]{5,4,3,2,1,0:T(8,128)(2,1)S(1)}, u32[]{:S(2)}, u32[]{:S(2)}) %collective-permute-start.7) | collective-permute-done | bytes 103456 | tf_op jit(solution)/shard_map/ppermute | solution.py:19
  41.2 2.9 %collective-permute-start.9 = (bf16[1,8,2,2,16,101]{5,4,3,2,1,0:T(8,128)(2,1)S(1)}, bf16[1,8,2,2,16,101]{5,4,3,2,1,0:T(8,128)(2,1)S(1)}, u32[]{:S(2)}, u32[]{:S(2)}) collective-permute-start(bf16[1,8,2,2,16,101]{5,4,3,2,1,0:T(8,128)(2,1)S(1)} %constant_dynamic-slice_fusion.1), channel_id=1, source_target_pairs={{28,0},{0,4},{4,8},{8,12},{12,16},{16,20},{20,24},{24,28},{29,1},{... | collective-permute-start | bytes 310280 | tf_op jit(solution)/shard_map/ppermute | solution.py:19
  45.6 2.4 %collective-permute-done.9 = bf16[1,8,2,2,16,101]{5,4,3,2,1,0:T(8,128)(2,1)S(1)} collective-permute-done((bf16[1,8,2,2,16,101]{5,4,3,2,1,0:T(8,128)(2,1)S(1)}, bf16[1,8,2,2,16,101]{5,4,3,2,1,0:T(8,128)(2,1)S(1)}, u32[]{:S(2)}, u32[]{:S(2)}) %collective-permute-start.9) | collective-permute-done | bytes 103456 | tf_op jit(solution)/shard_map/ppermute | solution.py:19
  48.1 3.4 %collective-permute-start.11 = (bf16[2,8,2,2,16,101]{5,4,3,2,1,0:T(8,128)(2,1)S(1)}, bf16[2,8,2,2,16,101]{5,4,3,2,1,0:T(8,128)(2,1)S(1)}, u32[]{:S(2)}, u32[]{:S(2)}) collective-permute-start(bf16[2,8,2,2,16,101]{5,4,3,2,1,0:T(8,128)(2,1)S(1)} %constant_dynamic-slice_fusion), channel_id=1, source_target_pairs={{28,0},{0,4},{4,8},{8,12},{12,16},{16,20},{20,24},{24,28},{29,1},{... | collective-permute-start | bytes 620552 | tf_op jit(solution)/shard_map/ppermute | solution.py:19
  54.4 1.5 %copy.13 = bf16[101,2,4,8,2,64]{0,5,4,3,2,1:T(8,128)(2,1)} copy(bf16[101,2,4,8,2,64]{0,5,1,4,3,2:T(8,128)(2,1)S(1)} %maximum_bitcast_fusion) | data formatting | bytes 3309568 | tf_op jit(solution)/shard_map/transpose | solution.py:222
  55.9 3.9 %copy.15 = bf16[101,128,64]{1,2,0:T(8,128)(2,1)S(1)} copy(bf16[101,128,64]{0,2,1:T(8,128)(2,1)} %bitcast.102) | data formatting | bytes 3309568 | tf_op jit(solution)/shard_map/reshape | solution.py:222
  59.9 4.5 %collective-permute-done.14 = bf16[2,8,2,2,16,101]{5,4,3,2,1,0:T(8,128)(2,1)S(1)} collective-permute-done((bf16[2,8,2,2,16,101]{5,4,3,2,1,0:T(8,128)(2,1)S(1)}, bf16[2,8,2,2,16,101]{5,4,3,2,1,0:T(8,128)(2,1)S(1)}, u32[]{:S(2)}, u32[]{:S(2)}) %collective-permute-start.14) | collective-permute-done | bytes 206880 | tf_op jit(solution)/shard_map/ppermute | solution.py:19
  65.5 2.2 %copy.14 = bf16[101,32,128]{2,1,0:T(8,128)(2,1)} copy(bf16[101,32,128]{0,1,2:T(8,128)(2,1)S(1)} %bitcast.105) | data formatting | bytes 1654784 | tf_op jit(solution)/shard_map/reshape | solution.py:231
  68.6 2.2 %copy.18 = bf16[101,32,128]{2,1,0:T(8,128)(2,1)} copy(bf16[101,32,128]{0,1,2:T(8,128)(2,1)S(1)} %bitcast.106) | data formatting | bytes 1654784 | tf_op jit(solution)/shard_map/reshape | solution.py:231
  72.9 2.1 %fusion.4 = f32[1,64,16,128]{3,1,2,0:T(8,128)S(1)} fusion(f32[101,2,16,64]{3,2,1,0:T(8,128)S(1)} %bitcast.104, f32[1,101,128]{2,1,0:T(8,128)S(1)} %copy-done.8, f32[1,101,128]{2,1,0:T(8,128)S(1)} %copy-done.7), kind=kOutput, calls=%fused_computation.6 | convolution fusion | flops 158885120 | bytes 1455104 | tf_op jit(solution)/shard_map/fcij,cfl->jil/dot_general | solution.py:235
  75.0 2.1 %fusion.7 = f32[1,64,16,128]{3,1,2,0:T(8,128)S(1)} fusion(f32[101,2,16,64]{3,2,1,0:T(8,128)S(1)} %bitcast.103, f32[1,101,128]{2,1,0:T(8,128)S(1)} %copy-done.8, f32[1,101,128]{2,1,0:T(8,128)S(1)} %copy-done.7), kind=kOutput, calls=%fused_computation.7 | convolution fusion | flops 158885120 | bytes 1455104 | tf_op jit(solution)/shard_map/fcij,cfl->jil/dot_general | solution.py:235
  77.2 1.6 %copy.21 = f32[2,64,16,128]{3,2,1,0:T(8,128)} copy(f32[2,64,16,128]{3,1,2,0:T(8,128)S(1)} %pad_maximum_fusion.1) | data formatting | bytes 2097152 | tf_op jit(solution)/shard_map/stack | solution.py:237
  (85 shorter events, 16.4 us)
Async XLA Ops:
  0.0 2.7 %copy-start.2 = (f32[1,400,512]{2,1,0:T(8,128)S(1)}, f32[1,400,512]{2,1,0:T(8,128)}, u32[]{:S(2)}) copy-start(f32[1,400,512]{2,1,0:T(8,128)} %param.3) | copy-start | bytes 2457604
  3.5 1.4 %copy-start.10 = (s32[512]{0:T(512)S(1)}, s32[512]{0:T(512)}, u32[]{:S(2)}) copy-start(s32[512]{0:T(512)} %param.4) | copy-start | bytes 6148
  5.8 8.2 %collective-permute-start = (bf16[2,2,64,101]{3,2,1,0:T(8,128)(2,1)S(1)}, bf16[2,2,64,101]{3,2,1,0:T(8,128)(2,1)S(1)}, u32[]{:S(2)}, u32[]{:S(2)}) collective-permute-start(bf16[2,2,64,101]{3,2,1,0:T(8,128)(2,1)S(1)} %get-tuple-element.15), channel_id=1, source_target_pairs={{28,0},{0,4},{4,8},{8,12},{12,16},{16,20},{20,24},{24,28},{29,1},{... | collective-permute-start | bytes 155144 | tf_op jit(solution)/shard_map/ppermute | solution.py:19
  7.4 8.5 %collective-permute-start.1 = (bf16[2,2,64,101]{3,2,1,0:T(8,128)(2,1)S(1)}, bf16[2,2,64,101]{3,2,1,0:T(8,128)(2,1)S(1)}, u32[]{:S(2)}, u32[]{:S(2)}) collective-permute-start(bf16[2,2,64,101]{3,2,1,0:T(8,128)(2,1)S(1)} %get-tuple-element.14), channel_id=1, source_target_pairs={{24,0},{28,4},{0,8},{4,12},{8,16},{12,20},{16,24},{20,28},{25,1},{... | collective-permute-start | bytes 155144 | tf_op jit(solution)/shard_map/ppermute | solution.py:19
  9.0 8.4 %collective-permute-start.2 = (bf16[2,2,64,101]{3,2,1,0:T(8,128)(2,1)S(1)}, bf16[2,2,64,101]{3,2,1,0:T(8,128)(2,1)S(1)}, u32[]{:S(2)}, u32[]{:S(2)}) collective-permute-start(bf16[2,2,64,101]{3,2,1,0:T(8,128)(2,1)S(1)} %get-tuple-element.13), channel_id=1, source_target_pairs={{20,0},{24,4},{28,8},{0,12},{4,16},{8,20},{12,24},{16,28},{21,1},{... | collective-permute-start | bytes 155144 | tf_op jit(solution)/shard_map/ppermute | solution.py:19
  11.5 7.6 %collective-permute-start.3 = (bf16[2,2,64,101]{3,2,1,0:T(8,128)(2,1)S(1)}, bf16[2,2,64,101]{3,2,1,0:T(8,128)(2,1)S(1)}, u32[]{:S(2)}, u32[]{:S(2)}) collective-permute-start(bf16[2,2,64,101]{3,2,1,0:T(8,128)(2,1)S(1)} %get-tuple-element.12), channel_id=1, source_target_pairs={{16,0},{20,4},{24,8},{28,12},{0,16},{4,20},{8,24},{12,28},{17,1},{... | collective-permute-start | bytes 155144 | tf_op jit(solution)/shard_map/ppermute | solution.py:19
  11.9 9.0 %collective-permute-start.4 = (bf16[2,2,64,101]{3,2,1,0:T(8,128)(2,1)S(1)}, bf16[2,2,64,101]{3,2,1,0:T(8,128)(2,1)S(1)}, u32[]{:S(2)}, u32[]{:S(2)}) collective-permute-start(bf16[2,2,64,101]{3,2,1,0:T(8,128)(2,1)S(1)} %get-tuple-element.11), channel_id=1, source_target_pairs={{12,0},{16,4},{20,8},{24,12},{28,16},{0,20},{4,24},{8,28},{13,1},{... | collective-permute-start | bytes 155144 | tf_op jit(solution)/shard_map/ppermute | solution.py:19
  14.1 6.8 %collective-permute-start.5 = (bf16[2,2,64,101]{3,2,1,0:T(8,128)(2,1)S(1)}, bf16[2,2,64,101]{3,2,1,0:T(8,128)(2,1)S(1)}, u32[]{:S(2)}, u32[]{:S(2)}) collective-permute-start(bf16[2,2,64,101]{3,2,1,0:T(8,128)(2,1)S(1)} %get-tuple-element.10), channel_id=1, source_target_pairs={{8,0},{12,4},{16,8},{20,12},{24,16},{28,20},{0,24},{4,28},{9,1},{1... | collective-permute-start | bytes 155144 | tf_op jit(solution)/shard_map/ppermute | solution.py:19
  15.9 6.0 %collective-permute-start.6 = (bf16[2,2,64,101]{3,2,1,0:T(8,128)(2,1)S(1)}, bf16[2,2,64,101]{3,2,1,0:T(8,128)(2,1)S(1)}, u32[]{:S(2)}, u32[]{:S(2)}) collective-permute-start(bf16[2,2,64,101]{3,2,1,0:T(8,128)(2,1)S(1)} %get-tuple-element.9), channel_id=1, source_target_pairs={{4,0},{8,4},{12,8},{16,12},{20,16},{24,20},{28,24},{0,28},{5,1},{9... | collective-permute-start | bytes 155144 | tf_op jit(solution)/shard_map/ppermute | solution.py:19
  22.0 12.9 %collective-permute-start.8 = (bf16[1,8,2,2,64,101]{5,4,3,2,1,0:T(8,128)(2,1)S(1)}, bf16[1,8,2,2,64,101]{5,4,3,2,1,0:T(8,128)(2,1)S(1)}, u32[]{:S(2)}, u32[]{:S(2)}) collective-permute-start(bf16[1,8,2,2,64,101]{5,4,3,2,1,0:T(8,128)(2,1)S(1)} %bitcast.111), channel_id=1, source_target_pairs={{0,2},{1,3},{2,0},{3,1},{4,6},{5,7},{6,4},{7,5},{8,10},{9,11},{10,... | collective-permute-start | bytes 1241096 | tf_op jit(solution)/shard_map/ppermute | solution.py:217
  35.1 12.9 %collective-permute-start.10 = (bf16[2,8,2,2,64,101]{5,4,3,2,1,0:T(8,128)(2,1)S(1)}, bf16[2,8,2,2,64,101]{5,4,3,2,1,0:T(8,128)(2,1)S(1)}, u32[]{:S(2)}, u32[]{:S(2)}) collective-permute-start(bf16[2,8,2,2,64,101]{5,4,3,2,1,0:T(8,128)(2,1)S(1)} %pad_maximum_fusion), channel_id=1, source_target_pairs={{0,1},{1,0},{2,3},{3,2},{4,5},{5,4},{6,7},{7,6},{8,9},{9,8},{10,11... | collective-permute-start | bytes 2482184 | tf_op jit(solution)/shard_map/ppermute | solution.py:217
  35.2 5.9 %collective-permute-start.7 = (bf16[1,8,2,2,16,101]{5,4,3,2,1,0:T(8,128)(2,1)S(1)}, bf16[1,8,2,2,16,101]{5,4,3,2,1,0:T(8,128)(2,1)S(1)}, u32[]{:S(2)}, u32[]{:S(2)}) collective-permute-start(bf16[1,8,2,2,16,101]{5,4,3,2,1,0:T(8,128)(2,1)S(1)} %dynamic-slice_bitcast_fusion), channel_id=1, source_target_pairs={{28,0},{0,4},{4,8},{8,12},{12,16},{16,20},{20,24},{24,28},{29,1},{... | collective-permute-start | bytes 310280 | tf_op jit(solution)/shard_map/ppermute | solution.py:19
  37.6 7.4 %collective-permute-start.12 = (bf16[1,8,2,2,16,101]{5,4,3,2,1,0:T(8,128)(2,1)S(1)}, bf16[1,8,2,2,16,101]{5,4,3,2,1,0:T(8,128)(2,1)S(1)}, u32[]{:S(2)}, u32[]{:S(2)}) collective-permute-start(bf16[1,8,2,2,16,101]{5,4,3,2,1,0:T(8,128)(2,1)S(1)} %dynamic-slice_bitcast_fusion), channel_id=1, source_target_pairs={{24,0},{28,4},{0,8},{4,12},{8,16},{12,20},{16,24},{20,28},{25,1},{... | collective-permute-start | bytes 310280 | tf_op jit(solution)/shard_map/ppermute | solution.py:19
  41.2 6.7 %collective-permute-start.9 = (bf16[1,8,2,2,16,101]{5,4,3,2,1,0:T(8,128)(2,1)S(1)}, bf16[1,8,2,2,16,101]{5,4,3,2,1,0:T(8,128)(2,1)S(1)}, u32[]{:S(2)}, u32[]{:S(2)}) collective-permute-start(bf16[1,8,2,2,16,101]{5,4,3,2,1,0:T(8,128)(2,1)S(1)} %constant_dynamic-slice_fusion.1), channel_id=1, source_target_pairs={{28,0},{0,4},{4,8},{8,12},{12,16},{16,20},{20,24},{24,28},{29,1},{... | collective-permute-start | bytes 310280 | tf_op jit(solution)/shard_map/ppermute | solution.py:19
  45.0 6.8 %collective-permute-start.13 = (bf16[1,8,2,2,16,101]{5,4,3,2,1,0:T(8,128)(2,1)S(1)}, bf16[1,8,2,2,16,101]{5,4,3,2,1,0:T(8,128)(2,1)S(1)}, u32[]{:S(2)}, u32[]{:S(2)}) collective-permute-start(bf16[1,8,2,2,16,101]{5,4,3,2,1,0:T(8,128)(2,1)S(1)} %constant_dynamic-slice_fusion.1), channel_id=1, source_target_pairs={{24,0},{28,4},{0,8},{4,12},{8,16},{12,20},{16,24},{20,28},{25,1},{... | collective-permute-start | bytes 310280 | tf_op jit(solution)/shard_map/ppermute | solution.py:19
  48.0 3.9 %copy-start.5 = (bf16[4,8,2,2,16,101]{5,4,3,2,1,0:T(8,128)(2,1)}, bf16[4,8,2,2,16,101]{5,4,3,2,1,0:T(8,128)(2,1)S(1)}, u32[]{:S(2)}) copy-start(bf16[4,8,2,2,16,101]{5,4,3,2,1,0:T(8,128)(2,1)S(1)} %constant_dynamic-update-slice_fusion.1) | copy-start | bytes 1241092
  48.1 11.8 %collective-permute-start.11 = (bf16[2,8,2,2,16,101]{5,4,3,2,1,0:T(8,128)(2,1)S(1)}, bf16[2,8,2,2,16,101]{5,4,3,2,1,0:T(8,128)(2,1)S(1)}, u32[]{:S(2)}, u32[]{:S(2)}) collective-permute-start(bf16[2,8,2,2,16,101]{5,4,3,2,1,0:T(8,128)(2,1)S(1)} %constant_dynamic-slice_fusion), channel_id=1, source_target_pairs={{28,0},{0,4},{4,8},{8,12},{12,16},{16,20},{20,24},{24,28},{29,1},{... | collective-permute-start | bytes 620552 | tf_op jit(solution)/shard_map/ppermute | solution.py:19
  52.7 11.8 %collective-permute-start.14 = (bf16[2,8,2,2,16,101]{5,4,3,2,1,0:T(8,128)(2,1)S(1)}, bf16[2,8,2,2,16,101]{5,4,3,2,1,0:T(8,128)(2,1)S(1)}, u32[]{:S(2)}, u32[]{:S(2)}) collective-permute-start(bf16[2,8,2,2,16,101]{5,4,3,2,1,0:T(8,128)(2,1)S(1)} %constant_dynamic-slice_fusion), channel_id=1, source_target_pairs={{24,0},{28,4},{0,8},{4,12},{8,16},{12,20},{16,24},{20,28},{25,1},{... | collective-permute-start | bytes 620552 | tf_op jit(solution)/shard_map/ppermute | solution.py:19
  55.9 3.9 %copy-start.6 = (bf16[4,8,2,2,16,101]{5,4,3,2,1,0:T(8,128)(2,1)S(1)}, bf16[4,8,2,2,16,101]{5,4,3,2,1,0:T(8,128)(2,1)}, u32[]{:S(2)}) copy-start(bf16[4,8,2,2,16,101]{5,4,3,2,1,0:T(8,128)(2,1)} %copy-done.5) | copy-start | bytes 1241092
  55.9 8.5 %copy-start.4 = (bf16[4,8,2,2,16,101]{5,4,3,2,1,0:T(8,128)(2,1)S(1)}, bf16[4,8,2,2,16,101]{5,4,3,2,1,0:T(8,128)(2,1)}, u32[]{:S(2)}) copy-start(bf16[4,8,2,2,16,101]{5,4,3,2,1,0:T(8,128)(2,1)} %copy-done.3) | copy-start | bytes 1241092
  68.3 2.5 %copy-start = (bf16[101,32,128]{2,1,0:T(8,128)(2,1)S(1)}, bf16[101,32,128]{2,1,0:T(8,128)(2,1)}, u32[]{:S(2)}) copy-start(bf16[101,32,128]{2,1,0:T(8,128)(2,1)} %copy.14) | copy-start | bytes 2482180
  70.8 1.1 %copy-start.1 = (bf16[101,32,128]{2,1,0:T(8,128)(2,1)S(1)}, bf16[101,32,128]{2,1,0:T(8,128)(2,1)}, u32[]{:S(2)}) copy-start(bf16[101,32,128]{2,1,0:T(8,128)(2,1)} %copy.18) | copy-start | bytes 2482180
  71.9 1.0 %copy-start.7 = (f32[1,101,128]{2,1,0:T(8,128)S(1)}, f32[1,101,128]{2,1,0:T(8,128)}, u32[]{:S(2)}) copy-start(f32[1,101,128]{2,1,0:T(8,128)} %get-tuple-element.18) | copy-start | bytes 155140
  71.9 1.0 %copy-start.8 = (f32[1,101,128]{2,1,0:T(8,128)S(1)}, f32[1,101,128]{2,1,0:T(8,128)}, u32[]{:S(2)}) copy-start(f32[1,101,128]{2,1,0:T(8,128)} %get-tuple-element.19) | copy-start | bytes 155140
  (2 other events, 1.7 us)

commit v10 on v5

--- a/solution.py
+++ b/solution.py
@@ -4,6 +4,7 @@
 import jax.numpy as jnp
 from jax import lax
 from jax.sharding import PartitionSpec as P
+
 
 L = 200
 FB = 101
@@ -117,30 +118,59 @@
     slice_width = block_width // tm_count
     windows = records.reshape(samples // L, L, channels)
     spectra = whiten_planes(windows, live_mask, lax.Precision.HIGH)
-    sorted_spec = jnp.take(spectra, chan_order, axis=2)
+    picks = (chan_order[:, None] == jnp.arange(channels, dtype=chan_order.dtype)[None, :])
+    sorted_spec = jnp.einsum(
+        "kh,wchf->wckf", picks.astype(jnp.bfloat16), spectra, preferred_element_type=jnp.float32
+    ).astype(jnp.bfloat16)
     sorted_spec = sorted_spec.reshape(spectra.shape[0], 2, chan_count, block_width, FB)
     sorted_spec = jnp.moveaxis(sorted_spec, 2, 0)
-    pieces = []
-    for distance in range(chan_count):
-        target = jnp.mod(chan_position + distance, chan_count)
-        piece = lax.dynamic_index_in_dim(sorted_spec, target, 0, keepdims=False)
-        pieces.append(piece if distance == 0 else shifted(piece, "chan", distance))
-    own = jnp.stack(pieces)
+    if chan_count % 2 == 0 and chan_count > 2:
+        outer = chan_count // 2
+        outer_position, inner_position = chan_position // 2, chan_position % 2
+        outer_index = jnp.arange(outer, dtype=jnp.int32)
+        theirs = jnp.take(sorted_spec, outer_index * 2 + (1 - inner_position), axis=0)
+        mine = jnp.take(sorted_spec, outer_index * 2 + inner_position, axis=0)
+        arrived = lax.ppermute(theirs, "chan", [(i, i ^ 1) for i in range(chan_count)])
+        held = jnp.stack([mine, arrived], axis=1)
+        pieces = []
+        for distance in range(outer):
+            target = jnp.mod(outer_position + distance, outer)
+            piece = lax.dynamic_index_in_dim(held, target, 0, keepdims=False)
+            pieces.append(piece if distance == 0 else shifted(piece, "chan", 2 * distance))
+        by_shift = jnp.stack(pieces).reshape((chan_count,) + held.shape[2:])
+        source = jnp.arange(chan_count, dtype=jnp.int32)
+        slot = jnp.mod(outer_position - source // 2, outer) * 2 + jnp.bitwise_xor(source % 2, inner_position)
+        own = jnp.take(by_shift, slot, axis=0)
+    else:
+        pieces = []
+        for distance in range(chan_count):
+            target = jnp.mod(chan_position + distance, chan_count)
+            piece = lax.dynamic_index_in_dim(sorted_spec, target, 0, keepdims=False)
+            pieces.append(piece if distance == 0 else shifted(piece, "chan", distance))
+        by_shift = jnp.stack(pieces)
+        source = jnp.arange(chan_count, dtype=jnp.int32)
+        own = jnp.take(by_shift, jnp.mod(chan_position - source, chan_count), axis=0)
+    offsets = [max(1, round_index * chan_count // 4) for round_index in range(ROUNDS)]
+
+    def send_slices(group):
+        piece = lax.dynamic_slice_in_dim(group, tm_position * slice_width, slice_width, axis=4)
+        return [shifted(piece, "chan", offset) for offset in offsets]
+
     gathered = own[None]
+    partner_groups = [send_slices(gathered)]
     step = tm_count // 2
     while step >= 1:
         route = [(q, q ^ step) for q in range(tm_count)]
-        gathered = jnp.concatenate([gathered, lax.ppermute(gathered, "tm", route)], axis=0)
+        arrived = lax.ppermute(gathered, "tm", route)
+        partner_groups.append(send_slices(arrived))
+        gathered = jnp.concatenate([gathered, arrived], axis=0)
         step //= 2
     windows_all = gathered.shape[0] * gathered.shape[1] * gathered.shape[2]
     own_spec = jnp.transpose(gathered, (5, 3, 0, 1, 2, 4)).reshape(FB, 2 * windows_all, block_width)
-    my_slice = lax.dynamic_slice_in_dim(gathered, tm_position * slice_width, slice_width, axis=4)
     inverse = inverse_table()
     results = []
     for round_index in range(ROUNDS):
-        offset = max(1, round_index * chan_count // 4)
-        partner = shifted(my_slice, "chan", offset)
-        partner = jnp.roll(partner, offset, axis=1)
+        partner = jnp.concatenate([group[round_index] for group in partner_groups], axis=0)
         rotated = jnp.stack([-partner[:, :, :, 1], partner[:, :, :, 0]], axis=3)
         both = jnp.stack([partner, rotated])
         both = jnp.transpose(both, (6, 0, 5, 4, 1, 2, 3)).reshape(FB, 2 * slice_width, 2 * windows_all)

time: 81.8 us -> 89.1 us (1.089); the launches traced: 81.4 us -> 87.7 us
  waiting for transfers between devices: 33.2 us -> 37 us
  starting transfers between devices: 15.2 us -> 17.6 us
    ppermute x2 -> x3, waiting for transfers between devices: 14.9 us -> 19.9 us  [the longest x2 13.2 us: on_device_local(): arrived = lax.ppermute(gathered, 'tm', route)]
    slice x4 -> x0, local copies, waits for them, and re-layouts: 1.98 us -> none  [on_device_local(): partner = jnp.roll(partner, offset, axis=1)]
    ppermute x9, starting transfers between devices: 14.5 us -> 16.4 us  [shifted(): return lax.ppermute(block, axis, route)]
    concatenate x0 -> x2, local copies, waits for them, and re-layouts: none -> 1.71 us  [on_device_local(): jnp.concatenate([group[round_index] for group in partner_groups], axis=0)]
    ppermute x9, waiting for transfers between devices: 18.3 us -> 17.1 us  [shifted(): return lax.ppermute(block, axis, route)]
    neg x2, other arithmetic: 0.27 us -> 1.19 us  [on_device_local(): rotated = jnp.stack([-partner[:, :, :, 1], partner[:, :, :, 0]], axis=3)]
    gather x2 -> x3, local copies, waits for them, and re-layouts: 2.36 us -> 1.84 us  [the longest x1 0.65 us: on_device_local(): own = jnp.take(by_shift, slot, axis=0)]
  transfers between devices with their start and end apart: 11 -> 12, of which waited for: 7 -> 9; matrix products, arithmetic and copies ran while one was open for 11% -> 12% of each run, Pallas kernels for 0% -> 0%
where the time goes in v10:
time: 89.1 us; the launch traced here: 87.7 us
  waiting for transfers between devices  37 us (42%)
  starting transfers between devices  17.6 us (20%)
  local copies, waits for them, and re-layouts  16.8 us (19%)
  matrix products  8.79 us (10%)
  other arithmetic  6.99 us (8%)
    ppermute x9, waiting for transfers between devices, shifted(): return lax.ppermute(block, axis, route)  17.1 us
    ppermute x9, starting transfers between devices, shifted(): return lax.ppermute(block, axis, route)  16.4 us
    ppermute x2, waiting for transfers between devices, on_device_local(): arrived = lax.ppermute(gathered, 'tm', route)  13.2 us
    ppermute x1, waiting for transfers between devices, on_device_local(): lax.ppermute(theirs, 'chan', [(i, i ^ 1) for i in range(chan_count)])  6.76 us
    dot_general x2, matrix products, on_device_local(): jnp.einsum('fcij,cfl->jil', sums, inverse, precision=lax.Precision.HIGH)  4.19 us
    reshape x1, local copies, waits for them, and re-layouts, on_device_local(): jnp.transpose(gathered, (5, 3, 0, 1, 2, 4))  3.79 us
    reshape x2, local copies, waits for them, and re-layouts, on_device_local(): jnp.transpose(both, (6, 0, 5, 4, 1, 2, 3))  3.62 us
    dot_general x2, matrix products, on_device_local(): jnp.einsum('fnk,fkj->fnj', both, own_spec, preferred_element_type=jnp.flo...  1.94 us
  transfers between devices with their start and end apart: 12, of which 9 were waited for; matrix products, arithmetic and copies ran while one was open for 12% of the time, Pallas kernels for 0%

profile of v10, /device:TPU:6, one launch (start us, length us, event | category | flops | bytes accessed | tf_op | source)
XLA Modules:
  0.0 87.7 jit_solution(16837824684768441041)
XLA Ops:
  0.2 1.3 %reduce_sum.36 = f32[2,512]{1,0:T(2,128)S(1)} reduce(f32[2,200,512]{2,1,0:T(8,128)} %bitcast.100, f32[]{:T(128)} %constant.171.clone.1), dimensions={1}, to_apply=%region_0.0 | reduce | flops 203776 | bytes 823300 | tf_op jit(solution)/shard_map/reduce_sum | solution.py:98
  1.5 1.3 %multiply_reduce_fusion = f32[2,512]{1,0:T(2,128)S(1)} fusion(f32[2,200,512]{2,1,0:T(8,128)} %bitcast.101, f32[2,512]{1,0:T(2,128)S(1)} %broadcast_multiply_fusion.1), kind=kLoop, calls=%fused_computation.22 | loop fusion | flops 613376 | bytes 827392 | tf_op jit(solution)/shard_map/reduce_sum | solution.py:100
  7.9 6.8 %collective-permute-done = bf16[4,2,2,64,101]{4,3,2,1,0:T(8,128)(2,1)S(1)} collective-permute-done((bf16[4,2,2,64,101]{4,3,2,1,0:T(8,128)(2,1)S(1)}, bf16[4,2,2,64,101]{4,3,2,1,0:T(8,128)(2,1)S(1)}, u32[]{:S(2)}, u32[]{:S(2)}) %collective-permute-start) | collective-permute-done | bytes 206880 | tf_op jit(solution)/shard_map/ppermute | solution.py:133
  14.8 1.6 %collective-permute-start.1 = (bf16[2,2,2,64,101]{4,3,2,1,0:T(8,128)(2,1)S(1)}, bf16[2,2,2,64,101]{4,3,2,1,0:T(8,128)(2,1)S(1)}, u32[]{:S(2)}, u32[]{:S(2)}) collective-permute-start(bf16[2,2,2,64,101]{4,3,2,1,0:T(8,128)(2,1)S(1)} %get-tuple-element.11), channel_id=1, source_target_pairs={{24,0},{28,4},{0,8},{4,12},{8,16},{12,20},{16,24},{20,28},{25,1},{... | collective-permute-start | bytes 310280 | tf_op jit(solution)/shard_map/ppermute | solution.py:19
  16.4 2.6 %collective-permute-start.2 = (bf16[2,2,2,64,101]{4,3,2,1,0:T(8,128)(2,1)S(1)}, bf16[2,2,2,64,101]{4,3,2,1,0:T(8,128)(2,1)S(1)}, u32[]{:S(2)}, u32[]{:S(2)}) collective-permute-start(bf16[2,2,2,64,101]{4,3,2,1,0:T(8,128)(2,1)S(1)} %get-tuple-element.12), channel_id=1, source_target_pairs={{16,0},{20,4},{24,8},{28,12},{0,16},{4,20},{8,24},{12,28},{17,1},{... | collective-permute-start | bytes 310280 | tf_op jit(solution)/shard_map/ppermute | solution.py:19
  19.0 1.3 %collective-permute-start.3 = (bf16[2,2,2,64,101]{4,3,2,1,0:T(8,128)(2,1)S(1)}, bf16[2,2,2,64,101]{4,3,2,1,0:T(8,128)(2,1)S(1)}, u32[]{:S(2)}, u32[]{:S(2)}) collective-permute-start(bf16[2,2,2,64,101]{4,3,2,1,0:T(8,128)(2,1)S(1)} %get-tuple-element.13), channel_id=1, source_target_pairs={{8,0},{12,4},{16,8},{20,12},{24,16},{28,20},{0,24},{4,28},{9,1},{1... | collective-permute-start | bytes 310280 | tf_op jit(solution)/shard_map/ppermute | solution.py:19
  20.4 2.8 %collective-permute-done.1 = bf16[2,2,2,64,101]{4,3,2,1,0:T(8,128)(2,1)S(1)} collective-permute-done((bf16[2,2,2,64,101]{4,3,2,1,0:T(8,128)(2,1)S(1)}, bf16[2,2,2,64,101]{4,3,2,1,0:T(8,128)(2,1)S(1)}, u32[]{:S(2)}, u32[]{:S(2)}) %collective-permute-start.1) | collective-permute-done | bytes 103456 | tf_op jit(solution)/shard_map/ppermute | solution.py:19
  23.1 3.7 %collective-permute-done.2 = bf16[2,2,2,64,101]{4,3,2,1,0:T(8,128)(2,1)S(1)} collective-permute-done((bf16[2,2,2,64,101]{4,3,2,1,0:T(8,128)(2,1)S(1)}, bf16[2,2,2,64,101]{4,3,2,1,0:T(8,128)(2,1)S(1)}, u32[]{:S(2)}, u32[]{:S(2)}) %collective-permute-start.2) | collective-permute-done | bytes 103456 | tf_op jit(solution)/shard_map/ppermute | solution.py:19
  28.5 13.2 %collective-permute-done.5 = bf16[1,8,2,2,64,101]{5,4,3,2,1,0:T(8,128)(2,1)S(1)} collective-permute-done((bf16[1,8,2,2,64,101]{5,4,3,2,1,0:T(8,128)(2,1)S(1)}, bf16[1,8,2,2,64,101]{5,4,3,2,1,0:T(8,128)(2,1)S(1)}, u32[]{:S(2)}, u32[]{:S(2)}) %collective-permute-start.5) | collective-permute-done | bytes 413728 | tf_op jit(solution)/shard_map/ppermute | solution.py:164
  42.1 3.3 %collective-permute-start.4 = (bf16[1,8,2,2,16,101]{5,4,3,2,1,0:T(8,128)(2,1)S(1)}, bf16[1,8,2,2,16,101]{5,4,3,2,1,0:T(8,128)(2,1)S(1)}, u32[]{:S(2)}, u32[]{:S(2)}) collective-permute-start(bf16[1,8,2,2,16,101]{5,4,3,2,1,0:T(8,128)(2,1)S(1)} %fusion.30), channel_id=1, source_target_pairs={{28,0},{0,4},{4,8},{8,12},{12,16},{16,20},{20,24},{24,28},{29,1},{... | collective-permute-start | bytes 310280 | tf_op jit(solution)/shard_map/ppermute | solution.py:19
  46.4 2.9 %collective-permute-done.4 = bf16[1,8,2,2,16,101]{5,4,3,2,1,0:T(8,128)(2,1)S(1)} collective-permute-done((bf16[1,8,2,2,16,101]{5,4,3,2,1,0:T(8,128)(2,1)S(1)}, bf16[1,8,2,2,16,101]{5,4,3,2,1,0:T(8,128)(2,1)S(1)}, u32[]{:S(2)}, u32[]{:S(2)}) %collective-permute-start.4) | collective-permute-done | bytes 103456 | tf_op jit(solution)/shard_map/ppermute | solution.py:19
  49.3 3.4 %collective-permute-start.6 = (bf16[1,8,2,2,16,101]{5,4,3,2,1,0:T(8,128)(2,1)S(1)}, bf16[1,8,2,2,16,101]{5,4,3,2,1,0:T(8,128)(2,1)S(1)}, u32[]{:S(2)}, u32[]{:S(2)}) collective-permute-start(bf16[1,8,2,2,16,101]{5,4,3,2,1,0:T(8,128)(2,1)S(1)} %constant_dynamic-slice_fusion.1), channel_id=1, source_target_pairs={{28,0},{0,4},{4,8},{8,12},{12,16},{16,20},{20,24},{24,28},{29,1},{... | collective-permute-start | bytes 310280 | tf_op jit(solution)/shard_map/ppermute | solution.py:19
  54.2 2.4 %collective-permute-done.6 = bf16[1,8,2,2,16,101]{5,4,3,2,1,0:T(8,128)(2,1)S(1)} collective-permute-done((bf16[1,8,2,2,16,101]{5,4,3,2,1,0:T(8,128)(2,1)S(1)}, bf16[1,8,2,2,16,101]{5,4,3,2,1,0:T(8,128)(2,1)S(1)}, u32[]{:S(2)}, u32[]{:S(2)}) %collective-permute-start.6) | collective-permute-done | bytes 103456 | tf_op jit(solution)/shard_map/ppermute | solution.py:19
  57.4 3.4 %collective-permute-start.8 = (bf16[2,8,2,2,16,101]{5,4,3,2,1,0:T(8,128)(2,1)}, bf16[2,8,2,2,16,101]{5,4,3,2,1,0:T(8,128)(2,1)S(1)}, u32[]{:S(2)}, u32[]{:S(2)}) collective-permute-start(bf16[2,8,2,2,16,101]{5,4,3,2,1,0:T(8,128)(2,1)} %constant_dynamic-slice_fusion), channel_id=1, source_target_pairs={{28,0},{0,4},{4,8},{8,12},{12,16},{16,20},{20,24},{24,28},{29,1},{... | collective-permute-start | bytes 620552 | tf_op jit(solution)/shard_map/ppermute | solution.py:19
  62.1 1.5 %copy.18 = bf16[101,2,4,8,2,64]{0,5,4,3,2,1:T(8,128)(2,1)} copy(bf16[101,2,4,8,2,64]{0,5,1,4,3,2:T(8,128)(2,1)S(1)} %maximum_bitcast_fusion) | data formatting | bytes 3309568 | tf_op jit(solution)/shard_map/transpose | solution.py:169
  63.7 3.8 %copy.20 = bf16[101,128,64]{1,2,0:T(8,128)(2,1)S(1)} copy(bf16[101,128,64]{0,2,1:T(8,128)(2,1)} %bitcast.95) | data formatting | bytes 3309568 | tf_op jit(solution)/shard_map/reshape | solution.py:169
  68.3 1.5 %copy.19 = bf16[101,32,128]{2,1,0:T(8,128)(2,1)S(1)} copy(bf16[101,32,128]{0,1,2:T(8,128)(2,1)S(1)} %bitcast.98) | data formatting | bytes 1654784 | tf_op jit(solution)/shard_map/reshape | solution.py:176
  69.7 4.3 %collective-permute-done.11 = bf16[2,8,2,2,16,101]{5,4,3,2,1,0:T(8,128)(2,1)} collective-permute-done((bf16[2,8,2,2,16,101]{5,4,3,2,1,0:T(8,128)(2,1)}, bf16[2,8,2,2,16,101]{5,4,3,2,1,0:T(8,128)(2,1)}, u32[]{:S(2)}, u32[]{:S(2)}) %collective-permute-start.11) | collective-permute-done | bytes 206880 | tf_op jit(solution)/shard_map/ppermute | solution.py:19
  74.0 1.7 %constant_dynamic-update-slice_fusion.3 = bf16[4,8,2,2,16,101]{5,4,3,2,1,0:T(8,128)(2,1)} fusion(bf16[4,8,2,2,16,101]{5,4,3,2,1,0:T(8,128)(2,1)} %copy-done.2, bf16[2,8,2,2,16,101]{5,4,3,2,1,0:T(8,128)(2,1)} %collective-permute-done.11), kind=kLoop, calls=%fused_computation.96 | loop fusion | bytes 524288 | tf_op jit(solution)/shard_map/concatenate | solution.py:173
  75.7 1.1 %slice_negate_fusion = (bf16[4,8,2,1,16,101]{5,4,3,2,1,0:T(8,128)(2,1)S(1)}, bf16[4,8,2,1,16,101]{5,4,3,2,1,0:T(8,128)(2,1)S(1)}) fusion(bf16[4,8,2,2,16,101]{5,4,3,2,1,0:T(8,128)(2,1)} %constant_dynamic-update-slice_fusion.3), kind=kLoop, calls=%fused_computation.45 | loop fusion | flops 103424 | bytes 827392 | tf_op jit(solution)/shard_map/neg | solution.py:174
  77.5 2.2 %copy.23 = bf16[101,32,128]{2,1,0:T(8,128)(2,1)} copy(bf16[101,32,128]{0,1,2:T(8,128)(2,1)S(1)} %bitcast.99) | data formatting | bytes 1654784 | tf_op jit(solution)/shard_map/reshape | solution.py:176
  81.8 2.1 %fusion.4 = f32[1,64,16,128]{3,1,2,0:T(8,128)S(1)} fusion(f32[101,2,16,64]{3,2,1,0:T(8,128)S(1)} %bitcast.97, f32[1,101,128]{2,1,0:T(8,128)S(1)} %copy-done.5, f32[1,101,128]{2,1,0:T(8,128)S(1)} %copy-done.4), kind=kOutput, calls=%fused_computation.9 | convolution fusion | flops 158885120 | bytes 1455104 | tf_op jit(solution)/shard_map/fcij,cfl->jil/dot_general | solution.py:180
  83.9 2.1 %fusion.7 = f32[1,64,16,128]{3,1,2,0:T(8,128)S(1)} fusion(f32[101,2,16,64]{3,2,1,0:T(8,128)S(1)} %bitcast.96, f32[1,101,128]{2,1,0:T(8,128)S(1)} %copy-done.5, f32[1,101,128]{2,1,0:T(8,128)S(1)} %copy-done.4), kind=kOutput, calls=%fused_computation.10 | convolution fusion | flops 158885120 | bytes 1455104 | tf_op jit(solution)/shard_map/fcij,cfl->jil/dot_general | solution.py:180
  86.1 1.6 %copy.26 = f32[2,64,16,128]{3,2,1,0:T(8,128)} copy(f32[2,64,16,128]{3,1,2,0:T(8,128)S(1)} %pad_maximum_fusion.1) | data formatting | bytes 2097152 | tf_op jit(solution)/shard_map/stack | solution.py:182
  (78 shorter events, 15.4 us)
Async XLA Ops:
  0.0 2.7 %copy-start.1 = (f32[1,400,512]{2,1,0:T(8,128)S(1)}, f32[1,400,512]{2,1,0:T(8,128)}, u32[]{:S(2)}) copy-start(f32[1,400,512]{2,1,0:T(8,128)} %param.5) | copy-start | bytes 2457604
  3.5 0.9 %copy-start.6 = (s32[512]{0:T(512)S(1)}, s32[512]{0:T(512)}, u32[]{:S(2)}) copy-start(s32[512]{0:T(512)} %param.7) | copy-start | bytes 6148
  3.6 1.4 %copy-start.7 = (s32[512]{0:T(512)S(1)}, s32[512]{0:T(512)}, u32[]{:S(2)}) copy-start(s32[512]{0:T(512)} %param.6) | copy-start | bytes 6148
  6.5 8.1 %collective-permute-start = (bf16[4,2,2,64,101]{4,3,2,1,0:T(8,128)(2,1)S(1)}, bf16[4,2,2,64,101]{4,3,2,1,0:T(8,128)(2,1)S(1)}, u32[]{:S(2)}, u32[]{:S(2)}) collective-permute-start(bf16[4,2,2,64,101]{4,3,2,1,0:T(8,128)(2,1)S(1)} %broadcast_select_fusion), channel_id=1, source_target_pairs={{0,4},{4,0},{8,12},{12,8},{16,20},{20,16},{24,28},{28,24},{1,5},{5... | collective-permute-start | bytes 620552 | tf_op jit(solution)/shard_map/ppermute | solution.py:133
  14.8 8.4 %collective-permute-start.1 = (bf16[2,2,2,64,101]{4,3,2,1,0:T(8,128)(2,1)S(1)}, bf16[2,2,2,64,101]{4,3,2,1,0:T(8,128)(2,1)S(1)}, u32[]{:S(2)}, u32[]{:S(2)}) collective-permute-start(bf16[2,2,2,64,101]{4,3,2,1,0:T(8,128)(2,1)S(1)} %get-tuple-element.11), channel_id=1, source_target_pairs={{24,0},{28,4},{0,8},{4,12},{8,16},{12,20},{16,24},{20,28},{25,1},{... | collective-permute-start | bytes 310280 | tf_op jit(solution)/shard_map/ppermute | solution.py:19
  16.4 10.5 %collective-permute-start.2 = (bf16[2,2,2,64,101]{4,3,2,1,0:T(8,128)(2,1)S(1)}, bf16[2,2,2,64,101]{4,3,2,1,0:T(8,128)(2,1)S(1)}, u32[]{:S(2)}, u32[]{:S(2)}) collective-permute-start(bf16[2,2,2,64,101]{4,3,2,1,0:T(8,128)(2,1)S(1)} %get-tuple-element.12), channel_id=1, source_target_pairs={{16,0},{20,4},{24,8},{28,12},{0,16},{4,20},{8,24},{12,28},{17,1},{... | collective-permute-start | bytes 310280 | tf_op jit(solution)/shard_map/ppermute | solution.py:19
  19.0 7.9 %collective-permute-start.3 = (bf16[2,2,2,64,101]{4,3,2,1,0:T(8,128)(2,1)S(1)}, bf16[2,2,2,64,101]{4,3,2,1,0:T(8,128)(2,1)S(1)}, u32[]{:S(2)}, u32[]{:S(2)}) collective-permute-start(bf16[2,2,2,64,101]{4,3,2,1,0:T(8,128)(2,1)S(1)} %get-tuple-element.13), channel_id=1, source_target_pairs={{8,0},{12,4},{16,8},{20,12},{24,16},{28,20},{0,24},{4,28},{9,1},{1... | collective-permute-start | bytes 310280 | tf_op jit(solution)/shard_map/ppermute | solution.py:19
  27.9 13.8 %collective-permute-start.5 = (bf16[1,8,2,2,64,101]{5,4,3,2,1,0:T(8,128)(2,1)S(1)}, bf16[1,8,2,2,64,101]{5,4,3,2,1,0:T(8,128)(2,1)S(1)}, u32[]{:S(2)}, u32[]{:S(2)}) collective-permute-start(bf16[1,8,2,2,64,101]{5,4,3,2,1,0:T(8,128)(2,1)S(1)} %bitcast_select_fusion), channel_id=1, source_target_pairs={{0,2},{1,3},{2,0},{3,1},{4,6},{5,7},{6,4},{7,5},{8,10},{9,11},{10,... | collective-permute-start | bytes 1241096 | tf_op jit(solution)/shard_map/ppermute | solution.py:164
  41.9 14.7 %collective-permute-start.7 = (bf16[2,8,2,2,64,101]{5,4,3,2,1,0:T(8,128)(2,1)S(1)}, bf16[2,8,2,2,64,101]{5,4,3,2,1,0:T(8,128)(2,1)S(1)}, u32[]{:S(2)}, u32[]{:S(2)}) collective-permute-start(bf16[2,8,2,2,64,101]{5,4,3,2,1,0:T(8,128)(2,1)S(1)} %pad_maximum_fusion), channel_id=1, source_target_pairs={{0,1},{1,0},{2,3},{3,2},{4,5},{5,4},{6,7},{7,6},{8,9},{9,8},{10,11... | collective-permute-start | bytes 2482184 | tf_op jit(solution)/shard_map/ppermute | solution.py:164
  42.1 7.2 %collective-permute-start.4 = (bf16[1,8,2,2,16,101]{5,4,3,2,1,0:T(8,128)(2,1)S(1)}, bf16[1,8,2,2,16,101]{5,4,3,2,1,0:T(8,128)(2,1)S(1)}, u32[]{:S(2)}, u32[]{:S(2)}) collective-permute-start(bf16[1,8,2,2,16,101]{5,4,3,2,1,0:T(8,128)(2,1)S(1)} %fusion.30), channel_id=1, source_target_pairs={{28,0},{0,4},{4,8},{8,12},{12,16},{16,20},{20,24},{24,28},{29,1},{... | collective-permute-start | bytes 310280 | tf_op jit(solution)/shard_map/ppermute | solution.py:19
  46.3 7.4 %collective-permute-start.9 = (bf16[1,8,2,2,16,101]{5,4,3,2,1,0:T(8,128)(2,1)S(1)}, bf16[1,8,2,2,16,101]{5,4,3,2,1,0:T(8,128)(2,1)S(1)}, u32[]{:S(2)}, u32[]{:S(2)}) collective-permute-start(bf16[1,8,2,2,16,101]{5,4,3,2,1,0:T(8,128)(2,1)S(1)} %fusion.30), channel_id=1, source_target_pairs={{24,0},{28,4},{0,8},{4,12},{8,16},{12,20},{16,24},{20,28},{25,1},{... | collective-permute-start | bytes 310280 | tf_op jit(solution)/shard_map/ppermute | solution.py:19
  49.3 7.3 %collective-permute-start.6 = (bf16[1,8,2,2,16,101]{5,4,3,2,1,0:T(8,128)(2,1)S(1)}, bf16[1,8,2,2,16,101]{5,4,3,2,1,0:T(8,128)(2,1)S(1)}, u32[]{:S(2)}, u32[]{:S(2)}) collective-permute-start(bf16[1,8,2,2,16,101]{5,4,3,2,1,0:T(8,128)(2,1)S(1)} %constant_dynamic-slice_fusion.1), channel_id=1, source_target_pairs={{28,0},{0,4},{4,8},{8,12},{12,16},{16,20},{20,24},{24,28},{29,1},{... | collective-permute-start | bytes 310280 | tf_op jit(solution)/shard_map/ppermute | solution.py:19
  53.7 7.1 %collective-permute-start.10 = (bf16[1,8,2,2,16,101]{5,4,3,2,1,0:T(8,128)(2,1)S(1)}, bf16[1,8,2,2,16,101]{5,4,3,2,1,0:T(8,128)(2,1)S(1)}, u32[]{:S(2)}, u32[]{:S(2)}) collective-permute-start(bf16[1,8,2,2,16,101]{5,4,3,2,1,0:T(8,128)(2,1)S(1)} %constant_dynamic-slice_fusion.1), channel_id=1, source_target_pairs={{24,0},{28,4},{0,8},{4,12},{8,16},{12,20},{16,24},{20,28},{25,1},{... | collective-permute-start | bytes 310280 | tf_op jit(solution)/shard_map/ppermute | solution.py:19
  57.4 10.1 %collective-permute-start.8 = (bf16[2,8,2,2,16,101]{5,4,3,2,1,0:T(8,128)(2,1)}, bf16[2,8,2,2,16,101]{5,4,3,2,1,0:T(8,128)(2,1)S(1)}, u32[]{:S(2)}, u32[]{:S(2)}) collective-permute-start(bf16[2,8,2,2,16,101]{5,4,3,2,1,0:T(8,128)(2,1)} %constant_dynamic-slice_fusion), channel_id=1, source_target_pairs={{28,0},{0,4},{4,8},{8,12},{12,16},{16,20},{20,24},{24,28},{29,1},{... | collective-permute-start | bytes 620552 | tf_op jit(solution)/shard_map/ppermute | solution.py:19
  60.8 0.8 copy-start.2
  61.6 12.4 %collective-permute-start.11 = (bf16[2,8,2,2,16,101]{5,4,3,2,1,0:T(8,128)(2,1)}, bf16[2,8,2,2,16,101]{5,4,3,2,1,0:T(8,128)(2,1)}, u32[]{:S(2)}, u32[]{:S(2)}) collective-permute-start(bf16[2,8,2,2,16,101]{5,4,3,2,1,0:T(8,128)(2,1)} %constant_dynamic-slice_fusion), channel_id=1, source_target_pairs={{24,0},{28,4},{0,8},{4,12},{8,16},{12,20},{16,24},{20,28},{25,1},{... | collective-permute-start | bytes 620552 | tf_op jit(solution)/shard_map/ppermute | solution.py:19
  75.7 1.3 %copy-start.3 = (bf16[4,8,2,2,16,101]{5,4,3,2,1,0:T(8,128)(2,1)S(1)}, bf16[4,8,2,2,16,101]{5,4,3,2,1,0:T(8,128)(2,1)}, u32[]{:S(2)}) copy-start(bf16[4,8,2,2,16,101]{5,4,3,2,1,0:T(8,128)(2,1)} %constant_dynamic-update-slice_fusion.3) | copy-start | bytes 1241092
  79.6 1.1 %copy-start = (bf16[101,32,128]{2,1,0:T(8,128)(2,1)S(1)}, bf16[101,32,128]{2,1,0:T(8,128)(2,1)}, u32[]{:S(2)}) copy-start(bf16[101,32,128]{2,1,0:T(8,128)(2,1)} %copy.23) | copy-start | bytes 2482180
  80.8 1.0 %copy-start.4 = (f32[1,101,128]{2,1,0:T(8,128)S(1)}, f32[1,101,128]{2,1,0:T(8,128)}, u32[]{:S(2)}) copy-start(f32[1,101,128]{2,1,0:T(8,128)} %get-tuple-element.16) | copy-start | bytes 155140
  80.8 1.0 %copy-start.5 = (f32[1,101,128]{2,1,0:T(8,128)S(1)}, f32[1,101,128]{2,1,0:T(8,128)}, u32[]{:S(2)}) copy-start(f32[1,101,128]{2,1,0:T(8,128)} %get-tuple-element.17) | copy-start | bytes 155140

commit v11 on v5

--- a/solution.py
+++ b/solution.py
@@ -4,6 +4,7 @@
 import jax.numpy as jnp
 from jax import lax
 from jax.sharding import PartitionSpec as P
+
 
 L = 200
 FB = 101
@@ -117,7 +118,10 @@
     slice_width = block_width // tm_count
     windows = records.reshape(samples // L, L, channels)
     spectra = whiten_planes(windows, live_mask, lax.Precision.HIGH)
-    sorted_spec = jnp.take(spectra, chan_order, axis=2)
+    picks = (chan_order[:, None] == jnp.arange(channels, dtype=chan_order.dtype)[None, :])
+    sorted_spec = jnp.einsum(
+        "kh,wchf->wckf", picks.astype(jnp.bfloat16), spectra, preferred_element_type=jnp.float32
+    ).astype(jnp.bfloat16)
     sorted_spec = sorted_spec.reshape(spectra.shape[0], 2, chan_count, block_width, FB)
     sorted_spec = jnp.moveaxis(sorted_spec, 2, 0)
     pieces = []
@@ -126,20 +130,46 @@
         piece = lax.dynamic_index_in_dim(sorted_spec, target, 0, keepdims=False)
         pieces.append(piece if distance == 0 else shifted(piece, "chan", distance))
     own = jnp.stack(pieces)
+    offsets = [max(1, round_index * chan_count // 4) for round_index in range(ROUNDS)]
+
+    def send_slices(group):
+        piece = lax.dynamic_slice_in_dim(group, tm_position * slice_width, slice_width, axis=4)
+        return [shifted(piece, "chan", offset) for offset in offsets]
+
     gathered = own[None]
+    partner_groups = [send_slices(gathered)]
     step = tm_count // 2
+    grid = [(c, q) for c in range(chan_count) for q in range(tm_count)]
+
+    def send_from_neighbour(group, mask):
+        piece = lax.dynamic_slice_in_dim(
+            group, jnp.bitwise_xor(tm_position, mask) * slice_width, slice_width, axis=4
+        )
+        sent = []
+        for offset in offsets:
+            route = [
+                (c * tm_count + q, ((c + offset) % chan_count) * tm_count + (q ^ mask))
+                for c, q in grid
+            ]
+            sent.append(lax.ppermute(piece, ("chan", "tm"), route))
+        return sent
+
     while step >= 1:
         route = [(q, q ^ step) for q in range(tm_count)]
-        gathered = jnp.concatenate([gathered, lax.ppermute(gathered, "tm", route)], axis=0)
+        arrived = lax.ppermute(gathered, "tm", route)
+        if step == 1:
+            partner_groups.append(send_from_neighbour(gathered, step))
+        else:
+            partner_groups.append(send_slices(arrived))
+        gathered = jnp.concatenate([gathered, arrived], axis=0)
         step //= 2
     windows_all = gathered.shape[0] * gathered.shape[1] * gathered.shape[2]
     own_spec = jnp.transpose(gathered, (5, 3, 0, 1, 2, 4)).reshape(FB, 2 * windows_all, block_width)
-    my_slice = lax.dynamic_slice_in_dim(gathered, tm_position * slice_width, slice_width, axis=4)
     inverse = inverse_table()
     results = []
     for round_index in range(ROUNDS):
-        offset = max(1, round_index * chan_count // 4)
-        partner = shifted(my_slice, "chan", offset)
+        offset = offsets[round_index]
+        partner = jnp.concatenate([group[round_index] for group in partner_groups], axis=0)
         partner = jnp.roll(partner, offset, axis=1)
         rotated = jnp.stack([-partner[:, :, :, 1], partner[:, :, :, 0]], axis=3)
         both = jnp.stack([partner, rotated])

time: 81.8 us -> 76.2 us (0.932)
  local copies, waits for them, and re-layouts: 17.3 us -> 12 us
  waiting for transfers between devices: 33.2 us -> 28.6 us
  starting transfers between devices: 15.2 us -> 18.6 us
    ppermute x2 -> x4, waiting for transfers between devices: 14.9 us -> 3.44 us  [the longest x2 3.44 us: on_device_local(): arrived = lax.ppermute(gathered, 'tm', route)]
    ppermute x9 -> x11, waiting for transfers between devices: 18.3 us -> 25.2 us  [shifted(): return lax.ppermute(block, axis, route)]
    ppermute x2 -> x4, starting transfers between devices: 0.67 us -> 3.07 us  [the longest x2 2.13 us: send_from_neighbour(): sent.append(lax.ppermute(piece, ('chan', 'tm'), route))]
    gather x2 -> x0, local copies, waits for them, and re-layouts: 2.36 us -> none  [on_device_local(): sorted_spec = jnp.take(spectra, chan_order, axis=2)]
    slice x4, local copies, waits for them, and re-layouts: 1.98 us -> 0.08 us  [on_device_local(): partner = jnp.roll(partner, offset, axis=1)]
    transpose x1, other arithmetic: 0.49 us -> 1.7 us  [on_device_local(): jnp.transpose(gathered, (5, 3, 0, 1, 2, 4))]
    concatenate x1 -> x2, other arithmetic: 0.24 us -> 1.27 us  [on_device_local(): gathered = jnp.concatenate([gathered, arrived], axis=0)]
    ppermute x9 -> x11, starting transfers between devices: 14.5 us -> 15.5 us  [shifted(): return lax.ppermute(block, axis, route)]
  transfers between devices with their start and end apart: 11 -> 15, of which waited for: 7 -> 8; matrix products, arithmetic and copies ran while one was open for 11% -> 9% of each run, Pallas kernels for 0% -> 0%
where the time goes in v11:
time: 76.2 us; the launch traced here: 75.6 us
  waiting for transfers between devices  28.6 us (38%)
  starting transfers between devices  18.6 us (24%)
  local copies, waits for them, and re-layouts  12 us (16%)
  matrix products  8.79 us (12%)
  other arithmetic  7.16 us (9%)
    ppermute x11, waiting for transfers between devices, shifted(): return lax.ppermute(block, axis, route)  25.2 us
    ppermute x11, starting transfers between devices, shifted(): return lax.ppermute(block, axis, route)  15.5 us
    dot_general x2, matrix products, on_device_local(): jnp.einsum('fcij,cfl->jil', sums, inverse, precision=lax.Precision.HIGH)  4.19 us
    reshape x1, local copies, waits for them, and re-layouts, on_device_local(): jnp.transpose(gathered, (5, 3, 0, 1, 2, 4))  3.79 us
    reshape x2, local copies, waits for them, and re-layouts, on_device_local(): jnp.transpose(both, (6, 0, 5, 4, 1, 2, 3))  3.66 us
    ppermute x2, waiting for transfers between devices, on_device_local(): arrived = lax.ppermute(gathered, 'tm', route)  3.44 us
    ppermute x2, starting transfers between devices, send_from_neighbour(): sent.append(lax.ppermute(piece, ('chan', 'tm'), route))  2.13 us
    dot_general x2, matrix products, on_device_local(): jnp.einsum('fnk,fkj->fnj', both, own_spec, preferred_element_type=jnp.flo...  1.94 us
  transfers between devices with their start and end apart: 15, of which 8 were waited for; matrix products, arithmetic and copies ran while one was open for 9% of the time, Pallas kernels for 0%

profile of v11, /device:TPU:6, one launch (start us, length us, event | category | flops | bytes accessed | tf_op | source)
XLA Modules:
  0.0 75.6 jit_solution(102857210919634712)
XLA Ops:
  0.1 1.3 %reduce_sum.36 = f32[2,512]{1,0:T(2,128)S(1)} reduce(f32[2,200,512]{2,1,0:T(8,128)} %bitcast.111, f32[]{:T(128)} %constant.117.clone.1), dimensions={1}, to_apply=%region_0.0 | reduce | flops 203776 | bytes 823300 | tf_op jit(solution)/shard_map/reduce_sum | solution.py:98
  5.8 1.6 %collective-permute-start = (bf16[2,2,64,101]{3,2,1,0:T(8,128)(2,1)S(1)}, bf16[2,2,64,101]{3,2,1,0:T(8,128)(2,1)S(1)}, u32[]{:S(2)}, u32[]{:S(2)}) collective-permute-start(bf16[2,2,64,101]{3,2,1,0:T(8,128)(2,1)S(1)} %get-tuple-element.15), channel_id=1, source_target_pairs={{28,0},{0,4},{4,8},{8,12},{12,16},{16,20},{20,24},{24,28},{29,1},{... | collective-permute-start | bytes 155144 | tf_op jit(solution)/shard_map/ppermute | solution.py:19
  7.4 1.6 %collective-permute-start.1 = (bf16[2,2,64,101]{3,2,1,0:T(8,128)(2,1)S(1)}, bf16[2,2,64,101]{3,2,1,0:T(8,128)(2,1)S(1)}, u32[]{:S(2)}, u32[]{:S(2)}) collective-permute-start(bf16[2,2,64,101]{3,2,1,0:T(8,128)(2,1)S(1)} %get-tuple-element.14), channel_id=1, source_target_pairs={{24,0},{28,4},{0,8},{4,12},{8,16},{12,20},{16,24},{20,28},{25,1},{... | collective-permute-start | bytes 155144 | tf_op jit(solution)/shard_map/ppermute | solution.py:19
  9.0 2.5 %collective-permute-start.2 = (bf16[2,2,64,101]{3,2,1,0:T(8,128)(2,1)S(1)}, bf16[2,2,64,101]{3,2,1,0:T(8,128)(2,1)S(1)}, u32[]{:S(2)}, u32[]{:S(2)}) collective-permute-start(bf16[2,2,64,101]{3,2,1,0:T(8,128)(2,1)S(1)} %get-tuple-element.13), channel_id=1, source_target_pairs={{20,0},{24,4},{28,8},{0,12},{4,16},{8,20},{12,24},{16,28},{21,1},{... | collective-permute-start | bytes 155144 | tf_op jit(solution)/shard_map/ppermute | solution.py:19
  11.9 2.2 %collective-permute-start.4 = (bf16[2,2,64,101]{3,2,1,0:T(8,128)(2,1)S(1)}, bf16[2,2,64,101]{3,2,1,0:T(8,128)(2,1)S(1)}, u32[]{:S(2)}, u32[]{:S(2)}) collective-permute-start(bf16[2,2,64,101]{3,2,1,0:T(8,128)(2,1)S(1)} %get-tuple-element.11), channel_id=1, source_target_pairs={{12,0},{16,4},{20,8},{24,12},{28,16},{0,20},{4,24},{8,28},{13,1},{... | collective-permute-start | bytes 155144 | tf_op jit(solution)/shard_map/ppermute | solution.py:19
  14.1 1.9 %collective-permute-start.5 = (bf16[2,2,64,101]{3,2,1,0:T(8,128)(2,1)S(1)}, bf16[2,2,64,101]{3,2,1,0:T(8,128)(2,1)S(1)}, u32[]{:S(2)}, u32[]{:S(2)}) collective-permute-start(bf16[2,2,64,101]{3,2,1,0:T(8,128)(2,1)S(1)} %get-tuple-element.10), channel_id=1, source_target_pairs={{8,0},{12,4},{16,8},{20,12},{24,16},{28,20},{0,24},{4,28},{9,1},{1... | collective-permute-start | bytes 155144 | tf_op jit(solution)/shard_map/ppermute | solution.py:19
  16.0 1.5 %collective-permute-start.6 = (bf16[2,2,64,101]{3,2,1,0:T(8,128)(2,1)S(1)}, bf16[2,2,64,101]{3,2,1,0:T(8,128)(2,1)S(1)}, u32[]{:S(2)}, u32[]{:S(2)}) collective-permute-start(bf16[2,2,64,101]{3,2,1,0:T(8,128)(2,1)S(1)} %get-tuple-element.9), channel_id=1, source_target_pairs={{4,0},{8,4},{12,8},{16,12},{20,16},{24,20},{28,24},{0,28},{5,1},{9... | collective-permute-start | bytes 155144 | tf_op jit(solution)/shard_map/ppermute | solution.py:19
  17.5 1.6 %collective-permute-done.3 = bf16[2,2,64,101]{3,2,1,0:T(8,128)(2,1)S(1)} collective-permute-done((bf16[2,2,64,101]{3,2,1,0:T(8,128)(2,1)S(1)}, bf16[2,2,64,101]{3,2,1,0:T(8,128)(2,1)S(1)}, u32[]{:S(2)}, u32[]{:S(2)}) %collective-permute-start.3) | collective-permute-done | bytes 51744 | tf_op jit(solution)/shard_map/ppermute | solution.py:19
  19.1 1.8 %collective-permute-done.4 = bf16[2,2,64,101]{3,2,1,0:T(8,128)(2,1)S(1)} collective-permute-done((bf16[2,2,64,101]{3,2,1,0:T(8,128)(2,1)S(1)}, bf16[2,2,64,101]{3,2,1,0:T(8,128)(2,1)S(1)}, u32[]{:S(2)}, u32[]{:S(2)}) %collective-permute-start.4) | collective-permute-done | bytes 51744 | tf_op jit(solution)/shard_map/ppermute | solution.py:19
  23.8 1.3 %collective-permute-start.12 = (bf16[1,8,2,2,16,101]{5,4,3,2,1,0:T(8,128)(2,1)S(1)}, bf16[1,8,2,2,16,101]{5,4,3,2,1,0:T(8,128)(2,1)S(1)}, u32[]{:S(2)}, u32[]{:S(2)}) collective-permute-start(bf16[1,8,2,2,16,101]{5,4,3,2,1,0:T(8,128)(2,1)S(1)} %dynamic-slice_bitcast_fusion), channel_id=1, source_target_pairs={{24,0},{28,4},{0,8},{4,12},{8,16},{12,20},{16,24},{20,28},{25,1},{... | collective-permute-start | bytes 310280 | tf_op jit(solution)/shard_map/ppermute | solution.py:19
  25.1 2.5 %collective-permute-done.7 = bf16[1,8,2,2,16,101]{5,4,3,2,1,0:T(8,128)(2,1)S(1)} collective-permute-done((bf16[1,8,2,2,16,101]{5,4,3,2,1,0:T(8,128)(2,1)S(1)}, bf16[1,8,2,2,16,101]{5,4,3,2,1,0:T(8,128)(2,1)S(1)}, u32[]{:S(2)}, u32[]{:S(2)}) %collective-permute-start.7) | collective-permute-done | bytes 103456 | tf_op jit(solution)/shard_map/ppermute | solution.py:19
  27.6 3.8 %collective-permute-done.12 = bf16[1,8,2,2,16,101]{5,4,3,2,1,0:T(8,128)(2,1)S(1)} collective-permute-done((bf16[1,8,2,2,16,101]{5,4,3,2,1,0:T(8,128)(2,1)S(1)}, bf16[1,8,2,2,16,101]{5,4,3,2,1,0:T(8,128)(2,1)S(1)}, u32[]{:S(2)}, u32[]{:S(2)}) %collective-permute-start.12) | collective-permute-done | bytes 103456 | tf_op jit(solution)/shard_map/ppermute | solution.py:19
  31.4 3.4 %collective-permute-done.8 = bf16[1,8,2,2,64,101]{5,4,3,2,1,0:T(8,128)(2,1)S(1)} collective-permute-done((bf16[1,8,2,2,64,101]{5,4,3,2,1,0:T(8,128)(2,1)S(1)}, bf16[1,8,2,2,64,101]{5,4,3,2,1,0:T(8,128)(2,1)S(1)}, u32[]{:S(2)}, u32[]{:S(2)}) %collective-permute-start.8) | collective-permute-done | bytes 413728 | tf_op jit(solution)/shard_map/ppermute | solution.py:159
  35.0 2.1 %collective-permute-start.14 = (bf16[2,8,2,2,16,101]{5,4,3,2,1,0:T(8,128)(2,1)S(1)}, bf16[2,8,2,2,16,101]{5,4,3,2,1,0:T(8,128)(2,1)S(1)}, u32[]{:S(2)}, u32[]{:S(2)}) collective-permute-start(bf16[2,8,2,2,16,101]{5,4,3,2,1,0:T(8,128)(2,1)S(1)} %fusion.28), channel_id=1, source_target_pairs={{0,9},{1,8},{2,11},{3,10},{4,13},{5,12},{6,15},{7,14},{8,17},{9,16... | collective-permute-start | bytes 620552 | tf_op jit(solution)/shard_map/ppermute | solution.py:154
  40.4 8.9 %collective-permute-done.9 = bf16[1,8,2,2,16,101]{5,4,3,2,1,0:T(8,128)(2,1)S(1)} collective-permute-done((bf16[1,8,2,2,16,101]{5,4,3,2,1,0:T(8,128)(2,1)S(1)}, bf16[1,8,2,2,16,101]{5,4,3,2,1,0:T(8,128)(2,1)S(1)}, u32[]{:S(2)}, u32[]{:S(2)}) %collective-permute-start.9) | collective-permute-done | bytes 103456 | tf_op jit(solution)/shard_map/ppermute | solution.py:19
  49.3 5.6 %collective-permute-done.13 = bf16[1,8,2,2,16,101]{5,4,3,2,1,0:T(8,128)(2,1)S(1)} collective-permute-done((bf16[1,8,2,2,16,101]{5,4,3,2,1,0:T(8,128)(2,1)S(1)}, bf16[1,8,2,2,16,101]{5,4,3,2,1,0:T(8,128)(2,1)S(1)}, u32[]{:S(2)}, u32[]{:S(2)}) %collective-permute-start.13) | collective-permute-done | bytes 103456 | tf_op jit(solution)/shard_map/ppermute | solution.py:19
  56.0 1.5 %copy.14 = bf16[101,32,128]{2,1,0:T(8,128)(2,1)S(1)} copy(bf16[101,32,128]{0,1,2:T(8,128)(2,1)S(1)} %bitcast.109) | data formatting | bytes 1654784 | tf_op jit(solution)/shard_map/reshape | solution.py:176
  58.3 2.2 %copy.18 = bf16[101,32,128]{2,1,0:T(8,128)(2,1)} copy(bf16[101,32,128]{0,1,2:T(8,128)(2,1)S(1)} %bitcast.110) | data formatting | bytes 1654784 | tf_op jit(solution)/shard_map/reshape | solution.py:176
  60.5 1.7 %maximum_bitcast_fusion = bf16[101,2,4,8,2,64]{0,5,1,4,3,2:T(8,128)(2,1)S(1)} fusion(bf16[2,8,2,2,64,101]{5,4,3,2,1,0:T(8,128)(2,1)} %collective-permute-done.11, bf16[1,8,2,2,64,101]{5,4,3,2,1,0:T(8,128)(2,1)S(1)} %collective-permute-done.8, bf16[1,8,2,2,64,101]{5,4,3,2,1,0:T(8,128)(2,1)S(1)} %bitcast.108), kind=kLoop, calls=%fused_computation | loop fusion | flops 1654784 | bytes 3309568 | tf_op jit(solution)/shard_map/transpose | solution.py:167
  62.2 1.5 %copy.13 = bf16[101,2,4,8,2,64]{0,5,4,3,2,1:T(8,128)(2,1)} copy(bf16[101,2,4,8,2,64]{0,5,1,4,3,2:T(8,128)(2,1)S(1)} %maximum_bitcast_fusion) | data formatting | bytes 3309568 | tf_op jit(solution)/shard_map/transpose | solution.py:167
  63.8 3.8 %copy.15 = bf16[101,128,64]{1,2,0:T(8,128)(2,1)S(1)} copy(bf16[101,128,64]{0,2,1:T(8,128)(2,1)} %bitcast.102) | data formatting | bytes 3309568 | tf_op jit(solution)/shard_map/reshape | solution.py:167
  69.7 2.1 %fusion.4 = f32[1,64,16,128]{3,1,2,0:T(8,128)S(1)} fusion(f32[101,2,16,64]{3,2,1,0:T(8,128)S(1)} %bitcast.104, f32[1,101,128]{2,1,0:T(8,128)S(1)} %get-tuple-element.19, f32[1,101,128]{2,1,0:T(8,128)S(1)} %get-tuple-element.18), kind=kOutput, calls=%fused_computation.6 | convolution fusion | flops 158885120 | bytes 1455104 | tf_op jit(solution)/shard_map/fcij,cfl->jil/dot_general | solution.py:180
  71.8 2.1 %fusion.7 = f32[1,64,16,128]{3,1,2,0:T(8,128)S(1)} fusion(f32[101,2,16,64]{3,2,1,0:T(8,128)S(1)} %bitcast.103, f32[1,101,128]{2,1,0:T(8,128)S(1)} %get-tuple-element.19, f32[1,101,128]{2,1,0:T(8,128)S(1)} %get-tuple-element.18), kind=kOutput, calls=%fused_computation.7 | convolution fusion | flops 158885120 | bytes 1455104 | tf_op jit(solution)/shard_map/fcij,cfl->jil/dot_general | solution.py:180
  74.0 1.6 %copy.21 = f32[2,64,16,128]{3,2,1,0:T(8,128)} copy(f32[2,64,16,128]{3,1,2,0:T(8,128)S(1)} %pad_maximum_fusion.1) | data formatting | bytes 2097152 | tf_op jit(solution)/shard_map/stack | solution.py:182
  (71 shorter events, 15.3 us)
Async XLA Ops:
  0.0 2.7 %copy-start.1 = (f32[1,400,512]{2,1,0:T(8,128)S(1)}, f32[1,400,512]{2,1,0:T(8,128)}, u32[]{:S(2)}) copy-start(f32[1,400,512]{2,1,0:T(8,128)} %param.3) | copy-start | bytes 2457604
  3.5 0.9 %copy-start.2 = (s32[512]{0:T(512)S(1)}, s32[512]{0:T(512)}, u32[]{:S(2)}) copy-start(s32[512]{0:T(512)} %param.5) | copy-start | bytes 6148
  3.5 1.4 %copy-start.3 = (s32[512]{0:T(512)S(1)}, s32[512]{0:T(512)}, u32[]{:S(2)}) copy-start(s32[512]{0:T(512)} %param.4) | copy-start | bytes 6148
  5.8 8.2 %collective-permute-start = (bf16[2,2,64,101]{3,2,1,0:T(8,128)(2,1)S(1)}, bf16[2,2,64,101]{3,2,1,0:T(8,128)(2,1)S(1)}, u32[]{:S(2)}, u32[]{:S(2)}) collective-permute-start(bf16[2,2,64,101]{3,2,1,0:T(8,128)(2,1)S(1)} %get-tuple-element.15), channel_id=1, source_target_pairs={{28,0},{0,4},{4,8},{8,12},{12,16},{16,20},{20,24},{24,28},{29,1},{... | collective-permute-start | bytes 155144 | tf_op jit(solution)/shard_map/ppermute | solution.py:19
  7.4 8.6 %collective-permute-start.1 = (bf16[2,2,64,101]{3,2,1,0:T(8,128)(2,1)S(1)}, bf16[2,2,64,101]{3,2,1,0:T(8,128)(2,1)S(1)}, u32[]{:S(2)}, u32[]{:S(2)}) collective-permute-start(bf16[2,2,64,101]{3,2,1,0:T(8,128)(2,1)S(1)} %get-tuple-element.14), channel_id=1, source_target_pairs={{24,0},{28,4},{0,8},{4,12},{8,16},{12,20},{16,24},{20,28},{25,1},{... | collective-permute-start | bytes 155144 | tf_op jit(solution)/shard_map/ppermute | solution.py:19
  9.0 8.5 %collective-permute-start.2 = (bf16[2,2,64,101]{3,2,1,0:T(8,128)(2,1)S(1)}, bf16[2,2,64,101]{3,2,1,0:T(8,128)(2,1)S(1)}, u32[]{:S(2)}, u32[]{:S(2)}) collective-permute-start(bf16[2,2,64,101]{3,2,1,0:T(8,128)(2,1)S(1)} %get-tuple-element.13), channel_id=1, source_target_pairs={{20,0},{24,4},{28,8},{0,12},{4,16},{8,20},{12,24},{16,28},{21,1},{... | collective-permute-start | bytes 155144 | tf_op jit(solution)/shard_map/ppermute | solution.py:19
  11.5 7.6 %collective-permute-start.3 = (bf16[2,2,64,101]{3,2,1,0:T(8,128)(2,1)S(1)}, bf16[2,2,64,101]{3,2,1,0:T(8,128)(2,1)S(1)}, u32[]{:S(2)}, u32[]{:S(2)}) collective-permute-start(bf16[2,2,64,101]{3,2,1,0:T(8,128)(2,1)S(1)} %get-tuple-element.12), channel_id=1, source_target_pairs={{16,0},{20,4},{24,8},{28,12},{0,16},{4,20},{8,24},{12,28},{17,1},{... | collective-permute-start | bytes 155144 | tf_op jit(solution)/shard_map/ppermute | solution.py:19
  11.9 9.0 %collective-permute-start.4 = (bf16[2,2,64,101]{3,2,1,0:T(8,128)(2,1)S(1)}, bf16[2,2,64,101]{3,2,1,0:T(8,128)(2,1)S(1)}, u32[]{:S(2)}, u32[]{:S(2)}) collective-permute-start(bf16[2,2,64,101]{3,2,1,0:T(8,128)(2,1)S(1)} %get-tuple-element.11), channel_id=1, source_target_pairs={{12,0},{16,4},{20,8},{24,12},{28,16},{0,20},{4,24},{8,28},{13,1},{... | collective-permute-start | bytes 155144 | tf_op jit(solution)/shard_map/ppermute | solution.py:19
  14.1 6.8 %collective-permute-start.5 = (bf16[2,2,64,101]{3,2,1,0:T(8,128)(2,1)S(1)}, bf16[2,2,64,101]{3,2,1,0:T(8,128)(2,1)S(1)}, u32[]{:S(2)}, u32[]{:S(2)}) collective-permute-start(bf16[2,2,64,101]{3,2,1,0:T(8,128)(2,1)S(1)} %get-tuple-element.10), channel_id=1, source_target_pairs={{8,0},{12,4},{16,8},{20,12},{24,16},{28,20},{0,24},{4,28},{9,1},{1... | collective-permute-start | bytes 155144 | tf_op jit(solution)/shard_map/ppermute | solution.py:19
  16.0 6.0 %collective-permute-start.6 = (bf16[2,2,64,101]{3,2,1,0:T(8,128)(2,1)S(1)}, bf16[2,2,64,101]{3,2,1,0:T(8,128)(2,1)S(1)}, u32[]{:S(2)}, u32[]{:S(2)}) collective-permute-start(bf16[2,2,64,101]{3,2,1,0:T(8,128)(2,1)S(1)} %get-tuple-element.9), channel_id=1, source_target_pairs={{4,0},{8,4},{12,8},{16,12},{20,16},{24,20},{28,24},{0,28},{5,1},{9... | collective-permute-start | bytes 155144 | tf_op jit(solution)/shard_map/ppermute | solution.py:19
  22.0 12.9 %collective-permute-start.8 = (bf16[1,8,2,2,64,101]{5,4,3,2,1,0:T(8,128)(2,1)S(1)}, bf16[1,8,2,2,64,101]{5,4,3,2,1,0:T(8,128)(2,1)S(1)}, u32[]{:S(2)}, u32[]{:S(2)}) collective-permute-start(bf16[1,8,2,2,64,101]{5,4,3,2,1,0:T(8,128)(2,1)S(1)} %bitcast.105), channel_id=1, source_target_pairs={{0,2},{1,3},{2,0},{3,1},{4,6},{5,7},{6,4},{7,5},{8,10},{9,11},{10,... | collective-permute-start | bytes 1241096 | tf_op jit(solution)/shard_map/ppermute | solution.py:159
  22.6 5.0 %collective-permute-start.7 = (bf16[1,8,2,2,16,101]{5,4,3,2,1,0:T(8,128)(2,1)S(1)}, bf16[1,8,2,2,16,101]{5,4,3,2,1,0:T(8,128)(2,1)S(1)}, u32[]{:S(2)}, u32[]{:S(2)}) collective-permute-start(bf16[1,8,2,2,16,101]{5,4,3,2,1,0:T(8,128)(2,1)S(1)} %dynamic-slice_bitcast_fusion), channel_id=1, source_target_pairs={{28,0},{0,4},{4,8},{8,12},{12,16},{16,20},{20,24},{24,28},{29,1},{... | collective-permute-start | bytes 310280 | tf_op jit(solution)/shard_map/ppermute | solution.py:19
  23.8 7.6 %collective-permute-start.12 = (bf16[1,8,2,2,16,101]{5,4,3,2,1,0:T(8,128)(2,1)S(1)}, bf16[1,8,2,2,16,101]{5,4,3,2,1,0:T(8,128)(2,1)S(1)}, u32[]{:S(2)}, u32[]{:S(2)}) collective-permute-start(bf16[1,8,2,2,16,101]{5,4,3,2,1,0:T(8,128)(2,1)S(1)} %dynamic-slice_bitcast_fusion), channel_id=1, source_target_pairs={{24,0},{28,4},{0,8},{4,12},{8,16},{12,20},{16,24},{20,28},{25,1},{... | collective-permute-start | bytes 310280 | tf_op jit(solution)/shard_map/ppermute | solution.py:19
  34.9 19.9 %collective-permute-start.10 = (bf16[2,8,2,2,16,101]{5,4,3,2,1,0:T(8,128)(2,1)S(1)}, bf16[2,8,2,2,16,101]{5,4,3,2,1,0:T(8,128)(2,1)S(1)}, u32[]{:S(2)}, u32[]{:S(2)}) collective-permute-start(bf16[2,8,2,2,16,101]{5,4,3,2,1,0:T(8,128)(2,1)S(1)} %fusion.28), channel_id=1, source_target_pairs={{0,5},{1,4},{2,7},{3,6},{4,9},{5,8},{6,11},{7,10},{8,13},{9,12},{1... | collective-permute-start | bytes 620552 | tf_op jit(solution)/shard_map/ppermute | solution.py:154
  35.0 19.9 %collective-permute-start.14 = (bf16[2,8,2,2,16,101]{5,4,3,2,1,0:T(8,128)(2,1)S(1)}, bf16[2,8,2,2,16,101]{5,4,3,2,1,0:T(8,128)(2,1)S(1)}, u32[]{:S(2)}, u32[]{:S(2)}) collective-permute-start(bf16[2,8,2,2,16,101]{5,4,3,2,1,0:T(8,128)(2,1)S(1)} %fusion.28), channel_id=1, source_target_pairs={{0,9},{1,8},{2,11},{3,10},{4,13},{5,12},{6,15},{7,14},{8,17},{9,16... | collective-permute-start | bytes 620552 | tf_op jit(solution)/shard_map/ppermute | solution.py:154
  37.1 12.2 %collective-permute-start.9 = (bf16[1,8,2,2,16,101]{5,4,3,2,1,0:T(8,128)(2,1)S(1)}, bf16[1,8,2,2,16,101]{5,4,3,2,1,0:T(8,128)(2,1)S(1)}, u32[]{:S(2)}, u32[]{:S(2)}) collective-permute-start(bf16[1,8,2,2,16,101]{5,4,3,2,1,0:T(8,128)(2,1)S(1)} %constant_dynamic-slice_fusion), channel_id=1, source_target_pairs={{28,0},{0,4},{4,8},{8,12},{12,16},{16,20},{20,24},{24,28},{29,1},{... | collective-permute-start | bytes 310280 | tf_op jit(solution)/shard_map/ppermute | solution.py:19
  37.9 16.9 %collective-permute-start.13 = (bf16[1,8,2,2,16,101]{5,4,3,2,1,0:T(8,128)(2,1)S(1)}, bf16[1,8,2,2,16,101]{5,4,3,2,1,0:T(8,128)(2,1)S(1)}, u32[]{:S(2)}, u32[]{:S(2)}) collective-permute-start(bf16[1,8,2,2,16,101]{5,4,3,2,1,0:T(8,128)(2,1)S(1)} %constant_dynamic-slice_fusion), channel_id=1, source_target_pairs={{24,0},{28,4},{0,8},{4,12},{8,16},{12,20},{16,24},{20,28},{25,1},{... | collective-permute-start | bytes 310280 | tf_op jit(solution)/shard_map/ppermute | solution.py:19
  40.1 20.5 %collective-permute-start.11 = (bf16[2,8,2,2,64,101]{5,4,3,2,1,0:T(8,128)(2,1)}, bf16[2,8,2,2,64,101]{5,4,3,2,1,0:T(8,128)(2,1)}, u32[]{:S(2)}, u32[]{:S(2)}) collective-permute-start(bf16[2,8,2,2,64,101]{5,4,3,2,1,0:T(8,128)(2,1)} %pad_maximum_fusion), channel_id=1, source_target_pairs={{0,1},{1,0},{2,3},{3,2},{4,5},{5,4},{6,7},{7,6},{8,9},{9,8},{10,11... | collective-permute-start | bytes 2482184 | tf_op jit(solution)/shard_map/ppermute | solution.py:159
  67.6 1.1 %copy-start = (bf16[101,32,128]{2,1,0:T(8,128)(2,1)S(1)}, bf16[101,32,128]{2,1,0:T(8,128)(2,1)}, u32[]{:S(2)}) copy-start(bf16[101,32,128]{2,1,0:T(8,128)(2,1)} %copy.18) | copy-start | bytes 2482180

commit v12 on v11

--- a/solution.py
+++ b/solution.py
@@ -129,16 +129,15 @@
         target = jnp.mod(chan_position + distance, chan_count)
         piece = lax.dynamic_index_in_dim(sorted_spec, target, 0, keepdims=False)
         pieces.append(piece if distance == 0 else shifted(piece, "chan", distance))
-    own = jnp.stack(pieces)
+    by_shift = jnp.stack(pieces)
+    source = jnp.arange(chan_count, dtype=jnp.int32)
+    own = jnp.take(by_shift, jnp.mod(chan_position - source, chan_count), axis=0)
     offsets = [max(1, round_index * chan_count // 4) for round_index in range(ROUNDS)]
 
     def send_slices(group):
         piece = lax.dynamic_slice_in_dim(group, tm_position * slice_width, slice_width, axis=4)
         return [shifted(piece, "chan", offset) for offset in offsets]
 
-    gathered = own[None]
-    partner_groups = [send_slices(gathered)]
-    step = tm_count // 2
     grid = [(c, q) for c in range(chan_count) for q in range(tm_count)]
 
     def send_from_neighbour(group, mask):
@@ -154,27 +153,43 @@
             sent.append(lax.ppermute(piece, ("chan", "tm"), route))
         return sent
 
-    while step >= 1:
-        route = [(q, q ^ step) for q in range(tm_count)]
-        arrived = lax.ppermute(gathered, "tm", route)
-        if step == 1:
-            partner_groups.append(send_from_neighbour(gathered, step))
-        else:
+    gathered = own[None]
+    if tm_count == 4:
+        slot0 = send_slices(gathered)
+        slot2 = send_from_neighbour(gathered, 1)
+        arrived = lax.ppermute(gathered, "tm", [(q, q ^ 2) for q in range(tm_count)])
+        slot1 = send_slices(arrived)
+        slot3 = send_from_neighbour(arrived, 1)
+        gathered = jnp.concatenate([gathered, arrived], axis=0)
+        arrived = lax.ppermute(gathered, "tm", [(q, q ^ 1) for q in range(tm_count)])
+        own_groups = [gathered, arrived]
+        partner_sets = [[slot0, slot1], [slot2, slot3]]
+    else:
+        partner_groups = [send_slices(gathered)]
+        step = tm_count // 2
+        while step >= 1:
+            route = [(q, q ^ step) for q in range(tm_count)]
+            arrived = lax.ppermute(gathered, "tm", route)
             partner_groups.append(send_slices(arrived))
-        gathered = jnp.concatenate([gathered, arrived], axis=0)
-        step //= 2
-    windows_all = gathered.shape[0] * gathered.shape[1] * gathered.shape[2]
-    own_spec = jnp.transpose(gathered, (5, 3, 0, 1, 2, 4)).reshape(FB, 2 * windows_all, block_width)
+            gathered = jnp.concatenate([gathered, arrived], axis=0)
+            step //= 2
+        own_groups = [gathered]
+        partner_sets = [partner_groups]
+    own_specs = []
+    for group in own_groups:
+        width = 2 * group.shape[0] * group.shape[1] * group.shape[2]
+        own_specs.append(jnp.transpose(group, (5, 3, 0, 1, 2, 4)).reshape(FB, width, block_width))
     inverse = inverse_table()
     results = []
     for round_index in range(ROUNDS):
-        offset = offsets[round_index]
-        partner = jnp.concatenate([group[round_index] for group in partner_groups], axis=0)
-        partner = jnp.roll(partner, offset, axis=1)
-        rotated = jnp.stack([-partner[:, :, :, 1], partner[:, :, :, 0]], axis=3)
-        both = jnp.stack([partner, rotated])
-        both = jnp.transpose(both, (6, 0, 5, 4, 1, 2, 3)).reshape(FB, 2 * slice_width, 2 * windows_all)
-        sums = jnp.einsum("fnk,fkj->fnj", both, own_spec, preferred_element_type=jnp.float32)
+        sums = None
+        for pieces_of_half, own_spec in zip(partner_sets, own_specs):
+            partner = jnp.concatenate([piece[round_index] for piece in pieces_of_half], axis=0)
+            rotated = jnp.stack([-partner[:, :, :, 1], partner[:, :, :, 0]], axis=3)
+            both = jnp.stack([partner, rotated])
+            both = jnp.transpose(both, (6, 0, 5, 4, 1, 2, 3)).reshape(FB, 2 * slice_width, own_spec.shape[1])
+            term = jnp.einsum("fnk,fkj->fnj", both, own_spec, preferred_element_type=jnp.float32)
+            sums = term if sums is None else sums + term
         sums = sums.reshape(FB, 2, slice_width, block_width)
         results.append(
             jnp.einsum("fcij,cfl->jil", sums, inverse, precision=lax.Precision.HIGH)

time: 76.2 us -> 88.3 us (1.16)
  the two profiles are of different devices: /device:TPU:6 before, /device:TPU:1 now
where the time goes in v12:
time: 88.3 us; the launch traced here: 87.9 us
  local copies, waits for them, and re-layouts  24.5 us (28%)
  starting transfers between devices  24.5 us (28%)
  waiting for transfers between devices  17.6 us (20%)
  matrix products  12.1 us (14%)
  other arithmetic  8.74 us (10%)
    ppermute x11, starting transfers between devices, shifted(): return lax.ppermute(block, axis, route)  15.1 us
    ppermute x11, waiting for transfers between devices, shifted(): return lax.ppermute(block, axis, route)  10.4 us
    reshape x4, local copies, waits for them, and re-layouts, on_device_local(): jnp.transpose(both, (6, 0, 5, 4, 1, 2, 3))  8.59 us
    ppermute x4, starting transfers between devices, send_from_neighbour(): sent.append(lax.ppermute(piece, ('chan', 'tm'), route))  8.08 us
    transpose x2, local copies, waits for them, and re-layouts, on_device_local(): jnp.transpose(group, (5, 3, 0, 1, 2, 4)).reshape(FB, width, block_width)  6.68 us
    dot_general x4, matrix products, on_device_local(): jnp.einsum('fnk,fkj->fnj', both, own_spec, preferred_element_type=jnp.flo...  5.21 us
    concatenate x4, local copies, waits for them, and re-layouts, on_device_local(): jnp.concatenate([piece[round_index] for piece in pieces_of_half], axis=0)  4.33 us
    dot_general x2, matrix products, on_device_local(): jnp.einsum('fcij,cfl->jil', sums, inverse, precision=lax.Precision.HIGH)  4.18 us
  transfers between devices with their start and end apart: 17, of which 7 were waited for; matrix products, arithmetic and copies ran while one was open for 28% of the time, Pallas kernels for 0%

profile of v12, /device:TPU:1, one launch (start us, length us, event | category | flops | bytes accessed | tf_op | source)
XLA Modules:
  0.0 87.9 jit_solution(4294002752081795855)
XLA Ops:
  5.8 2.1 %collective-permute-start = (bf16[2,2,64,101]{3,2,1,0:T(8,128)(2,1)S(1)}, bf16[2,2,64,101]{3,2,1,0:T(8,128)(2,1)S(1)}, u32[]{:S(2)}, u32[]{:S(2)}) collective-permute-start(bf16[2,2,64,101]{3,2,1,0:T(8,128)(2,1)S(1)} %get-tuple-element.17), channel_id=1, source_target_pairs={{28,0},{0,4},{4,8},{8,12},{12,16},{16,20},{20,24},{24,28},{29,1},{... | collective-permute-start | bytes 155144 | tf_op jit(solution)/shard_map/ppermute | solution.py:19
  9.2 2.2 %collective-permute-start.2 = (bf16[2,2,64,101]{3,2,1,0:T(8,128)(2,1)S(1)}, bf16[2,2,64,101]{3,2,1,0:T(8,128)(2,1)S(1)}, u32[]{:S(2)}, u32[]{:S(2)}) collective-permute-start(bf16[2,2,64,101]{3,2,1,0:T(8,128)(2,1)S(1)} %get-tuple-element.15), channel_id=1, source_target_pairs={{20,0},{24,4},{28,8},{0,12},{4,16},{8,20},{12,24},{16,28},{21,1},{... | collective-permute-start | bytes 155144 | tf_op jit(solution)/shard_map/ppermute | solution.py:19
  12.5 2.4 %collective-permute-start.4 = (bf16[2,2,64,101]{3,2,1,0:T(8,128)(2,1)S(1)}, bf16[2,2,64,101]{3,2,1,0:T(8,128)(2,1)S(1)}, u32[]{:S(2)}, u32[]{:S(2)}) collective-permute-start(bf16[2,2,64,101]{3,2,1,0:T(8,128)(2,1)S(1)} %get-tuple-element.13), channel_id=1, source_target_pairs={{12,0},{16,4},{20,8},{24,12},{28,16},{0,20},{4,24},{8,28},{13,1},{... | collective-permute-start | bytes 155144 | tf_op jit(solution)/shard_map/ppermute | solution.py:19
  21.5 4.7 %collective-permute-start.10 = (bf16[1,8,2,2,16,101]{5,4,3,2,1,0:T(8,128)(2,1)S(1)}, bf16[1,8,2,2,16,101]{5,4,3,2,1,0:T(8,128)(2,1)S(1)}, u32[]{:S(2)}, u32[]{:S(2)}) collective-permute-start(bf16[1,8,2,2,16,101]{5,4,3,2,1,0:T(8,128)(2,1)S(1)} %get-tuple-element.9), channel_id=1, source_target_pairs={{0,5},{1,4},{2,7},{3,6},{4,9},{5,8},{6,11},{7,10},{8,13},{9,12},{1... | collective-permute-start | bytes 310280 | tf_op jit(solution)/shard_map/ppermute | solution.py:153
  27.4 1.4 %collective-permute-start.13 = (bf16[1,8,2,2,16,101]{5,4,3,2,1,0:T(8,128)(2,1)S(1)}, bf16[1,8,2,2,16,101]{5,4,3,2,1,0:T(8,128)(2,1)S(1)}, u32[]{:S(2)}, u32[]{:S(2)}) collective-permute-start(bf16[1,8,2,2,16,101]{5,4,3,2,1,0:T(8,128)(2,1)S(1)} %get-tuple-element.10), channel_id=1, source_target_pairs={{24,0},{28,4},{0,8},{4,12},{8,16},{12,20},{16,24},{20,28},{25,1},{... | collective-permute-start | bytes 310280 | tf_op jit(solution)/shard_map/ppermute | solution.py:19
  28.8 3.8 %collective-permute-done.10 = bf16[1,8,2,2,16,101]{5,4,3,2,1,0:T(8,128)(2,1)S(1)} collective-permute-done((bf16[1,8,2,2,16,101]{5,4,3,2,1,0:T(8,128)(2,1)S(1)}, bf16[1,8,2,2,16,101]{5,4,3,2,1,0:T(8,128)(2,1)S(1)}, u32[]{:S(2)}, u32[]{:S(2)}) %collective-permute-start.10) | collective-permute-done | bytes 103456 | tf_op jit(solution)/shard_map/ppermute | solution.py:153
  33.2 5.0 %collective-permute-done.7 = bf16[1,8,2,2,16,101]{5,4,3,2,1,0:T(8,128)(2,1)S(1)} collective-permute-done((bf16[1,8,2,2,16,101]{5,4,3,2,1,0:T(8,128)(2,1)S(1)}, bf16[1,8,2,2,16,101]{5,4,3,2,1,0:T(8,128)(2,1)S(1)}, u32[]{:S(2)}, u32[]{:S(2)}) %collective-permute-start.7) | collective-permute-done | bytes 103456 | tf_op jit(solution)/shard_map/ppermute | solution.py:19
  38.2 3.3 %collective-permute-done.8 = bf16[1,8,2,2,64,101]{5,4,3,2,1,0:T(8,128)(2,1)S(1)} collective-permute-done((bf16[1,8,2,2,64,101]{5,4,3,2,1,0:T(8,128)(2,1)S(1)}, bf16[1,8,2,2,64,101]{5,4,3,2,1,0:T(8,128)(2,1)S(1)}, u32[]{:S(2)}, u32[]{:S(2)}) %collective-permute-start.8) | collective-permute-done | bytes 413728 | tf_op jit(solution)/shard_map/ppermute | solution.py:160
  42.3 2.6 %collective-permute-start.11 = (bf16[1,8,2,2,16,101]{5,4,3,2,1,0:T(8,128)(2,1)}, bf16[1,8,2,2,16,101]{5,4,3,2,1,0:T(8,128)(2,1)}, u32[]{:S(2)}, u32[]{:S(2)}) collective-permute-start(bf16[1,8,2,2,16,101]{5,4,3,2,1,0:T(8,128)(2,1)} %get-tuple-element.7), channel_id=1, source_target_pairs={{0,5},{1,4},{2,7},{3,6},{4,9},{5,8},{6,11},{7,10},{8,13},{9,12},{1... | collective-permute-start | bytes 310280 | tf_op jit(solution)/shard_map/ppermute | solution.py:153
  45.5 1.5 %collective-permute-start.14 = (bf16[1,8,2,2,16,101]{5,4,3,2,1,0:T(8,128)(2,1)}, bf16[1,8,2,2,16,101]{5,4,3,2,1,0:T(8,128)(2,1)}, u32[]{:S(2)}, u32[]{:S(2)}) collective-permute-start(bf16[1,8,2,2,16,101]{5,4,3,2,1,0:T(8,128)(2,1)} %get-tuple-element.8), channel_id=1, source_target_pairs={{24,0},{28,4},{0,8},{4,12},{8,16},{12,20},{16,24},{20,28},{25,1},{... | collective-permute-start | bytes 310280 | tf_op jit(solution)/shard_map/ppermute | solution.py:19
  48.3 2.3 %copy.15 = bf16[101,2,2,8,2,64]{5,4,3,2,1,0:T(2,128)(2,1)S(1)} copy(bf16[101,2,2,8,2,64]{0,5,1,4,3,2:T(8,128)(2,1)S(1)} %get-tuple-element.6) | data formatting | bytes 1654784 | tf_op jit(solution)/shard_map/transpose | solution.py:181
  50.6 1.3 %collective-permute-start.12 = (bf16[2,8,2,2,64,101]{5,4,3,2,1,0:T(8,128)(2,1)}, bf16[2,8,2,2,64,101]{5,4,3,2,1,0:T(8,128)(2,1)}, u32[]{:S(2)}, u32[]{:S(2)}) collective-permute-start(bf16[2,8,2,2,64,101]{5,4,3,2,1,0:T(8,128)(2,1)} %get-tuple-element.5), channel_id=1, source_target_pairs={{0,1},{1,0},{2,3},{3,2},{4,5},{5,4},{6,7},{7,6},{8,9},{9,8},{10,11... | collective-permute-start | bytes 2482184 | tf_op jit(solution)/shard_map/ppermute | solution.py:164
  51.9 1.6 %constant_dynamic-update-slice_fusion.2 = bf16[2,8,2,2,16,101]{5,4,3,2,1,0:T(8,128)(2,1)} fusion(bf16[2,8,2,2,16,101]{5,4,3,2,1,0:T(8,128)(2,1)} %constant_dynamic-update-slice_fusion.3, bf16[1,8,2,2,16,101]{5,4,3,2,1,0:T(8,128)(2,1)} %collective-permute-done.11), kind=kLoop, calls=%fused_computation.95 | loop fusion | bytes 262144 | tf_op jit(solution)/shard_map/concatenate | solution.py:187
  54.5 3.1 %collective-permute-done.9 = bf16[1,8,2,2,16,101]{5,4,3,2,1,0:T(8,128)(2,1)} collective-permute-done((bf16[1,8,2,2,16,101]{5,4,3,2,1,0:T(8,128)(2,1)}, bf16[1,8,2,2,16,101]{5,4,3,2,1,0:T(8,128)(2,1)}, u32[]{:S(2)}, u32[]{:S(2)}) %collective-permute-start.9) | collective-permute-done | bytes 103456 | tf_op jit(solution)/shard_map/ppermute | solution.py:19
  62.1 2.4 %copy.19 = bf16[101,32,64]{2,1,0:T(8,128)(2,1)} copy(bf16[101,32,64]{0,1,2:T(8,128)(2,1)S(1)} %bitcast.135) | data formatting | bytes 827392 | tf_op jit(solution)/shard_map/reshape | solution.py:190
  64.5 1.5 %copy.16 = bf16[101,32,64]{2,1,0:T(8,128)(2,1)S(1)} copy(bf16[101,32,64]{0,1,2:T(8,128)(2,1)S(1)} %bitcast.136) | data formatting | bytes 827392 | tf_op jit(solution)/shard_map/reshape | solution.py:190
  66.1 2.3 %copy.24 = bf16[101,32,64]{2,1,0:T(8,128)(2,1)} copy(bf16[101,32,64]{0,1,2:T(8,128)(2,1)S(1)} %bitcast.137) | data formatting | bytes 827392 | tf_op jit(solution)/shard_map/reshape | solution.py:190
  69.7 2.4 %copy.22 = bf16[101,32,64]{2,1,0:T(8,128)(2,1)} copy(bf16[101,32,64]{0,1,2:T(8,128)(2,1)S(1)} %bitcast.138) | data formatting | bytes 827392 | tf_op jit(solution)/shard_map/reshape | solution.py:190
  72.1 1.8 %fusion.67 = f32[101,32,64]{2,1,0:T(8,128)} fusion(bf16[101,32,64]{2,1,0:T(8,128)(2,1)S(1)} %copy.16, bf16[101,64,64]{2,1,0:T(8,128)(2,1)S(1)} %bitcast.125), kind=kOutput, calls=%fused_computation.135 | convolution fusion | flops 26476544 | bytes 2068480 | tf_op jit(solution)/shard_map/fnk,fkj->fnj/dot_general | solution.py:191
  74.4 4.4 %copy.18 = bf16[101,2,2,8,2,64]{5,4,3,2,1,0:T(2,128)(2,1)S(1)} copy(bf16[101,2,2,8,2,64]{0,5,1,4,3,2:T(8,128)(2,1)} %bitcast.39) | data formatting | bytes 1654784 | tf_op jit(solution)/shard_map/transpose | solution.py:181
  78.8 2.3 %convolution_add_fusion.1 = f32[101,32,64]{2,1,0:T(8,128)S(1)} fusion(f32[101,32,64]{2,1,0:T(8,128)} %fusion.67, bf16[101,32,64]{2,1,0:T(8,128)(2,1)} %copy.19, bf16[101,64,64]{2,1,0:T(8,128)(2,1)S(1)} %bitcast.123), kind=kOutput, calls=%fused_computation.6 | convolution fusion | flops 26683392 | bytes 2895872 | tf_op jit(solution)/shard_map/fnk,fkj->fnj/dot_general | solution.py:191
  82.0 2.1 %fusion.4 = f32[1,64,16,128]{3,1,2,0:T(8,128)S(1)} fusion(f32[101,2,16,64]{3,2,1,0:T(8,128)S(1)} %bitcast.128, f32[1,101,128]{2,1,0:T(8,128)S(1)} %copy-done.6, f32[1,101,128]{2,1,0:T(8,128)S(1)} %copy-done.5), kind=kOutput, calls=%fused_computation.8 | convolution fusion | flops 158885120 | bytes 1455104 | tf_op jit(solution)/shard_map/fcij,cfl->jil/dot_general | solution.py:195
  84.1 2.1 %fusion.7 = f32[1,64,16,128]{3,1,2,0:T(8,128)S(1)} fusion(f32[101,2,16,64]{3,2,1,0:T(8,128)S(1)} %bitcast.127, f32[1,101,128]{2,1,0:T(8,128)S(1)} %copy-done.6, f32[1,101,128]{2,1,0:T(8,128)S(1)} %copy-done.5), kind=kOutput, calls=%fused_computation.9 | convolution fusion | flops 158885120 | bytes 1455104 | tf_op jit(solution)/shard_map/fcij,cfl->jil/dot_general | solution.py:195
  86.3 1.6 %copy.26 = f32[2,64,16,128]{3,2,1,0:T(8,128)} copy(f32[2,64,16,128]{3,1,2,0:T(8,128)S(1)} %pad_maximum_fusion.1) | data formatting | bytes 2097152 | tf_op jit(solution)/shard_map/stack | solution.py:197
  (99 shorter events, 27.2 us)
Async XLA Ops:
  0.0 2.7 %copy-start.2 = (f32[1,400,512]{2,1,0:T(8,128)S(1)}, f32[1,400,512]{2,1,0:T(8,128)}, u32[]{:S(2)}) copy-start(f32[1,400,512]{2,1,0:T(8,128)} %param.3) | copy-start | bytes 2457604
  3.5 0.9 %copy-start.7 = (s32[512]{0:T(512)S(1)}, s32[512]{0:T(512)}, u32[]{:S(2)}) copy-start(s32[512]{0:T(512)} %param.5) | copy-start | bytes 6148
  3.5 1.4 %copy-start.8 = (s32[512]{0:T(512)S(1)}, s32[512]{0:T(512)}, u32[]{:S(2)}) copy-start(s32[512]{0:T(512)} %param.4) | copy-start | bytes 6148
  5.8 10.0 %collective-permute-start = (bf16[2,2,64,101]{3,2,1,0:T(8,128)(2,1)S(1)}, bf16[2,2,64,101]{3,2,1,0:T(8,128)(2,1)S(1)}, u32[]{:S(2)}, u32[]{:S(2)}) collective-permute-start(bf16[2,2,64,101]{3,2,1,0:T(8,128)(2,1)S(1)} %get-tuple-element.17), channel_id=1, source_target_pairs={{28,0},{0,4},{4,8},{8,12},{12,16},{16,20},{20,24},{24,28},{29,1},{... | collective-permute-start | bytes 155144 | tf_op jit(solution)/shard_map/ppermute | solution.py:19
  7.9 9.0 %collective-permute-start.1 = (bf16[2,2,64,101]{3,2,1,0:T(8,128)(2,1)S(1)}, bf16[2,2,64,101]{3,2,1,0:T(8,128)(2,1)S(1)}, u32[]{:S(2)}, u32[]{:S(2)}) collective-permute-start(bf16[2,2,64,101]{3,2,1,0:T(8,128)(2,1)S(1)} %get-tuple-element.16), channel_id=1, source_target_pairs={{24,0},{28,4},{0,8},{4,12},{8,16},{12,20},{16,24},{20,28},{25,1},{... | collective-permute-start | bytes 155144 | tf_op jit(solution)/shard_map/ppermute | solution.py:19
  9.2 9.9 %collective-permute-start.2 = (bf16[2,2,64,101]{3,2,1,0:T(8,128)(2,1)S(1)}, bf16[2,2,64,101]{3,2,1,0:T(8,128)(2,1)S(1)}, u32[]{:S(2)}, u32[]{:S(2)}) collective-permute-start(bf16[2,2,64,101]{3,2,1,0:T(8,128)(2,1)S(1)} %get-tuple-element.15), channel_id=1, source_target_pairs={{20,0},{24,4},{28,8},{0,12},{4,16},{8,20},{12,24},{16,28},{21,1},{... | collective-permute-start | bytes 155144 | tf_op jit(solution)/shard_map/ppermute | solution.py:19
  11.5 7.8 %collective-permute-start.3 = (bf16[2,2,64,101]{3,2,1,0:T(8,128)(2,1)S(1)}, bf16[2,2,64,101]{3,2,1,0:T(8,128)(2,1)S(1)}, u32[]{:S(2)}, u32[]{:S(2)}) collective-permute-start(bf16[2,2,64,101]{3,2,1,0:T(8,128)(2,1)S(1)} %get-tuple-element.14), channel_id=1, source_target_pairs={{16,0},{20,4},{24,8},{28,12},{0,16},{4,20},{8,24},{12,28},{17,1},{... | collective-permute-start | bytes 155144 | tf_op jit(solution)/shard_map/ppermute | solution.py:19
  12.5 6.9 %collective-permute-start.4 = (bf16[2,2,64,101]{3,2,1,0:T(8,128)(2,1)S(1)}, bf16[2,2,64,101]{3,2,1,0:T(8,128)(2,1)S(1)}, u32[]{:S(2)}, u32[]{:S(2)}) collective-permute-start(bf16[2,2,64,101]{3,2,1,0:T(8,128)(2,1)S(1)} %get-tuple-element.13), channel_id=1, source_target_pairs={{12,0},{16,4},{20,8},{24,12},{28,16},{0,20},{4,24},{8,28},{13,1},{... | collective-permute-start | bytes 155144 | tf_op jit(solution)/shard_map/ppermute | solution.py:19
  15.8 4.8 %collective-permute-start.5 = (bf16[2,2,64,101]{3,2,1,0:T(8,128)(2,1)S(1)}, bf16[2,2,64,101]{3,2,1,0:T(8,128)(2,1)S(1)}, u32[]{:S(2)}, u32[]{:S(2)}) collective-permute-start(bf16[2,2,64,101]{3,2,1,0:T(8,128)(2,1)S(1)} %get-tuple-element.12), channel_id=1, source_target_pairs={{8,0},{12,4},{16,8},{20,12},{24,16},{28,20},{0,24},{4,28},{9,1},{1... | collective-permute-start | bytes 155144 | tf_op jit(solution)/shard_map/ppermute | solution.py:19
  17.0 3.7 %collective-permute-start.6 = (bf16[2,2,64,101]{3,2,1,0:T(8,128)(2,1)S(1)}, bf16[2,2,64,101]{3,2,1,0:T(8,128)(2,1)S(1)}, u32[]{:S(2)}, u32[]{:S(2)}) collective-permute-start(bf16[2,2,64,101]{3,2,1,0:T(8,128)(2,1)S(1)} %get-tuple-element.11), channel_id=1, source_target_pairs={{4,0},{8,4},{12,8},{16,12},{20,16},{24,20},{28,24},{0,28},{5,1},{9... | collective-permute-start | bytes 155144 | tf_op jit(solution)/shard_map/ppermute | solution.py:19
  21.5 11.1 %collective-permute-start.10 = (bf16[1,8,2,2,16,101]{5,4,3,2,1,0:T(8,128)(2,1)S(1)}, bf16[1,8,2,2,16,101]{5,4,3,2,1,0:T(8,128)(2,1)S(1)}, u32[]{:S(2)}, u32[]{:S(2)}) collective-permute-start(bf16[1,8,2,2,16,101]{5,4,3,2,1,0:T(8,128)(2,1)S(1)} %get-tuple-element.9), channel_id=1, source_target_pairs={{0,5},{1,4},{2,7},{3,6},{4,9},{5,8},{6,11},{7,10},{8,13},{9,12},{1... | collective-permute-start | bytes 310280 | tf_op jit(solution)/shard_map/ppermute | solution.py:153
  26.3 11.9 %collective-permute-start.15 = (bf16[1,8,2,2,16,101]{5,4,3,2,1,0:T(8,128)(2,1)S(1)}, bf16[1,8,2,2,16,101]{5,4,3,2,1,0:T(8,128)(2,1)S(1)}, u32[]{:S(2)}, u32[]{:S(2)}) collective-permute-start(bf16[1,8,2,2,16,101]{5,4,3,2,1,0:T(8,128)(2,1)S(1)} %get-tuple-element.9), channel_id=1, source_target_pairs={{0,9},{1,8},{2,11},{3,10},{4,13},{5,12},{6,15},{7,14},{8,17},{9,16... | collective-permute-start | bytes 310280 | tf_op jit(solution)/shard_map/ppermute | solution.py:153
  27.1 11.1 %collective-permute-start.7 = (bf16[1,8,2,2,16,101]{5,4,3,2,1,0:T(8,128)(2,1)S(1)}, bf16[1,8,2,2,16,101]{5,4,3,2,1,0:T(8,128)(2,1)S(1)}, u32[]{:S(2)}, u32[]{:S(2)}) collective-permute-start(bf16[1,8,2,2,16,101]{5,4,3,2,1,0:T(8,128)(2,1)S(1)} %get-tuple-element.10), channel_id=1, source_target_pairs={{28,0},{0,4},{4,8},{8,12},{12,16},{16,20},{20,24},{24,28},{29,1},{... | collective-permute-start | bytes 310280 | tf_op jit(solution)/shard_map/ppermute | solution.py:19
  27.4 10.9 %collective-permute-start.13 = (bf16[1,8,2,2,16,101]{5,4,3,2,1,0:T(8,128)(2,1)S(1)}, bf16[1,8,2,2,16,101]{5,4,3,2,1,0:T(8,128)(2,1)S(1)}, u32[]{:S(2)}, u32[]{:S(2)}) collective-permute-start(bf16[1,8,2,2,16,101]{5,4,3,2,1,0:T(8,128)(2,1)S(1)} %get-tuple-element.10), channel_id=1, source_target_pairs={{24,0},{28,4},{0,8},{4,12},{8,16},{12,20},{16,24},{20,28},{25,1},{... | collective-permute-start | bytes 310280 | tf_op jit(solution)/shard_map/ppermute | solution.py:19
  28.7 12.8 %collective-permute-start.8 = (bf16[1,8,2,2,64,101]{5,4,3,2,1,0:T(8,128)(2,1)S(1)}, bf16[1,8,2,2,64,101]{5,4,3,2,1,0:T(8,128)(2,1)S(1)}, u32[]{:S(2)}, u32[]{:S(2)}) collective-permute-start(bf16[1,8,2,2,64,101]{5,4,3,2,1,0:T(8,128)(2,1)S(1)} %bitcast_select_fusion), channel_id=1, source_target_pairs={{0,2},{1,3},{2,0},{3,1},{4,6},{5,7},{6,4},{7,5},{8,10},{9,11},{10,... | collective-permute-start | bytes 1241096 | tf_op jit(solution)/shard_map/ppermute | solution.py:160
  42.3 9.6 %collective-permute-start.11 = (bf16[1,8,2,2,16,101]{5,4,3,2,1,0:T(8,128)(2,1)}, bf16[1,8,2,2,16,101]{5,4,3,2,1,0:T(8,128)(2,1)}, u32[]{:S(2)}, u32[]{:S(2)}) collective-permute-start(bf16[1,8,2,2,16,101]{5,4,3,2,1,0:T(8,128)(2,1)} %get-tuple-element.7), channel_id=1, source_target_pairs={{0,5},{1,4},{2,7},{3,6},{4,9},{5,8},{6,11},{7,10},{8,13},{9,12},{1... | collective-permute-start | bytes 310280 | tf_op jit(solution)/shard_map/ppermute | solution.py:153
  44.9 13.6 %collective-permute-start.16 = (bf16[1,8,2,2,16,101]{5,4,3,2,1,0:T(8,128)(2,1)}, bf16[1,8,2,2,16,101]{5,4,3,2,1,0:T(8,128)(2,1)}, u32[]{:S(2)}, u32[]{:S(2)}) collective-permute-start(bf16[1,8,2,2,16,101]{5,4,3,2,1,0:T(8,128)(2,1)} %get-tuple-element.7), channel_id=1, source_target_pairs={{0,9},{1,8},{2,11},{3,10},{4,13},{5,12},{6,15},{7,14},{8,17},{9,16... | collective-permute-start | bytes 310280 | tf_op jit(solution)/shard_map/ppermute | solution.py:153
  44.9 12.6 %collective-permute-start.9 = (bf16[1,8,2,2,16,101]{5,4,3,2,1,0:T(8,128)(2,1)}, bf16[1,8,2,2,16,101]{5,4,3,2,1,0:T(8,128)(2,1)}, u32[]{:S(2)}, u32[]{:S(2)}) collective-permute-start(bf16[1,8,2,2,16,101]{5,4,3,2,1,0:T(8,128)(2,1)} %get-tuple-element.8), channel_id=1, source_target_pairs={{28,0},{0,4},{4,8},{8,12},{12,16},{16,20},{20,24},{24,28},{29,1},{... | collective-permute-start | bytes 310280 | tf_op jit(solution)/shard_map/ppermute | solution.py:19
  45.5 14.0 %collective-permute-start.14 = (bf16[1,8,2,2,16,101]{5,4,3,2,1,0:T(8,128)(2,1)}, bf16[1,8,2,2,16,101]{5,4,3,2,1,0:T(8,128)(2,1)}, u32[]{:S(2)}, u32[]{:S(2)}) collective-permute-start(bf16[1,8,2,2,16,101]{5,4,3,2,1,0:T(8,128)(2,1)} %get-tuple-element.8), channel_id=1, source_target_pairs={{24,0},{28,4},{0,8},{4,12},{8,16},{12,20},{16,24},{20,28},{25,1},{... | collective-permute-start | bytes 310280 | tf_op jit(solution)/shard_map/ppermute | solution.py:19
  50.6 23.8 %collective-permute-start.12 = (bf16[2,8,2,2,64,101]{5,4,3,2,1,0:T(8,128)(2,1)}, bf16[2,8,2,2,64,101]{5,4,3,2,1,0:T(8,128)(2,1)}, u32[]{:S(2)}, u32[]{:S(2)}) collective-permute-start(bf16[2,8,2,2,64,101]{5,4,3,2,1,0:T(8,128)(2,1)} %get-tuple-element.5), channel_id=1, source_target_pairs={{0,1},{1,0},{2,3},{3,2},{4,5},{5,4},{6,7},{7,6},{8,9},{9,8},{10,11... | collective-permute-start | bytes 2482184 | tf_op jit(solution)/shard_map/ppermute | solution.py:164
  53.5 7.1 %copy-start.4 = (bf16[2,8,2,2,16,101]{5,4,3,2,1,0:T(8,128)(2,1)S(1)}, bf16[2,8,2,2,16,101]{5,4,3,2,1,0:T(8,128)(2,1)}, u32[]{:S(2)}) copy-start(bf16[2,8,2,2,16,101]{5,4,3,2,1,0:T(8,128)(2,1)} %constant_dynamic-update-slice_fusion.2) | copy-start | bytes 620548
  72.1 1.8 %copy-start.1 = (bf16[101,32,64]{2,1,0:T(8,128)(2,1)S(1)}, bf16[101,32,64]{2,1,0:T(8,128)(2,1)}, u32[]{:S(2)}) copy-start(bf16[101,32,64]{2,1,0:T(8,128)(2,1)} %copy.22) | copy-start | bytes 1241092
  78.8 2.3 %copy-start = (bf16[101,32,64]{2,1,0:T(8,128)(2,1)S(1)}, bf16[101,32,64]{2,1,0:T(8,128)(2,1)}, u32[]{:S(2)}) copy-start(bf16[101,32,64]{2,1,0:T(8,128)(2,1)} %copy.24) | copy-start | bytes 1241092
  81.1 0.8 copy-start.6
  (2 other events, 1.5 us)

commit v13 on v11

--- a/solution.py
+++ b/solution.py
@@ -136,9 +136,6 @@
         piece = lax.dynamic_slice_in_dim(group, tm_position * slice_width, slice_width, axis=4)
         return [shifted(piece, "chan", offset) for offset in offsets]
 
-    gathered = own[None]
-    partner_groups = [send_slices(gathered)]
-    step = tm_count // 2
     grid = [(c, q) for c in range(chan_count) for q in range(tm_count)]
 
     def send_from_neighbour(group, mask):
@@ -154,15 +151,26 @@
             sent.append(lax.ppermute(piece, ("chan", "tm"), route))
         return sent
 
-    while step >= 1:
-        route = [(q, q ^ step) for q in range(tm_count)]
-        arrived = lax.ppermute(gathered, "tm", route)
-        if step == 1:
-            partner_groups.append(send_from_neighbour(gathered, step))
-        else:
+    gathered = own[None]
+    if tm_count == 4:
+        slot0 = send_slices(gathered)
+        slot2 = send_from_neighbour(gathered, 1)
+        arrived = lax.ppermute(gathered, "tm", [(q, q ^ 2) for q in range(tm_count)])
+        slot1 = send_slices(arrived)
+        slot3 = send_from_neighbour(arrived, 1)
+        gathered = jnp.concatenate([gathered, arrived], axis=0)
+        arrived = lax.ppermute(gathered, "tm", [(q, q ^ 1) for q in range(tm_count)])
+        gathered = jnp.concatenate([gathered, arrived], axis=0)
+        partner_groups = [slot0, slot1, slot2, slot3]
+    else:
+        partner_groups = [send_slices(gathered)]
+        step = tm_count // 2
+        while step >= 1:
+            route = [(q, q ^ step) for q in range(tm_count)]
+            arrived = lax.ppermute(gathered, "tm", route)
             partner_groups.append(send_slices(arrived))
-        gathered = jnp.concatenate([gathered, arrived], axis=0)
-        step //= 2
+            gathered = jnp.concatenate([gathered, arrived], axis=0)
+            step //= 2
     windows_all = gathered.shape[0] * gathered.shape[1] * gathered.shape[2]
     own_spec = jnp.transpose(gathered, (5, 3, 0, 1, 2, 4)).reshape(FB, 2 * windows_all, block_width)
     inverse = inverse_table()
@@ -177,7 +185,7 @@
         sums = jnp.einsum("fnk,fkj->fnj", both, own_spec, preferred_element_type=jnp.float32)
         sums = sums.reshape(FB, 2, slice_width, block_width)
         results.append(
-            jnp.einsum("fcij,cfl->jil", sums, inverse, precision=lax.Precision.HIGH)
+            jnp.einsum("fcij,cfl->jil", sums, inverse, precision=lax.Precision.DEFAULT)
         )
     return jnp.stack(results)
 

time: 76.2 us -> 69.8 us (0.916)
  the two profiles are of different devices: /device:TPU:6 before, /device:TPU:0 now
where the time goes in v13:
time: 69.8 us; the launch traced here: 69.4 us
  starting transfers between devices  28.5 us (41%)
  waiting for transfers between devices  14.5 us (21%)
  local copies, waits for them, and re-layouts  12.1 us (17%)
  other arithmetic  7.13 us (10%)
  matrix products  6.76 us (10%)
    ppermute x11, starting transfers between devices, shifted(): return lax.ppermute(block, axis, route)  24.4 us
    ppermute x11, waiting for transfers between devices, shifted(): return lax.ppermute(block, axis, route)  7.97 us
    ppermute x4, waiting for transfers between devices, send_from_neighbour(): sent.append(lax.ppermute(piece, ('chan', 'tm'), route))  5.78 us
    reshape x1, local copies, waits for them, and re-layouts, on_device_local(): jnp.transpose(gathered, (5, 3, 0, 1, 2, 4))  3.79 us
    reshape x2, local copies, waits for them, and re-layouts, on_device_local(): jnp.transpose(both, (6, 0, 5, 4, 1, 2, 3))  3.67 us
    dot_general x2, matrix products, on_device_local(): jnp.einsum('fnk,fkj->fnj', both, own_spec, preferred_element_type=jnp.flo...  1.93 us
    dot_general x1, matrix products, whiten_planes(): jnp.einsum('wlk,lg->wkg', normed, table[:, :FB], precision=precision)  1.93 us
    transpose x1, other arithmetic, on_device_local(): jnp.transpose(gathered, (5, 3, 0, 1, 2, 4))  1.71 us
  transfers between devices with their start and end apart: 17, of which 10 were waited for; matrix products, arithmetic and copies ran while one was open for 10% of the time, Pallas kernels for 0%

profile of v13, /device:TPU:0, one launch (start us, length us, event | category | flops | bytes accessed | tf_op | source)
XLA Modules:
  0.0 69.4 jit_solution(11999178016509947766)
XLA Ops:
  1.4 1.3 %multiply_reduce_fusion = f32[2,512]{1,0:T(2,128)S(1)} fusion(f32[2,200,512]{2,1,0:T(8,128)} %bitcast.113, f32[2,512]{1,0:T(2,128)S(1)} %broadcast_multiply_fusion.1), kind=kLoop, calls=%fused_computation.22 | loop fusion | flops 613376 | bytes 827392 | tf_op jit(solution)/shard_map/reduce_sum | solution.py:100
  2.7 1.9 %fusion.21 = f32[2,512,101]{1,2,0:T(8,128)S(1)} fusion(f32[2,200,512]{2,1,0:T(8,128)} %bitcast.114, f32[2,512]{1,0:T(2,128)S(1)} %add_sqrt_fusion, f32[2,512]{1,0:T(2,128)S(1)} %broadcast_multiply_fusion.1), kind=kOutput, calls=%fused_computation.42 | convolution fusion | flops 124700200 | bytes 1241088 | tf_op jit(solution)/shard_map/wlk,lg->wkg/dot_general | solution.py:102
  7.0 3.1 %collective-permute-start = (bf16[2,2,64,101]{3,2,1,0:T(8,128)(2,1)S(1)}, bf16[2,2,64,101]{3,2,1,0:T(8,128)(2,1)S(1)}, u32[]{:S(2)}, u32[]{:S(2)}) collective-permute-start(bf16[2,2,64,101]{3,2,1,0:T(8,128)(2,1)S(1)} %get-tuple-element.19), channel_id=1, source_target_pairs={{28,0},{0,4},{4,8},{8,12},{12,16},{16,20},{20,24},{24,28},{29,1},{... | collective-permute-start | bytes 155144 | tf_op jit(solution)/shard_map/ppermute | solution.py:19
  10.0 1.6 %collective-permute-start.1 = (bf16[2,2,64,101]{3,2,1,0:T(8,128)(2,1)S(1)}, bf16[2,2,64,101]{3,2,1,0:T(8,128)(2,1)S(1)}, u32[]{:S(2)}, u32[]{:S(2)}) collective-permute-start(bf16[2,2,64,101]{3,2,1,0:T(8,128)(2,1)S(1)} %get-tuple-element.18), channel_id=1, source_target_pairs={{24,0},{28,4},{0,8},{4,12},{8,16},{12,20},{16,24},{20,28},{25,1},{... | collective-permute-start | bytes 155144 | tf_op jit(solution)/shard_map/ppermute | solution.py:19
  11.6 2.5 %collective-permute-start.2 = (bf16[2,2,64,101]{3,2,1,0:T(8,128)(2,1)S(1)}, bf16[2,2,64,101]{3,2,1,0:T(8,128)(2,1)S(1)}, u32[]{:S(2)}, u32[]{:S(2)}) collective-permute-start(bf16[2,2,64,101]{3,2,1,0:T(8,128)(2,1)S(1)} %get-tuple-element.17), channel_id=1, source_target_pairs={{20,0},{24,4},{28,8},{0,12},{4,16},{8,20},{12,24},{16,28},{21,1},{... | collective-permute-start | bytes 155144 | tf_op jit(solution)/shard_map/ppermute | solution.py:19
  15.4 2.7 %collective-permute-start.4 = (bf16[2,2,64,101]{3,2,1,0:T(8,128)(2,1)S(1)}, bf16[2,2,64,101]{3,2,1,0:T(8,128)(2,1)S(1)}, u32[]{:S(2)}, u32[]{:S(2)}) collective-permute-start(bf16[2,2,64,101]{3,2,1,0:T(8,128)(2,1)S(1)} %get-tuple-element.15), channel_id=1, source_target_pairs={{12,0},{16,4},{20,8},{24,12},{28,16},{0,20},{4,24},{8,28},{13,1},{... | collective-permute-start | bytes 155144 | tf_op jit(solution)/shard_map/ppermute | solution.py:19
  18.1 1.4 %collective-permute-start.5 = (bf16[2,2,64,101]{3,2,1,0:T(8,128)(2,1)S(1)}, bf16[2,2,64,101]{3,2,1,0:T(8,128)(2,1)S(1)}, u32[]{:S(2)}, u32[]{:S(2)}) collective-permute-start(bf16[2,2,64,101]{3,2,1,0:T(8,128)(2,1)S(1)} %get-tuple-element.14), channel_id=1, source_target_pairs={{8,0},{12,4},{16,8},{20,12},{24,16},{28,20},{0,24},{4,28},{9,1},{1... | collective-permute-start | bytes 155144 | tf_op jit(solution)/shard_map/ppermute | solution.py:19
  19.5 1.5 %collective-permute-start.6 = (bf16[2,2,64,101]{3,2,1,0:T(8,128)(2,1)S(1)}, bf16[2,2,64,101]{3,2,1,0:T(8,128)(2,1)S(1)}, u32[]{:S(2)}, u32[]{:S(2)}) collective-permute-start(bf16[2,2,64,101]{3,2,1,0:T(8,128)(2,1)S(1)} %get-tuple-element.13), channel_id=1, source_target_pairs={{4,0},{8,4},{12,8},{16,12},{20,16},{24,20},{28,24},{0,28},{5,1},{9... | collective-permute-start | bytes 155144 | tf_op jit(solution)/shard_map/ppermute | solution.py:19
  24.0 1.6 %collective-permute-start.8 = (bf16[1,8,2,2,64,101]{5,4,3,2,1,0:T(8,128)(2,1)S(1)}, bf16[1,8,2,2,64,101]{5,4,3,2,1,0:T(8,128)(2,1)S(1)}, u32[]{:S(2)}, u32[]{:S(2)}) collective-permute-start(bf16[1,8,2,2,64,101]{5,4,3,2,1,0:T(8,128)(2,1)S(1)} %bitcast.107), channel_id=1, source_target_pairs={{0,2},{1,3},{2,0},{3,1},{4,6},{5,7},{6,4},{7,5},{8,10},{9,11},{10,... | collective-permute-start | bytes 1241096 | tf_op jit(solution)/shard_map/ppermute | solution.py:158
  25.6 2.2 %collective-permute-start.7 = (bf16[1,8,2,2,16,101]{5,4,3,2,1,0:T(8,128)(2,1)S(1)}, bf16[1,8,2,2,16,101]{5,4,3,2,1,0:T(8,128)(2,1)S(1)}, u32[]{:S(2)}, u32[]{:S(2)}) collective-permute-start(bf16[1,8,2,2,16,101]{5,4,3,2,1,0:T(8,128)(2,1)S(1)} %get-tuple-element.12), channel_id=1, source_target_pairs={{28,0},{0,4},{4,8},{8,12},{12,16},{16,20},{20,24},{24,28},{29,1},{... | collective-permute-start | bytes 310280 | tf_op jit(solution)/shard_map/ppermute | solution.py:19
  28.0 2.0 %collective-permute-start.13 = (bf16[1,8,2,2,16,101]{5,4,3,2,1,0:T(8,128)(2,1)S(1)}, bf16[1,8,2,2,16,101]{5,4,3,2,1,0:T(8,128)(2,1)S(1)}, u32[]{:S(2)}, u32[]{:S(2)}) collective-permute-start(bf16[1,8,2,2,16,101]{5,4,3,2,1,0:T(8,128)(2,1)S(1)} %get-tuple-element.12), channel_id=1, source_target_pairs={{24,0},{28,4},{0,8},{4,12},{8,16},{12,20},{16,24},{20,28},{25,1},{... | collective-permute-start | bytes 310280 | tf_op jit(solution)/shard_map/ppermute | solution.py:19
  30.0 1.4 %collective-permute-start.15 = (bf16[1,8,2,2,16,101]{5,4,3,2,1,0:T(8,128)(2,1)S(1)}, bf16[1,8,2,2,16,101]{5,4,3,2,1,0:T(8,128)(2,1)S(1)}, u32[]{:S(2)}, u32[]{:S(2)}) collective-permute-start(bf16[1,8,2,2,16,101]{5,4,3,2,1,0:T(8,128)(2,1)S(1)} %get-tuple-element.11), channel_id=1, source_target_pairs={{0,9},{1,8},{2,11},{3,10},{4,13},{5,12},{6,15},{7,14},{8,17},{9,16... | collective-permute-start | bytes 310280 | tf_op jit(solution)/shard_map/ppermute | solution.py:151
  31.5 3.1 %collective-permute-done.7 = bf16[1,8,2,2,16,101]{5,4,3,2,1,0:T(8,128)(2,1)S(1)} collective-permute-done((bf16[1,8,2,2,16,101]{5,4,3,2,1,0:T(8,128)(2,1)S(1)}, bf16[1,8,2,2,16,101]{5,4,3,2,1,0:T(8,128)(2,1)S(1)}, u32[]{:S(2)}, u32[]{:S(2)}) %collective-permute-start.7) | collective-permute-done | bytes 103456 | tf_op jit(solution)/shard_map/ppermute | solution.py:19
  35.7 3.5 %collective-permute-start.9 = (bf16[1,8,2,2,16,101]{5,4,3,2,1,0:T(8,128)(2,1)S(1)}, bf16[1,8,2,2,16,101]{5,4,3,2,1,0:T(8,128)(2,1)S(1)}, u32[]{:S(2)}, u32[]{:S(2)}) collective-permute-start(bf16[1,8,2,2,16,101]{5,4,3,2,1,0:T(8,128)(2,1)S(1)} %get-tuple-element.10), channel_id=1, source_target_pairs={{28,0},{0,4},{4,8},{8,12},{12,16},{16,20},{20,24},{24,28},{29,1},{... | collective-permute-start | bytes 310280 | tf_op jit(solution)/shard_map/ppermute | solution.py:19
  39.1 2.8 %collective-permute-start.14 = (bf16[1,8,2,2,16,101]{5,4,3,2,1,0:T(8,128)(2,1)S(1)}, bf16[1,8,2,2,16,101]{5,4,3,2,1,0:T(8,128)(2,1)S(1)}, u32[]{:S(2)}, u32[]{:S(2)}) collective-permute-start(bf16[1,8,2,2,16,101]{5,4,3,2,1,0:T(8,128)(2,1)S(1)} %get-tuple-element.10), channel_id=1, source_target_pairs={{24,0},{28,4},{0,8},{4,12},{8,16},{12,20},{16,24},{20,28},{25,1},{... | collective-permute-start | bytes 310280 | tf_op jit(solution)/shard_map/ppermute | solution.py:19
  43.1 1.7 %collective-permute-done.9 = bf16[1,8,2,2,16,101]{5,4,3,2,1,0:T(8,128)(2,1)S(1)} collective-permute-done((bf16[1,8,2,2,16,101]{5,4,3,2,1,0:T(8,128)(2,1)S(1)}, bf16[1,8,2,2,16,101]{5,4,3,2,1,0:T(8,128)(2,1)S(1)}, u32[]{:S(2)}, u32[]{:S(2)}) %collective-permute-start.9) | collective-permute-done | bytes 103456 | tf_op jit(solution)/shard_map/ppermute | solution.py:19
  46.0 4.4 %collective-permute-done.11 = bf16[1,8,2,2,16,101]{5,4,3,2,1,0:T(8,128)(2,1)S(1)} collective-permute-done((bf16[1,8,2,2,16,101]{5,4,3,2,1,0:T(8,128)(2,1)S(1)}, bf16[1,8,2,2,16,101]{5,4,3,2,1,0:T(8,128)(2,1)S(1)}, u32[]{:S(2)}, u32[]{:S(2)}) %collective-permute-start.11) | collective-permute-done | bytes 103456 | tf_op jit(solution)/shard_map/ppermute | solution.py:151
  50.5 1.4 %collective-permute-done.16 = bf16[1,8,2,2,16,101]{5,4,3,2,1,0:T(8,128)(2,1)S(1)} collective-permute-done((bf16[1,8,2,2,16,101]{5,4,3,2,1,0:T(8,128)(2,1)S(1)}, bf16[1,8,2,2,16,101]{5,4,3,2,1,0:T(8,128)(2,1)S(1)}, u32[]{:S(2)}, u32[]{:S(2)}) %collective-permute-start.16) | collective-permute-done | bytes 103456 | tf_op jit(solution)/shard_map/ppermute | solution.py:151
  52.9 1.5 %copy.14 = bf16[101,32,128]{2,1,0:T(8,128)(2,1)S(1)} copy(bf16[101,32,128]{0,1,2:T(8,128)(2,1)S(1)} %bitcast.105) | data formatting | bytes 1654784 | tf_op jit(solution)/shard_map/reshape | solution.py:184
  55.3 2.2 %copy.18 = bf16[101,32,128]{2,1,0:T(8,128)(2,1)} copy(bf16[101,32,128]{0,1,2:T(8,128)(2,1)S(1)} %bitcast.106) | data formatting | bytes 1654784 | tf_op jit(solution)/shard_map/reshape | solution.py:184
  57.5 1.7 %maximum_bitcast_fusion = bf16[101,2,4,8,2,64]{0,5,1,4,3,2:T(8,128)(2,1)S(1)} fusion(bf16[2,8,2,2,64,101]{5,4,3,2,1,0:T(8,128)(2,1)} %collective-permute-done.12, bf16[1,8,2,2,64,101]{5,4,3,2,1,0:T(8,128)(2,1)S(1)} %collective-permute-done.8, bf16[1,8,2,2,64,101]{5,4,3,2,1,0:T(8,128)(2,1)S(1)} %bitcast.109), kind=kLoop, calls=%fused_computation | loop fusion | flops 1654784 | bytes 3309568 | tf_op jit(solution)/shard_map/transpose | solution.py:175
  59.2 1.5 %copy.13 = bf16[101,2,4,8,2,64]{0,5,4,3,2,1:T(8,128)(2,1)} copy(bf16[101,2,4,8,2,64]{0,5,1,4,3,2:T(8,128)(2,1)S(1)} %maximum_bitcast_fusion) | data formatting | bytes 3309568 | tf_op jit(solution)/shard_map/transpose | solution.py:175
  60.8 3.8 %copy.15 = bf16[101,128,64]{1,2,0:T(8,128)(2,1)S(1)} copy(bf16[101,128,64]{0,2,1:T(8,128)(2,1)} %bitcast.104) | data formatting | bytes 3309568 | tf_op jit(solution)/shard_map/reshape | solution.py:175
  67.8 1.6 %copy.21 = f32[2,64,16,128]{3,2,1,0:T(8,128)} copy(f32[2,64,16,128]{3,1,2,0:T(8,128)S(1)} %pad_maximum_fusion.1) | data formatting | bytes 2097152 | tf_op jit(solution)/shard_map/stack | solution.py:190
  (76 shorter events, 16.8 us)
Async XLA Ops:
  1.3 3.3 %copy-start.1 = (f32[1,400,512]{2,1,0:T(8,128)S(1)}, f32[1,400,512]{2,1,0:T(8,128)}, u32[]{:S(2)}) copy-start(f32[1,400,512]{2,1,0:T(8,128)} %param.3) | copy-start | bytes 2457604
  4.7 0.9 %copy-start.2 = (s32[512]{0:T(512)S(1)}, s32[512]{0:T(512)}, u32[]{:S(2)}) copy-start(s32[512]{0:T(512)} %param.5) | copy-start | bytes 6148
  4.7 1.4 %copy-start.3 = (s32[512]{0:T(512)S(1)}, s32[512]{0:T(512)}, u32[]{:S(2)}) copy-start(s32[512]{0:T(512)} %param.4) | copy-start | bytes 6148
  7.0 11.1 %collective-permute-start = (bf16[2,2,64,101]{3,2,1,0:T(8,128)(2,1)S(1)}, bf16[2,2,64,101]{3,2,1,0:T(8,128)(2,1)S(1)}, u32[]{:S(2)}, u32[]{:S(2)}) collective-permute-start(bf16[2,2,64,101]{3,2,1,0:T(8,128)(2,1)S(1)} %get-tuple-element.19), channel_id=1, source_target_pairs={{28,0},{0,4},{4,8},{8,12},{12,16},{16,20},{20,24},{24,28},{29,1},{... | collective-permute-start | bytes 155144 | tf_op jit(solution)/shard_map/ppermute | solution.py:19
  10.0 9.4 %collective-permute-start.1 = (bf16[2,2,64,101]{3,2,1,0:T(8,128)(2,1)S(1)}, bf16[2,2,64,101]{3,2,1,0:T(8,128)(2,1)S(1)}, u32[]{:S(2)}, u32[]{:S(2)}) collective-permute-start(bf16[2,2,64,101]{3,2,1,0:T(8,128)(2,1)S(1)} %get-tuple-element.18), channel_id=1, source_target_pairs={{24,0},{28,4},{0,8},{4,12},{8,16},{12,20},{16,24},{20,28},{25,1},{... | collective-permute-start | bytes 155144 | tf_op jit(solution)/shard_map/ppermute | solution.py:19
  11.6 9.7 %collective-permute-start.2 = (bf16[2,2,64,101]{3,2,1,0:T(8,128)(2,1)S(1)}, bf16[2,2,64,101]{3,2,1,0:T(8,128)(2,1)S(1)}, u32[]{:S(2)}, u32[]{:S(2)}) collective-permute-start(bf16[2,2,64,101]{3,2,1,0:T(8,128)(2,1)S(1)} %get-tuple-element.17), channel_id=1, source_target_pairs={{20,0},{24,4},{28,8},{0,12},{4,16},{8,20},{12,24},{16,28},{21,1},{... | collective-permute-start | bytes 155144 | tf_op jit(solution)/shard_map/ppermute | solution.py:19
  14.1 7.8 %collective-permute-start.3 = (bf16[2,2,64,101]{3,2,1,0:T(8,128)(2,1)S(1)}, bf16[2,2,64,101]{3,2,1,0:T(8,128)(2,1)S(1)}, u32[]{:S(2)}, u32[]{:S(2)}) collective-permute-start(bf16[2,2,64,101]{3,2,1,0:T(8,128)(2,1)S(1)} %get-tuple-element.16), channel_id=1, source_target_pairs={{16,0},{20,4},{24,8},{28,12},{0,16},{4,20},{8,24},{12,28},{17,1},{... | collective-permute-start | bytes 155144 | tf_op jit(solution)/shard_map/ppermute | solution.py:19
  15.4 7.4 %collective-permute-start.4 = (bf16[2,2,64,101]{3,2,1,0:T(8,128)(2,1)S(1)}, bf16[2,2,64,101]{3,2,1,0:T(8,128)(2,1)S(1)}, u32[]{:S(2)}, u32[]{:S(2)}) collective-permute-start(bf16[2,2,64,101]{3,2,1,0:T(8,128)(2,1)S(1)} %get-tuple-element.15), channel_id=1, source_target_pairs={{12,0},{16,4},{20,8},{24,12},{28,16},{0,20},{4,24},{8,28},{13,1},{... | collective-permute-start | bytes 155144 | tf_op jit(solution)/shard_map/ppermute | solution.py:19
  18.1 5.9 %collective-permute-start.5 = (bf16[2,2,64,101]{3,2,1,0:T(8,128)(2,1)S(1)}, bf16[2,2,64,101]{3,2,1,0:T(8,128)(2,1)S(1)}, u32[]{:S(2)}, u32[]{:S(2)}) collective-permute-start(bf16[2,2,64,101]{3,2,1,0:T(8,128)(2,1)S(1)} %get-tuple-element.14), channel_id=1, source_target_pairs={{8,0},{12,4},{16,8},{20,12},{24,16},{28,20},{0,24},{4,28},{9,1},{1... | collective-permute-start | bytes 155144 | tf_op jit(solution)/shard_map/ppermute | solution.py:19
  19.5 4.5 %collective-permute-start.6 = (bf16[2,2,64,101]{3,2,1,0:T(8,128)(2,1)S(1)}, bf16[2,2,64,101]{3,2,1,0:T(8,128)(2,1)S(1)}, u32[]{:S(2)}, u32[]{:S(2)}) collective-permute-start(bf16[2,2,64,101]{3,2,1,0:T(8,128)(2,1)S(1)} %get-tuple-element.13), channel_id=1, source_target_pairs={{4,0},{8,4},{12,8},{16,12},{20,16},{24,20},{28,24},{0,28},{5,1},{9... | collective-permute-start | bytes 155144 | tf_op jit(solution)/shard_map/ppermute | solution.py:19
  24.0 11.6 %collective-permute-start.8 = (bf16[1,8,2,2,64,101]{5,4,3,2,1,0:T(8,128)(2,1)S(1)}, bf16[1,8,2,2,64,101]{5,4,3,2,1,0:T(8,128)(2,1)S(1)}, u32[]{:S(2)}, u32[]{:S(2)}) collective-permute-start(bf16[1,8,2,2,64,101]{5,4,3,2,1,0:T(8,128)(2,1)S(1)} %bitcast.107), channel_id=1, source_target_pairs={{0,2},{1,3},{2,0},{3,1},{4,6},{5,7},{6,4},{7,5},{8,10},{9,11},{10,... | collective-permute-start | bytes 1241096 | tf_op jit(solution)/shard_map/ppermute | solution.py:158
  25.6 9.0 %collective-permute-start.7 = (bf16[1,8,2,2,16,101]{5,4,3,2,1,0:T(8,128)(2,1)S(1)}, bf16[1,8,2,2,16,101]{5,4,3,2,1,0:T(8,128)(2,1)S(1)}, u32[]{:S(2)}, u32[]{:S(2)}) collective-permute-start(bf16[1,8,2,2,16,101]{5,4,3,2,1,0:T(8,128)(2,1)S(1)} %get-tuple-element.12), channel_id=1, source_target_pairs={{28,0},{0,4},{4,8},{8,12},{12,16},{16,20},{20,24},{24,28},{29,1},{... | collective-permute-start | bytes 310280 | tf_op jit(solution)/shard_map/ppermute | solution.py:19
  28.0 6.8 %collective-permute-start.13 = (bf16[1,8,2,2,16,101]{5,4,3,2,1,0:T(8,128)(2,1)S(1)}, bf16[1,8,2,2,16,101]{5,4,3,2,1,0:T(8,128)(2,1)S(1)}, u32[]{:S(2)}, u32[]{:S(2)}) collective-permute-start(bf16[1,8,2,2,16,101]{5,4,3,2,1,0:T(8,128)(2,1)S(1)} %get-tuple-element.12), channel_id=1, source_target_pairs={{24,0},{28,4},{0,8},{4,12},{8,16},{12,20},{16,24},{20,28},{25,1},{... | collective-permute-start | bytes 310280 | tf_op jit(solution)/shard_map/ppermute | solution.py:19
  30.0 14.8 %collective-permute-start.10 = (bf16[1,8,2,2,16,101]{5,4,3,2,1,0:T(8,128)(2,1)S(1)}, bf16[1,8,2,2,16,101]{5,4,3,2,1,0:T(8,128)(2,1)S(1)}, u32[]{:S(2)}, u32[]{:S(2)}) collective-permute-start(bf16[1,8,2,2,16,101]{5,4,3,2,1,0:T(8,128)(2,1)S(1)} %get-tuple-element.11), channel_id=1, source_target_pairs={{0,5},{1,4},{2,7},{3,6},{4,9},{5,8},{6,11},{7,10},{8,13},{9,12},{1... | collective-permute-start | bytes 310280 | tf_op jit(solution)/shard_map/ppermute | solution.py:151
  30.0 20.4 %collective-permute-start.15 = (bf16[1,8,2,2,16,101]{5,4,3,2,1,0:T(8,128)(2,1)S(1)}, bf16[1,8,2,2,16,101]{5,4,3,2,1,0:T(8,128)(2,1)S(1)}, u32[]{:S(2)}, u32[]{:S(2)}) collective-permute-start(bf16[1,8,2,2,16,101]{5,4,3,2,1,0:T(8,128)(2,1)S(1)} %get-tuple-element.11), channel_id=1, source_target_pairs={{0,9},{1,8},{2,11},{3,10},{4,13},{5,12},{6,15},{7,14},{8,17},{9,16... | collective-permute-start | bytes 310280 | tf_op jit(solution)/shard_map/ppermute | solution.py:151
  35.7 9.1 %collective-permute-start.9 = (bf16[1,8,2,2,16,101]{5,4,3,2,1,0:T(8,128)(2,1)S(1)}, bf16[1,8,2,2,16,101]{5,4,3,2,1,0:T(8,128)(2,1)S(1)}, u32[]{:S(2)}, u32[]{:S(2)}) collective-permute-start(bf16[1,8,2,2,16,101]{5,4,3,2,1,0:T(8,128)(2,1)S(1)} %get-tuple-element.10), channel_id=1, source_target_pairs={{28,0},{0,4},{4,8},{8,12},{12,16},{16,20},{20,24},{24,28},{29,1},{... | collective-permute-start | bytes 310280 | tf_op jit(solution)/shard_map/ppermute | solution.py:19
  39.1 11.3 %collective-permute-start.14 = (bf16[1,8,2,2,16,101]{5,4,3,2,1,0:T(8,128)(2,1)S(1)}, bf16[1,8,2,2,16,101]{5,4,3,2,1,0:T(8,128)(2,1)S(1)}, u32[]{:S(2)}, u32[]{:S(2)}) collective-permute-start(bf16[1,8,2,2,16,101]{5,4,3,2,1,0:T(8,128)(2,1)S(1)} %get-tuple-element.10), channel_id=1, source_target_pairs={{24,0},{28,4},{0,8},{4,12},{8,16},{12,20},{16,24},{20,28},{25,1},{... | collective-permute-start | bytes 310280 | tf_op jit(solution)/shard_map/ppermute | solution.py:19
  41.9 8.5 %collective-permute-start.11 = (bf16[1,8,2,2,16,101]{5,4,3,2,1,0:T(8,128)(2,1)S(1)}, bf16[1,8,2,2,16,101]{5,4,3,2,1,0:T(8,128)(2,1)S(1)}, u32[]{:S(2)}, u32[]{:S(2)}) collective-permute-start(bf16[1,8,2,2,16,101]{5,4,3,2,1,0:T(8,128)(2,1)S(1)} %get-tuple-element.9), channel_id=1, source_target_pairs={{0,5},{1,4},{2,7},{3,6},{4,9},{5,8},{6,11},{7,10},{8,13},{9,12},{1... | collective-permute-start | bytes 310280 | tf_op jit(solution)/shard_map/ppermute | solution.py:151
  44.8 7.1 %collective-permute-start.16 = (bf16[1,8,2,2,16,101]{5,4,3,2,1,0:T(8,128)(2,1)S(1)}, bf16[1,8,2,2,16,101]{5,4,3,2,1,0:T(8,128)(2,1)S(1)}, u32[]{:S(2)}, u32[]{:S(2)}) collective-permute-start(bf16[1,8,2,2,16,101]{5,4,3,2,1,0:T(8,128)(2,1)S(1)} %get-tuple-element.9), channel_id=1, source_target_pairs={{0,9},{1,8},{2,11},{3,10},{4,13},{5,12},{6,15},{7,14},{8,17},{9,16... | collective-permute-start | bytes 310280 | tf_op jit(solution)/shard_map/ppermute | solution.py:151
  44.8 12.7 %collective-permute-start.12 = (bf16[2,8,2,2,64,101]{5,4,3,2,1,0:T(8,128)(2,1)}, bf16[2,8,2,2,64,101]{5,4,3,2,1,0:T(8,128)(2,1)}, u32[]{:S(2)}, u32[]{:S(2)}) collective-permute-start(bf16[2,8,2,2,64,101]{5,4,3,2,1,0:T(8,128)(2,1)} %pad_maximum_fusion), channel_id=1, source_target_pairs={{0,1},{1,0},{2,3},{3,2},{4,5},{5,4},{6,7},{7,6},{8,9},{9,8},{10,11... | collective-permute-start | bytes 2482184 | tf_op jit(solution)/shard_map/ppermute | solution.py:162
  64.5 1.1 %copy-start = (bf16[101,32,128]{2,1,0:T(8,128)(2,1)S(1)}, bf16[101,32,128]{2,1,0:T(8,128)(2,1)}, u32[]{:S(2)}) copy-start(bf16[101,32,128]{2,1,0:T(8,128)(2,1)} %copy.18) | copy-start | bytes 2482180

commit v14 on v13

--- a/solution.py
+++ b/solution.py
@@ -128,7 +128,10 @@
     for distance in range(chan_count):
         target = jnp.mod(chan_position + distance, chan_count)
         piece = lax.dynamic_index_in_dim(sorted_spec, target, 0, keepdims=False)
-        pieces.append(piece if distance == 0 else shifted(piece, "chan", distance))
+        if distance == 0:
+            pieces.append(piece)
+        else:
+            pieces.append(shifted(piece, "chan", distance))
     own = jnp.stack(pieces)
     offsets = [max(1, round_index * chan_count // 4) for round_index in range(ROUNDS)]
 
@@ -185,7 +188,7 @@
         sums = jnp.einsum("fnk,fkj->fnj", both, own_spec, preferred_element_type=jnp.float32)
         sums = sums.reshape(FB, 2, slice_width, block_width)
         results.append(
-            jnp.einsum("fcij,cfl->jil", sums, inverse, precision=lax.Precision.DEFAULT)
+            jnp.einsum("fcij,cfl->jil", sums, inverse, precision=lax.Precision.HIGH)
         )
     return jnp.stack(results)
 

time: 69.8 us -> 71.8 us (1.029)
  matrix products: 6.76 us -> 8.8 us
    dot_general x2, matrix products: 1.03 us -> 4.19 us  [on_device_local(): jnp.einsum('fcij,cfl->jil', sums, inverse, precision=lax.Precision.HIGH)]
    dot_general x1, matrix products: 1.93 us -> 0.79 us  [whiten_planes(): jnp.einsum('wlk,lg->wkg', normed, table[:, :FB], precision=precision)]
where the time goes in v14:
time: 71.8 us; the launch traced here: 71.5 us
  starting transfers between devices  28.5 us (40%)
  waiting for transfers between devices  14.6 us (20%)
  local copies, waits for them, and re-layouts  12.1 us (17%)
  matrix products  8.8 us (12%)
  other arithmetic  7.12 us (10%)
    ppermute x11, starting transfers between devices, shifted(): return lax.ppermute(block, axis, route)  24.3 us
    ppermute x11, waiting for transfers between devices, shifted(): return lax.ppermute(block, axis, route)  7.95 us
    ppermute x4, waiting for transfers between devices, send_from_neighbour(): sent.append(lax.ppermute(piece, ('chan', 'tm'), route))  5.83 us
    dot_general x2, matrix products, on_device_local(): jnp.einsum('fcij,cfl->jil', sums, inverse, precision=lax.Precision.HIGH)  4.19 us
    reshape x1, local copies, waits for them, and re-layouts, on_device_local(): jnp.transpose(gathered, (5, 3, 0, 1, 2, 4))  3.79 us
    reshape x2, local copies, waits for them, and re-layouts, on_device_local(): jnp.transpose(both, (6, 0, 5, 4, 1, 2, 3))  3.67 us
    dot_general x2, matrix products, on_device_local(): jnp.einsum('fnk,fkj->fnj', both, own_spec, preferred_element_type=jnp.flo...  1.95 us
    transpose x1, other arithmetic, on_device_local(): jnp.transpose(gathered, (5, 3, 0, 1, 2, 4))  1.71 us
  transfers between devices with their start and end apart: 17, of which 10 were waited for; matrix products, arithmetic and copies ran while one was open for 10% of the time, Pallas kernels for 0%

profile of v14, /device:TPU:0, one launch (start us, length us, event | category | flops | bytes accessed | tf_op | source)
XLA Modules:
  0.0 71.5 jit_solution(16327788903902587892)
XLA Ops:
  5.8 3.0 %collective-permute-start = (bf16[2,2,64,101]{3,2,1,0:T(8,128)(2,1)S(1)}, bf16[2,2,64,101]{3,2,1,0:T(8,128)(2,1)S(1)}, u32[]{:S(2)}, u32[]{:S(2)}) collective-permute-start(bf16[2,2,64,101]{3,2,1,0:T(8,128)(2,1)S(1)} %get-tuple-element.19), channel_id=1, source_target_pairs={{28,0},{0,4},{4,8},{8,12},{12,16},{16,20},{20,24},{24,28},{29,1},{... | collective-permute-start | bytes 155144 | tf_op jit(solution)/shard_map/ppermute | solution.py:19
  8.9 1.6 %collective-permute-start.1 = (bf16[2,2,64,101]{3,2,1,0:T(8,128)(2,1)S(1)}, bf16[2,2,64,101]{3,2,1,0:T(8,128)(2,1)S(1)}, u32[]{:S(2)}, u32[]{:S(2)}) collective-permute-start(bf16[2,2,64,101]{3,2,1,0:T(8,128)(2,1)S(1)} %get-tuple-element.18), channel_id=1, source_target_pairs={{24,0},{28,4},{0,8},{4,12},{8,16},{12,20},{16,24},{20,28},{25,1},{... | collective-permute-start | bytes 155144 | tf_op jit(solution)/shard_map/ppermute | solution.py:19
  10.5 2.5 %collective-permute-start.2 = (bf16[2,2,64,101]{3,2,1,0:T(8,128)(2,1)S(1)}, bf16[2,2,64,101]{3,2,1,0:T(8,128)(2,1)S(1)}, u32[]{:S(2)}, u32[]{:S(2)}) collective-permute-start(bf16[2,2,64,101]{3,2,1,0:T(8,128)(2,1)S(1)} %get-tuple-element.17), channel_id=1, source_target_pairs={{20,0},{24,4},{28,8},{0,12},{4,16},{8,20},{12,24},{16,28},{21,1},{... | collective-permute-start | bytes 155144 | tf_op jit(solution)/shard_map/ppermute | solution.py:19
  14.2 2.6 %collective-permute-start.4 = (bf16[2,2,64,101]{3,2,1,0:T(8,128)(2,1)S(1)}, bf16[2,2,64,101]{3,2,1,0:T(8,128)(2,1)S(1)}, u32[]{:S(2)}, u32[]{:S(2)}) collective-permute-start(bf16[2,2,64,101]{3,2,1,0:T(8,128)(2,1)S(1)} %get-tuple-element.15), channel_id=1, source_target_pairs={{12,0},{16,4},{20,8},{24,12},{28,16},{0,20},{4,24},{8,28},{13,1},{... | collective-permute-start | bytes 155144 | tf_op jit(solution)/shard_map/ppermute | solution.py:19
  16.9 1.4 %collective-permute-start.5 = (bf16[2,2,64,101]{3,2,1,0:T(8,128)(2,1)S(1)}, bf16[2,2,64,101]{3,2,1,0:T(8,128)(2,1)S(1)}, u32[]{:S(2)}, u32[]{:S(2)}) collective-permute-start(bf16[2,2,64,101]{3,2,1,0:T(8,128)(2,1)S(1)} %get-tuple-element.14), channel_id=1, source_target_pairs={{8,0},{12,4},{16,8},{20,12},{24,16},{28,20},{0,24},{4,28},{9,1},{1... | collective-permute-start | bytes 155144 | tf_op jit(solution)/shard_map/ppermute | solution.py:19
  18.4 1.5 %collective-permute-start.6 = (bf16[2,2,64,101]{3,2,1,0:T(8,128)(2,1)S(1)}, bf16[2,2,64,101]{3,2,1,0:T(8,128)(2,1)S(1)}, u32[]{:S(2)}, u32[]{:S(2)}) collective-permute-start(bf16[2,2,64,101]{3,2,1,0:T(8,128)(2,1)S(1)} %get-tuple-element.13), channel_id=1, source_target_pairs={{4,0},{8,4},{12,8},{16,12},{20,16},{24,20},{28,24},{0,28},{5,1},{9... | collective-permute-start | bytes 155144 | tf_op jit(solution)/shard_map/ppermute | solution.py:19
  22.9 1.6 %collective-permute-start.8 = (bf16[1,8,2,2,64,101]{5,4,3,2,1,0:T(8,128)(2,1)S(1)}, bf16[1,8,2,2,64,101]{5,4,3,2,1,0:T(8,128)(2,1)S(1)}, u32[]{:S(2)}, u32[]{:S(2)}) collective-permute-start(bf16[1,8,2,2,64,101]{5,4,3,2,1,0:T(8,128)(2,1)S(1)} %bitcast.109), channel_id=1, source_target_pairs={{0,2},{1,3},{2,0},{3,1},{4,6},{5,7},{6,4},{7,5},{8,10},{9,11},{10,... | collective-permute-start | bytes 1241096 | tf_op jit(solution)/shard_map/ppermute | solution.py:161
  24.5 2.2 %collective-permute-start.7 = (bf16[1,8,2,2,16,101]{5,4,3,2,1,0:T(8,128)(2,1)S(1)}, bf16[1,8,2,2,16,101]{5,4,3,2,1,0:T(8,128)(2,1)S(1)}, u32[]{:S(2)}, u32[]{:S(2)}) collective-permute-start(bf16[1,8,2,2,16,101]{5,4,3,2,1,0:T(8,128)(2,1)S(1)} %get-tuple-element.12), channel_id=1, source_target_pairs={{28,0},{0,4},{4,8},{8,12},{12,16},{16,20},{20,24},{24,28},{29,1},{... | collective-permute-start | bytes 310280 | tf_op jit(solution)/shard_map/ppermute | solution.py:19
  26.9 2.0 %collective-permute-start.13 = (bf16[1,8,2,2,16,101]{5,4,3,2,1,0:T(8,128)(2,1)S(1)}, bf16[1,8,2,2,16,101]{5,4,3,2,1,0:T(8,128)(2,1)S(1)}, u32[]{:S(2)}, u32[]{:S(2)}) collective-permute-start(bf16[1,8,2,2,16,101]{5,4,3,2,1,0:T(8,128)(2,1)S(1)} %get-tuple-element.12), channel_id=1, source_target_pairs={{24,0},{28,4},{0,8},{4,12},{8,16},{12,20},{16,24},{20,28},{25,1},{... | collective-permute-start | bytes 310280 | tf_op jit(solution)/shard_map/ppermute | solution.py:19
  28.9 1.4 %collective-permute-start.15 = (bf16[1,8,2,2,16,101]{5,4,3,2,1,0:T(8,128)(2,1)S(1)}, bf16[1,8,2,2,16,101]{5,4,3,2,1,0:T(8,128)(2,1)S(1)}, u32[]{:S(2)}, u32[]{:S(2)}) collective-permute-start(bf16[1,8,2,2,16,101]{5,4,3,2,1,0:T(8,128)(2,1)S(1)} %get-tuple-element.11), channel_id=1, source_target_pairs={{0,9},{1,8},{2,11},{3,10},{4,13},{5,12},{6,15},{7,14},{8,17},{9,16... | collective-permute-start | bytes 310280 | tf_op jit(solution)/shard_map/ppermute | solution.py:154
  30.4 3.1 %collective-permute-done.7 = bf16[1,8,2,2,16,101]{5,4,3,2,1,0:T(8,128)(2,1)S(1)} collective-permute-done((bf16[1,8,2,2,16,101]{5,4,3,2,1,0:T(8,128)(2,1)S(1)}, bf16[1,8,2,2,16,101]{5,4,3,2,1,0:T(8,128)(2,1)S(1)}, u32[]{:S(2)}, u32[]{:S(2)}) %collective-permute-start.7) | collective-permute-done | bytes 103456 | tf_op jit(solution)/shard_map/ppermute | solution.py:19
  34.5 3.5 %collective-permute-start.9 = (bf16[1,8,2,2,16,101]{5,4,3,2,1,0:T(8,128)(2,1)S(1)}, bf16[1,8,2,2,16,101]{5,4,3,2,1,0:T(8,128)(2,1)S(1)}, u32[]{:S(2)}, u32[]{:S(2)}) collective-permute-start(bf16[1,8,2,2,16,101]{5,4,3,2,1,0:T(8,128)(2,1)S(1)} %get-tuple-element.10), channel_id=1, source_target_pairs={{28,0},{0,4},{4,8},{8,12},{12,16},{16,20},{20,24},{24,28},{29,1},{... | collective-permute-start | bytes 310280 | tf_op jit(solution)/shard_map/ppermute | solution.py:19
  38.0 2.8 %collective-permute-start.14 = (bf16[1,8,2,2,16,101]{5,4,3,2,1,0:T(8,128)(2,1)S(1)}, bf16[1,8,2,2,16,101]{5,4,3,2,1,0:T(8,128)(2,1)S(1)}, u32[]{:S(2)}, u32[]{:S(2)}) collective-permute-start(bf16[1,8,2,2,16,101]{5,4,3,2,1,0:T(8,128)(2,1)S(1)} %get-tuple-element.10), channel_id=1, source_target_pairs={{24,0},{28,4},{0,8},{4,12},{8,16},{12,20},{16,24},{20,28},{25,1},{... | collective-permute-start | bytes 310280 | tf_op jit(solution)/shard_map/ppermute | solution.py:19
  42.0 1.7 %collective-permute-done.9 = bf16[1,8,2,2,16,101]{5,4,3,2,1,0:T(8,128)(2,1)S(1)} collective-permute-done((bf16[1,8,2,2,16,101]{5,4,3,2,1,0:T(8,128)(2,1)S(1)}, bf16[1,8,2,2,16,101]{5,4,3,2,1,0:T(8,128)(2,1)S(1)}, u32[]{:S(2)}, u32[]{:S(2)}) %collective-permute-start.9) | collective-permute-done | bytes 103456 | tf_op jit(solution)/shard_map/ppermute | solution.py:19
  44.9 4.4 %collective-permute-done.11 = bf16[1,8,2,2,16,101]{5,4,3,2,1,0:T(8,128)(2,1)S(1)} collective-permute-done((bf16[1,8,2,2,16,101]{5,4,3,2,1,0:T(8,128)(2,1)S(1)}, bf16[1,8,2,2,16,101]{5,4,3,2,1,0:T(8,128)(2,1)S(1)}, u32[]{:S(2)}, u32[]{:S(2)}) %collective-permute-start.11) | collective-permute-done | bytes 103456 | tf_op jit(solution)/shard_map/ppermute | solution.py:154
  49.4 1.4 %collective-permute-done.16 = bf16[1,8,2,2,16,101]{5,4,3,2,1,0:T(8,128)(2,1)S(1)} collective-permute-done((bf16[1,8,2,2,16,101]{5,4,3,2,1,0:T(8,128)(2,1)S(1)}, bf16[1,8,2,2,16,101]{5,4,3,2,1,0:T(8,128)(2,1)S(1)}, u32[]{:S(2)}, u32[]{:S(2)}) %collective-permute-start.16) | collective-permute-done | bytes 103456 | tf_op jit(solution)/shard_map/ppermute | solution.py:154
  51.8 1.5 %copy.14 = bf16[101,32,128]{2,1,0:T(8,128)(2,1)S(1)} copy(bf16[101,32,128]{0,1,2:T(8,128)(2,1)S(1)} %bitcast.107) | data formatting | bytes 1654784 | tf_op jit(solution)/shard_map/reshape | solution.py:187
  54.2 2.2 %copy.18 = bf16[101,32,128]{2,1,0:T(8,128)(2,1)} copy(bf16[101,32,128]{0,1,2:T(8,128)(2,1)S(1)} %bitcast.108) | data formatting | bytes 1654784 | tf_op jit(solution)/shard_map/reshape | solution.py:187
  56.4 1.7 %maximum_bitcast_fusion = bf16[101,2,4,8,2,64]{0,5,1,4,3,2:T(8,128)(2,1)S(1)} fusion(bf16[2,8,2,2,64,101]{5,4,3,2,1,0:T(8,128)(2,1)} %collective-permute-done.12, bf16[1,8,2,2,64,101]{5,4,3,2,1,0:T(8,128)(2,1)S(1)} %collective-permute-done.8, bf16[1,8,2,2,64,101]{5,4,3,2,1,0:T(8,128)(2,1)S(1)} %bitcast.111), kind=kLoop, calls=%fused_computation | loop fusion | flops 1654784 | bytes 3309568 | tf_op jit(solution)/shard_map/transpose | solution.py:178
  58.1 1.5 %copy.13 = bf16[101,2,4,8,2,64]{0,5,4,3,2,1:T(8,128)(2,1)} copy(bf16[101,2,4,8,2,64]{0,5,1,4,3,2:T(8,128)(2,1)S(1)} %maximum_bitcast_fusion) | data formatting | bytes 3309568 | tf_op jit(solution)/shard_map/transpose | solution.py:178
  59.6 3.8 %copy.15 = bf16[101,128,64]{1,2,0:T(8,128)(2,1)S(1)} copy(bf16[101,128,64]{0,2,1:T(8,128)(2,1)} %bitcast.104) | data formatting | bytes 3309568 | tf_op jit(solution)/shard_map/reshape | solution.py:178
  65.6 2.1 %fusion.4 = f32[1,64,16,128]{3,1,2,0:T(8,128)S(1)} fusion(f32[101,2,16,64]{3,2,1,0:T(8,128)S(1)} %bitcast.106, f32[1,101,128]{2,1,0:T(8,128)S(1)} %get-tuple-element.23, f32[1,101,128]{2,1,0:T(8,128)S(1)} %get-tuple-element.22), kind=kOutput, calls=%fused_computation.6 | convolution fusion | flops 158885120 | bytes 1455104 | tf_op jit(solution)/shard_map/fcij,cfl->jil/dot_general | solution.py:191
  67.7 2.1 %fusion.7 = f32[1,64,16,128]{3,1,2,0:T(8,128)S(1)} fusion(f32[101,2,16,64]{3,2,1,0:T(8,128)S(1)} %bitcast.105, f32[1,101,128]{2,1,0:T(8,128)S(1)} %get-tuple-element.23, f32[1,101,128]{2,1,0:T(8,128)S(1)} %get-tuple-element.22), kind=kOutput, calls=%fused_computation.7 | convolution fusion | flops 158885120 | bytes 1455104 | tf_op jit(solution)/shard_map/fcij,cfl->jil/dot_general | solution.py:191
  69.9 1.6 %copy.21 = f32[2,64,16,128]{3,2,1,0:T(8,128)} copy(f32[2,64,16,128]{3,1,2,0:T(8,128)S(1)} %pad_maximum_fusion.1) | data formatting | bytes 2097152 | tf_op jit(solution)/shard_map/stack | solution.py:193
  (76 shorter events, 17.9 us)
Async XLA Ops:
  0.0 2.7 %copy-start.1 = (f32[1,400,512]{2,1,0:T(8,128)S(1)}, f32[1,400,512]{2,1,0:T(8,128)}, u32[]{:S(2)}) copy-start(f32[1,400,512]{2,1,0:T(8,128)} %param.3) | copy-start | bytes 2457604
  3.5 0.9 %copy-start.2 = (s32[512]{0:T(512)S(1)}, s32[512]{0:T(512)}, u32[]{:S(2)}) copy-start(s32[512]{0:T(512)} %param.5) | copy-start | bytes 6148
  3.5 1.4 %copy-start.3 = (s32[512]{0:T(512)S(1)}, s32[512]{0:T(512)}, u32[]{:S(2)}) copy-start(s32[512]{0:T(512)} %param.4) | copy-start | bytes 6148
  5.8 11.1 %collective-permute-start = (bf16[2,2,64,101]{3,2,1,0:T(8,128)(2,1)S(1)}, bf16[2,2,64,101]{3,2,1,0:T(8,128)(2,1)S(1)}, u32[]{:S(2)}, u32[]{:S(2)}) collective-permute-start(bf16[2,2,64,101]{3,2,1,0:T(8,128)(2,1)S(1)} %get-tuple-element.19), channel_id=1, source_target_pairs={{28,0},{0,4},{4,8},{8,12},{12,16},{16,20},{20,24},{24,28},{29,1},{... | collective-permute-start | bytes 155144 | tf_op jit(solution)/shard_map/ppermute | solution.py:19
  8.9 9.5 %collective-permute-start.1 = (bf16[2,2,64,101]{3,2,1,0:T(8,128)(2,1)S(1)}, bf16[2,2,64,101]{3,2,1,0:T(8,128)(2,1)S(1)}, u32[]{:S(2)}, u32[]{:S(2)}) collective-permute-start(bf16[2,2,64,101]{3,2,1,0:T(8,128)(2,1)S(1)} %get-tuple-element.18), channel_id=1, source_target_pairs={{24,0},{28,4},{0,8},{4,12},{8,16},{12,20},{16,24},{20,28},{25,1},{... | collective-permute-start | bytes 155144 | tf_op jit(solution)/shard_map/ppermute | solution.py:19
  10.5 9.7 %collective-permute-start.2 = (bf16[2,2,64,101]{3,2,1,0:T(8,128)(2,1)S(1)}, bf16[2,2,64,101]{3,2,1,0:T(8,128)(2,1)S(1)}, u32[]{:S(2)}, u32[]{:S(2)}) collective-permute-start(bf16[2,2,64,101]{3,2,1,0:T(8,128)(2,1)S(1)} %get-tuple-element.17), channel_id=1, source_target_pairs={{20,0},{24,4},{28,8},{0,12},{4,16},{8,20},{12,24},{16,28},{21,1},{... | collective-permute-start | bytes 155144 | tf_op jit(solution)/shard_map/ppermute | solution.py:19
  13.0 7.8 %collective-permute-start.3 = (bf16[2,2,64,101]{3,2,1,0:T(8,128)(2,1)S(1)}, bf16[2,2,64,101]{3,2,1,0:T(8,128)(2,1)S(1)}, u32[]{:S(2)}, u32[]{:S(2)}) collective-permute-start(bf16[2,2,64,101]{3,2,1,0:T(8,128)(2,1)S(1)} %get-tuple-element.16), channel_id=1, source_target_pairs={{16,0},{20,4},{24,8},{28,12},{0,16},{4,20},{8,24},{12,28},{17,1},{... | collective-permute-start | bytes 155144 | tf_op jit(solution)/shard_map/ppermute | solution.py:19
  14.2 7.4 %collective-permute-start.4 = (bf16[2,2,64,101]{3,2,1,0:T(8,128)(2,1)S(1)}, bf16[2,2,64,101]{3,2,1,0:T(8,128)(2,1)S(1)}, u32[]{:S(2)}, u32[]{:S(2)}) collective-permute-start(bf16[2,2,64,101]{3,2,1,0:T(8,128)(2,1)S(1)} %get-tuple-element.15), channel_id=1, source_target_pairs={{12,0},{16,4},{20,8},{24,12},{28,16},{0,20},{4,24},{8,28},{13,1},{... | collective-permute-start | bytes 155144 | tf_op jit(solution)/shard_map/ppermute | solution.py:19
  16.9 5.9 %collective-permute-start.5 = (bf16[2,2,64,101]{3,2,1,0:T(8,128)(2,1)S(1)}, bf16[2,2,64,101]{3,2,1,0:T(8,128)(2,1)S(1)}, u32[]{:S(2)}, u32[]{:S(2)}) collective-permute-start(bf16[2,2,64,101]{3,2,1,0:T(8,128)(2,1)S(1)} %get-tuple-element.14), channel_id=1, source_target_pairs={{8,0},{12,4},{16,8},{20,12},{24,16},{28,20},{0,24},{4,28},{9,1},{1... | collective-permute-start | bytes 155144 | tf_op jit(solution)/shard_map/ppermute | solution.py:19
  18.4 4.5 %collective-permute-start.6 = (bf16[2,2,64,101]{3,2,1,0:T(8,128)(2,1)S(1)}, bf16[2,2,64,101]{3,2,1,0:T(8,128)(2,1)S(1)}, u32[]{:S(2)}, u32[]{:S(2)}) collective-permute-start(bf16[2,2,64,101]{3,2,1,0:T(8,128)(2,1)S(1)} %get-tuple-element.13), channel_id=1, source_target_pairs={{4,0},{8,4},{12,8},{16,12},{20,16},{24,20},{28,24},{0,28},{5,1},{9... | collective-permute-start | bytes 155144 | tf_op jit(solution)/shard_map/ppermute | solution.py:19
  22.9 11.6 %collective-permute-start.8 = (bf16[1,8,2,2,64,101]{5,4,3,2,1,0:T(8,128)(2,1)S(1)}, bf16[1,8,2,2,64,101]{5,4,3,2,1,0:T(8,128)(2,1)S(1)}, u32[]{:S(2)}, u32[]{:S(2)}) collective-permute-start(bf16[1,8,2,2,64,101]{5,4,3,2,1,0:T(8,128)(2,1)S(1)} %bitcast.109), channel_id=1, source_target_pairs={{0,2},{1,3},{2,0},{3,1},{4,6},{5,7},{6,4},{7,5},{8,10},{9,11},{10,... | collective-permute-start | bytes 1241096 | tf_op jit(solution)/shard_map/ppermute | solution.py:161
  24.5 9.0 %collective-permute-start.7 = (bf16[1,8,2,2,16,101]{5,4,3,2,1,0:T(8,128)(2,1)S(1)}, bf16[1,8,2,2,16,101]{5,4,3,2,1,0:T(8,128)(2,1)S(1)}, u32[]{:S(2)}, u32[]{:S(2)}) collective-permute-start(bf16[1,8,2,2,16,101]{5,4,3,2,1,0:T(8,128)(2,1)S(1)} %get-tuple-element.12), channel_id=1, source_target_pairs={{28,0},{0,4},{4,8},{8,12},{12,16},{16,20},{20,24},{24,28},{29,1},{... | collective-permute-start | bytes 310280 | tf_op jit(solution)/shard_map/ppermute | solution.py:19
  26.9 6.8 %collective-permute-start.13 = (bf16[1,8,2,2,16,101]{5,4,3,2,1,0:T(8,128)(2,1)S(1)}, bf16[1,8,2,2,16,101]{5,4,3,2,1,0:T(8,128)(2,1)S(1)}, u32[]{:S(2)}, u32[]{:S(2)}) collective-permute-start(bf16[1,8,2,2,16,101]{5,4,3,2,1,0:T(8,128)(2,1)S(1)} %get-tuple-element.12), channel_id=1, source_target_pairs={{24,0},{28,4},{0,8},{4,12},{8,16},{12,20},{16,24},{20,28},{25,1},{... | collective-permute-start | bytes 310280 | tf_op jit(solution)/shard_map/ppermute | solution.py:19
  28.9 14.8 %collective-permute-start.10 = (bf16[1,8,2,2,16,101]{5,4,3,2,1,0:T(8,128)(2,1)S(1)}, bf16[1,8,2,2,16,101]{5,4,3,2,1,0:T(8,128)(2,1)S(1)}, u32[]{:S(2)}, u32[]{:S(2)}) collective-permute-start(bf16[1,8,2,2,16,101]{5,4,3,2,1,0:T(8,128)(2,1)S(1)} %get-tuple-element.11), channel_id=1, source_target_pairs={{0,5},{1,4},{2,7},{3,6},{4,9},{5,8},{6,11},{7,10},{8,13},{9,12},{1... | collective-permute-start | bytes 310280 | tf_op jit(solution)/shard_map/ppermute | solution.py:154
  28.9 20.4 %collective-permute-start.15 = (bf16[1,8,2,2,16,101]{5,4,3,2,1,0:T(8,128)(2,1)S(1)}, bf16[1,8,2,2,16,101]{5,4,3,2,1,0:T(8,128)(2,1)S(1)}, u32[]{:S(2)}, u32[]{:S(2)}) collective-permute-start(bf16[1,8,2,2,16,101]{5,4,3,2,1,0:T(8,128)(2,1)S(1)} %get-tuple-element.11), channel_id=1, source_target_pairs={{0,9},{1,8},{2,11},{3,10},{4,13},{5,12},{6,15},{7,14},{8,17},{9,16... | collective-permute-start | bytes 310280 | tf_op jit(solution)/shard_map/ppermute | solution.py:154
  34.5 9.1 %collective-permute-start.9 = (bf16[1,8,2,2,16,101]{5,4,3,2,1,0:T(8,128)(2,1)S(1)}, bf16[1,8,2,2,16,101]{5,4,3,2,1,0:T(8,128)(2,1)S(1)}, u32[]{:S(2)}, u32[]{:S(2)}) collective-permute-start(bf16[1,8,2,2,16,101]{5,4,3,2,1,0:T(8,128)(2,1)S(1)} %get-tuple-element.10), channel_id=1, source_target_pairs={{28,0},{0,4},{4,8},{8,12},{12,16},{16,20},{20,24},{24,28},{29,1},{... | collective-permute-start | bytes 310280 | tf_op jit(solution)/shard_map/ppermute | solution.py:19
  38.0 11.3 %collective-permute-start.14 = (bf16[1,8,2,2,16,101]{5,4,3,2,1,0:T(8,128)(2,1)S(1)}, bf16[1,8,2,2,16,101]{5,4,3,2,1,0:T(8,128)(2,1)S(1)}, u32[]{:S(2)}, u32[]{:S(2)}) collective-permute-start(bf16[1,8,2,2,16,101]{5,4,3,2,1,0:T(8,128)(2,1)S(1)} %get-tuple-element.10), channel_id=1, source_target_pairs={{24,0},{28,4},{0,8},{4,12},{8,16},{12,20},{16,24},{20,28},{25,1},{... | collective-permute-start | bytes 310280 | tf_op jit(solution)/shard_map/ppermute | solution.py:19
  40.8 8.5 %collective-permute-start.11 = (bf16[1,8,2,2,16,101]{5,4,3,2,1,0:T(8,128)(2,1)S(1)}, bf16[1,8,2,2,16,101]{5,4,3,2,1,0:T(8,128)(2,1)S(1)}, u32[]{:S(2)}, u32[]{:S(2)}) collective-permute-start(bf16[1,8,2,2,16,101]{5,4,3,2,1,0:T(8,128)(2,1)S(1)} %get-tuple-element.9), channel_id=1, source_target_pairs={{0,5},{1,4},{2,7},{3,6},{4,9},{5,8},{6,11},{7,10},{8,13},{9,12},{1... | collective-permute-start | bytes 310280 | tf_op jit(solution)/shard_map/ppermute | solution.py:154
  43.6 7.1 %collective-permute-start.16 = (bf16[1,8,2,2,16,101]{5,4,3,2,1,0:T(8,128)(2,1)S(1)}, bf16[1,8,2,2,16,101]{5,4,3,2,1,0:T(8,128)(2,1)S(1)}, u32[]{:S(2)}, u32[]{:S(2)}) collective-permute-start(bf16[1,8,2,2,16,101]{5,4,3,2,1,0:T(8,128)(2,1)S(1)} %get-tuple-element.9), channel_id=1, source_target_pairs={{0,9},{1,8},{2,11},{3,10},{4,13},{5,12},{6,15},{7,14},{8,17},{9,16... | collective-permute-start | bytes 310280 | tf_op jit(solution)/shard_map/ppermute | solution.py:154
  43.7 12.7 %collective-permute-start.12 = (bf16[2,8,2,2,64,101]{5,4,3,2,1,0:T(8,128)(2,1)}, bf16[2,8,2,2,64,101]{5,4,3,2,1,0:T(8,128)(2,1)}, u32[]{:S(2)}, u32[]{:S(2)}) collective-permute-start(bf16[2,8,2,2,64,101]{5,4,3,2,1,0:T(8,128)(2,1)} %pad_maximum_fusion), channel_id=1, source_target_pairs={{0,1},{1,0},{2,3},{3,2},{4,5},{5,4},{6,7},{7,6},{8,9},{9,8},{10,11... | collective-permute-start | bytes 2482184 | tf_op jit(solution)/shard_map/ppermute | solution.py:165
  63.4 1.1 %copy-start = (bf16[101,32,128]{2,1,0:T(8,128)(2,1)S(1)}, bf16[101,32,128]{2,1,0:T(8,128)(2,1)}, u32[]{:S(2)}) copy-start(bf16[101,32,128]{2,1,0:T(8,128)(2,1)} %copy.18) | copy-start | bytes 2482180

commit v15 on v13

--- a/solution.py
+++ b/solution.py
@@ -183,11 +183,9 @@
         both = jnp.stack([partner, rotated])
         both = jnp.transpose(both, (6, 0, 5, 4, 1, 2, 3)).reshape(FB, 2 * slice_width, 2 * windows_all)
         sums = jnp.einsum("fnk,fkj->fnj", both, own_spec, preferred_element_type=jnp.float32)
-        sums = sums.reshape(FB, 2, slice_width, block_width)
-        results.append(
-            jnp.einsum("fcij,cfl->jil", sums, inverse, precision=lax.Precision.DEFAULT)
-        )
-    return jnp.stack(results)
+        results.append(sums.reshape(FB, 2, slice_width, block_width))
+    sums = jnp.stack(results, axis=2)
+    return jnp.einsum("fcrij,cfl->rjil", sums, inverse, precision=lax.Precision.HIGH)
 
 
 def on_device(records, chan_order, live_mask):

time: 69.8 us -> 77.9 us (1.12)
  local copies, waits for them, and re-layouts: 12.1 us -> 16.7 us
  matrix products: 6.76 us -> 10.3 us
    another operation x1 -> x2, local copies, waits for them, and re-layouts: 1.59 us -> 4.12 us  [on_device_local(): sums = jnp.stack(results, axis=2)]
    dot_general x2, matrix products: 1.93 us -> 4.23 us  [on_device_local(): jnp.einsum('fnk,fkj->fnj', both, own_spec, preferred_element_type=jnp.flo...]
    transpose x0 -> x1, local copies, waits for them, and re-layouts: none -> 1.58 us  [on_device_local(): jnp.einsum('fcrij,cfl->rjil', sums, inverse, precision=lax.Precision.HIGH)]
    dot_general x2 -> x1, matrix products: 1.03 us -> 2.26 us  [on_device_local(): jnp.einsum('fcrij,cfl->rjil', sums, inverse, precision=lax.Precision.HIGH)]
where the time goes in v15:
time: 77.9 us; the launch traced here: 77.5 us
  starting transfers between devices  28.5 us (37%)
  local copies, waits for them, and re-layouts  16.7 us (21%)
  waiting for transfers between devices  14.5 us (19%)
  matrix products  10.3 us (13%)
  other arithmetic  7 us (9%)
    ppermute x11, starting transfers between devices, shifted(): return lax.ppermute(block, axis, route)  24.4 us
    ppermute x11, waiting for transfers between devices, shifted(): return lax.ppermute(block, axis, route)  7.97 us
    ppermute x4, waiting for transfers between devices, send_from_neighbour(): sent.append(lax.ppermute(piece, ('chan', 'tm'), route))  5.78 us
    reshape x2, local copies, waits for them, and re-layouts, on_device_local(): jnp.transpose(both, (6, 0, 5, 4, 1, 2, 3))  4.39 us
    dot_general x2, matrix products, on_device_local(): jnp.einsum('fnk,fkj->fnj', both, own_spec, preferred_element_type=jnp.flo...  4.23 us
    another operation x2, local copies, waits for them, and re-layouts, on_device_local(): sums = jnp.stack(results, axis=2)  4.12 us
    reshape x1, local copies, waits for them, and re-layouts, on_device_local(): jnp.transpose(gathered, (5, 3, 0, 1, 2, 4))  3.79 us
    dot_general x1, matrix products, on_device_local(): jnp.einsum('fcrij,cfl->rjil', sums, inverse, precision=lax.Precision.HIGH)  2.26 us
  transfers between devices with their start and end apart: 17, of which 10 were waited for; matrix products, arithmetic and copies ran while one was open for 10% of the time, Pallas kernels for 0%

profile of v15, /device:TPU:0, one launch (start us, length us, event | category | flops | bytes accessed | tf_op | source)
XLA Modules:
  0.0 77.5 jit_solution(18127932149923678355)
XLA Ops:
  2.7 1.9 %fusion.18 = f32[2,512,101]{1,2,0:T(8,128)S(1)} fusion(f32[2,200,512]{2,1,0:T(8,128)} %bitcast.105, f32[2,512]{1,0:T(2,128)S(1)} %add_sqrt_fusion, f32[2,512]{1,0:T(2,128)S(1)} %broadcast_multiply_fusion.1), kind=kOutput, calls=%fused_computation.40 | convolution fusion | flops 124700200 | bytes 1241088 | tf_op jit(solution)/shard_map/wlk,lg->wkg/dot_general | solution.py:102
  7.0 3.1 %collective-permute-start = (bf16[2,2,64,101]{3,2,1,0:T(8,128)(2,1)S(1)}, bf16[2,2,64,101]{3,2,1,0:T(8,128)(2,1)S(1)}, u32[]{:S(2)}, u32[]{:S(2)}) collective-permute-start(bf16[2,2,64,101]{3,2,1,0:T(8,128)(2,1)S(1)} %get-tuple-element.19), channel_id=1, source_target_pairs={{28,0},{0,4},{4,8},{8,12},{12,16},{16,20},{20,24},{24,28},{29,1},{... | collective-permute-start | bytes 155144 | tf_op jit(solution)/shard_map/ppermute | solution.py:19
  10.0 1.6 %collective-permute-start.1 = (bf16[2,2,64,101]{3,2,1,0:T(8,128)(2,1)S(1)}, bf16[2,2,64,101]{3,2,1,0:T(8,128)(2,1)S(1)}, u32[]{:S(2)}, u32[]{:S(2)}) collective-permute-start(bf16[2,2,64,101]{3,2,1,0:T(8,128)(2,1)S(1)} %get-tuple-element.18), channel_id=1, source_target_pairs={{24,0},{28,4},{0,8},{4,12},{8,16},{12,20},{16,24},{20,28},{25,1},{... | collective-permute-start | bytes 155144 | tf_op jit(solution)/shard_map/ppermute | solution.py:19
  11.6 2.5 %collective-permute-start.2 = (bf16[2,2,64,101]{3,2,1,0:T(8,128)(2,1)S(1)}, bf16[2,2,64,101]{3,2,1,0:T(8,128)(2,1)S(1)}, u32[]{:S(2)}, u32[]{:S(2)}) collective-permute-start(bf16[2,2,64,101]{3,2,1,0:T(8,128)(2,1)S(1)} %get-tuple-element.17), channel_id=1, source_target_pairs={{20,0},{24,4},{28,8},{0,12},{4,16},{8,20},{12,24},{16,28},{21,1},{... | collective-permute-start | bytes 155144 | tf_op jit(solution)/shard_map/ppermute | solution.py:19
  15.4 2.7 %collective-permute-start.4 = (bf16[2,2,64,101]{3,2,1,0:T(8,128)(2,1)S(1)}, bf16[2,2,64,101]{3,2,1,0:T(8,128)(2,1)S(1)}, u32[]{:S(2)}, u32[]{:S(2)}) collective-permute-start(bf16[2,2,64,101]{3,2,1,0:T(8,128)(2,1)S(1)} %get-tuple-element.15), channel_id=1, source_target_pairs={{12,0},{16,4},{20,8},{24,12},{28,16},{0,20},{4,24},{8,28},{13,1},{... | collective-permute-start | bytes 155144 | tf_op jit(solution)/shard_map/ppermute | solution.py:19
  24.0 1.6 %collective-permute-start.8 = (bf16[1,8,2,2,64,101]{5,4,3,2,1,0:T(8,128)(2,1)S(1)}, bf16[1,8,2,2,64,101]{5,4,3,2,1,0:T(8,128)(2,1)S(1)}, u32[]{:S(2)}, u32[]{:S(2)}) collective-permute-start(bf16[1,8,2,2,64,101]{5,4,3,2,1,0:T(8,128)(2,1)S(1)} %bitcast.100), channel_id=1, source_target_pairs={{0,2},{1,3},{2,0},{3,1},{4,6},{5,7},{6,4},{7,5},{8,10},{9,11},{10,... | collective-permute-start | bytes 1241096 | tf_op jit(solution)/shard_map/ppermute | solution.py:158
  25.6 2.2 %collective-permute-start.7 = (bf16[1,8,2,2,16,101]{5,4,3,2,1,0:T(8,128)(2,1)S(1)}, bf16[1,8,2,2,16,101]{5,4,3,2,1,0:T(8,128)(2,1)S(1)}, u32[]{:S(2)}, u32[]{:S(2)}) collective-permute-start(bf16[1,8,2,2,16,101]{5,4,3,2,1,0:T(8,128)(2,1)S(1)} %get-tuple-element.12), channel_id=1, source_target_pairs={{28,0},{0,4},{4,8},{8,12},{12,16},{16,20},{20,24},{24,28},{29,1},{... | collective-permute-start | bytes 310280 | tf_op jit(solution)/shard_map/ppermute | solution.py:19
  28.0 2.0 %collective-permute-start.13 = (bf16[1,8,2,2,16,101]{5,4,3,2,1,0:T(8,128)(2,1)S(1)}, bf16[1,8,2,2,16,101]{5,4,3,2,1,0:T(8,128)(2,1)S(1)}, u32[]{:S(2)}, u32[]{:S(2)}) collective-permute-start(bf16[1,8,2,2,16,101]{5,4,3,2,1,0:T(8,128)(2,1)S(1)} %get-tuple-element.12), channel_id=1, source_target_pairs={{24,0},{28,4},{0,8},{4,12},{8,16},{12,20},{16,24},{20,28},{25,1},{... | collective-permute-start | bytes 310280 | tf_op jit(solution)/shard_map/ppermute | solution.py:19
  31.5 3.1 %collective-permute-done.7 = bf16[1,8,2,2,16,101]{5,4,3,2,1,0:T(8,128)(2,1)S(1)} collective-permute-done((bf16[1,8,2,2,16,101]{5,4,3,2,1,0:T(8,128)(2,1)S(1)}, bf16[1,8,2,2,16,101]{5,4,3,2,1,0:T(8,128)(2,1)S(1)}, u32[]{:S(2)}, u32[]{:S(2)}) %collective-permute-start.7) | collective-permute-done | bytes 103456 | tf_op jit(solution)/shard_map/ppermute | solution.py:19
  35.7 3.5 %collective-permute-start.9 = (bf16[1,8,2,2,16,101]{5,4,3,2,1,0:T(8,128)(2,1)S(1)}, bf16[1,8,2,2,16,101]{5,4,3,2,1,0:T(8,128)(2,1)S(1)}, u32[]{:S(2)}, u32[]{:S(2)}) collective-permute-start(bf16[1,8,2,2,16,101]{5,4,3,2,1,0:T(8,128)(2,1)S(1)} %get-tuple-element.10), channel_id=1, source_target_pairs={{28,0},{0,4},{4,8},{8,12},{12,16},{16,20},{20,24},{24,28},{29,1},{... | collective-permute-start | bytes 310280 | tf_op jit(solution)/shard_map/ppermute | solution.py:19
  39.1 2.8 %collective-permute-start.14 = (bf16[1,8,2,2,16,101]{5,4,3,2,1,0:T(8,128)(2,1)S(1)}, bf16[1,8,2,2,16,101]{5,4,3,2,1,0:T(8,128)(2,1)S(1)}, u32[]{:S(2)}, u32[]{:S(2)}) collective-permute-start(bf16[1,8,2,2,16,101]{5,4,3,2,1,0:T(8,128)(2,1)S(1)} %get-tuple-element.10), channel_id=1, source_target_pairs={{24,0},{28,4},{0,8},{4,12},{8,16},{12,20},{16,24},{20,28},{25,1},{... | collective-permute-start | bytes 310280 | tf_op jit(solution)/shard_map/ppermute | solution.py:19
  43.1 1.7 %collective-permute-done.9 = bf16[1,8,2,2,16,101]{5,4,3,2,1,0:T(8,128)(2,1)S(1)} collective-permute-done((bf16[1,8,2,2,16,101]{5,4,3,2,1,0:T(8,128)(2,1)S(1)}, bf16[1,8,2,2,16,101]{5,4,3,2,1,0:T(8,128)(2,1)S(1)}, u32[]{:S(2)}, u32[]{:S(2)}) %collective-permute-start.9) | collective-permute-done | bytes 103456 | tf_op jit(solution)/shard_map/ppermute | solution.py:19
  46.0 4.4 %collective-permute-done.11 = bf16[1,8,2,2,16,101]{5,4,3,2,1,0:T(8,128)(2,1)S(1)} collective-permute-done((bf16[1,8,2,2,16,101]{5,4,3,2,1,0:T(8,128)(2,1)S(1)}, bf16[1,8,2,2,16,101]{5,4,3,2,1,0:T(8,128)(2,1)S(1)}, u32[]{:S(2)}, u32[]{:S(2)}) %collective-permute-start.11) | collective-permute-done | bytes 103456 | tf_op jit(solution)/shard_map/ppermute | solution.py:151
  52.9 2.2 %copy.14 = bf16[101,32,128]{2,1,0:T(8,128)(2,1)} copy(bf16[101,32,128]{0,1,2:T(8,128)(2,1)S(1)} %bitcast.98) | data formatting | bytes 1654784 | tf_op jit(solution)/shard_map/reshape | solution.py:184
  56.0 2.2 %copy.17 = bf16[101,32,128]{2,1,0:T(8,128)(2,1)} copy(bf16[101,32,128]{0,1,2:T(8,128)(2,1)S(1)} %bitcast.99) | data formatting | bytes 1654784 | tf_op jit(solution)/shard_map/reshape | solution.py:184
  58.2 1.7 %maximum_bitcast_fusion = bf16[101,2,4,8,2,64]{0,5,1,4,3,2:T(8,128)(2,1)S(1)} fusion(bf16[2,8,2,2,64,101]{5,4,3,2,1,0:T(8,128)(2,1)} %collective-permute-done.12, bf16[1,8,2,2,64,101]{5,4,3,2,1,0:T(8,128)(2,1)S(1)} %collective-permute-done.8, bf16[1,8,2,2,64,101]{5,4,3,2,1,0:T(8,128)(2,1)S(1)} %bitcast.102), kind=kLoop, calls=%fused_computation | loop fusion | flops 1654784 | bytes 3309568 | tf_op jit(solution)/shard_map/transpose | solution.py:175
  59.9 1.5 %copy.13 = bf16[101,2,4,8,2,64]{0,5,4,3,2,1:T(8,128)(2,1)} copy(bf16[101,2,4,8,2,64]{0,5,1,4,3,2:T(8,128)(2,1)S(1)} %maximum_bitcast_fusion) | data formatting | bytes 3309568 | tf_op jit(solution)/shard_map/transpose | solution.py:175
  61.4 3.8 %copy.15 = bf16[101,128,64]{1,2,0:T(8,128)(2,1)S(1)} copy(bf16[101,128,64]{0,2,1:T(8,128)(2,1)} %bitcast.95) | data formatting | bytes 3309568 | tf_op jit(solution)/shard_map/reshape | solution.py:175
  65.2 2.1 %fusion.69 = f32[101,32,64]{2,1,0:T(8,128)S(1)} fusion(bf16[101,32,128]{2,1,0:T(8,128)(2,1)} %copy.14, bf16[101,128,64]{1,2,0:T(8,128)(2,1)S(1)} %copy.15), kind=kOutput, calls=%fused_computation.126 | convolution fusion | flops 52953088 | bytes 3309568 | tf_op jit(solution)/shard_map/fnk,fkj->fnj/dot_general | solution.py:185
  67.4 2.1 %copy.19 = f32[101,2,1,16,64]{0,4,1,3,2:T(8,128)} copy(f32[101,2,1,16,64]{4,3,1,0,2:T(8,128)S(1)} %bitcast.97) | data formatting | bytes 1654784 | tf_op jit(solution)/shard_map/stack;reshape | solution.py:187
  69.4 2.1 %fusion.70 = f32[101,32,64]{2,1,0:T(8,128)S(1)} fusion(bf16[101,32,128]{2,1,0:T(8,128)(2,1)} %copy.17, bf16[101,128,64]{1,2,0:T(8,128)(2,1)S(1)} %copy.15), kind=kOutput, calls=%fused_computation.127 | convolution fusion | flops 52953088 | bytes 3309568 | tf_op jit(solution)/shard_map/fnk,fkj->fnj/dot_general | solution.py:185
  71.5 2.1 %copy.20 = f32[101,2,1,16,64]{0,4,1,3,2:T(8,128)} copy(f32[101,2,1,16,64]{4,3,1,0,2:T(8,128)S(1)} %bitcast.96) | data formatting | bytes 1654784 | tf_op jit(solution)/shard_map/stack;reshape | solution.py:187
  73.6 2.3 %fusion.4 = f32[2,64,16,128]{3,1,2,0:T(8,128)S(1)} fusion(f32[101,2,1,16,64]{0,4,1,3,2:T(8,128)} %copy.20, f32[101,2,1,16,64]{0,4,1,3,2:T(8,128)S(1)} %copy-done, f32[1,101,128]{2,1,0:T(8,128)S(1)} %get-tuple-element.23, f32[1,101,128]{2,1,0:T(8,128)S(1)} %get-tuple-element.22), kind=kOutput, calls=%fused_computation.5 | convolution fusion | flops 318158080 | bytes 2806784 | tf_op jit(solution)/shard_map/fcrij,cfl->rjil/dot_general | solution.py:188
  75.9 1.6 %copy.21 = f32[2,64,16,128]{3,2,1,0:T(8,128)} copy(f32[2,64,16,128]{3,1,2,0:T(8,128)S(1)} %fusion.4) | data formatting | bytes 2097152 | tf_op jit(solution)/shard_map/fcrij,cfl->rjil/transpose | solution.py:188
  (76 shorter events, 20.6 us)
Async XLA Ops:
  1.3 3.3 %copy-start.1 = (f32[1,400,512]{2,1,0:T(8,128)S(1)}, f32[1,400,512]{2,1,0:T(8,128)}, u32[]{:S(2)}) copy-start(f32[1,400,512]{2,1,0:T(8,128)} %param.3) | copy-start | bytes 2457604
  4.7 0.9 %copy-start.2 = (s32[512]{0:T(512)S(1)}, s32[512]{0:T(512)}, u32[]{:S(2)}) copy-start(s32[512]{0:T(512)} %param.5) | copy-start | bytes 6148
  4.7 1.4 %copy-start.3 = (s32[512]{0:T(512)S(1)}, s32[512]{0:T(512)}, u32[]{:S(2)}) copy-start(s32[512]{0:T(512)} %param.4) | copy-start | bytes 6148
  7.0 11.1 %collective-permute-start = (bf16[2,2,64,101]{3,2,1,0:T(8,128)(2,1)S(1)}, bf16[2,2,64,101]{3,2,1,0:T(8,128)(2,1)S(1)}, u32[]{:S(2)}, u32[]{:S(2)}) collective-permute-start(bf16[2,2,64,101]{3,2,1,0:T(8,128)(2,1)S(1)} %get-tuple-element.19), channel_id=1, source_target_pairs={{28,0},{0,4},{4,8},{8,12},{12,16},{16,20},{20,24},{24,28},{29,1},{... | collective-permute-start | bytes 155144 | tf_op jit(solution)/shard_map/ppermute | solution.py:19
  10.0 9.4 %collective-permute-start.1 = (bf16[2,2,64,101]{3,2,1,0:T(8,128)(2,1)S(1)}, bf16[2,2,64,101]{3,2,1,0:T(8,128)(2,1)S(1)}, u32[]{:S(2)}, u32[]{:S(2)}) collective-permute-start(bf16[2,2,64,101]{3,2,1,0:T(8,128)(2,1)S(1)} %get-tuple-element.18), channel_id=1, source_target_pairs={{24,0},{28,4},{0,8},{4,12},{8,16},{12,20},{16,24},{20,28},{25,1},{... | collective-permute-start | bytes 155144 | tf_op jit(solution)/shard_map/ppermute | solution.py:19
  11.6 9.7 %collective-permute-start.2 = (bf16[2,2,64,101]{3,2,1,0:T(8,128)(2,1)S(1)}, bf16[2,2,64,101]{3,2,1,0:T(8,128)(2,1)S(1)}, u32[]{:S(2)}, u32[]{:S(2)}) collective-permute-start(bf16[2,2,64,101]{3,2,1,0:T(8,128)(2,1)S(1)} %get-tuple-element.17), channel_id=1, source_target_pairs={{20,0},{24,4},{28,8},{0,12},{4,16},{8,20},{12,24},{16,28},{21,1},{... | collective-permute-start | bytes 155144 | tf_op jit(solution)/shard_map/ppermute | solution.py:19
  14.1 7.8 %collective-permute-start.3 = (bf16[2,2,64,101]{3,2,1,0:T(8,128)(2,1)S(1)}, bf16[2,2,64,101]{3,2,1,0:T(8,128)(2,1)S(1)}, u32[]{:S(2)}, u32[]{:S(2)}) collective-permute-start(bf16[2,2,64,101]{3,2,1,0:T(8,128)(2,1)S(1)} %get-tuple-element.16), channel_id=1, source_target_pairs={{16,0},{20,4},{24,8},{28,12},{0,16},{4,20},{8,24},{12,28},{17,1},{... | collective-permute-start | bytes 155144 | tf_op jit(solution)/shard_map/ppermute | solution.py:19
  15.4 7.4 %collective-permute-start.4 = (bf16[2,2,64,101]{3,2,1,0:T(8,128)(2,1)S(1)}, bf16[2,2,64,101]{3,2,1,0:T(8,128)(2,1)S(1)}, u32[]{:S(2)}, u32[]{:S(2)}) collective-permute-start(bf16[2,2,64,101]{3,2,1,0:T(8,128)(2,1)S(1)} %get-tuple-element.15), channel_id=1, source_target_pairs={{12,0},{16,4},{20,8},{24,12},{28,16},{0,20},{4,24},{8,28},{13,1},{... | collective-permute-start | bytes 155144 | tf_op jit(solution)/shard_map/ppermute | solution.py:19
  18.1 5.9 %collective-permute-start.5 = (bf16[2,2,64,101]{3,2,1,0:T(8,128)(2,1)S(1)}, bf16[2,2,64,101]{3,2,1,0:T(8,128)(2,1)S(1)}, u32[]{:S(2)}, u32[]{:S(2)}) collective-permute-start(bf16[2,2,64,101]{3,2,1,0:T(8,128)(2,1)S(1)} %get-tuple-element.14), channel_id=1, source_target_pairs={{8,0},{12,4},{16,8},{20,12},{24,16},{28,20},{0,24},{4,28},{9,1},{1... | collective-permute-start | bytes 155144 | tf_op jit(solution)/shard_map/ppermute | solution.py:19
  19.5 4.5 %collective-permute-start.6 = (bf16[2,2,64,101]{3,2,1,0:T(8,128)(2,1)S(1)}, bf16[2,2,64,101]{3,2,1,0:T(8,128)(2,1)S(1)}, u32[]{:S(2)}, u32[]{:S(2)}) collective-permute-start(bf16[2,2,64,101]{3,2,1,0:T(8,128)(2,1)S(1)} %get-tuple-element.13), channel_id=1, source_target_pairs={{4,0},{8,4},{12,8},{16,12},{20,16},{24,20},{28,24},{0,28},{5,1},{9... | collective-permute-start | bytes 155144 | tf_op jit(solution)/shard_map/ppermute | solution.py:19
  24.0 11.6 %collective-permute-start.8 = (bf16[1,8,2,2,64,101]{5,4,3,2,1,0:T(8,128)(2,1)S(1)}, bf16[1,8,2,2,64,101]{5,4,3,2,1,0:T(8,128)(2,1)S(1)}, u32[]{:S(2)}, u32[]{:S(2)}) collective-permute-start(bf16[1,8,2,2,64,101]{5,4,3,2,1,0:T(8,128)(2,1)S(1)} %bitcast.100), channel_id=1, source_target_pairs={{0,2},{1,3},{2,0},{3,1},{4,6},{5,7},{6,4},{7,5},{8,10},{9,11},{10,... | collective-permute-start | bytes 1241096 | tf_op jit(solution)/shard_map/ppermute | solution.py:158
  25.6 9.0 %collective-permute-start.7 = (bf16[1,8,2,2,16,101]{5,4,3,2,1,0:T(8,128)(2,1)S(1)}, bf16[1,8,2,2,16,101]{5,4,3,2,1,0:T(8,128)(2,1)S(1)}, u32[]{:S(2)}, u32[]{:S(2)}) collective-permute-start(bf16[1,8,2,2,16,101]{5,4,3,2,1,0:T(8,128)(2,1)S(1)} %get-tuple-element.12), channel_id=1, source_target_pairs={{28,0},{0,4},{4,8},{8,12},{12,16},{16,20},{20,24},{24,28},{29,1},{... | collective-permute-start | bytes 310280 | tf_op jit(solution)/shard_map/ppermute | solution.py:19
  28.0 6.8 %collective-permute-start.13 = (bf16[1,8,2,2,16,101]{5,4,3,2,1,0:T(8,128)(2,1)S(1)}, bf16[1,8,2,2,16,101]{5,4,3,2,1,0:T(8,128)(2,1)S(1)}, u32[]{:S(2)}, u32[]{:S(2)}) collective-permute-start(bf16[1,8,2,2,16,101]{5,4,3,2,1,0:T(8,128)(2,1)S(1)} %get-tuple-element.12), channel_id=1, source_target_pairs={{24,0},{28,4},{0,8},{4,12},{8,16},{12,20},{16,24},{20,28},{25,1},{... | collective-permute-start | bytes 310280 | tf_op jit(solution)/shard_map/ppermute | solution.py:19
  30.0 14.8 %collective-permute-start.10 = (bf16[1,8,2,2,16,101]{5,4,3,2,1,0:T(8,128)(2,1)S(1)}, bf16[1,8,2,2,16,101]{5,4,3,2,1,0:T(8,128)(2,1)S(1)}, u32[]{:S(2)}, u32[]{:S(2)}) collective-permute-start(bf16[1,8,2,2,16,101]{5,4,3,2,1,0:T(8,128)(2,1)S(1)} %get-tuple-element.11), channel_id=1, source_target_pairs={{0,5},{1,4},{2,7},{3,6},{4,9},{5,8},{6,11},{7,10},{8,13},{9,12},{1... | collective-permute-start | bytes 310280 | tf_op jit(solution)/shard_map/ppermute | solution.py:151
  30.0 20.4 %collective-permute-start.15 = (bf16[1,8,2,2,16,101]{5,4,3,2,1,0:T(8,128)(2,1)S(1)}, bf16[1,8,2,2,16,101]{5,4,3,2,1,0:T(8,128)(2,1)S(1)}, u32[]{:S(2)}, u32[]{:S(2)}) collective-permute-start(bf16[1,8,2,2,16,101]{5,4,3,2,1,0:T(8,128)(2,1)S(1)} %get-tuple-element.11), channel_id=1, source_target_pairs={{0,9},{1,8},{2,11},{3,10},{4,13},{5,12},{6,15},{7,14},{8,17},{9,16... | collective-permute-start | bytes 310280 | tf_op jit(solution)/shard_map/ppermute | solution.py:151
  35.7 9.1 %collective-permute-start.9 = (bf16[1,8,2,2,16,101]{5,4,3,2,1,0:T(8,128)(2,1)S(1)}, bf16[1,8,2,2,16,101]{5,4,3,2,1,0:T(8,128)(2,1)S(1)}, u32[]{:S(2)}, u32[]{:S(2)}) collective-permute-start(bf16[1,8,2,2,16,101]{5,4,3,2,1,0:T(8,128)(2,1)S(1)} %get-tuple-element.10), channel_id=1, source_target_pairs={{28,0},{0,4},{4,8},{8,12},{12,16},{16,20},{20,24},{24,28},{29,1},{... | collective-permute-start | bytes 310280 | tf_op jit(solution)/shard_map/ppermute | solution.py:19
  39.1 11.3 %collective-permute-start.14 = (bf16[1,8,2,2,16,101]{5,4,3,2,1,0:T(8,128)(2,1)S(1)}, bf16[1,8,2,2,16,101]{5,4,3,2,1,0:T(8,128)(2,1)S(1)}, u32[]{:S(2)}, u32[]{:S(2)}) collective-permute-start(bf16[1,8,2,2,16,101]{5,4,3,2,1,0:T(8,128)(2,1)S(1)} %get-tuple-element.10), channel_id=1, source_target_pairs={{24,0},{28,4},{0,8},{4,12},{8,16},{12,20},{16,24},{20,28},{25,1},{... | collective-permute-start | bytes 310280 | tf_op jit(solution)/shard_map/ppermute | solution.py:19
  41.9 8.5 %collective-permute-start.11 = (bf16[1,8,2,2,16,101]{5,4,3,2,1,0:T(8,128)(2,1)S(1)}, bf16[1,8,2,2,16,101]{5,4,3,2,1,0:T(8,128)(2,1)S(1)}, u32[]{:S(2)}, u32[]{:S(2)}) collective-permute-start(bf16[1,8,2,2,16,101]{5,4,3,2,1,0:T(8,128)(2,1)S(1)} %get-tuple-element.9), channel_id=1, source_target_pairs={{0,5},{1,4},{2,7},{3,6},{4,9},{5,8},{6,11},{7,10},{8,13},{9,12},{1... | collective-permute-start | bytes 310280 | tf_op jit(solution)/shard_map/ppermute | solution.py:151
  44.8 7.1 %collective-permute-start.16 = (bf16[1,8,2,2,16,101]{5,4,3,2,1,0:T(8,128)(2,1)S(1)}, bf16[1,8,2,2,16,101]{5,4,3,2,1,0:T(8,128)(2,1)S(1)}, u32[]{:S(2)}, u32[]{:S(2)}) collective-permute-start(bf16[1,8,2,2,16,101]{5,4,3,2,1,0:T(8,128)(2,1)S(1)} %get-tuple-element.9), channel_id=1, source_target_pairs={{0,9},{1,8},{2,11},{3,10},{4,13},{5,12},{6,15},{7,14},{8,17},{9,16... | collective-permute-start | bytes 310280 | tf_op jit(solution)/shard_map/ppermute | solution.py:151
  44.8 13.4 %collective-permute-start.12 = (bf16[2,8,2,2,64,101]{5,4,3,2,1,0:T(8,128)(2,1)}, bf16[2,8,2,2,64,101]{5,4,3,2,1,0:T(8,128)(2,1)}, u32[]{:S(2)}, u32[]{:S(2)}) collective-permute-start(bf16[2,8,2,2,64,101]{5,4,3,2,1,0:T(8,128)(2,1)} %pad_maximum_fusion), channel_id=1, source_target_pairs={{0,1},{1,0},{2,3},{3,2},{4,5},{5,4},{6,7},{7,6},{8,9},{9,8},{10,11... | collective-permute-start | bytes 2482184 | tf_op jit(solution)/shard_map/ppermute | solution.py:162
  71.5 2.1 %copy-start = (f32[101,2,1,16,64]{0,4,1,3,2:T(8,128)S(1)}, f32[101,2,1,16,64]{0,4,1,3,2:T(8,128)}, u32[]{:S(2)}) copy-start(f32[101,2,1,16,64]{0,4,1,3,2:T(8,128)} %copy.19) | copy-start | bytes 2482180

commit v16 on v13

--- a/solution.py
+++ b/solution.py
@@ -99,13 +99,13 @@
     centred = windows - window_mean
     normed = centred / jnp.sqrt(jnp.mean(centred * centred, axis=-2, keepdims=True) + 1e-05)
     table = forward_table()
-    real_part = jnp.einsum("wlk,lg->wkg", normed, table[:, :FB], precision=precision)
-    imag_part = jnp.einsum("wlk,lg->wkg", normed, table[:, FB:], precision=precision)
+    both_parts = jnp.einsum("wlk,lcg->wckg", normed, table.reshape(L, 2, FB), precision=precision)
+    real_part, imag_part = both_parts[:, 0], both_parts[:, 1]
     power = real_part * real_part + imag_part * imag_part
     smoothed = jnp.einsum("wkf,fg->wkg", power, smoothing_table(), precision=precision)
     mean_power = jnp.mean(power, axis=-1, keepdims=True)
     scale = live.astype(jnp.float32)[:, None] / jnp.sqrt(smoothed + 0.1 * mean_power + 1e-05)
-    return jnp.stack([real_part * scale, imag_part * scale], axis=1).astype(jnp.bfloat16)
+    return (both_parts * scale[:, None]).astype(jnp.bfloat16)
 
 
 def on_device_local(records, chan_order, live_mask):
@@ -185,7 +185,7 @@
         sums = jnp.einsum("fnk,fkj->fnj", both, own_spec, preferred_element_type=jnp.float32)
         sums = sums.reshape(FB, 2, slice_width, block_width)
         results.append(
-            jnp.einsum("fcij,cfl->jil", sums, inverse, precision=lax.Precision.DEFAULT)
+            jnp.einsum("fcij,cfl->jil", sums, inverse, precision=lax.Precision.HIGH)
         )
     return jnp.stack(results)
 

time: 69.8 us -> 69.7 us (level)
  matrix products: 6.76 us -> 7.69 us
  other arithmetic: 7.13 us -> 6.39 us
    reduce_sum x1, other arithmetic: 1.33 us -> 0.11 us  [whiten_planes(): jnp.mean(centred * centred, axis=-2, keepdims=True) + 1e-05]
    dot_general x4 -> x3, matrix products: 3.8 us -> 4.76 us  [the longest x2 4.19 us: on_device_local(): jnp.einsum('fcij,cfl->jil', sums, inverse, precision=lax.Precision.HIGH)]
where the time goes in v16:
time: 69.7 us; the launch traced here: 69.4 us
  starting transfers between devices  28.6 us (41%)
  waiting for transfers between devices  14.2 us (20%)
  local copies, waits for them, and re-layouts  12.2 us (18%)
  matrix products  7.69 us (11%)
  other arithmetic  6.39 us (9%)
    ppermute x11, starting transfers between devices, shifted(): return lax.ppermute(block, axis, route)  24.4 us
    ppermute x11, waiting for transfers between devices, shifted(): return lax.ppermute(block, axis, route)  7.95 us
    ppermute x4, waiting for transfers between devices, send_from_neighbour(): sent.append(lax.ppermute(piece, ('chan', 'tm'), route))  5.47 us
    dot_general x2, matrix products, on_device_local(): jnp.einsum('fcij,cfl->jil', sums, inverse, precision=lax.Precision.HIGH)  4.19 us
    reshape x1, local copies, waits for them, and re-layouts, on_device_local(): jnp.transpose(gathered, (5, 3, 0, 1, 2, 4))  3.79 us
    reshape x2, local copies, waits for them, and re-layouts, on_device_local(): jnp.transpose(both, (6, 0, 5, 4, 1, 2, 3))  3.67 us
    dot_general x2, matrix products, on_device_local(): jnp.einsum('fnk,fkj->fnj', both, own_spec, preferred_element_type=jnp.flo...  1.95 us
    transpose x1, other arithmetic, on_device_local(): jnp.transpose(gathered, (5, 3, 0, 1, 2, 4))  1.71 us
  transfers between devices with their start and end apart: 17, of which 10 were waited for; matrix products, arithmetic and copies ran while one was open for 10% of the time, Pallas kernels for 0%

profile of v16, /device:TPU:0, one launch (start us, length us, event | category | flops | bytes accessed | tf_op | source)
XLA Modules:
  0.0 69.4 jit_solution(1599938936054011702)
XLA Ops:
  4.1 3.1 %collective-permute-start = (bf16[2,2,64,101]{3,2,1,0:T(8,128)(2,1)S(1)}, bf16[2,2,64,101]{3,2,1,0:T(8,128)(2,1)S(1)}, u32[]{:S(2)}, u32[]{:S(2)}) collective-permute-start(bf16[2,2,64,101]{3,2,1,0:T(8,128)(2,1)S(1)} %get-tuple-element.19), channel_id=1, source_target_pairs={{28,0},{0,4},{4,8},{8,12},{12,16},{16,20},{20,24},{24,28},{29,1},{... | collective-permute-start | bytes 155144 | tf_op jit(solution)/shard_map/ppermute | solution.py:19
  7.1 1.6 %collective-permute-start.1 = (bf16[2,2,64,101]{3,2,1,0:T(8,128)(2,1)S(1)}, bf16[2,2,64,101]{3,2,1,0:T(8,128)(2,1)S(1)}, u32[]{:S(2)}, u32[]{:S(2)}) collective-permute-start(bf16[2,2,64,101]{3,2,1,0:T(8,128)(2,1)S(1)} %get-tuple-element.18), channel_id=1, source_target_pairs={{24,0},{28,4},{0,8},{4,12},{8,16},{12,20},{16,24},{20,28},{25,1},{... | collective-permute-start | bytes 155144 | tf_op jit(solution)/shard_map/ppermute | solution.py:19
  8.7 2.5 %collective-permute-start.2 = (bf16[2,2,64,101]{3,2,1,0:T(8,128)(2,1)S(1)}, bf16[2,2,64,101]{3,2,1,0:T(8,128)(2,1)S(1)}, u32[]{:S(2)}, u32[]{:S(2)}) collective-permute-start(bf16[2,2,64,101]{3,2,1,0:T(8,128)(2,1)S(1)} %get-tuple-element.17), channel_id=1, source_target_pairs={{20,0},{24,4},{28,8},{0,12},{4,16},{8,20},{12,24},{16,28},{21,1},{... | collective-permute-start | bytes 155144 | tf_op jit(solution)/shard_map/ppermute | solution.py:19
  11.2 1.2 %collective-permute-start.3 = (bf16[2,2,64,101]{3,2,1,0:T(8,128)(2,1)S(1)}, bf16[2,2,64,101]{3,2,1,0:T(8,128)(2,1)S(1)}, u32[]{:S(2)}, u32[]{:S(2)}) collective-permute-start(bf16[2,2,64,101]{3,2,1,0:T(8,128)(2,1)S(1)} %get-tuple-element.16), channel_id=1, source_target_pairs={{16,0},{20,4},{24,8},{28,12},{0,16},{4,20},{8,24},{12,28},{17,1},{... | collective-permute-start | bytes 155144 | tf_op jit(solution)/shard_map/ppermute | solution.py:19
  12.5 2.6 %collective-permute-start.4 = (bf16[2,2,64,101]{3,2,1,0:T(8,128)(2,1)S(1)}, bf16[2,2,64,101]{3,2,1,0:T(8,128)(2,1)S(1)}, u32[]{:S(2)}, u32[]{:S(2)}) collective-permute-start(bf16[2,2,64,101]{3,2,1,0:T(8,128)(2,1)S(1)} %get-tuple-element.15), channel_id=1, source_target_pairs={{12,0},{16,4},{20,8},{24,12},{28,16},{0,20},{4,24},{8,28},{13,1},{... | collective-permute-start | bytes 155144 | tf_op jit(solution)/shard_map/ppermute | solution.py:19
  15.2 1.4 %collective-permute-start.5 = (bf16[2,2,64,101]{3,2,1,0:T(8,128)(2,1)S(1)}, bf16[2,2,64,101]{3,2,1,0:T(8,128)(2,1)S(1)}, u32[]{:S(2)}, u32[]{:S(2)}) collective-permute-start(bf16[2,2,64,101]{3,2,1,0:T(8,128)(2,1)S(1)} %get-tuple-element.14), channel_id=1, source_target_pairs={{8,0},{12,4},{16,8},{20,12},{24,16},{28,20},{0,24},{4,28},{9,1},{1... | collective-permute-start | bytes 155144 | tf_op jit(solution)/shard_map/ppermute | solution.py:19
  16.6 1.5 %collective-permute-start.6 = (bf16[2,2,64,101]{3,2,1,0:T(8,128)(2,1)S(1)}, bf16[2,2,64,101]{3,2,1,0:T(8,128)(2,1)S(1)}, u32[]{:S(2)}, u32[]{:S(2)}) collective-permute-start(bf16[2,2,64,101]{3,2,1,0:T(8,128)(2,1)S(1)} %get-tuple-element.13), channel_id=1, source_target_pairs={{4,0},{8,4},{12,8},{16,12},{20,16},{24,20},{28,24},{0,28},{5,1},{9... | collective-permute-start | bytes 155144 | tf_op jit(solution)/shard_map/ppermute | solution.py:19
  21.1 1.6 %collective-permute-start.8 = (bf16[1,8,2,2,64,101]{5,4,3,2,1,0:T(8,128)(2,1)S(1)}, bf16[1,8,2,2,64,101]{5,4,3,2,1,0:T(8,128)(2,1)S(1)}, u32[]{:S(2)}, u32[]{:S(2)}) collective-permute-start(bf16[1,8,2,2,64,101]{5,4,3,2,1,0:T(8,128)(2,1)S(1)} %bitcast.108), channel_id=1, source_target_pairs={{0,2},{1,3},{2,0},{3,1},{4,6},{5,7},{6,4},{7,5},{8,10},{9,11},{10,... | collective-permute-start | bytes 1241096 | tf_op jit(solution)/shard_map/ppermute | solution.py:158
  22.7 2.2 %collective-permute-start.7 = (bf16[1,8,2,2,16,101]{5,4,3,2,1,0:T(8,128)(2,1)S(1)}, bf16[1,8,2,2,16,101]{5,4,3,2,1,0:T(8,128)(2,1)S(1)}, u32[]{:S(2)}, u32[]{:S(2)}) collective-permute-start(bf16[1,8,2,2,16,101]{5,4,3,2,1,0:T(8,128)(2,1)S(1)} %get-tuple-element.12), channel_id=1, source_target_pairs={{28,0},{0,4},{4,8},{8,12},{12,16},{16,20},{20,24},{24,28},{29,1},{... | collective-permute-start | bytes 310280 | tf_op jit(solution)/shard_map/ppermute | solution.py:19
  25.1 2.0 %collective-permute-start.13 = (bf16[1,8,2,2,16,101]{5,4,3,2,1,0:T(8,128)(2,1)S(1)}, bf16[1,8,2,2,16,101]{5,4,3,2,1,0:T(8,128)(2,1)S(1)}, u32[]{:S(2)}, u32[]{:S(2)}) collective-permute-start(bf16[1,8,2,2,16,101]{5,4,3,2,1,0:T(8,128)(2,1)S(1)} %get-tuple-element.12), channel_id=1, source_target_pairs={{24,0},{28,4},{0,8},{4,12},{8,16},{12,20},{16,24},{20,28},{25,1},{... | collective-permute-start | bytes 310280 | tf_op jit(solution)/shard_map/ppermute | solution.py:19
  27.1 1.4 %collective-permute-start.15 = (bf16[1,8,2,2,16,101]{5,4,3,2,1,0:T(8,128)(2,1)S(1)}, bf16[1,8,2,2,16,101]{5,4,3,2,1,0:T(8,128)(2,1)S(1)}, u32[]{:S(2)}, u32[]{:S(2)}) collective-permute-start(bf16[1,8,2,2,16,101]{5,4,3,2,1,0:T(8,128)(2,1)S(1)} %get-tuple-element.11), channel_id=1, source_target_pairs={{0,9},{1,8},{2,11},{3,10},{4,13},{5,12},{6,15},{7,14},{8,17},{9,16... | collective-permute-start | bytes 310280 | tf_op jit(solution)/shard_map/ppermute | solution.py:151
  28.6 3.1 %collective-permute-done.7 = bf16[1,8,2,2,16,101]{5,4,3,2,1,0:T(8,128)(2,1)S(1)} collective-permute-done((bf16[1,8,2,2,16,101]{5,4,3,2,1,0:T(8,128)(2,1)S(1)}, bf16[1,8,2,2,16,101]{5,4,3,2,1,0:T(8,128)(2,1)S(1)}, u32[]{:S(2)}, u32[]{:S(2)}) %collective-permute-start.7) | collective-permute-done | bytes 103456 | tf_op jit(solution)/shard_map/ppermute | solution.py:19
  32.8 3.5 %collective-permute-start.9 = (bf16[1,8,2,2,16,101]{5,4,3,2,1,0:T(8,128)(2,1)S(1)}, bf16[1,8,2,2,16,101]{5,4,3,2,1,0:T(8,128)(2,1)S(1)}, u32[]{:S(2)}, u32[]{:S(2)}) collective-permute-start(bf16[1,8,2,2,16,101]{5,4,3,2,1,0:T(8,128)(2,1)S(1)} %get-tuple-element.10), channel_id=1, source_target_pairs={{28,0},{0,4},{4,8},{8,12},{12,16},{16,20},{20,24},{24,28},{29,1},{... | collective-permute-start | bytes 310280 | tf_op jit(solution)/shard_map/ppermute | solution.py:19
  36.2 2.8 %collective-permute-start.14 = (bf16[1,8,2,2,16,101]{5,4,3,2,1,0:T(8,128)(2,1)S(1)}, bf16[1,8,2,2,16,101]{5,4,3,2,1,0:T(8,128)(2,1)S(1)}, u32[]{:S(2)}, u32[]{:S(2)}) collective-permute-start(bf16[1,8,2,2,16,101]{5,4,3,2,1,0:T(8,128)(2,1)S(1)} %get-tuple-element.10), channel_id=1, source_target_pairs={{24,0},{28,4},{0,8},{4,12},{8,16},{12,20},{16,24},{20,28},{25,1},{... | collective-permute-start | bytes 310280 | tf_op jit(solution)/shard_map/ppermute | solution.py:19
  40.2 1.6 %collective-permute-done.9 = bf16[1,8,2,2,16,101]{5,4,3,2,1,0:T(8,128)(2,1)S(1)} collective-permute-done((bf16[1,8,2,2,16,101]{5,4,3,2,1,0:T(8,128)(2,1)S(1)}, bf16[1,8,2,2,16,101]{5,4,3,2,1,0:T(8,128)(2,1)S(1)}, u32[]{:S(2)}, u32[]{:S(2)}) %collective-permute-start.9) | collective-permute-done | bytes 103456 | tf_op jit(solution)/shard_map/ppermute | solution.py:19
  43.1 4.4 %collective-permute-done.11 = bf16[1,8,2,2,16,101]{5,4,3,2,1,0:T(8,128)(2,1)S(1)} collective-permute-done((bf16[1,8,2,2,16,101]{5,4,3,2,1,0:T(8,128)(2,1)S(1)}, bf16[1,8,2,2,16,101]{5,4,3,2,1,0:T(8,128)(2,1)S(1)}, u32[]{:S(2)}, u32[]{:S(2)}) %collective-permute-start.11) | collective-permute-done | bytes 103456 | tf_op jit(solution)/shard_map/ppermute | solution.py:151
  49.7 1.5 %copy.27 = bf16[101,32,128]{2,1,0:T(8,128)(2,1)S(1)} copy(bf16[101,32,128]{0,1,2:T(8,128)(2,1)S(1)} %bitcast.106) | data formatting | bytes 1654784 | tf_op jit(solution)/shard_map/reshape | solution.py:184
  52.1 2.2 %copy.31 = bf16[101,32,128]{2,1,0:T(8,128)(2,1)} copy(bf16[101,32,128]{0,1,2:T(8,128)(2,1)S(1)} %bitcast.107) | data formatting | bytes 1654784 | tf_op jit(solution)/shard_map/reshape | solution.py:184
  54.3 1.7 %maximum_bitcast_fusion = bf16[101,2,4,8,2,64]{0,5,1,4,3,2:T(8,128)(2,1)S(1)} fusion(bf16[2,8,2,2,64,101]{5,4,3,2,1,0:T(8,128)(2,1)} %collective-permute-done.12, bf16[1,8,2,2,64,101]{5,4,3,2,1,0:T(8,128)(2,1)S(1)} %collective-permute-done.8, bf16[1,8,2,2,64,101]{5,4,3,2,1,0:T(8,128)(2,1)S(1)} %bitcast.110), kind=kLoop, calls=%fused_computation | loop fusion | flops 1654784 | bytes 3309568 | tf_op jit(solution)/shard_map/transpose | solution.py:175
  56.0 1.6 %copy.26 = bf16[101,2,4,8,2,64]{0,5,4,3,2,1:T(8,128)(2,1)} copy(bf16[101,2,4,8,2,64]{0,5,1,4,3,2:T(8,128)(2,1)S(1)} %maximum_bitcast_fusion) | data formatting | bytes 3309568 | tf_op jit(solution)/shard_map/transpose | solution.py:175
  57.6 3.8 %copy.28 = bf16[101,128,64]{1,2,0:T(8,128)(2,1)S(1)} copy(bf16[101,128,64]{0,2,1:T(8,128)(2,1)} %bitcast.103) | data formatting | bytes 3309568 | tf_op jit(solution)/shard_map/reshape | solution.py:175
  63.5 2.1 %fusion.4 = f32[1,64,16,128]{3,1,2,0:T(8,128)S(1)} fusion(f32[101,2,16,64]{3,2,1,0:T(8,128)S(1)} %bitcast.105, f32[1,101,128]{2,1,0:T(8,128)S(1)} %get-tuple-element.21, f32[1,101,128]{2,1,0:T(8,128)S(1)} %get-tuple-element.20), kind=kOutput, calls=%fused_computation.7 | convolution fusion | flops 158885120 | bytes 1455104 | tf_op jit(solution)/shard_map/fcij,cfl->jil/dot_general | solution.py:188
  65.6 2.1 %fusion.7 = f32[1,64,16,128]{3,1,2,0:T(8,128)S(1)} fusion(f32[101,2,16,64]{3,2,1,0:T(8,128)S(1)} %bitcast.104, f32[1,101,128]{2,1,0:T(8,128)S(1)} %get-tuple-element.21, f32[1,101,128]{2,1,0:T(8,128)S(1)} %get-tuple-element.20), kind=kOutput, calls=%fused_computation.8 | convolution fusion | flops 158885120 | bytes 1455104 | tf_op jit(solution)/shard_map/fcij,cfl->jil/dot_general | solution.py:188
  67.8 1.6 %copy.34 = f32[2,64,16,128]{3,2,1,0:T(8,128)} copy(f32[2,64,16,128]{3,1,2,0:T(8,128)S(1)} %pad_maximum_fusion.1) | data formatting | bytes 2097152 | tf_op jit(solution)/shard_map/stack | solution.py:190
  (79 shorter events, 16.0 us)
Async XLA Ops:
  0.0 1.7 %copy-start.1 = (f32[1,400,512]{2,1,0:T(8,128)S(1)}, f32[1,400,512]{2,1,0:T(8,128)}, u32[]{:S(2)}) copy-start(f32[1,400,512]{2,1,0:T(8,128)} %param.3) | copy-start | bytes 2457604
  1.8 0.7 %copy-start.3 = (s32[512]{0:T(512)S(1)}, s32[512]{0:T(512)}, u32[]{:S(2)}) copy-start(s32[512]{0:T(512)} %param.5) | copy-start | bytes 6148
  2.4 0.7 copy-start.2
  4.1 11.1 %collective-permute-start = (bf16[2,2,64,101]{3,2,1,0:T(8,128)(2,1)S(1)}, bf16[2,2,64,101]{3,2,1,0:T(8,128)(2,1)S(1)}, u32[]{:S(2)}, u32[]{:S(2)}) collective-permute-start(bf16[2,2,64,101]{3,2,1,0:T(8,128)(2,1)S(1)} %get-tuple-element.19), channel_id=1, source_target_pairs={{28,0},{0,4},{4,8},{8,12},{12,16},{16,20},{20,24},{24,28},{29,1},{... | collective-permute-start | bytes 155144 | tf_op jit(solution)/shard_map/ppermute | solution.py:19
  7.1 9.4 %collective-permute-start.1 = (bf16[2,2,64,101]{3,2,1,0:T(8,128)(2,1)S(1)}, bf16[2,2,64,101]{3,2,1,0:T(8,128)(2,1)S(1)}, u32[]{:S(2)}, u32[]{:S(2)}) collective-permute-start(bf16[2,2,64,101]{3,2,1,0:T(8,128)(2,1)S(1)} %get-tuple-element.18), channel_id=1, source_target_pairs={{24,0},{28,4},{0,8},{4,12},{8,16},{12,20},{16,24},{20,28},{25,1},{... | collective-permute-start | bytes 155144 | tf_op jit(solution)/shard_map/ppermute | solution.py:19
  8.7 9.7 %collective-permute-start.2 = (bf16[2,2,64,101]{3,2,1,0:T(8,128)(2,1)S(1)}, bf16[2,2,64,101]{3,2,1,0:T(8,128)(2,1)S(1)}, u32[]{:S(2)}, u32[]{:S(2)}) collective-permute-start(bf16[2,2,64,101]{3,2,1,0:T(8,128)(2,1)S(1)} %get-tuple-element.17), channel_id=1, source_target_pairs={{20,0},{24,4},{28,8},{0,12},{4,16},{8,20},{12,24},{16,28},{21,1},{... | collective-permute-start | bytes 155144 | tf_op jit(solution)/shard_map/ppermute | solution.py:19
  11.2 7.8 %collective-permute-start.3 = (bf16[2,2,64,101]{3,2,1,0:T(8,128)(2,1)S(1)}, bf16[2,2,64,101]{3,2,1,0:T(8,128)(2,1)S(1)}, u32[]{:S(2)}, u32[]{:S(2)}) collective-permute-start(bf16[2,2,64,101]{3,2,1,0:T(8,128)(2,1)S(1)} %get-tuple-element.16), channel_id=1, source_target_pairs={{16,0},{20,4},{24,8},{28,12},{0,16},{4,20},{8,24},{12,28},{17,1},{... | collective-permute-start | bytes 155144 | tf_op jit(solution)/shard_map/ppermute | solution.py:19
  12.5 7.4 %collective-permute-start.4 = (bf16[2,2,64,101]{3,2,1,0:T(8,128)(2,1)S(1)}, bf16[2,2,64,101]{3,2,1,0:T(8,128)(2,1)S(1)}, u32[]{:S(2)}, u32[]{:S(2)}) collective-permute-start(bf16[2,2,64,101]{3,2,1,0:T(8,128)(2,1)S(1)} %get-tuple-element.15), channel_id=1, source_target_pairs={{12,0},{16,4},{20,8},{24,12},{28,16},{0,20},{4,24},{8,28},{13,1},{... | collective-permute-start | bytes 155144 | tf_op jit(solution)/shard_map/ppermute | solution.py:19
  15.2 5.9 %collective-permute-start.5 = (bf16[2,2,64,101]{3,2,1,0:T(8,128)(2,1)S(1)}, bf16[2,2,64,101]{3,2,1,0:T(8,128)(2,1)S(1)}, u32[]{:S(2)}, u32[]{:S(2)}) collective-permute-start(bf16[2,2,64,101]{3,2,1,0:T(8,128)(2,1)S(1)} %get-tuple-element.14), channel_id=1, source_target_pairs={{8,0},{12,4},{16,8},{20,12},{24,16},{28,20},{0,24},{4,28},{9,1},{1... | collective-permute-start | bytes 155144 | tf_op jit(solution)/shard_map/ppermute | solution.py:19
  16.6 4.5 %collective-permute-start.6 = (bf16[2,2,64,101]{3,2,1,0:T(8,128)(2,1)S(1)}, bf16[2,2,64,101]{3,2,1,0:T(8,128)(2,1)S(1)}, u32[]{:S(2)}, u32[]{:S(2)}) collective-permute-start(bf16[2,2,64,101]{3,2,1,0:T(8,128)(2,1)S(1)} %get-tuple-element.13), channel_id=1, source_target_pairs={{4,0},{8,4},{12,8},{16,12},{20,16},{24,20},{28,24},{0,28},{5,1},{9... | collective-permute-start | bytes 155144 | tf_op jit(solution)/shard_map/ppermute | solution.py:19
  21.1 11.6 %collective-permute-start.8 = (bf16[1,8,2,2,64,101]{5,4,3,2,1,0:T(8,128)(2,1)S(1)}, bf16[1,8,2,2,64,101]{5,4,3,2,1,0:T(8,128)(2,1)S(1)}, u32[]{:S(2)}, u32[]{:S(2)}) collective-permute-start(bf16[1,8,2,2,64,101]{5,4,3,2,1,0:T(8,128)(2,1)S(1)} %bitcast.108), channel_id=1, source_target_pairs={{0,2},{1,3},{2,0},{3,1},{4,6},{5,7},{6,4},{7,5},{8,10},{9,11},{10,... | collective-permute-start | bytes 1241096 | tf_op jit(solution)/shard_map/ppermute | solution.py:158
  22.7 9.0 %collective-permute-start.7 = (bf16[1,8,2,2,16,101]{5,4,3,2,1,0:T(8,128)(2,1)S(1)}, bf16[1,8,2,2,16,101]{5,4,3,2,1,0:T(8,128)(2,1)S(1)}, u32[]{:S(2)}, u32[]{:S(2)}) collective-permute-start(bf16[1,8,2,2,16,101]{5,4,3,2,1,0:T(8,128)(2,1)S(1)} %get-tuple-element.12), channel_id=1, source_target_pairs={{28,0},{0,4},{4,8},{8,12},{12,16},{16,20},{20,24},{24,28},{29,1},{... | collective-permute-start | bytes 310280 | tf_op jit(solution)/shard_map/ppermute | solution.py:19
  25.1 6.8 %collective-permute-start.13 = (bf16[1,8,2,2,16,101]{5,4,3,2,1,0:T(8,128)(2,1)S(1)}, bf16[1,8,2,2,16,101]{5,4,3,2,1,0:T(8,128)(2,1)S(1)}, u32[]{:S(2)}, u32[]{:S(2)}) collective-permute-start(bf16[1,8,2,2,16,101]{5,4,3,2,1,0:T(8,128)(2,1)S(1)} %get-tuple-element.12), channel_id=1, source_target_pairs={{24,0},{28,4},{0,8},{4,12},{8,16},{12,20},{16,24},{20,28},{25,1},{... | collective-permute-start | bytes 310280 | tf_op jit(solution)/shard_map/ppermute | solution.py:19
  27.1 14.8 %collective-permute-start.10 = (bf16[1,8,2,2,16,101]{5,4,3,2,1,0:T(8,128)(2,1)S(1)}, bf16[1,8,2,2,16,101]{5,4,3,2,1,0:T(8,128)(2,1)S(1)}, u32[]{:S(2)}, u32[]{:S(2)}) collective-permute-start(bf16[1,8,2,2,16,101]{5,4,3,2,1,0:T(8,128)(2,1)S(1)} %get-tuple-element.11), channel_id=1, source_target_pairs={{0,5},{1,4},{2,7},{3,6},{4,9},{5,8},{6,11},{7,10},{8,13},{9,12},{1... | collective-permute-start | bytes 310280 | tf_op jit(solution)/shard_map/ppermute | solution.py:151
  27.1 20.7 %collective-permute-start.15 = (bf16[1,8,2,2,16,101]{5,4,3,2,1,0:T(8,128)(2,1)S(1)}, bf16[1,8,2,2,16,101]{5,4,3,2,1,0:T(8,128)(2,1)S(1)}, u32[]{:S(2)}, u32[]{:S(2)}) collective-permute-start(bf16[1,8,2,2,16,101]{5,4,3,2,1,0:T(8,128)(2,1)S(1)} %get-tuple-element.11), channel_id=1, source_target_pairs={{0,9},{1,8},{2,11},{3,10},{4,13},{5,12},{6,15},{7,14},{8,17},{9,16... | collective-permute-start | bytes 310280 | tf_op jit(solution)/shard_map/ppermute | solution.py:151
  32.8 9.1 %collective-permute-start.9 = (bf16[1,8,2,2,16,101]{5,4,3,2,1,0:T(8,128)(2,1)S(1)}, bf16[1,8,2,2,16,101]{5,4,3,2,1,0:T(8,128)(2,1)S(1)}, u32[]{:S(2)}, u32[]{:S(2)}) collective-permute-start(bf16[1,8,2,2,16,101]{5,4,3,2,1,0:T(8,128)(2,1)S(1)} %get-tuple-element.10), channel_id=1, source_target_pairs={{28,0},{0,4},{4,8},{8,12},{12,16},{16,20},{20,24},{24,28},{29,1},{... | collective-permute-start | bytes 310280 | tf_op jit(solution)/shard_map/ppermute | solution.py:19
  36.2 11.6 %collective-permute-start.14 = (bf16[1,8,2,2,16,101]{5,4,3,2,1,0:T(8,128)(2,1)S(1)}, bf16[1,8,2,2,16,101]{5,4,3,2,1,0:T(8,128)(2,1)S(1)}, u32[]{:S(2)}, u32[]{:S(2)}) collective-permute-start(bf16[1,8,2,2,16,101]{5,4,3,2,1,0:T(8,128)(2,1)S(1)} %get-tuple-element.10), channel_id=1, source_target_pairs={{24,0},{28,4},{0,8},{4,12},{8,16},{12,20},{16,24},{20,28},{25,1},{... | collective-permute-start | bytes 310280 | tf_op jit(solution)/shard_map/ppermute | solution.py:19
  39.0 8.5 %collective-permute-start.11 = (bf16[1,8,2,2,16,101]{5,4,3,2,1,0:T(8,128)(2,1)S(1)}, bf16[1,8,2,2,16,101]{5,4,3,2,1,0:T(8,128)(2,1)S(1)}, u32[]{:S(2)}, u32[]{:S(2)}) collective-permute-start(bf16[1,8,2,2,16,101]{5,4,3,2,1,0:T(8,128)(2,1)S(1)} %get-tuple-element.9), channel_id=1, source_target_pairs={{0,5},{1,4},{2,7},{3,6},{4,9},{5,8},{6,11},{7,10},{8,13},{9,12},{1... | collective-permute-start | bytes 310280 | tf_op jit(solution)/shard_map/ppermute | solution.py:151
  41.9 7.1 %collective-permute-start.16 = (bf16[1,8,2,2,16,101]{5,4,3,2,1,0:T(8,128)(2,1)S(1)}, bf16[1,8,2,2,16,101]{5,4,3,2,1,0:T(8,128)(2,1)S(1)}, u32[]{:S(2)}, u32[]{:S(2)}) collective-permute-start(bf16[1,8,2,2,16,101]{5,4,3,2,1,0:T(8,128)(2,1)S(1)} %get-tuple-element.9), channel_id=1, source_target_pairs={{0,9},{1,8},{2,11},{3,10},{4,13},{5,12},{6,15},{7,14},{8,17},{9,16... | collective-permute-start | bytes 310280 | tf_op jit(solution)/shard_map/ppermute | solution.py:151
  41.9 12.4 %collective-permute-start.12 = (bf16[2,8,2,2,64,101]{5,4,3,2,1,0:T(8,128)(2,1)}, bf16[2,8,2,2,64,101]{5,4,3,2,1,0:T(8,128)(2,1)}, u32[]{:S(2)}, u32[]{:S(2)}) collective-permute-start(bf16[2,8,2,2,64,101]{5,4,3,2,1,0:T(8,128)(2,1)} %pad_maximum_fusion), channel_id=1, source_target_pairs={{0,1},{1,0},{2,3},{3,2},{4,5},{5,4},{6,7},{7,6},{8,9},{9,8},{10,11... | collective-permute-start | bytes 2482184 | tf_op jit(solution)/shard_map/ppermute | solution.py:162
  61.4 1.1 %copy-start = (bf16[101,32,128]{2,1,0:T(8,128)(2,1)S(1)}, bf16[101,32,128]{2,1,0:T(8,128)(2,1)}, u32[]{:S(2)}) copy-start(bf16[101,32,128]{2,1,0:T(8,128)(2,1)} %copy.31) | copy-start | bytes 2482180
